TPU v7x, 32 devices: a whole 2x2x4 slice. The times are simulated.
32 devices in a mesh: stream: 4 (over y, core), cross: 2 (over x), gore: 4 (over z).
Axes of the slice: x: 2, y: 2, z: 4, core: 2. Of those that a mesh axis runs over, the one named last changes fastest.
Arguments:
- density: float32 [16, 8, 512], P('stream', 'cross', 'gore'), may hold values from 1 to 2
- momentum_energy: float32 [4, 16, 8, 512], P(None, 'stream', 'cross', 'gore'), may hold values from -6 to 6
- viscosity: float32 [16, 8, 512], P('stream', 'cross', 'gore'), may hold values from 0.02 to 0.15
- records: float32 [8, 2048, 128], P(None, ('stream', 'cross', 'gore')), may hold values from -6 to 6
- cell_ids: int32 [2048, 128], P(('stream', 'cross', 'gore')), may hold values from 0 to 2047
- routes: int32 [2048, 1], P(('stream', 'cross', 'gore')), may hold values from 0 to 7; in each aligned block of 64 rows (0 to 63, 64 to 127, ...) at most 16 rows name the same one
- lengths: int32 [2048], P(('stream', 'cross', 'gore')), may hold values from 1 to 128, 163840 in all
Outputs:
- new_state: float32 [5, 16, 8, 512], P(None, 'stream', 'cross', 'gore')
- face_loads: float32 [3, 2048, 128], P(None, ('stream', 'cross', 'gore'))
Inputs may be any that keep to these rules, and one draw needn't show every extreme that they name: `routes`: among the 64 tiles of one device no fluid block is named more than 16 times, and some block exactly 16 times. `lengths`: some tile is full.
All inputs are finite; a program needn't handle non-finite values. No bound on the sum of `lengths` on one device may be relied on, other than what follows from the above.
Results may differ from a plain program's by a relative error of at most 0.0003.
Values sent between devices are 32-bit elements; how exact they have to be, the bound alone decides.
No kernel may reach another device: no remote copies, remote signals or barrier semaphores. Data moves between devices by JAX's collectives and lax.ppermute only.
A program may use at most 64 MiB of HBM per device.

v0:
```python
import math

import jax
import jax.numpy as jnp
from jax import lax
from jax.sharding import PartitionSpec as P


def with_halo(block, sides, width):
    for axis, dim in sides:
        count = lax.axis_size(axis)
        forward = [(i, i + 1) for i in range(count - 1)]
        backward = [(target, source) for source, target in forward]
        low = lax.ppermute(
            lax.slice_in_dim(block, block.shape[dim] - width, None, axis=dim), axis, forward
        )
        high = lax.ppermute(lax.slice_in_dim(block, 0, width, axis=dim), axis, backward)
        block = jnp.concatenate([low, block, high], axis=dim)
    return block


def harmonic(first_visc, second_visc):
    summed = first_visc + second_visc
    denominator = jnp.where(summed > 0, summed, 1.0)
    return 2.0 * first_visc * second_visc / denominator


def shifted(values, leading, spatial, offset):
    value_portions = [slice(None)] * leading
    for position in range(3):
        extent = values.shape[leading + position]
        if position == spatial:
            value_portions.append(slice(1 + offset, extent - 1 + offset))
        else:
            value_portions.append(slice(1, extent - 1))
    return values[tuple(value_portions)]


def viscous(field, visc):
    centre = shifted(field, 1, 0, 0)
    centre_visc = shifted(visc, 0, 0, 0)
    change = jnp.zeros_like(centre)
    for spatial in range(3):
        for offset in (1, -1):
            face_visc = harmonic(centre_visc, shifted(visc, 0, spatial, offset))
            change = change + face_visc[None] * (shifted(field, 1, spatial, offset) - centre)
    return change


def inside_mask(place, count, cells_dev, extent):
    first = place * cells_dev - 1
    coords = first + lax.iota(jnp.int32, extent)
    return (coords >= 0) & (coords < count * cells_dev)


def split_tables(cell_block, plane_count, vertical_cells):
    plane_index = cell_block // vertical_cells
    depth_index = cell_block % vertical_cells
    plane_onehot = (
        plane_index[:, None]
        == lax.broadcasted_iota(jnp.int32, (cell_block.shape[0], plane_count), 1)
    ).astype(jnp.float32)
    depth_onehot = (
        depth_index[:, None]
        == lax.broadcasted_iota(jnp.int32, (cell_block.shape[0], vertical_cells), 1)
    ).astype(jnp.float32)
    return (plane_onehot, depth_onehot)


def accumulate_source(cell_slots, value_slots, plane_count, vertical_cells, group):
    slot_total, row_count = cell_slots.shape
    comps = value_slots.shape[0]
    turns = slot_total // group
    cell_blocks = cell_slots.reshape(turns, group * row_count)
    value_blocks = value_slots.reshape(comps, turns, group * row_count).transpose(1, 0, 2)

    def add_block(total, value_portions):
        cell_block, value_block = value_portions
        plane_onehot, depth_onehot = split_tables(cell_block, plane_count, vertical_cells)
        spread = value_block.T[:, :, None] * depth_onehot[:, None, :]
        spread = spread.reshape(cell_block.shape[0], comps * vertical_cells)
        added = lax.dot_general(
            plane_onehot,
            spread,
            (((0,), (0,)), ((), ())),
            precision=lax.Precision.HIGHEST,
            preferred_element_type=jnp.float32,
        )
        return (total + added, None)

    start = jnp.zeros((plane_count, comps * vertical_cells), jnp.float32)
    total, _ = lax.scan(add_block, start, (cell_blocks, value_blocks))
    return total.reshape(plane_count, comps, vertical_cells).transpose(1, 0, 2)


def read_cells(cell_slots, field_planes, vertical_cells, group):
    slot_total, row_count = cell_slots.shape
    plane_count = field_planes.shape[0]
    turns = slot_total // group
    cell_blocks = cell_slots.reshape(turns, group * row_count)

    def read_block(carry, cell_block):
        plane_onehot, depth_onehot = split_tables(cell_block, plane_count, vertical_cells)
        picked = jnp.dot(
            plane_onehot,
            field_planes,
            precision=lax.Precision.HIGHEST,
            preferred_element_type=jnp.float32,
        )
        return (carry, jnp.sum(picked * depth_onehot, axis=1))

    _, values = lax.scan(read_block, jnp.zeros((), jnp.float32), cell_blocks)
    return values.reshape(slot_total, row_count)


def shards(density, momentum_energy, viscosity, records, cell_ids, routes, lengths):
    fluid_state = jnp.concatenate([density[None], momentum_energy], 0)
    cells_x, cells_y, vertical_cells = density.shape
    plane_count = cells_x * cells_y
    tile_count = records.shape[1]
    row_count = records.shape[2]
    stream_count = lax.axis_size("stream")
    cross_count = lax.axis_size("cross")
    blocks = stream_count * cross_count
    capacity = max(2, 2 * tile_count // blocks)
    slot_total = blocks * capacity
    group = math.gcd(slot_total, 16)
    live_rows = lax.broadcasted_iota(jnp.int32, (tile_count, row_count), 1) < lengths[:, None]
    masked_values = jnp.where(live_rows[None], records, 0.0)
    target = routes[:, 0]
    onehot = (target[:, None] == lax.broadcasted_iota(jnp.int32, (tile_count, blocks), 1)).astype(
        jnp.float32
    )
    lower = (
        lax.broadcasted_iota(jnp.int32, (tile_count, tile_count), 1)
        < lax.broadcasted_iota(jnp.int32, (tile_count, tile_count), 0)
    ).astype(jnp.float32)
    before = jnp.dot(
        lower, onehot, precision=lax.Precision.HIGHEST, preferred_element_type=jnp.float32
    )
    slot_rank = jnp.sum(before * onehot, axis=1).astype(jnp.int32)
    slot_index = target * capacity + slot_rank
    placement_plan = (
        slot_index[:, None] == lax.broadcasted_iota(jnp.int32, (tile_count, slot_total), 1)
    ).astype(jnp.float32)
    outbound_values = jnp.einsum(
        "hn,ahq->anq", placement_plan, masked_values, precision=lax.Precision.HIGHEST
    )
    out_cells = jnp.einsum(
        "ts,tr->sr", placement_plan, cell_ids.astype(jnp.float32), precision=lax.Precision.HIGHEST
    )
    out_cells = out_cells.astype(jnp.int32)[None]
    arrived, arrived_cells = (
        lax.all_to_all(
            outbound_values, ("stream", "cross"), split_axis=1, concat_axis=1, tiled=True
        ),
        lax.all_to_all(out_cells, ("stream", "cross"), split_axis=1, concat_axis=1, tiled=True),
    )
    cell_slots = arrived_cells[0]
    source_rows = jnp.concatenate([jnp.abs(arrived[0:1]), arrived[1:5]], 0)
    source = accumulate_source(cell_slots, source_rows, plane_count, vertical_cells, group)
    source = source.reshape(5, cells_x, cells_y, vertical_cells)
    stacked = jnp.concatenate([fluid_state, viscosity[None], source], 0)
    padded = with_halo(stacked, (("stream", 1), ("cross", 2), ("gore", 3)), 2)
    state_wide = padded[0:5]
    visc_wide = padded[5]
    source_wide = padded[6:11]
    middle_wide = (
        shifted(state_wide, 1, 0, 0)
        + viscous(state_wide, visc_wide)
        + shifted(source_wide, 1, 0, 0)
    )
    inside_x = inside_mask(lax.axis_index("stream"), lax.axis_size("stream"), cells_x, cells_x + 2)
    inside_y = inside_mask(lax.axis_index("cross"), lax.axis_size("cross"), cells_y, cells_y + 2)
    inside_z = inside_mask(
        lax.axis_index("gore"), lax.axis_size("gore"), vertical_cells, vertical_cells + 2
    )
    inside = inside_x[:, None, None] & inside_y[None, :, None] & inside_z[None, None, :]
    middle_wide = jnp.where(inside[None], middle_wide, 0.0)
    visc_pad = shifted(visc_wide, 0, 0, 0)
    new_state = shifted(middle_wide, 1, 0, 0) + viscous(middle_wide, visc_pad)
    flat_state = new_state.reshape(5, plane_count, vertical_cells)
    kinetic = (
        flat_state[1] * flat_state[1]
        + flat_state[2] * flat_state[2]
        + flat_state[3] * flat_state[3]
    )
    pressure = 0.4 * (flat_state[4] - 0.5 * kinetic / flat_state[0])
    face_pressure = read_cells(cell_slots, pressure, vertical_cells, group)
    slot_values = arrived[5:8] * face_pressure[None]
    returned_values = lax.all_to_all(
        slot_values, ("stream", "cross"), split_axis=1, concat_axis=1, tiled=True
    )
    local_owned_values = jnp.einsum(
        "dm,pml->pdl", placement_plan, returned_values, precision=lax.Precision.HIGHEST
    )
    return (new_state, local_owned_values)


def solution(mesh):
    placed = (
        P("stream", "cross", "gore"),
        P(None, "stream", "cross", "gore"),
        P("stream", "cross", "gore"),
        P(None, ("stream", "cross", "gore"), None),
        P(("stream", "cross", "gore"), None),
        P(("stream", "cross", "gore"), None),
        P(("stream", "cross", "gore")),
    )
    return jax.shard_map(
        shards,
        mesh=mesh,
        in_specs=placed,
        out_specs=(P(None, "stream", "cross", "gore"), P(None, ("stream", "cross", "gore"), None)),
        check_vma=False,
    )
```

profile of v0, /device:TPU:1, one launch (start us, length us, event | category | flops | bytes accessed | tf_op | source)
XLA Modules:
  0.0 149.8 jit_solution(6206015372374661185)
XLA Ops:
  3.9 5.2 %all-to-all-start = ((s32[1,128,128]{2,0,1:T(1,128)}), s32[1,128,128]{2,0,1:T(1,128)S(1)}, u32[]{:S(2)}, u32[]{:S(2)}) async-start(s32[1,128,128]{2,0,1:T(1,128)} %bitcast.8), calls=%async_computation | async-start | bytes 131072 | tf_op jit(solution)/shard_map/all_to_all | solution.py:157
  13.6 3.8 %all-to-all-start.1 = ((f32[8,128,128]{2,0,1:T(8,128)}), f32[8,128,128]{2,0,1:T(8,128)S(1)}, u32[]{:S(2)}, u32[]{:S(2)}) async-start(f32[8,128,128]{2,0,1:T(8,128)} %copy.18), calls=%async_computation.1 | async-start | bytes 1048576 | tf_op jit(solution)/shard_map/all_to_all | solution.py:154
  18.8 7.0 %all-to-all-done.1 = f32[8,128,128]{2,0,1:T(8,128)S(1)} async-done(((f32[8,128,128]{2,0,1:T(8,128)}), f32[8,128,128]{2,0,1:T(8,128)S(1)}, u32[]{:S(2)}, u32[]{:S(2)}) %all-to-all-start.1) | async-done | bytes 524320 | tf_op jit(solution)/shard_map/all_to_all | solution.py:154
  26.2 67.1 %while.26 = (s32[]{:T(128)}, f32[16,640]{1,0:T(8,128)S(1)}, s32[8,2048]{1,0:T(8,128)S(1)}, f32[8,5,2048]{2,0,1:T(8,128)S(1)}, s32[]{:T(128)}, /*index=5*/s32[]{:T(128)}) while((s32[]{:T(128)}, f32[16,640]{1,0:T(8,128)S(1)}, s32[8,2048]{1,0:T(8,128)S(1)}, f32[8,5,2048]{2,0,1:T(8,128)S(1)}, s32[]{:T(128)}, /*index=5*/s32[]{:T(128)}) %tuple.84), condition=%wide.region_2.3_spmd.clone, body=%wide.region_1.2_spmd.clone.sunk | while | flops 253618176 | bytes 12927063 | solution.py:92
  26.4 2.9 %broadcast_multiply_fusion.3 = f32[2048,5,128]{0,2,1:T(8,128)} fusion(f32[2048,128]{0,1:T(8,128)S(1)} %fusion.83, f32[2048,5]{0,1:T(8,128)S(1)} %bitcast.54), kind=kLoop, calls=%fused_computation.14.clone.1 | loop fusion | flops 1310720 | bytes 6332416 | tf_op jit(solution)/shard_map/while/body/eval_jaxpr/mul | solution.py:80
  29.4 5.2 %convolution_add_fusion.2 = f32[16,640]{1,0:T(8,128)S(1)} fusion(f32[2048,640]{0,1:T(8,128)} %bitcast.53, s32[2048]{0:T(1024)S(1)} %get-tuple-element.238, f32[16,640]{1,0:T(8,128)S(1)} %get-tuple-element.246, pred[]{:T(512)S(6)} %compare.27), kind=kOutput, calls=%fused_computation.15.clone.1 | convolution fusion | flops 251744256 | bytes 5332993 | tf_op jit(solution)/shard_map/while/body/eval_jaxpr/dot_general | solution.py:82
  34.8 2.9 %broadcast_multiply_fusion.3 = f32[2048,5,128]{0,2,1:T(8,128)} fusion(f32[2048,128]{0,1:T(8,128)S(1)} %fusion.83, f32[2048,5]{0,1:T(8,128)S(1)} %bitcast.54), kind=kLoop, calls=%fused_computation.14.clone.1 | loop fusion | flops 1310720 | bytes 6332416 | tf_op jit(solution)/shard_map/while/body/eval_jaxpr/mul | solution.py:80
  37.8 5.2 %convolution_add_fusion.2 = f32[16,640]{1,0:T(8,128)S(1)} fusion(f32[2048,640]{0,1:T(8,128)} %bitcast.53, s32[2048]{0:T(1024)S(1)} %get-tuple-element.238, f32[16,640]{1,0:T(8,128)S(1)} %get-tuple-element.246, pred[]{:T(512)S(6)} %compare.27), kind=kOutput, calls=%fused_computation.15.clone.1 | convolution fusion | flops 251744256 | bytes 5332993 | tf_op jit(solution)/shard_map/while/body/eval_jaxpr/dot_general | solution.py:82
  43.2 2.9 %broadcast_multiply_fusion.3 = f32[2048,5,128]{0,2,1:T(8,128)} fusion(f32[2048,128]{0,1:T(8,128)S(1)} %fusion.83, f32[2048,5]{0,1:T(8,128)S(1)} %bitcast.54), kind=kLoop, calls=%fused_computation.14.clone.1 | loop fusion | flops 1310720 | bytes 6332416 | tf_op jit(solution)/shard_map/while/body/eval_jaxpr/mul | solution.py:80
  46.2 5.2 %convolution_add_fusion.2 = f32[16,640]{1,0:T(8,128)S(1)} fusion(f32[2048,640]{0,1:T(8,128)} %bitcast.53, s32[2048]{0:T(1024)S(1)} %get-tuple-element.238, f32[16,640]{1,0:T(8,128)S(1)} %get-tuple-element.246, pred[]{:T(512)S(6)} %compare.27), kind=kOutput, calls=%fused_computation.15.clone.1 | convolution fusion | flops 251744256 | bytes 5332993 | tf_op jit(solution)/shard_map/while/body/eval_jaxpr/dot_general | solution.py:82
  51.6 2.9 %broadcast_multiply_fusion.3 = f32[2048,5,128]{0,2,1:T(8,128)} fusion(f32[2048,128]{0,1:T(8,128)S(1)} %fusion.83, f32[2048,5]{0,1:T(8,128)S(1)} %bitcast.54), kind=kLoop, calls=%fused_computation.14.clone.1 | loop fusion | flops 1310720 | bytes 6332416 | tf_op jit(solution)/shard_map/while/body/eval_jaxpr/mul | solution.py:80
  54.6 5.2 %convolution_add_fusion.2 = f32[16,640]{1,0:T(8,128)S(1)} fusion(f32[2048,640]{0,1:T(8,128)} %bitcast.53, s32[2048]{0:T(1024)S(1)} %get-tuple-element.238, f32[16,640]{1,0:T(8,128)S(1)} %get-tuple-element.246, pred[]{:T(512)S(6)} %compare.27), kind=kOutput, calls=%fused_computation.15.clone.1 | convolution fusion | flops 251744256 | bytes 5332993 | tf_op jit(solution)/shard_map/while/body/eval_jaxpr/dot_general | solution.py:82
  60.0 2.9 %broadcast_multiply_fusion.3 = f32[2048,5,128]{0,2,1:T(8,128)} fusion(f32[2048,128]{0,1:T(8,128)S(1)} %fusion.83, f32[2048,5]{0,1:T(8,128)S(1)} %bitcast.54), kind=kLoop, calls=%fused_computation.14.clone.1 | loop fusion | flops 1310720 | bytes 6332416 | tf_op jit(solution)/shard_map/while/body/eval_jaxpr/mul | solution.py:80
  63.0 5.2 %convolution_add_fusion.2 = f32[16,640]{1,0:T(8,128)S(1)} fusion(f32[2048,640]{0,1:T(8,128)} %bitcast.53, s32[2048]{0:T(1024)S(1)} %get-tuple-element.238, f32[16,640]{1,0:T(8,128)S(1)} %get-tuple-element.246, pred[]{:T(512)S(6)} %compare.27), kind=kOutput, calls=%fused_computation.15.clone.1 | convolution fusion | flops 251744256 | bytes 5332993 | tf_op jit(solution)/shard_map/while/body/eval_jaxpr/dot_general | solution.py:82
  71.3 5.2 %convolution_add_fusion.2 = f32[16,640]{1,0:T(8,128)S(1)} fusion(f32[2048,640]{0,1:T(8,128)} %bitcast.53, s32[2048]{0:T(1024)S(1)} %get-tuple-element.238, f32[16,640]{1,0:T(8,128)S(1)} %get-tuple-element.246, pred[]{:T(512)S(6)} %compare.27), kind=kOutput, calls=%fused_computation.15.clone.1 | convolution fusion | flops 251744256 | bytes 5332993 | tf_op jit(solution)/shard_map/while/body/eval_jaxpr/dot_general | solution.py:82
  79.7 5.2 %convolution_add_fusion.2 = f32[16,640]{1,0:T(8,128)S(1)} fusion(f32[2048,640]{0,1:T(8,128)} %bitcast.53, s32[2048]{0:T(1024)S(1)} %get-tuple-element.238, f32[16,640]{1,0:T(8,128)S(1)} %get-tuple-element.246, pred[]{:T(512)S(6)} %compare.27), kind=kOutput, calls=%fused_computation.15.clone.1 | convolution fusion | flops 251744256 | bytes 5332993 | tf_op jit(solution)/shard_map/while/body/eval_jaxpr/dot_general | solution.py:82
  88.1 5.2 %convolution_add_fusion.2 = f32[16,640]{1,0:T(8,128)S(1)} fusion(f32[2048,640]{0,1:T(8,128)} %bitcast.53, s32[2048]{0:T(1024)S(1)} %get-tuple-element.238, f32[16,640]{1,0:T(8,128)S(1)} %get-tuple-element.246, pred[]{:T(512)S(6)} %compare.27), kind=kOutput, calls=%fused_computation.15.clone.1 | convolution fusion | flops 251744256 | bytes 5332993 | tf_op jit(solution)/shard_map/while/body/eval_jaxpr/dot_general | solution.py:82
  98.3 3.4 %collective-permute-done.1 = f32[11,2,4,128]{3,2,1,0:T(4,128)S(1)} collective-permute-done((f32[11,2,4,128]{3,2,1,0:T(4,128)S(1)}, f32[11,2,4,128]{3,2,1,0:T(4,128)S(1)}, u32[]{:S(2)}, u32[]{:S(2)}) %collective-permute-start.1) | collective-permute-done | bytes 45088 | tf_op jit(solution)/shard_map/ppermute | solution.py:17
  106.1 3.7 %collective-permute-done.3 = f32[11,8,2,128]{3,2,1,0:T(2,128)S(1)} collective-permute-done((f32[11,8,2,128]{3,2,1,0:T(2,128)S(1)}, f32[11,8,2,128]{3,2,1,0:T(2,128)S(1)}, u32[]{:S(2)}, u32[]{:S(2)}) %collective-permute-start.3) | collective-permute-done | bytes 90144 | tf_op jit(solution)/shard_map/ppermute | solution.py:17
  110.9 3.2 %collective-permute-start.4 = (f32[11,8,8,2]{3,2,1,0:T(8,128)}, f32[11,8,8,2]{3,2,1,0:T(8,128)S(1)}, u32[]{:S(2)}, u32[]{:S(2)}) collective-permute-start(f32[11,8,8,2]{3,2,1,0:T(8,128)} %get-tuple-element.159), channel_id=1, source_target_pairs={{0,1},{1,2},{2,3},{4,5},{5,6},{6,7},{8,9},{9,10},{10,11},{12,13},{... | collective-permute-start | bytes 16904 | tf_op jit(solution)/shard_map/ppermute | solution.py:14
  115.6 6.7 %collective-permute-done.4 = f32[11,8,8,2]{3,2,1,0:T(8,128)S(1)} collective-permute-done((f32[11,8,8,2]{3,2,1,0:T(8,128)}, f32[11,8,8,2]{3,2,1,0:T(8,128)S(1)}, u32[]{:S(2)}, u32[]{:S(2)}) %collective-permute-start.4) | collective-permute-done | bytes 5664 | tf_op jit(solution)/shard_map/ppermute | solution.py:14
  122.2 4.0 %collective-permute-done.5 = f32[11,8,8,2]{3,2,1,0:T(8,128)S(1)} collective-permute-done((f32[11,8,8,2]{3,2,1,0:T(8,128)S(1)}, f32[11,8,8,2]{3,2,1,0:T(8,128)S(1)}, u32[]{:S(2)}, u32[]{:S(2)}) %collective-permute-start.5) | collective-permute-done | bytes 5664 | tf_op jit(solution)/shard_map/ppermute | solution.py:17
  128.2 11.7 %while.25 = (s32[]{:T(128)}, f32[8,2048]{1,0:T(8,128)S(1)}, s32[8,2048]{1,0:T(8,128)S(1)}, f32[16,128]{1,0:T(8,128)S(1)}, s32[]{:T(128)}, /*index=5*/s32[]{:T(128)}) while((s32[]{:T(128)}, f32[8,2048]{1,0:T(8,128)S(1)}, s32[8,2048]{1,0:T(8,128)S(1)}, f32[16,128]{1,0:T(8,128)S(1)}, s32[]{:T(128)}, /*index=5*/s32[]{:T(128)}) %tuple.86), condition=%wide.region_5.6_spmd, body=%wide.region_3.5_spmd.sunk | while | flops 51187712 | bytes 90189 | solution.py:112
  140.0 8.9 %all_to_all.15 = f32[3,128,128]{2,0,1:T(4,128)S(1)} all-to-all(f32[3,128,128]{2,0,1:T(4,128)S(1)} %slice_multiply_fusion), channel_id=1, replica_groups=mesh['stream'=4,'cross'=2,'gore'=4] {'stream','cross'}, dimensions={1} | all-to-all | bytes 393216 | tf_op jit(solution)/shard_map/all_to_all | solution.py:191
  (130 shorter events, 45.7 us)
Async XLA Ops:
  3.9 9.7 %all-to-all-start = ((s32[1,128,128]{2,0,1:T(1,128)}), s32[1,128,128]{2,0,1:T(1,128)S(1)}, u32[]{:S(2)}, u32[]{:S(2)}) async-start(s32[1,128,128]{2,0,1:T(1,128)} %bitcast.8), calls=%async_computation | async-start | bytes 131072 | tf_op jit(solution)/shard_map/all_to_all | solution.py:157
  13.6 12.2 %all-to-all-start.1 = ((f32[8,128,128]{2,0,1:T(8,128)}), f32[8,128,128]{2,0,1:T(8,128)S(1)}, u32[]{:S(2)}, u32[]{:S(2)}) async-start(f32[8,128,128]{2,0,1:T(8,128)} %copy.18), calls=%async_computation.1 | async-start | bytes 1048576 | tf_op jit(solution)/shard_map/all_to_all | solution.py:154
  26.2 67.2 %copy-start = (f32[4,4,4,128]{3,2,1,0:T(4,128)S(1)}, f32[4,4,4,128]{3,2,1,0:T(4,128)}, u32[]{:S(2)}) copy-start(f32[4,4,4,128]{3,2,1,0:T(4,128)} %param.12) | copy-start | bytes 98308
  26.2 67.2 %copy-start.1 = (f32[4,4,128]{2,1,0:T(4,128)S(1)}, f32[4,4,128]{2,1,0:T(4,128)}, u32[]{:S(2)}) copy-start(f32[4,4,128]{2,1,0:T(4,128)} %param.13) | copy-start | bytes 24580
  26.2 67.2 %copy-start.2 = (f32[4,4,128]{2,1,0:T(4,128)S(1)}, f32[4,4,128]{2,1,0:T(4,128)}, u32[]{:S(2)}) copy-start(f32[4,4,128]{2,1,0:T(4,128)} %param.11) | copy-start | bytes 24580
  93.5 4.8 %collective-permute-start = (f32[11,2,4,128]{3,2,1,0:T(4,128)S(1)}, f32[11,2,4,128]{3,2,1,0:T(4,128)S(1)}, u32[]{:S(2)}, u32[]{:S(2)}) collective-permute-start(f32[11,2,4,128]{3,2,1,0:T(4,128)S(1)} %get-tuple-element.163), channel_id=1, source_target_pairs={{0,8},{8,16},{16,24},{1,9},{9,17},{17,25},{2,10},{10,18},{18,26},{... | collective-permute-start | bytes 135176 | tf_op jit(solution)/shard_map/ppermute | solution.py:14
  96.4 5.4 %collective-permute-start.1 = (f32[11,2,4,128]{3,2,1,0:T(4,128)S(1)}, f32[11,2,4,128]{3,2,1,0:T(4,128)S(1)}, u32[]{:S(2)}, u32[]{:S(2)}) collective-permute-start(f32[11,2,4,128]{3,2,1,0:T(4,128)S(1)} %get-tuple-element.164), channel_id=1, source_target_pairs={{8,0},{16,8},{24,16},{9,1},{17,9},{25,17},{10,2},{18,10},{26,18},{... | collective-permute-start | bytes 135176 | tf_op jit(solution)/shard_map/ppermute | solution.py:17
  101.9 4.2 %collective-permute-start.2 = (f32[11,8,2,128]{3,2,1,0:T(2,128)S(1)}, f32[11,8,2,128]{3,2,1,0:T(2,128)S(1)}, u32[]{:S(2)}, u32[]{:S(2)}) collective-permute-start(f32[11,8,2,128]{3,2,1,0:T(2,128)S(1)} %get-tuple-element.161), channel_id=1, source_target_pairs={{0,4},{1,5},{2,6},{3,7},{8,12},{9,13},{10,14},{11,15},{16,20},{17,... | collective-permute-start | bytes 270344 | tf_op jit(solution)/shard_map/ppermute | solution.py:14
  104.5 5.3 %collective-permute-start.3 = (f32[11,8,2,128]{3,2,1,0:T(2,128)S(1)}, f32[11,8,2,128]{3,2,1,0:T(2,128)S(1)}, u32[]{:S(2)}, u32[]{:S(2)}) collective-permute-start(f32[11,8,2,128]{3,2,1,0:T(2,128)S(1)} %get-tuple-element.162), channel_id=1, source_target_pairs={{4,0},{5,1},{6,2},{7,3},{12,8},{13,9},{14,10},{15,11},{20,16},{21,... | collective-permute-start | bytes 270344 | tf_op jit(solution)/shard_map/ppermute | solution.py:17
  110.9 11.4 %collective-permute-start.4 = (f32[11,8,8,2]{3,2,1,0:T(8,128)}, f32[11,8,8,2]{3,2,1,0:T(8,128)S(1)}, u32[]{:S(2)}, u32[]{:S(2)}) collective-permute-start(f32[11,8,8,2]{3,2,1,0:T(8,128)} %get-tuple-element.159), channel_id=1, source_target_pairs={{0,1},{1,2},{2,3},{4,5},{5,6},{6,7},{8,9},{9,10},{10,11},{12,13},{... | collective-permute-start | bytes 16904 | tf_op jit(solution)/shard_map/ppermute | solution.py:14
  114.1 12.2 %collective-permute-start.5 = (f32[11,8,8,2]{3,2,1,0:T(8,128)S(1)}, f32[11,8,8,2]{3,2,1,0:T(8,128)S(1)}, u32[]{:S(2)}, u32[]{:S(2)}) collective-permute-start(f32[11,8,8,2]{3,2,1,0:T(8,128)S(1)} %get-tuple-element.160), channel_id=1, source_target_pairs={{1,0},{2,1},{3,2},{5,4},{6,5},{7,6},{9,8},{10,9},{11,10},{13,12},{... | collective-permute-start | bytes 16904 | tf_op jit(solution)/shard_map/ppermute | solution.py:17
  128.1 21.6 %copy-start.3 = (f32[5,4,4,128]{3,2,1,0:T(4,128)}, f32[5,4,4,128]{3,2,1,0:T(4,128)S(1)}, u32[]{:S(2)}) copy-start(f32[5,4,4,128]{3,2,1,0:T(4,128)S(1)} %fusion.38) | copy-start | bytes 122884
where the time goes:
time: 151 us; the launch traced here: 150 us
  matrix products  56.2 us (37%)
  other arithmetic  29.4 us (19%)
  waiting for transfers between devices  26.2 us (17%)
  starting transfers between devices  22.3 us (15%)
  blocking collectives  8.9 us (6%)
  local copies, waits for them, and re-layouts  5.08 us (3%)
    dot_general x8, matrix products, add_block(): lax.dot_general(plane_onehot, spread, (((0,), (0,)), ((), ())), precision...  41.7 us
    mul x8, other arithmetic, add_block(): spread = value_block.T[:, :, None] * depth_onehot[:, None, :]  23.6 us
    ppermute x3, waiting for transfers between devices, with_halo(): lax.ppermute(lax.slice_in_dim(block, 0, width, axis=dim), axis, backward)  11.2 us
    dot_general x8, matrix products, read_block(): jnp.dot(plane_onehot, field_planes, precision=lax.Precision.HIGHEST, pref...  9.5 us
    all_to_all x1, blocking collectives, shards(): lax.all_to_all(slot_values, ('stream', 'cross'), split_axis=1, concat_axi...  8.9 us
    ppermute x3, starting transfers between devices, with_halo(): lax.ppermute(lax.slice_in_dim(block, block.shape[dim] - width, None, axis...  8.79 us
    all_to_all x1, waiting for transfers between devices, shards(): lax.all_to_all(outbound_values, ('stream', 'cross'), split_axis=1, concat...  7.01 us
    ppermute x3, waiting for transfers between devices, with_halo(): lax.ppermute(lax.slice_in_dim(block, block.shape[dim] - width, None, axis...  6.85 us
  transfers between devices with their start and end apart: 8, of which 7 were waited for; matrix products, arithmetic and copies ran while one was open for 3% of the time, Pallas kernels for 0%

commit v1 on v0

v1 whole, which is shorter than its diff:
```python
import jax
import jax.numpy as jnp
from jax import lax
from jax.sharding import PartitionSpec as P


SIDES = (("stream", 1), ("cross", 2), ("gore", 3))


def face_halo(block):
    padded = jnp.pad(block, ((0, 0), (1, 1), (1, 1), (1, 1)))
    for axis, dim in SIDES:
        count = lax.axis_size(axis)
        forward = [(i, i + 1) for i in range(count - 1)]
        backward = [(target, source) for source, target in forward]
        extent = block.shape[dim]
        low = lax.ppermute(lax.slice_in_dim(block, extent - 1, None, axis=dim), axis, forward)
        high = lax.ppermute(lax.slice_in_dim(block, 0, 1, axis=dim), axis, backward)
        low_at = [slice(None)] + [slice(1, -1)] * 3
        high_at = list(low_at)
        low_at[dim] = slice(0, 1)
        high_at[dim] = slice(extent + 1, extent + 2)
        padded = padded.at[tuple(low_at)].set(low).at[tuple(high_at)].set(high)
    return padded


def harmonic(first_visc, second_visc):
    summed = first_visc + second_visc
    denominator = jnp.where(summed > 0, summed, 1.0)
    return 2.0 * first_visc * second_visc / denominator


def shifted(values, leading, spatial, offset):
    value_portions = [slice(None)] * leading
    for position in range(3):
        extent = values.shape[leading + position]
        if position == spatial:
            value_portions.append(slice(1 + offset, extent - 1 + offset))
        else:
            value_portions.append(slice(1, extent - 1))
    return values[tuple(value_portions)]


def viscous(field, visc):
    centre = shifted(field, 1, 0, 0)
    centre_visc = shifted(visc, 0, 0, 0)
    change = jnp.zeros_like(centre)
    for spatial in range(3):
        for offset in (1, -1):
            face_visc = harmonic(centre_visc, shifted(visc, 0, spatial, offset))
            change = change + face_visc[None] * (shifted(field, 1, spatial, offset) - centre)
    return change


def split_high(values):
    scaled = values * jnp.float32(65537.0)
    high = scaled - (scaled - values)
    return (high, values - high)


def three_bf16(values):
    first, rest = split_high(values)
    second, third = split_high(rest)
    return tuple(part.astype(jnp.bfloat16) for part in (first, second, third))


def exact_dot(spec, values, onehot, values_first):
    stacked = jnp.stack(three_bf16(values), 0)
    left, right = spec.split("->")[0].split(",")
    output = spec.split("->")[1]
    if values_first:
        terms = jnp.einsum(
            "k" + left + "," + right + "->k" + output, stacked, onehot,
            preferred_element_type=jnp.float32,
        )
    else:
        terms = jnp.einsum(
            left + ",k" + right + "->k" + output, onehot, stacked,
            preferred_element_type=jnp.float32,
        )
    return terms[0] + terms[1] + terms[2]


def shards(density, momentum_energy, viscosity, records, cell_ids, routes, lengths):
    fluid_state = jnp.concatenate([density[None], momentum_energy], 0)
    cells_x, cells_y, vertical_cells = density.shape
    plane_count = cells_x * cells_y
    tile_count = records.shape[1]
    row_count = records.shape[2]
    blocks = lax.axis_size("stream") * lax.axis_size("cross")
    capacity = max(2, 2 * tile_count // blocks)
    slot_total = blocks * capacity
    faces = slot_total * row_count

    state_visc = face_halo(jnp.concatenate([fluid_state, viscosity[None]], 0))
    state_pad = state_visc[0:5]
    visc_pad = state_visc[5]

    live_rows = lax.broadcasted_iota(jnp.int32, (tile_count, row_count), 1) < lengths[:, None]
    masked_values = jnp.where(live_rows[None], records, 0.0)
    target = routes[:, 0]
    onehot = (target[:, None] == lax.broadcasted_iota(jnp.int32, (tile_count, blocks), 1)).astype(
        jnp.float32
    )
    lower = (
        lax.broadcasted_iota(jnp.int32, (tile_count, tile_count), 1)
        < lax.broadcasted_iota(jnp.int32, (tile_count, tile_count), 0)
    ).astype(jnp.float32)
    before = jnp.dot(
        lower, onehot, precision=lax.Precision.HIGHEST, preferred_element_type=jnp.float32
    )
    slot_rank = jnp.sum(before * onehot, axis=1).astype(jnp.int32)
    slot_index = target * capacity + slot_rank
    placement_plan = (
        slot_index[:, None] == lax.broadcasted_iota(jnp.int32, (tile_count, slot_total), 1)
    ).astype(jnp.float32)
    payload = jnp.concatenate(
        [
            jnp.abs(masked_values[0:1]),
            masked_values[1:5],
            cell_ids.astype(jnp.float32)[None],
        ],
        0,
    )
    outbound = jnp.einsum(
        "ts,ctr->csr", placement_plan, payload, precision=lax.Precision.HIGHEST
    )
    arrived = lax.all_to_all(outbound, ("stream", "cross"), split_axis=1, concat_axis=1, tiled=True)

    cells = jnp.round(arrived[5]).astype(jnp.int32).reshape(faces)
    plane = cells // vertical_cells
    depth = cells % vertical_cells
    depth_hot = (
        depth[:, None] == lax.broadcasted_iota(jnp.int32, (faces, vertical_cells), 1)
    )
    plane_rows = plane[None, :] == lax.broadcasted_iota(jnp.int32, (plane_count, faces), 0)
    spread = jnp.where(plane_rows[None], arrived[0:5].reshape(5, 1, faces), 0.0)
    source = jnp.einsum(
        "cpf,fd->cpd", spread, depth_hot.astype(jnp.float32), precision=lax.Precision.HIGHEST
    )
    source = source.reshape(5, cells_x, cells_y, vertical_cells)

    middle = shifted(state_pad, 1, 0, 0) + viscous(state_pad, visc_pad) + source
    middle_pad = face_halo(middle)
    new_state = middle + viscous(middle_pad, visc_pad)

    flat_state = new_state.reshape(5, plane_count, vertical_cells)
    kinetic = (
        flat_state[1] * flat_state[1]
        + flat_state[2] * flat_state[2]
        + flat_state[3] * flat_state[3]
    )
    pressure = 0.4 * (flat_state[4] - 0.5 * kinetic / flat_state[0])
    picked = exact_dot("fd,dp->fp", pressure.T, depth_hot.astype(jnp.bfloat16), False)
    plane_cols = plane[:, None] == lax.broadcasted_iota(jnp.int32, (faces, plane_count), 1)
    face_pressure = jnp.sum(jnp.where(plane_cols, picked, 0.0), axis=1)
    returned = lax.all_to_all(
        face_pressure.reshape(1, slot_total, row_count),
        ("stream", "cross"),
        split_axis=1,
        concat_axis=1,
        tiled=True,
    )
    home_pressure = jnp.einsum(
        "ts,sr->tr", placement_plan, returned[0], precision=lax.Precision.HIGHEST
    )
    face_loads = masked_values[5:8] * home_pressure[None]
    return (new_state, face_loads)


def solution(mesh):
    placed = (
        P("stream", "cross", "gore"),
        P(None, "stream", "cross", "gore"),
        P("stream", "cross", "gore"),
        P(None, ("stream", "cross", "gore"), None),
        P(("stream", "cross", "gore"), None),
        P(("stream", "cross", "gore"), None),
        P(("stream", "cross", "gore")),
    )
    return jax.shard_map(
        shards,
        mesh=mesh,
        in_specs=placed,
        out_specs=(P(None, "stream", "cross", "gore"), P(None, ("stream", "cross", "gore"), None)),
        check_vma=False,
    )
```

time: 151 us -> 94.7 us (0.63)
  matrix products: 56.2 us -> 7.98 us
  waiting for transfers between devices: 26.2 us -> 0.03 us
  local copies, waits for them, and re-layouts: 5.08 us -> 31.1 us
  other arithmetic: 29.4 us -> 6.14 us
  starting transfers between devices: 22.3 us -> 37 us
    dot_general x19 -> x4, matrix products: 55.4 us -> 7.11 us  [the longest x1 3.98 us: shards(): jnp.einsum('cpf,fd->cpd', spread, depth_hot.astype(jnp.float32), precisio...]
    scatter x0 -> x12, local copies, waits for them, and re-layouts: none -> 29.5 us  [face_halo(): padded = padded.at[tuple(low_at)].set(low).at[tuple(high_at)].set(high)]
    mul x9 -> x1, other arithmetic: 23.6 us -> 0.65 us  [shards(): face_loads = masked_values[5:8] * home_pressure[None]]
    ppermute x6 -> x12, starting transfers between devices: 13.3 us -> 31.8 us  [the longest x6 22.6 us: face_halo(): lax.ppermute(lax.slice_in_dim(block, extent - 1, None, axis=dim), axis, f...]
    ppermute x6 -> x12, waiting for transfers between devices: 18 us -> 0.03 us  [the longest x6 0.02 us: face_halo(): high = lax.ppermute(lax.slice_in_dim(block, 0, 1, axis=dim), axis, backward)]
    all_to_all x2 -> x1, waiting for transfers between devices: 8.16 us -> 0.01 us  [shards(): lax.all_to_all(outbound, ('stream', 'cross'), split_axis=1, concat_axis=1...]
    all_to_all x2 -> x1, starting transfers between devices: 9.02 us -> 5.22 us  [shards(): lax.all_to_all(outbound, ('stream', 'cross'), split_axis=1, concat_axis=1...]
    dynamic_update_slice x8 -> x0, local copies, waits for them, and re-layouts: 1.63 us -> none  [read_cells(): _, values = lax.scan(read_block, jnp.zeros((), jnp.float32), cell_blocks)]
  transfers between devices with their start and end apart: 8 -> 13, of which waited for: 7 -> 0; matrix products, arithmetic and copies ran while one was open for 3% -> 30% of each run, Pallas kernels for 0% -> 0%
where the time goes in v1:
time: 94.7 us; the launch traced here: 93.7 us
  starting transfers between devices  37 us (39%)
  local copies, waits for them, and re-layouts  31.1 us (33%)
  blocking collectives  10.3 us (11%)
  matrix products  7.98 us (8%)
  other arithmetic  6.14 us (6%)
  between operations  1.13 us (1%)
    scatter x12, local copies, waits for them, and re-layouts, face_halo(): padded = padded.at[tuple(low_at)].set(low).at[tuple(high_at)].set(high)  29.5 us
    ppermute x6, starting transfers between devices, face_halo(): lax.ppermute(lax.slice_in_dim(block, extent - 1, None, axis=dim), axis, f...  22.6 us
    all_to_all x1, blocking collectives, shards(): lax.all_to_all(face_pressure.reshape(1, slot_total, row_count), ('stream'...  10.3 us
    ppermute x6, starting transfers between devices, face_halo(): high = lax.ppermute(lax.slice_in_dim(block, 0, 1, axis=dim), axis, backward)  9.19 us
    all_to_all x1, starting transfers between devices, shards(): lax.all_to_all(outbound, ('stream', 'cross'), split_axis=1, concat_axis=1...  5.22 us
    dot_general x1, matrix products, shards(): jnp.einsum('cpf,fd->cpd', spread, depth_hot.astype(jnp.float32), precisio...  3.98 us
    dot_general x1, matrix products, exact_dot(): jnp.einsum(left + ',k' + right + '->k' + output, onehot, stacked, preferr...  2.4 us
  transfers between devices with their start and end apart: 13, of which 0 were waited for; matrix products, arithmetic and copies ran while one was open for 30% of the time, Pallas kernels for 0%

profile of v1, /device:TPU:1, one launch (start us, length us, event | category | flops | bytes accessed | tf_op | source)
XLA Modules:
  0.0 93.7 jit_solution(12657105326850253347)
XLA Ops:
  6.2 5.2 %all-to-all-start = ((f32[6,128,128]{2,0,1:T(8,128)}), f32[6,128,128]{2,0,1:T(8,128)S(1)}, u32[]{:S(2)}, u32[]{:S(2)}) async-start(f32[6,128,128]{2,0,1:T(8,128)} %copy.11), calls=%async_computation | async-start | bytes 1048576 | tf_op jit(solution)/shard_map/all_to_all | solution.py:128
  12.2 3.5 %collective-permute-start = (f32[6,1,4,128]{3,2,1,0:T(4,128)S(1)}, f32[6,1,4,128]{3,2,1,0:T(4,128)S(1)}, u32[]{:S(2)}, u32[]{:S(2)}) collective-permute-start(f32[6,1,4,128]{3,2,1,0:T(4,128)S(1)} %get-tuple-element.159), channel_id=1, source_target_pairs={{0,8},{8,16},{16,24},{1,9},{9,17},{17,25},{2,10},{10,18},{18,26},{... | collective-permute-start | bytes 36872 | tf_op jit(solution)/shard_map/ppermute | solution.py:17
  15.8 1.9 %collective-permute-start.1 = (f32[6,1,4,128]{3,2,1,0:T(4,128)S(1)}, f32[6,1,4,128]{3,2,1,0:T(4,128)S(1)}, u32[]{:S(2)}, u32[]{:S(2)}) collective-permute-start(f32[6,1,4,128]{3,2,1,0:T(4,128)S(1)} %get-tuple-element.158), channel_id=1, source_target_pairs={{8,0},{16,8},{24,16},{9,1},{17,9},{25,17},{10,2},{18,10},{26,18},{... | collective-permute-start | bytes 36872 | tf_op jit(solution)/shard_map/ppermute | solution.py:18
  17.7 3.1 %collective-permute-start.2 = (f32[6,4,1,128]{3,2,1,0:T(1,128)S(1)}, f32[6,4,1,128]{3,2,1,0:T(1,128)S(1)}, u32[]{:S(2)}, u32[]{:S(2)}) collective-permute-start(f32[6,4,1,128]{3,2,1,0:T(1,128)S(1)} %get-tuple-element.157), channel_id=1, source_target_pairs={{0,4},{1,5},{2,6},{3,7},{8,12},{9,13},{10,14},{11,15},{16,20},{17,... | collective-permute-start | bytes 36872 | tf_op jit(solution)/shard_map/ppermute | solution.py:17
  20.8 1.3 %collective-permute-start.3 = (f32[6,4,1,128]{3,2,1,0:T(1,128)S(1)}, f32[6,4,1,128]{3,2,1,0:T(1,128)S(1)}, u32[]{:S(2)}, u32[]{:S(2)}) collective-permute-start(f32[6,4,1,128]{3,2,1,0:T(1,128)S(1)} %get-tuple-element.156), channel_id=1, source_target_pairs={{4,0},{5,1},{6,2},{7,3},{12,8},{13,9},{14,10},{15,11},{20,16},{21,... | collective-permute-start | bytes 36872 | tf_op jit(solution)/shard_map/ppermute | solution.py:18
  22.2 3.2 %collective-permute-start.4 = (f32[6,4,4,1]{3,2,1,0:T(4,128)S(1)}, f32[6,4,4,1]{3,2,1,0:T(4,128)S(1)}, u32[]{:S(2)}, u32[]{:S(2)}) collective-permute-start(f32[6,4,4,1]{3,2,1,0:T(4,128)S(1)} %get-tuple-element.155), channel_id=1, source_target_pairs={{0,1},{1,2},{2,3},{4,5},{5,6},{6,7},{8,9},{9,10},{10,11},{12,13},{... | collective-permute-start | bytes 1160 | tf_op jit(solution)/shard_map/ppermute | solution.py:17
  26.9 2.1 %scatter.40 = f32[6,6,6,130]{3,2,1,0:T(8,128)S(1)} dynamic-update-slice(f32[6,6,6,130]{3,2,1,0:T(8,128)S(1)} %pad.56, f32[6,1,4,128]{3,2,1,0:T(4,128)S(1)} %collective-permute-done, s32[]{:T(128)} %constant.358.clone.1, s32[]{:T(128)} %constant.358.clone.1, s32[]{:T(128)} %constant.359.clone.1, s32[]{:T(128)} %constant.359.clone.1) | dynamic-update-slice | bytes 24580 | tf_op jit(solution)/shard_map/scatter | solution.py:23
  29.0 2.1 %scatter.41 = f32[6,6,6,130]{3,2,1,0:T(8,128)S(1)} dynamic-update-slice(f32[6,6,6,130]{3,2,1,0:T(8,128)S(1)} %scatter.40, f32[6,1,4,128]{3,2,1,0:T(4,128)S(1)} %collective-permute-done.1, s32[]{:T(128)} %constant.358.clone.1, s32[]{:T(128)} %constant.360.clone.1, s32[]{:T(128)} %constant.359.clone.1, s32[]{:T(128)} %constant.359.clone.1) | dynamic-update-slice | bytes 24580 | tf_op jit(solution)/shard_map/scatter | solution.py:23
  31.2 3.8 %scatter.44 = f32[6,6,6,130]{3,2,1,0:T(8,128)S(1)} dynamic-update-slice(f32[6,6,6,130]{3,2,1,0:T(8,128)S(1)} %scatter.41, f32[6,4,1,128]{3,2,1,0:T(1,128)S(1)} %collective-permute-done.2, s32[]{:T(128)} %constant.358.clone.1, s32[]{:T(128)} %constant.359.clone.1, s32[]{:T(128)} %constant.358.clone.1, s32[]{:T(128)} %constant.359.clone.1) | dynamic-update-slice | bytes 24580 | tf_op jit(solution)/shard_map/scatter | solution.py:23
  35.0 3.8 %scatter.45 = f32[6,6,6,130]{3,2,1,0:T(8,128)S(1)} dynamic-update-slice(f32[6,6,6,130]{3,2,1,0:T(8,128)S(1)} %scatter.44, f32[6,4,1,128]{3,2,1,0:T(1,128)S(1)} %collective-permute-done.3, s32[]{:T(128)} %constant.358.clone.1, s32[]{:T(128)} %constant.359.clone.1, s32[]{:T(128)} %constant.360.clone.1, s32[]{:T(128)} %constant.359.clone.1) | dynamic-update-slice | bytes 24580 | tf_op jit(solution)/shard_map/scatter | solution.py:23
  39.3 3.7 %scatter.49 = f32[6,6,6,130]{3,2,1,0:T(8,128)S(1)} dynamic-update-slice(f32[6,6,6,130]{3,2,1,0:T(8,128)S(1)} %scatter.46, f32[6,4,4,1]{3,2,1,0:T(4,128)S(1)} %collective-permute-done.5, s32[]{:T(128)} %constant.358.clone.1, s32[]{:T(128)} %constant.359.clone.1, s32[]{:T(128)} %constant.359.clone.1, s32[]{:T(128)} %constant.361.clone.1) | dynamic-update-slice | bytes 772 | tf_op jit(solution)/shard_map/scatter | solution.py:23
  44.0 4.0 %fusion.2 = f32[5,16,128]{2,1,0:T(8,128)S(1)} fusion(s32[16384]{0:T(1024)S(1)} %get-tuple-element.147, f32[5,16,16384]{2,1,0:T(8,128)S(1)} %fusion.94), kind=kOutput, calls=%fused_computation.3 | convolution fusion | flops 2015363072 | bytes 5349376 | tf_op jit(solution)/shard_map/cpf,fd->cpd/dot_general | solution.py:138
  48.2 4.2 %collective-permute-start.6 = (f32[5,1,4,128]{3,2,1,0:T(4,128)S(1)}, f32[5,1,4,128]{3,2,1,0:T(4,128)S(1)}, u32[]{:S(2)}, u32[]{:S(2)}) collective-permute-start(f32[5,1,4,128]{3,2,1,0:T(4,128)S(1)} %get-tuple-element.165), channel_id=1, source_target_pairs={{0,8},{8,16},{16,24},{1,9},{9,17},{17,25},{2,10},{10,18},{18,26},{... | collective-permute-start | bytes 30728 | tf_op jit(solution)/shard_map/ppermute | solution.py:17
  52.4 1.9 %collective-permute-start.7 = (f32[5,1,4,128]{3,2,1,0:T(4,128)S(1)}, f32[5,1,4,128]{3,2,1,0:T(4,128)S(1)}, u32[]{:S(2)}, u32[]{:S(2)}) collective-permute-start(f32[5,1,4,128]{3,2,1,0:T(4,128)S(1)} %get-tuple-element.164), channel_id=1, source_target_pairs={{8,0},{16,8},{24,16},{9,1},{17,9},{25,17},{10,2},{18,10},{26,18},{... | collective-permute-start | bytes 30728 | tf_op jit(solution)/shard_map/ppermute | solution.py:18
  54.3 4.3 %collective-permute-start.8 = (f32[5,4,1,128]{3,2,1,0:T(1,128)S(1)}, f32[5,4,1,128]{3,2,1,0:T(1,128)S(1)}, u32[]{:S(2)}, u32[]{:S(2)}) collective-permute-start(f32[5,4,1,128]{3,2,1,0:T(1,128)S(1)} %get-tuple-element.163), channel_id=1, source_target_pairs={{0,4},{1,5},{2,6},{3,7},{8,12},{9,13},{10,14},{11,15},{16,20},{17,... | collective-permute-start | bytes 30728 | tf_op jit(solution)/shard_map/ppermute | solution.py:17
  60.1 4.3 %collective-permute-start.10 = (f32[5,4,4,1]{3,2,1,0:T(4,128)S(1)}, f32[5,4,4,1]{3,2,1,0:T(4,128)S(1)}, u32[]{:S(2)}, u32[]{:S(2)}) collective-permute-start(f32[5,4,4,1]{3,2,1,0:T(4,128)S(1)} %get-tuple-element.161), channel_id=1, source_target_pairs={{0,1},{1,2},{2,3},{4,5},{5,6},{6,7},{8,9},{9,10},{10,11},{12,13},{... | collective-permute-start | bytes 968 | tf_op jit(solution)/shard_map/ppermute | solution.py:17
  64.4 1.5 %collective-permute-start.11 = (f32[5,4,4,1]{3,2,1,0:T(4,128)S(1)}, f32[5,4,4,1]{3,2,1,0:T(4,128)S(1)}, u32[]{:S(2)}, u32[]{:S(2)}) collective-permute-start(f32[5,4,4,1]{3,2,1,0:T(4,128)S(1)} %get-tuple-element.160), channel_id=1, source_target_pairs={{1,0},{2,1},{3,2},{5,4},{6,5},{7,6},{9,8},{10,9},{11,10},{13,12},{... | collective-permute-start | bytes 968 | tf_op jit(solution)/shard_map/ppermute | solution.py:18
  65.9 1.8 %scatter.50 = f32[5,6,6,130]{3,2,1,0:T(8,128)S(1)} dynamic-update-slice(f32[5,6,6,130]{3,2,1,0:T(8,128)S(1)} %pad.57, f32[5,1,4,128]{3,2,1,0:T(4,128)S(1)} %collective-permute-done.6, s32[]{:T(128)} %constant.358.clone.1, s32[]{:T(128)} %constant.358.clone.1, s32[]{:T(128)} %constant.359.clone.1, s32[]{:T(128)} %constant.359.clone.1) | dynamic-update-slice | bytes 20484 | tf_op jit(solution)/shard_map/scatter | solution.py:23
  67.7 1.8 %scatter.51 = f32[5,6,6,130]{3,2,1,0:T(8,128)S(1)} dynamic-update-slice(f32[5,6,6,130]{3,2,1,0:T(8,128)S(1)} %scatter.50, f32[5,1,4,128]{3,2,1,0:T(4,128)S(1)} %collective-permute-done.7, s32[]{:T(128)} %constant.358.clone.1, s32[]{:T(128)} %constant.360.clone.1, s32[]{:T(128)} %constant.359.clone.1, s32[]{:T(128)} %constant.359.clone.1) | dynamic-update-slice | bytes 20484 | tf_op jit(solution)/shard_map/scatter | solution.py:23
  69.5 3.2 %scatter.54 = f32[5,6,6,130]{3,2,1,0:T(8,128)S(1)} dynamic-update-slice(f32[5,6,6,130]{3,2,1,0:T(8,128)S(1)} %scatter.51, f32[5,4,1,128]{3,2,1,0:T(1,128)S(1)} %collective-permute-done.8, s32[]{:T(128)} %constant.358.clone.1, s32[]{:T(128)} %constant.359.clone.1, s32[]{:T(128)} %constant.358.clone.1, s32[]{:T(128)} %constant.359.clone.1) | dynamic-update-slice | bytes 20484 | tf_op jit(solution)/shard_map/scatter | solution.py:23
  72.7 3.2 %scatter.55 = f32[5,6,6,130]{3,2,1,0:T(8,128)S(1)} dynamic-update-slice(f32[5,6,6,130]{3,2,1,0:T(8,128)S(1)} %scatter.54, f32[5,4,1,128]{3,2,1,0:T(1,128)S(1)} %collective-permute-done.9, s32[]{:T(128)} %constant.358.clone.1, s32[]{:T(128)} %constant.359.clone.1, s32[]{:T(128)} %constant.360.clone.1, s32[]{:T(128)} %constant.359.clone.1) | dynamic-update-slice | bytes 20484 | tf_op jit(solution)/shard_map/scatter | solution.py:23
  76.3 3.1 %scatter.59 = f32[5,6,6,130]{3,2,1,0:T(8,128)S(1)} dynamic-update-slice(f32[5,6,6,130]{3,2,1,0:T(8,128)S(1)} %scatter.56, f32[5,4,4,1]{3,2,1,0:T(4,128)S(1)} %collective-permute-done.11, s32[]{:T(128)} %constant.358.clone.1, s32[]{:T(128)} %constant.359.clone.1, s32[]{:T(128)} %constant.359.clone.1, s32[]{:T(128)} %constant.361.clone.1) | dynamic-update-slice | bytes 644 | tf_op jit(solution)/shard_map/scatter | solution.py:23
  79.7 2.4 %convolution_bitcast_fusion = f32[3,16384,16]{1,2,0:T(8,128)S(1)} fusion(s32[16384]{0:T(1024)S(1)} %get-tuple-element.147, bf16[1,128,16]{1,2,0:T(8,128)(2,1)S(1)} %get-tuple-element.168, bf16[1,128,16]{1,2,0:T(8,128)(2,1)S(1)} %get-tuple-element.167, bf16[1,128,16]{1,2,0:T(8,128)(2,1)S(1)} %get-tuple-element.166), kind=kOutput, calls=%fused_computation | convolution fusion | flops 203436032 | bytes 3223552 | tf_op jit(solution)/shard_map/fd,kdp->kfp/dot_general | solution.py:77
  82.5 10.3 %all_to_all.10 = f32[1,128,128]{2,0,1:T(1,128)S(1)} all-to-all(f32[1,128,128]{2,0,1:T(1,128)S(1)} %bitcast.77), channel_id=1, replica_groups=mesh['stream'=4,'cross'=2,'gore'=4] {'stream','cross'}, dimensions={1} | all-to-all | bytes 131072 | tf_op jit(solution)/shard_map/all_to_all | solution.py:157
  (51 shorter events, 12.9 us)
Async XLA Ops:
  6.2 36.9 %all-to-all-start = ((f32[6,128,128]{2,0,1:T(8,128)}), f32[6,128,128]{2,0,1:T(8,128)S(1)}, u32[]{:S(2)}, u32[]{:S(2)}) async-start(f32[6,128,128]{2,0,1:T(8,128)} %copy.11), calls=%async_computation | async-start | bytes 1048576 | tf_op jit(solution)/shard_map/all_to_all | solution.py:128
  12.2 13.3 %collective-permute-start = (f32[6,1,4,128]{3,2,1,0:T(4,128)S(1)}, f32[6,1,4,128]{3,2,1,0:T(4,128)S(1)}, u32[]{:S(2)}, u32[]{:S(2)}) collective-permute-start(f32[6,1,4,128]{3,2,1,0:T(4,128)S(1)} %get-tuple-element.159), channel_id=1, source_target_pairs={{0,8},{8,16},{16,24},{1,9},{9,17},{17,25},{2,10},{10,18},{18,26},{... | collective-permute-start | bytes 36872 | tf_op jit(solution)/shard_map/ppermute | solution.py:17
  15.8 13.2 %collective-permute-start.1 = (f32[6,1,4,128]{3,2,1,0:T(4,128)S(1)}, f32[6,1,4,128]{3,2,1,0:T(4,128)S(1)}, u32[]{:S(2)}, u32[]{:S(2)}) collective-permute-start(f32[6,1,4,128]{3,2,1,0:T(4,128)S(1)} %get-tuple-element.158), channel_id=1, source_target_pairs={{8,0},{16,8},{24,16},{9,1},{17,9},{25,17},{10,2},{18,10},{26,18},{... | collective-permute-start | bytes 36872 | tf_op jit(solution)/shard_map/ppermute | solution.py:18
  17.7 13.4 %collective-permute-start.2 = (f32[6,4,1,128]{3,2,1,0:T(1,128)S(1)}, f32[6,4,1,128]{3,2,1,0:T(1,128)S(1)}, u32[]{:S(2)}, u32[]{:S(2)}) collective-permute-start(f32[6,4,1,128]{3,2,1,0:T(1,128)S(1)} %get-tuple-element.157), channel_id=1, source_target_pairs={{0,4},{1,5},{2,6},{3,7},{8,12},{9,13},{10,14},{11,15},{16,20},{17,... | collective-permute-start | bytes 36872 | tf_op jit(solution)/shard_map/ppermute | solution.py:17
  20.8 14.1 %collective-permute-start.3 = (f32[6,4,1,128]{3,2,1,0:T(1,128)S(1)}, f32[6,4,1,128]{3,2,1,0:T(1,128)S(1)}, u32[]{:S(2)}, u32[]{:S(2)}) collective-permute-start(f32[6,4,1,128]{3,2,1,0:T(1,128)S(1)} %get-tuple-element.156), channel_id=1, source_target_pairs={{4,0},{5,1},{6,2},{7,3},{12,8},{13,9},{14,10},{15,11},{20,16},{21,... | collective-permute-start | bytes 36872 | tf_op jit(solution)/shard_map/ppermute | solution.py:18
  22.2 16.5 %collective-permute-start.4 = (f32[6,4,4,1]{3,2,1,0:T(4,128)S(1)}, f32[6,4,4,1]{3,2,1,0:T(4,128)S(1)}, u32[]{:S(2)}, u32[]{:S(2)}) collective-permute-start(f32[6,4,4,1]{3,2,1,0:T(4,128)S(1)} %get-tuple-element.155), channel_id=1, source_target_pairs={{0,1},{1,2},{2,3},{4,5},{5,6},{6,7},{8,9},{9,10},{10,11},{12,13},{... | collective-permute-start | bytes 1160 | tf_op jit(solution)/shard_map/ppermute | solution.py:17
  25.6 13.7 %collective-permute-start.5 = (f32[6,4,4,1]{3,2,1,0:T(4,128)S(1)}, f32[6,4,4,1]{3,2,1,0:T(4,128)S(1)}, u32[]{:S(2)}, u32[]{:S(2)}) collective-permute-start(f32[6,4,4,1]{3,2,1,0:T(4,128)S(1)} %get-tuple-element.154), channel_id=1, source_target_pairs={{1,0},{2,1},{3,2},{5,4},{6,5},{7,6},{9,8},{10,9},{11,10},{13,12},{... | collective-permute-start | bytes 1160 | tf_op jit(solution)/shard_map/ppermute | solution.py:18
  48.2 16.2 %collective-permute-start.6 = (f32[5,1,4,128]{3,2,1,0:T(4,128)S(1)}, f32[5,1,4,128]{3,2,1,0:T(4,128)S(1)}, u32[]{:S(2)}, u32[]{:S(2)}) collective-permute-start(f32[5,1,4,128]{3,2,1,0:T(4,128)S(1)} %get-tuple-element.165), channel_id=1, source_target_pairs={{0,8},{8,16},{16,24},{1,9},{9,17},{17,25},{2,10},{10,18},{18,26},{... | collective-permute-start | bytes 30728 | tf_op jit(solution)/shard_map/ppermute | solution.py:17
  52.4 15.3 %collective-permute-start.7 = (f32[5,1,4,128]{3,2,1,0:T(4,128)S(1)}, f32[5,1,4,128]{3,2,1,0:T(4,128)S(1)}, u32[]{:S(2)}, u32[]{:S(2)}) collective-permute-start(f32[5,1,4,128]{3,2,1,0:T(4,128)S(1)} %get-tuple-element.164), channel_id=1, source_target_pairs={{8,0},{16,8},{24,16},{9,1},{17,9},{25,17},{10,2},{18,10},{26,18},{... | collective-permute-start | bytes 30728 | tf_op jit(solution)/shard_map/ppermute | solution.py:18
  54.3 15.2 %collective-permute-start.8 = (f32[5,4,1,128]{3,2,1,0:T(1,128)S(1)}, f32[5,4,1,128]{3,2,1,0:T(1,128)S(1)}, u32[]{:S(2)}, u32[]{:S(2)}) collective-permute-start(f32[5,4,1,128]{3,2,1,0:T(1,128)S(1)} %get-tuple-element.163), channel_id=1, source_target_pairs={{0,4},{1,5},{2,6},{3,7},{8,12},{9,13},{10,14},{11,15},{16,20},{17,... | collective-permute-start | bytes 30728 | tf_op jit(solution)/shard_map/ppermute | solution.py:17
  58.6 14.1 %collective-permute-start.9 = (f32[5,4,1,128]{3,2,1,0:T(1,128)S(1)}, f32[5,4,1,128]{3,2,1,0:T(1,128)S(1)}, u32[]{:S(2)}, u32[]{:S(2)}) collective-permute-start(f32[5,4,1,128]{3,2,1,0:T(1,128)S(1)} %get-tuple-element.162), channel_id=1, source_target_pairs={{4,0},{5,1},{6,2},{7,3},{12,8},{13,9},{14,10},{15,11},{20,16},{21,... | collective-permute-start | bytes 30728 | tf_op jit(solution)/shard_map/ppermute | solution.py:18
  60.1 15.8 %collective-permute-start.10 = (f32[5,4,4,1]{3,2,1,0:T(4,128)S(1)}, f32[5,4,4,1]{3,2,1,0:T(4,128)S(1)}, u32[]{:S(2)}, u32[]{:S(2)}) collective-permute-start(f32[5,4,4,1]{3,2,1,0:T(4,128)S(1)} %get-tuple-element.161), channel_id=1, source_target_pairs={{0,1},{1,2},{2,3},{4,5},{5,6},{6,7},{8,9},{9,10},{10,11},{12,13},{... | collective-permute-start | bytes 968 | tf_op jit(solution)/shard_map/ppermute | solution.py:17
  64.4 11.9 %collective-permute-start.11 = (f32[5,4,4,1]{3,2,1,0:T(4,128)S(1)}, f32[5,4,4,1]{3,2,1,0:T(4,128)S(1)}, u32[]{:S(2)}, u32[]{:S(2)}) collective-permute-start(f32[5,4,4,1]{3,2,1,0:T(4,128)S(1)} %get-tuple-element.160), channel_id=1, source_target_pairs={{1,0},{2,1},{3,2},{5,4},{6,5},{7,6},{9,8},{10,9},{11,10},{13,12},{... | collective-permute-start | bytes 968 | tf_op jit(solution)/shard_map/ppermute | solution.py:18
  79.7 14.0 %copy-start = (f32[5,4,4,128]{3,2,1,0:T(4,128)}, f32[5,4,4,128]{3,2,1,0:T(4,128)S(1)}, u32[]{:S(2)}) copy-start(f32[5,4,4,128]{3,2,1,0:T(4,128)S(1)} %fusion.23) | copy-start | bytes 122884

commit v2 on v1

--- a/solution.py
+++ b/solution.py
@@ -8,7 +8,7 @@
 
 
 def face_halo(block):
-    padded = jnp.pad(block, ((0, 0), (1, 1), (1, 1), (1, 1)))
+    wide = block
     for axis, dim in SIDES:
         count = lax.axis_size(axis)
         forward = [(i, i + 1) for i in range(count - 1)]
@@ -16,12 +16,9 @@
         extent = block.shape[dim]
         low = lax.ppermute(lax.slice_in_dim(block, extent - 1, None, axis=dim), axis, forward)
         high = lax.ppermute(lax.slice_in_dim(block, 0, 1, axis=dim), axis, backward)
-        low_at = [slice(None)] + [slice(1, -1)] * 3
-        high_at = list(low_at)
-        low_at[dim] = slice(0, 1)
-        high_at[dim] = slice(extent + 1, extent + 2)
-        padded = padded.at[tuple(low_at)].set(low).at[tuple(high_at)].set(high)
-    return padded
+        widths = [(0, 0)] + [(1, 1) if d < dim else (0, 0) for d in range(1, 4)]
+        wide = jnp.concatenate([jnp.pad(low, widths), wide, jnp.pad(high, widths)], axis=dim)
+    return wide
 
 
 def harmonic(first_visc, second_visc):

time: 94.7 us -> 67.8 us (0.72)
  local copies, waits for them, and re-layouts: 31.1 us -> 1.46 us
  waiting for transfers between devices: 0.03 us -> 4.43 us
  blocking collectives: 10.3 us -> 7.52 us
  other arithmetic: 6.14 us -> 7.19 us
    scatter x12 -> x0, local copies, waits for them, and re-layouts: 29.5 us -> none  [face_halo(): padded = padded.at[tuple(low_at)].set(low).at[tuple(high_at)].set(high)]
    ppermute x6, waiting for transfers between devices: 0.02 us -> 3.83 us  [face_halo(): high = lax.ppermute(lax.slice_in_dim(block, 0, 1, axis=dim), axis, backward)]
    all_to_all x1, blocking collectives: 10.3 us -> 7.52 us  [shards(): lax.all_to_all(face_pressure.reshape(1, slot_total, row_count), ('stream'...]
    ppermute x6, starting transfers between devices: 9.19 us -> 10.4 us  [face_halo(): high = lax.ppermute(lax.slice_in_dim(block, 0, 1, axis=dim), axis, backward)]
    ppermute x6, starting transfers between devices: 22.6 us -> 21.4 us  [face_halo(): lax.ppermute(lax.slice_in_dim(block, extent - 1, None, axis=dim), axis, f...]
  transfers between devices with their start and end apart: 13 -> 13, of which waited for: 0 -> 2; matrix products, arithmetic and copies ran while one was open for 30% -> 3% of each run, Pallas kernels for 0% -> 0%
where the time goes in v2:
time: 67.8 us; the launch traced here: 66.7 us
  starting transfers between devices  37 us (55%)
  matrix products  7.97 us (12%)
  blocking collectives  7.52 us (11%)
  other arithmetic  7.19 us (11%)
  waiting for transfers between devices  4.43 us (7%)
  local copies, waits for them, and re-layouts  1.46 us (2%)
  between operations  1.08 us (2%)
    ppermute x6, starting transfers between devices, face_halo(): lax.ppermute(lax.slice_in_dim(block, extent - 1, None, axis=dim), axis, f...  21.4 us
    ppermute x6, starting transfers between devices, face_halo(): high = lax.ppermute(lax.slice_in_dim(block, 0, 1, axis=dim), axis, backward)  10.4 us
    all_to_all x1, blocking collectives, shards(): lax.all_to_all(face_pressure.reshape(1, slot_total, row_count), ('stream'...  7.52 us
    all_to_all x1, starting transfers between devices, shards(): lax.all_to_all(outbound, ('stream', 'cross'), split_axis=1, concat_axis=1...  5.22 us
    dot_general x1, matrix products, shards(): jnp.einsum('cpf,fd->cpd', spread, depth_hot.astype(jnp.float32), precisio...  3.97 us
    ppermute x6, waiting for transfers between devices, face_halo(): high = lax.ppermute(lax.slice_in_dim(block, 0, 1, axis=dim), axis, backward)  3.83 us
    dot_general x1, matrix products, exact_dot(): jnp.einsum(left + ',k' + right + '->k' + output, onehot, stacked, preferr...  2.4 us
    concatenate x2, other arithmetic, shards(): state_visc = face_halo(jnp.concatenate([fluid_state, viscosity[None]], 0))  1.67 us
  transfers between devices with their start and end apart: 13, of which 2 were waited for; matrix products, arithmetic and copies ran while one was open for 3% of the time, Pallas kernels for 0%

profile of v2, /device:TPU:1, one launch (start us, length us, event | category | flops | bytes accessed | tf_op | source)
XLA Modules:
  0.0 66.7 jit_solution(9919858535621362687)
XLA Ops:
  0.6 0.7 %iota_compare_fusion.6 = pred[64,128]{1,0:T(8,128)(4,1)S(1)} fusion(s32[64]{0:T(128)} %param.13), kind=kLoop, calls=%fused_computation.145 | loop fusion | flops 8192 | bytes 8448 | tf_op jit(solution)/shard_map/lt | solution.py:96
  1.4 1.0 %broadcast_select_fusion = f32[8,64,128]{2,1,0:T(8,128)S(1)} fusion(f32[8,64,128]{2,1,0:T(8,128)} %param.10, pred[64,128]{1,0:T(8,128)(4,1)S(1)} %iota_compare_fusion.6), kind=kLoop, calls=%fused_computation.31 | loop fusion | flops 65536 | bytes 532480 | tf_op jit(solution)/shard_map/jit(_where)/select_n | solution.py:97
  2.4 0.8 %convert_bitcast_fusion = f32[1,64,128]{2,1,0:T(8,128)S(1)} fusion(s32[64,128]{1,0:T(8,128)} %param.11), kind=kLoop, calls=%fused_computation.144 | loop fusion | flops 8192 | bytes 65536 | tf_op jit(solution)/shard_map/broadcast_in_dim | solution.py:118
  3.1 0.9 %fusion.10 = f32[64]{0:T(128)S(1)} fusion(s32[64]{0:T(128)} %bitcast.87), kind=kOutput, calls=%fused_computation.12 | convolution fusion | flops 71616 | bytes 512 | tf_op jit(solution)/shard_map/dot_general | solution.py:106
  5.2 1.0 %copy.11 = f32[6,128,128]{2,0,1:T(8,128)} copy(f32[6,128,128]{1,2,0:T(8,128)S(1)} %convolution_bitcast_fusion.1) | data formatting | bytes 786432 | tf_op jit(solution)/shard_map/ts,ctr->csr/transpose | solution.py:122
  6.2 5.2 %all-to-all-start = ((f32[6,128,128]{2,0,1:T(8,128)}), f32[6,128,128]{2,0,1:T(8,128)S(1)}, u32[]{:S(2)}, u32[]{:S(2)}) async-start(f32[6,128,128]{2,0,1:T(8,128)} %copy.11), calls=%async_computation | async-start | bytes 1048576 | tf_op jit(solution)/shard_map/all_to_all | solution.py:125
  11.4 0.8 %pad_maximum_fusion.6 = f32[6,4,4,128]{3,2,1,0:T(4,128)S(1)} fusion(f32[1,4,4,128]{3,2,1,0:T(4,128)} %bitcast.80, f32[4,4,4,128]{3,2,1,0:T(4,128)} %param.8, f32[1,4,4,128]{3,2,1,0:T(4,128)} %bitcast.83), kind=kLoop, calls=%fused_computation.49 | loop fusion | flops 24576 | bytes 98304 | tf_op jit(solution)/shard_map/concatenate | solution.py:92
  12.3 3.3 %collective-permute-start.1 = (f32[6,4,1,128]{3,2,1,0:T(1,128)S(1)}, f32[6,4,1,128]{3,2,1,0:T(1,128)S(1)}, u32[]{:S(2)}, u32[]{:S(2)}) collective-permute-start(f32[6,4,1,128]{3,2,1,0:T(1,128)S(1)} %get-tuple-element.13), channel_id=1, source_target_pairs={{0,4},{1,5},{2,6},{3,7},{8,12},{9,13},{10,14},{11,15},{16,20},{17,... | collective-permute-start | bytes 36872 | tf_op jit(solution)/shard_map/ppermute | solution.py:17
  15.6 1.3 %collective-permute-start.5 = (f32[6,4,4,1]{3,2,1,0:T(4,128)S(1)}, f32[6,4,4,1]{3,2,1,0:T(4,128)S(1)}, u32[]{:S(2)}, u32[]{:S(2)}) collective-permute-start(f32[6,4,4,1]{3,2,1,0:T(4,128)S(1)} %get-tuple-element.11), channel_id=1, source_target_pairs={{1,0},{2,1},{3,2},{5,4},{6,5},{7,6},{9,8},{10,9},{11,10},{13,12},{... | collective-permute-start | bytes 1160 | tf_op jit(solution)/shard_map/ppermute | solution.py:18
  17.0 2.5 %collective-permute-start.3 = (f32[6,1,4,128]{3,2,1,0:T(4,128)S(1)}, f32[6,1,4,128]{3,2,1,0:T(4,128)S(1)}, u32[]{:S(2)}, u32[]{:S(2)}) collective-permute-start(f32[6,1,4,128]{3,2,1,0:T(4,128)S(1)} %get-tuple-element.15), channel_id=1, source_target_pairs={{8,0},{16,8},{24,16},{9,1},{17,9},{25,17},{10,2},{18,10},{26,18},{... | collective-permute-start | bytes 36872 | tf_op jit(solution)/shard_map/ppermute | solution.py:18
  19.5 3.0 %collective-permute-start.2 = (f32[6,1,4,128]{3,2,1,0:T(4,128)S(1)}, f32[6,1,4,128]{3,2,1,0:T(4,128)S(1)}, u32[]{:S(2)}, u32[]{:S(2)}) collective-permute-start(f32[6,1,4,128]{3,2,1,0:T(4,128)S(1)} %get-tuple-element.14), channel_id=1, source_target_pairs={{0,8},{8,16},{16,24},{1,9},{9,17},{17,25},{2,10},{10,18},{18,26},{... | collective-permute-start | bytes 36872 | tf_op jit(solution)/shard_map/ppermute | solution.py:17
  22.5 1.3 %collective-permute-start.4 = (f32[6,4,1,128]{3,2,1,0:T(1,128)S(1)}, f32[6,4,1,128]{3,2,1,0:T(1,128)S(1)}, u32[]{:S(2)}, u32[]{:S(2)}) collective-permute-start(f32[6,4,1,128]{3,2,1,0:T(1,128)S(1)} %get-tuple-element.12), channel_id=1, source_target_pairs={{4,0},{5,1},{6,2},{7,3},{12,8},{13,9},{14,10},{15,11},{20,16},{21,... | collective-permute-start | bytes 36872 | tf_op jit(solution)/shard_map/ppermute | solution.py:18
  23.8 4.2 %collective-permute-start = (f32[6,4,4,1]{3,2,1,0:T(4,128)S(1)}, f32[6,4,4,1]{3,2,1,0:T(4,128)S(1)}, u32[]{:S(2)}, u32[]{:S(2)}) collective-permute-start(f32[6,4,4,1]{3,2,1,0:T(4,128)S(1)} %get-tuple-element.10), channel_id=1, source_target_pairs={{0,1},{1,2},{2,3},{4,5},{5,6},{6,7},{8,9},{9,10},{10,11},{12,13},{... | collective-permute-start | bytes 1160 | tf_op jit(solution)/shard_map/ppermute | solution.py:17
  28.1 0.9 %pad_maximum_fusion = f32[6,6,6,130]{3,2,1,0:T(8,128)S(1)} fusion(f32[1,4,4,128]{3,2,1,0:T(4,128)} %bitcast.81, f32[4,4,4,128]{3,2,1,0:T(4,128)} %param.8, f32[1,4,4,128]{3,2,1,0:T(4,128)} %bitcast.84), kind=kLoop, calls=%fused_computation.21 | loop fusion | flops 56160 | bytes 161472 | tf_op jit(solution)/shard_map/concatenate | solution.py:92
  30.8 4.0 %fusion.2 = f32[5,16,128]{2,1,0:T(8,128)S(1)} fusion(s32[16384]{0:T(1024)S(1)} %get-tuple-element.3, f32[5,16,16384]{2,1,0:T(8,128)S(1)} %fusion.121), kind=kOutput, calls=%fused_computation.3 | convolution fusion | flops 2015363072 | bytes 5349376 | tf_op jit(solution)/shard_map/cpf,fd->cpd/dot_general | solution.py:135
  35.1 1.3 %collective-permute-start.8 = (f32[5,4,1,128]{3,2,1,0:T(1,128)S(1)}, f32[5,4,1,128]{3,2,1,0:T(1,128)S(1)}, u32[]{:S(2)}, u32[]{:S(2)}) collective-permute-start(f32[5,4,1,128]{3,2,1,0:T(1,128)S(1)} %get-tuple-element.21), channel_id=1, source_target_pairs={{4,0},{5,1},{6,2},{7,3},{12,8},{13,9},{14,10},{15,11},{20,16},{21,... | collective-permute-start | bytes 30728 | tf_op jit(solution)/shard_map/ppermute | solution.py:18
  36.4 4.0 %collective-permute-start.9 = (f32[5,4,1,128]{3,2,1,0:T(1,128)S(1)}, f32[5,4,1,128]{3,2,1,0:T(1,128)S(1)}, u32[]{:S(2)}, u32[]{:S(2)}) collective-permute-start(f32[5,4,1,128]{3,2,1,0:T(1,128)S(1)} %get-tuple-element.20), channel_id=1, source_target_pairs={{0,4},{1,5},{2,6},{3,7},{8,12},{9,13},{10,14},{11,15},{16,20},{17,... | collective-permute-start | bytes 30728 | tf_op jit(solution)/shard_map/ppermute | solution.py:17
  40.3 2.7 %collective-permute-start.6 = (f32[5,1,4,128]{3,2,1,0:T(4,128)S(1)}, f32[5,1,4,128]{3,2,1,0:T(4,128)S(1)}, u32[]{:S(2)}, u32[]{:S(2)}) collective-permute-start(f32[5,1,4,128]{3,2,1,0:T(4,128)S(1)} %get-tuple-element.19), channel_id=1, source_target_pairs={{8,0},{16,8},{24,16},{9,1},{17,9},{25,17},{10,2},{18,10},{26,18},{... | collective-permute-start | bytes 30728 | tf_op jit(solution)/shard_map/ppermute | solution.py:18
  43.0 2.9 %collective-permute-start.7 = (f32[5,1,4,128]{3,2,1,0:T(4,128)S(1)}, f32[5,1,4,128]{3,2,1,0:T(4,128)S(1)}, u32[]{:S(2)}, u32[]{:S(2)}) collective-permute-start(f32[5,1,4,128]{3,2,1,0:T(4,128)S(1)} %get-tuple-element.18), channel_id=1, source_target_pairs={{0,8},{8,16},{16,24},{1,9},{9,17},{17,25},{2,10},{10,18},{18,26},{... | collective-permute-start | bytes 30728 | tf_op jit(solution)/shard_map/ppermute | solution.py:17
  46.0 4.0 %collective-permute-start.11 = (f32[5,4,4,1]{3,2,1,0:T(4,128)S(1)}, f32[5,4,4,1]{3,2,1,0:T(4,128)S(1)}, u32[]{:S(2)}, u32[]{:S(2)}) collective-permute-start(f32[5,4,4,1]{3,2,1,0:T(4,128)S(1)} %get-tuple-element.17), channel_id=1, source_target_pairs={{0,1},{1,2},{2,3},{4,5},{5,6},{6,7},{8,9},{9,10},{10,11},{12,13},{... | collective-permute-start | bytes 968 | tf_op jit(solution)/shard_map/ppermute | solution.py:17
  50.0 1.3 %collective-permute-start.10 = (f32[5,4,4,1]{3,2,1,0:T(4,128)S(1)}, f32[5,4,4,1]{3,2,1,0:T(4,128)S(1)}, u32[]{:S(2)}, u32[]{:S(2)}) collective-permute-start(f32[5,4,4,1]{3,2,1,0:T(4,128)S(1)} %get-tuple-element.16), channel_id=1, source_target_pairs={{1,0},{2,1},{3,2},{5,4},{6,5},{7,6},{9,8},{10,9},{11,10},{13,12},{... | collective-permute-start | bytes 968 | tf_op jit(solution)/shard_map/ppermute | solution.py:18
  51.4 3.8 %collective-permute-done.10 = f32[5,4,4,1]{3,2,1,0:T(4,128)S(1)} collective-permute-done((f32[5,4,4,1]{3,2,1,0:T(4,128)S(1)}, f32[5,4,4,1]{3,2,1,0:T(4,128)S(1)}, u32[]{:S(2)}, u32[]{:S(2)}) %collective-permute-start.10) | collective-permute-done | bytes 352 | tf_op jit(solution)/shard_map/ppermute | solution.py:18
  55.5 2.4 %convolution_bitcast_fusion = f32[3,16384,16]{1,2,0:T(8,128)S(1)} fusion(s32[16384]{0:T(1024)S(1)} %get-tuple-element.3, bf16[1,128,16]{1,2,0:T(8,128)(2,1)S(1)} %get-tuple-element.24, bf16[1,128,16]{1,2,0:T(8,128)(2,1)S(1)} %get-tuple-element.23, bf16[1,128,16]{1,2,0:T(8,128)(2,1)S(1)} %get-tuple-element.22), kind=kOutput, calls=%fused_computation | convolution fusion | flops 203436032 | bytes 3223552 | tf_op jit(solution)/shard_map/fd,kdp->kfp/dot_general | solution.py:74
  58.3 7.5 %all_to_all.10 = f32[1,128,128]{2,0,1:T(1,128)S(1)} all-to-all(f32[1,128,128]{2,0,1:T(1,128)S(1)} %bitcast.77), channel_id=1, replica_groups=mesh['stream'=4,'cross'=2,'gore'=4] {'stream','cross'}, dimensions={1} | all-to-all | bytes 131072 | tf_op jit(solution)/shard_map/all_to_all | solution.py:154
  (50 shorter events, 4.8 us)
Async XLA Ops:
  6.2 23.7 %all-to-all-start = ((f32[6,128,128]{2,0,1:T(8,128)}), f32[6,128,128]{2,0,1:T(8,128)S(1)}, u32[]{:S(2)}, u32[]{:S(2)}) async-start(f32[6,128,128]{2,0,1:T(8,128)} %copy.11), calls=%async_computation | async-start | bytes 1048576 | tf_op jit(solution)/shard_map/all_to_all | solution.py:125
  12.3 17.4 %collective-permute-start.1 = (f32[6,4,1,128]{3,2,1,0:T(1,128)S(1)}, f32[6,4,1,128]{3,2,1,0:T(1,128)S(1)}, u32[]{:S(2)}, u32[]{:S(2)}) collective-permute-start(f32[6,4,1,128]{3,2,1,0:T(1,128)S(1)} %get-tuple-element.13), channel_id=1, source_target_pairs={{0,4},{1,5},{2,6},{3,7},{8,12},{9,13},{10,14},{11,15},{16,20},{17,... | collective-permute-start | bytes 36872 | tf_op jit(solution)/shard_map/ppermute | solution.py:17
  15.6 8.2 %collective-permute-start.5 = (f32[6,4,4,1]{3,2,1,0:T(4,128)S(1)}, f32[6,4,4,1]{3,2,1,0:T(4,128)S(1)}, u32[]{:S(2)}, u32[]{:S(2)}) collective-permute-start(f32[6,4,4,1]{3,2,1,0:T(4,128)S(1)} %get-tuple-element.11), channel_id=1, source_target_pairs={{1,0},{2,1},{3,2},{5,4},{6,5},{7,6},{9,8},{10,9},{11,10},{13,12},{... | collective-permute-start | bytes 1160 | tf_op jit(solution)/shard_map/ppermute | solution.py:18
  17.0 12.7 %collective-permute-start.3 = (f32[6,1,4,128]{3,2,1,0:T(4,128)S(1)}, f32[6,1,4,128]{3,2,1,0:T(4,128)S(1)}, u32[]{:S(2)}, u32[]{:S(2)}) collective-permute-start(f32[6,1,4,128]{3,2,1,0:T(4,128)S(1)} %get-tuple-element.15), channel_id=1, source_target_pairs={{8,0},{16,8},{24,16},{9,1},{17,9},{25,17},{10,2},{18,10},{26,18},{... | collective-permute-start | bytes 36872 | tf_op jit(solution)/shard_map/ppermute | solution.py:18
  19.5 10.2 %collective-permute-start.2 = (f32[6,1,4,128]{3,2,1,0:T(4,128)S(1)}, f32[6,1,4,128]{3,2,1,0:T(4,128)S(1)}, u32[]{:S(2)}, u32[]{:S(2)}) collective-permute-start(f32[6,1,4,128]{3,2,1,0:T(4,128)S(1)} %get-tuple-element.14), channel_id=1, source_target_pairs={{0,8},{8,16},{16,24},{1,9},{9,17},{17,25},{2,10},{10,18},{18,26},{... | collective-permute-start | bytes 36872 | tf_op jit(solution)/shard_map/ppermute | solution.py:17
  22.5 7.1 %collective-permute-start.4 = (f32[6,4,1,128]{3,2,1,0:T(1,128)S(1)}, f32[6,4,1,128]{3,2,1,0:T(1,128)S(1)}, u32[]{:S(2)}, u32[]{:S(2)}) collective-permute-start(f32[6,4,1,128]{3,2,1,0:T(1,128)S(1)} %get-tuple-element.12), channel_id=1, source_target_pairs={{4,0},{5,1},{6,2},{7,3},{12,8},{13,9},{14,10},{15,11},{20,16},{21,... | collective-permute-start | bytes 36872 | tf_op jit(solution)/shard_map/ppermute | solution.py:18
  23.8 5.8 %collective-permute-start = (f32[6,4,4,1]{3,2,1,0:T(4,128)S(1)}, f32[6,4,4,1]{3,2,1,0:T(4,128)S(1)}, u32[]{:S(2)}, u32[]{:S(2)}) collective-permute-start(f32[6,4,4,1]{3,2,1,0:T(4,128)S(1)} %get-tuple-element.10), channel_id=1, source_target_pairs={{0,1},{1,2},{2,3},{4,5},{5,6},{6,7},{8,9},{9,10},{10,11},{12,13},{... | collective-permute-start | bytes 1160 | tf_op jit(solution)/shard_map/ppermute | solution.py:17
  30.3 4.5 %copy-start = (f32[4,4,4,128]{3,2,1,0:T(4,128)S(1)}, f32[4,4,4,128]{3,2,1,0:T(4,128)}, u32[]{:S(2)}) copy-start(f32[4,4,4,128]{3,2,1,0:T(4,128)} %param.8) | copy-start | bytes 98308
  30.3 4.5 %copy-start.2 = (f32[4,4,128]{2,1,0:T(4,128)S(1)}, f32[4,4,128]{2,1,0:T(4,128)}, u32[]{:S(2)}) copy-start(f32[4,4,128]{2,1,0:T(4,128)} %param.9) | copy-start | bytes 24580
  30.3 4.5 %copy-start.3 = (f32[4,4,128]{2,1,0:T(4,128)S(1)}, f32[4,4,128]{2,1,0:T(4,128)}, u32[]{:S(2)}) copy-start(f32[4,4,128]{2,1,0:T(4,128)} %param.7) | copy-start | bytes 24580
  35.1 14.9 %collective-permute-start.8 = (f32[5,4,1,128]{3,2,1,0:T(1,128)S(1)}, f32[5,4,1,128]{3,2,1,0:T(1,128)S(1)}, u32[]{:S(2)}, u32[]{:S(2)}) collective-permute-start(f32[5,4,1,128]{3,2,1,0:T(1,128)S(1)} %get-tuple-element.21), channel_id=1, source_target_pairs={{4,0},{5,1},{6,2},{7,3},{12,8},{13,9},{14,10},{15,11},{20,16},{21,... | collective-permute-start | bytes 30728 | tf_op jit(solution)/shard_map/ppermute | solution.py:18
  36.4 15.0 %collective-permute-start.9 = (f32[5,4,1,128]{3,2,1,0:T(1,128)S(1)}, f32[5,4,1,128]{3,2,1,0:T(1,128)S(1)}, u32[]{:S(2)}, u32[]{:S(2)}) collective-permute-start(f32[5,4,1,128]{3,2,1,0:T(1,128)S(1)} %get-tuple-element.20), channel_id=1, source_target_pairs={{0,4},{1,5},{2,6},{3,7},{8,12},{9,13},{10,14},{11,15},{16,20},{17,... | collective-permute-start | bytes 30728 | tf_op jit(solution)/shard_map/ppermute | solution.py:17
  40.3 14.8 %collective-permute-start.6 = (f32[5,1,4,128]{3,2,1,0:T(4,128)S(1)}, f32[5,1,4,128]{3,2,1,0:T(4,128)S(1)}, u32[]{:S(2)}, u32[]{:S(2)}) collective-permute-start(f32[5,1,4,128]{3,2,1,0:T(4,128)S(1)} %get-tuple-element.19), channel_id=1, source_target_pairs={{8,0},{16,8},{24,16},{9,1},{17,9},{25,17},{10,2},{18,10},{26,18},{... | collective-permute-start | bytes 30728 | tf_op jit(solution)/shard_map/ppermute | solution.py:18
  43.0 12.2 %collective-permute-start.7 = (f32[5,1,4,128]{3,2,1,0:T(4,128)S(1)}, f32[5,1,4,128]{3,2,1,0:T(4,128)S(1)}, u32[]{:S(2)}, u32[]{:S(2)}) collective-permute-start(f32[5,1,4,128]{3,2,1,0:T(4,128)S(1)} %get-tuple-element.18), channel_id=1, source_target_pairs={{0,8},{8,16},{16,24},{1,9},{9,17},{17,25},{2,10},{10,18},{18,26},{... | collective-permute-start | bytes 30728 | tf_op jit(solution)/shard_map/ppermute | solution.py:17
  46.0 5.3 %collective-permute-start.11 = (f32[5,4,4,1]{3,2,1,0:T(4,128)S(1)}, f32[5,4,4,1]{3,2,1,0:T(4,128)S(1)}, u32[]{:S(2)}, u32[]{:S(2)}) collective-permute-start(f32[5,4,4,1]{3,2,1,0:T(4,128)S(1)} %get-tuple-element.17), channel_id=1, source_target_pairs={{0,1},{1,2},{2,3},{4,5},{5,6},{6,7},{8,9},{9,10},{10,11},{12,13},{... | collective-permute-start | bytes 968 | tf_op jit(solution)/shard_map/ppermute | solution.py:17
  50.0 5.2 %collective-permute-start.10 = (f32[5,4,4,1]{3,2,1,0:T(4,128)S(1)}, f32[5,4,4,1]{3,2,1,0:T(4,128)S(1)}, u32[]{:S(2)}, u32[]{:S(2)}) collective-permute-start(f32[5,4,4,1]{3,2,1,0:T(4,128)S(1)} %get-tuple-element.16), channel_id=1, source_target_pairs={{1,0},{2,1},{3,2},{5,4},{6,5},{7,6},{9,8},{10,9},{11,10},{13,12},{... | collective-permute-start | bytes 968 | tf_op jit(solution)/shard_map/ppermute | solution.py:18
  55.4 11.2 %copy-start.1 = (f32[5,4,4,128]{3,2,1,0:T(4,128)}, f32[5,4,4,128]{3,2,1,0:T(4,128)S(1)}, u32[]{:S(2)}) copy-start(f32[5,4,4,128]{3,2,1,0:T(4,128)S(1)} %fusion.42) | copy-start | bytes 122884

commit v3 on v2

--- a/solution.py
+++ b/solution.py
@@ -11,11 +11,20 @@
     wide = block
     for axis, dim in SIDES:
         count = lax.axis_size(axis)
-        forward = [(i, i + 1) for i in range(count - 1)]
-        backward = [(target, source) for source, target in forward]
+        index = lax.axis_index(axis)
+        odd = index % 2 == 1
         extent = block.shape[dim]
-        low = lax.ppermute(lax.slice_in_dim(block, extent - 1, None, axis=dim), axis, forward)
-        high = lax.ppermute(lax.slice_in_dim(block, 0, 1, axis=dim), axis, backward)
+        last = lax.slice_in_dim(block, extent - 1, None, axis=dim)
+        first = lax.slice_in_dim(block, 0, 1, axis=dim)
+        pairs_a = [(i, i ^ 1) for i in range(count) if (i ^ 1) < count]
+        pairs_b = [(i, j) for i in range(1, count) for j in (i - 1, i + 1) if j >= 1 and j < count and (min(i, j) % 2 == 1)]
+        from_a = lax.ppermute(jnp.where(odd, first, last), axis, pairs_a)
+        if pairs_b:
+            from_b = lax.ppermute(jnp.where(odd, last, first), axis, pairs_b)
+        else:
+            from_b = jnp.zeros_like(from_a)
+        low = jnp.where(odd, from_a, from_b)
+        high = jnp.where(odd, from_b, from_a)
         widths = [(0, 0)] + [(1, 1) if d < dim else (0, 0) for d in range(1, 4)]
         wide = jnp.concatenate([jnp.pad(low, widths), wide, jnp.pad(high, widths)], axis=dim)
     return wide
@@ -87,7 +96,6 @@
     blocks = lax.axis_size("stream") * lax.axis_size("cross")
     capacity = max(2, 2 * tile_count // blocks)
     slot_total = blocks * capacity
-    faces = slot_total * row_count
 
     state_visc = face_halo(jnp.concatenate([fluid_state, viscosity[None]], 0))
     state_pad = state_visc[0:5]
@@ -120,20 +128,23 @@
         0,
     )
     outbound = jnp.einsum(
-        "ts,ctr->csr", placement_plan, payload, precision=lax.Precision.HIGHEST
+        "ts,ctr->scr", placement_plan, payload, precision=lax.Precision.HIGHEST
     )
-    arrived = lax.all_to_all(outbound, ("stream", "cross"), split_axis=1, concat_axis=1, tiled=True)
+    arrived = lax.all_to_all(outbound, ("stream", "cross"), split_axis=0, concat_axis=0, tiled=True)
 
-    cells = jnp.round(arrived[5]).astype(jnp.int32).reshape(faces)
+    cells = jnp.round(arrived[:, 5]).astype(jnp.int32)
     plane = cells // vertical_cells
     depth = cells % vertical_cells
     depth_hot = (
-        depth[:, None] == lax.broadcasted_iota(jnp.int32, (faces, vertical_cells), 1)
+        depth[:, :, None]
+        == lax.broadcasted_iota(jnp.int32, (slot_total, row_count, vertical_cells), 2)
     )
-    plane_rows = plane[None, :] == lax.broadcasted_iota(jnp.int32, (plane_count, faces), 0)
-    spread = jnp.where(plane_rows[None], arrived[0:5].reshape(5, 1, faces), 0.0)
+    plane_rows = plane[None] == lax.broadcasted_iota(
+        jnp.int32, (plane_count, slot_total, row_count), 0
+    )
+    spread = jnp.where(plane_rows[None], arrived[:, 0:5].transpose(1, 0, 2)[:, None], 0.0)
     source = jnp.einsum(
-        "cpf,fd->cpd", spread, depth_hot.astype(jnp.float32), precision=lax.Precision.HIGHEST
+        "cpsr,srd->cpd", spread, depth_hot.astype(jnp.float32), precision=lax.Precision.HIGHEST
     )
     source = source.reshape(5, cells_x, cells_y, vertical_cells)
 
@@ -148,9 +159,11 @@
         + flat_state[3] * flat_state[3]
     )
     pressure = 0.4 * (flat_state[4] - 0.5 * kinetic / flat_state[0])
-    picked = exact_dot("fd,dp->fp", pressure.T, depth_hot.astype(jnp.bfloat16), False)
-    plane_cols = plane[:, None] == lax.broadcasted_iota(jnp.int32, (faces, plane_count), 1)
-    face_pressure = jnp.sum(jnp.where(plane_cols, picked, 0.0), axis=1)
+    picked = exact_dot("srd,dp->srp", pressure.T, depth_hot.astype(jnp.bfloat16), False)
+    plane_cols = plane[:, :, None] == lax.broadcasted_iota(
+        jnp.int32, (slot_total, row_count, plane_count), 2
+    )
+    face_pressure = jnp.sum(jnp.where(plane_cols, picked, 0.0), axis=2)
     returned = lax.all_to_all(
         face_pressure.reshape(1, slot_total, row_count),
         ("stream", "cross"),

time: 67.8 us -> 61 us (0.90)
  starting transfers between devices: 37 us -> 22 us
  waiting for transfers between devices: 4.43 us -> 9.59 us
  matrix products: 7.97 us -> 10.1 us
  other arithmetic: 7.19 us -> 9.29 us
  blocking collectives: 7.52 us -> 6.62 us
    ppermute x12 -> x10, starting transfers between devices: 31.8 us -> 18.6 us  [the longest x6 12 us: face_halo(): from_a = lax.ppermute(jnp.where(odd, first, last), axis, pairs_a)]
    all_to_all x1, waiting for transfers between devices: 0.01 us -> 6.97 us  [shards(): lax.all_to_all(outbound, ('stream', 'cross'), split_axis=0, concat_axis=0...]
    eq x1 -> x2, other arithmetic: 0.14 us -> 2.93 us  [the longest x1 2.78 us: shards(): depth[:, :, None]]
    dot_general x2, matrix products: 4.49 us -> 6.59 us  [the longest x1 6.16 us: shards(): jnp.einsum('cpsr,srd->cpd', spread, depth_hot.astype(jnp.float32), precis...]
    ppermute x12 -> x10, waiting for transfers between devices: 4.43 us -> 2.62 us  [the longest x4 2.61 us: face_halo(): from_b = lax.ppermute(jnp.where(odd, last, first), axis, pairs_b)]
    all_to_all x1, starting transfers between devices: 5.22 us -> 3.44 us  [shards(): lax.all_to_all(outbound, ('stream', 'cross'), split_axis=0, concat_axis=0...]
    dot_general x0 -> x1, local copies, waits for them, and re-layouts: none -> 1.04 us  [shards(): jnp.einsum('ts,ctr->scr', placement_plan, payload, precision=lax.Precisio...]
    all_to_all x1, blocking collectives: 7.52 us -> 6.62 us  [shards(): lax.all_to_all(face_pressure.reshape(1, slot_total, row_count), ('stream'...]
  transfers between devices with their start and end apart: 13 -> 11, of which waited for: 2 -> 2; matrix products, arithmetic and copies ran while one was open for 3% -> 10% of each run, Pallas kernels for 0% -> 0%
where the time goes in v3:
time: 61 us; the launch traced here: 60.2 us
  starting transfers between devices  22 us (36%)
  matrix products  10.1 us (17%)
  waiting for transfers between devices  9.59 us (16%)
  other arithmetic  9.29 us (15%)
  blocking collectives  6.62 us (11%)
  local copies, waits for them, and re-layouts  1.47 us (2%)
  between operations  1.12 us (2%)
    ppermute x6, starting transfers between devices, face_halo(): from_a = lax.ppermute(jnp.where(odd, first, last), axis, pairs_a)  12 us
    all_to_all x1, waiting for transfers between devices, shards(): lax.all_to_all(outbound, ('stream', 'cross'), split_axis=0, concat_axis=0...  6.97 us
    all_to_all x1, blocking collectives, shards(): lax.all_to_all(face_pressure.reshape(1, slot_total, row_count), ('stream'...  6.62 us
    ppermute x4, starting transfers between devices, face_halo(): from_b = lax.ppermute(jnp.where(odd, last, first), axis, pairs_b)  6.6 us
    dot_general x1, matrix products, shards(): jnp.einsum('cpsr,srd->cpd', spread, depth_hot.astype(jnp.float32), precis...  6.16 us
    all_to_all x1, starting transfers between devices, shards(): lax.all_to_all(outbound, ('stream', 'cross'), split_axis=0, concat_axis=0...  3.44 us
    eq x1, other arithmetic, shards(): depth[:, :, None]  2.78 us
    ppermute x4, waiting for transfers between devices, face_halo(): from_b = lax.ppermute(jnp.where(odd, last, first), axis, pairs_b)  2.61 us
  transfers between devices with their start and end apart: 11, of which 2 were waited for; matrix products, arithmetic and copies ran while one was open for 10% of the time, Pallas kernels for 0%

profile of v3, /device:TPU:1, one launch (start us, length us, event | category | flops | bytes accessed | tf_op | source)
XLA Modules:
  0.0 60.2 jit_solution(1490734831515447886)
XLA Ops:
  0.7 0.8 %pad_maximum_fusion.6 = f32[6,4,4,128]{3,2,1,0:T(4,128)S(1)} fusion(f32[1,4,4,128]{3,2,1,0:T(4,128)} %bitcast.71, f32[4,4,4,128]{3,2,1,0:T(4,128)} %param.8, f32[1,4,4,128]{3,2,1,0:T(4,128)} %bitcast.74), kind=kLoop, calls=%fused_computation.50 | loop fusion | flops 24576 | bytes 98304 | tf_op jit(solution)/shard_map/concatenate | solution.py:100
  1.5 2.1 %collective-permute-start.2 = (f32[6,4,1,128]{3,2,1,0:T(1,128)S(1)}, f32[6,4,1,128]{3,2,1,0:T(1,128)S(1)}, u32[]{:S(2)}, u32[]{:S(2)}) collective-permute-start(f32[6,4,1,128]{3,2,1,0:T(1,128)S(1)} %broadcast_select_fusion.3), channel_id=1, source_target_pairs={{0,4},{4,0},{1,5},{5,1},{2,6},{6,2},{3,7},{7,3},{8,12},{12,8},{9,1... | collective-permute-start | bytes 36872 | tf_op jit(solution)/shard_map/ppermute | solution.py:21
  3.6 1.0 %collective-permute-start.3 = (f32[6,1,4,128]{3,2,1,0:T(4,128)S(1)}, f32[6,1,4,128]{3,2,1,0:T(4,128)S(1)}, u32[]{:S(2)}, u32[]{:S(2)}) collective-permute-start(f32[6,1,4,128]{3,2,1,0:T(4,128)S(1)} %get-tuple-element.16), channel_id=1, source_target_pairs={{0,8},{8,0},{16,24},{24,16},{1,9},{9,1},{17,25},{25,17},{2,10},{10... | collective-permute-start | bytes 36872 | tf_op jit(solution)/shard_map/ppermute | solution.py:21
  4.6 3.0 %collective-permute-start.4 = (f32[6,1,4,128]{3,2,1,0:T(4,128)S(1)}, f32[6,1,4,128]{3,2,1,0:T(4,128)S(1)}, u32[]{:S(2)}, u32[]{:S(2)}) collective-permute-start(f32[6,1,4,128]{3,2,1,0:T(4,128)S(1)} %get-tuple-element.17), channel_id=1, source_target_pairs={{8,16},{16,8},{9,17},{17,9},{10,18},{18,10},{11,19},{19,11},{12,20... | collective-permute-start | bytes 36872 | tf_op jit(solution)/shard_map/ppermute | solution.py:23
  7.7 1.4 %collective-permute-start = (f32[6,4,4,1]{3,2,1,0:T(4,128)S(1)}, f32[6,4,4,1]{3,2,1,0:T(4,128)S(1)}, u32[]{:S(2)}, u32[]{:S(2)}) collective-permute-start(f32[6,4,4,1]{3,2,1,0:T(4,128)S(1)} %get-tuple-element.14), channel_id=1, source_target_pairs={{0,1},{1,0},{2,3},{3,2},{4,5},{5,4},{6,7},{7,6},{8,9},{9,8},{10,11... | collective-permute-start | bytes 1160 | tf_op jit(solution)/shard_map/ppermute | solution.py:21
  9.1 0.7 %collective-permute-start.1 = (f32[6,4,4,1]{3,2,1,0:T(4,128)S(1)}, f32[6,4,4,1]{3,2,1,0:T(4,128)S(1)}, u32[]{:S(2)}, u32[]{:S(2)}) collective-permute-start(f32[6,4,4,1]{3,2,1,0:T(4,128)S(1)} %get-tuple-element.15), channel_id=1, source_target_pairs={{1,2},{2,1},{5,6},{6,5},{9,10},{10,9},{13,14},{14,13},{17,18},{18,... | collective-permute-start | bytes 1160 | tf_op jit(solution)/shard_map/ppermute | solution.py:23
  9.8 0.7 %iota_compare_fusion.4 = pred[64,128]{1,0:T(8,128)(4,1)S(1)} fusion(s32[64]{0:T(128)} %param.13), kind=kLoop, calls=%fused_computation.146 | loop fusion | flops 8192 | bytes 8448 | tf_op jit(solution)/shard_map/lt | solution.py:104
  10.5 1.0 %broadcast_select_fusion = f32[8,64,128]{2,1,0:T(8,128)S(1)} fusion(f32[8,64,128]{2,1,0:T(8,128)} %param.10, pred[64,128]{1,0:T(8,128)(4,1)S(1)} %iota_compare_fusion.4), kind=kLoop, calls=%fused_computation.32 | loop fusion | flops 65536 | bytes 532480 | tf_op jit(solution)/shard_map/jit(_where)/select_n | solution.py:105
  11.5 0.9 %fusion.12 = f32[64]{0:T(128)S(1)} fusion(s32[64]{0:T(128)} %bitcast.83), kind=kOutput, calls=%fused_computation.12 | convolution fusion | flops 71616 | bytes 512 | tf_op jit(solution)/shard_map/dot_general | solution.py:114
  12.4 0.7 %fusion.106 = s32[64]{0:T(128)S(1)} fusion(f32[64]{0:T(128)S(1)} %fusion.12, s32[64,1]{0,1:T(1,128)} %param.12), kind=kLoop, calls=%fused_computation.211 | loop fusion | flops 192 | bytes 768 | tf_op jit(solution)/shard_map/eq | solution.py:120
  13.0 0.8 %convert_bitcast_fusion = f32[1,64,128]{2,1,0:T(8,128)S(1)} fusion(s32[64,128]{1,0:T(8,128)} %param.11), kind=kLoop, calls=%fused_computation.145 | loop fusion | flops 8192 | bytes 65536 | tf_op jit(solution)/shard_map/broadcast_in_dim | solution.py:126
  14.2 1.0 %copy.12 = f32[128,6,128]{2,1,0:T(8,128)} copy(f32[128,6,128]{2,0,1:T(8,128)S(1)} %fusion.16) | data formatting | bytes 786432 | tf_op jit(solution)/shard_map/ts,ctr->scr/dot_general | solution.py:130
  15.3 3.4 %all-to-all-start = ((f32[128,6,128]{2,1,0:T(8,128)}), f32[128,6,128]{2,1,0:T(8,128)S(1)}, u32[]{:S(2)}, u32[]{:S(2)}) async-start(f32[128,6,128]{2,1,0:T(8,128)} %copy.12), calls=%async_computation | async-start | bytes 1048576 | tf_op jit(solution)/shard_map/all_to_all | solution.py:133
  19.3 7.0 %all-to-all-done = f32[128,6,128]{2,1,0:T(8,128)S(1)} async-done(((f32[128,6,128]{2,1,0:T(8,128)}), f32[128,6,128]{2,1,0:T(8,128)S(1)}, u32[]{:S(2)}, u32[]{:S(2)}) %all-to-all-start) | async-done | bytes 393248 | tf_op jit(solution)/shard_map/all_to_all | solution.py:133
  26.9 2.8 %iota_compare_fusion = pred[128,128,128]{2,1,0:T(32,128)(4,1)S(1)} fusion(s32[128,128]{1,0:T(8,128)S(1)} %get-tuple-element.7), kind=kLoop, calls=%fused_computation | loop fusion | flops 2097152 | bytes 2162688 | tf_op jit(solution)/shard_map/eq | solution.py:139
  29.7 6.2 %fusion.2 = f32[5,16,128,1]{2,1,3,0:T(8,128)S(1)} fusion(pred[128,128,128]{2,1,0:T(32,128)(4,1)S(1)} %iota_compare_fusion, f32[5,128,128]{1,2,0:T(8,128)S(1)} %copy.14, pred[16,128,128]{1,0,2:T(8,128)(4,1)S(1)} %iota_compare_fusion.2), kind=kOutput, calls=%fused_computation.3 | convolution fusion | flops 2014576640 | bytes 2727936 | tf_op jit(solution)/shard_map/cpsr,srd->cpd/dot_general | solution.py:146
  36.2 0.7 %collective-permute-start.8 = (f32[5,4,4,1]{3,2,1,0:T(4,128)S(1)}, f32[5,4,4,1]{3,2,1,0:T(4,128)S(1)}, u32[]{:S(2)}, u32[]{:S(2)}) collective-permute-start(f32[5,4,4,1]{3,2,1,0:T(4,128)S(1)} %get-tuple-element.20), channel_id=1, source_target_pairs={{1,2},{2,1},{5,6},{6,5},{9,10},{10,9},{13,14},{14,13},{17,18},{18,... | collective-permute-start | bytes 968 | tf_op jit(solution)/shard_map/ppermute | solution.py:23
  36.9 5.4 %collective-permute-start.9 = (f32[5,4,4,1]{3,2,1,0:T(4,128)S(1)}, f32[5,4,4,1]{3,2,1,0:T(4,128)S(1)}, u32[]{:S(2)}, u32[]{:S(2)}) collective-permute-start(f32[5,4,4,1]{3,2,1,0:T(4,128)S(1)} %get-tuple-element.21), channel_id=1, source_target_pairs={{0,1},{1,0},{2,3},{3,2},{4,5},{5,4},{6,7},{7,6},{8,9},{9,8},{10,11... | collective-permute-start | bytes 968 | tf_op jit(solution)/shard_map/ppermute | solution.py:21
  42.4 0.7 %collective-permute-start.7 = (f32[5,4,1,128]{3,2,1,0:T(1,128)S(1)}, f32[5,4,1,128]{3,2,1,0:T(1,128)S(1)}, u32[]{:S(2)}, u32[]{:S(2)}) collective-permute-start(f32[5,4,1,128]{3,2,1,0:T(1,128)S(1)} %broadcast_select_fusion.10), channel_id=1, source_target_pairs={{0,4},{4,0},{1,5},{5,1},{2,6},{6,2},{3,7},{7,3},{8,12},{12,8},{9,1... | collective-permute-start | bytes 30728 | tf_op jit(solution)/shard_map/ppermute | solution.py:21
  43.1 1.4 %collective-permute-start.6 = (f32[5,1,4,128]{3,2,1,0:T(4,128)S(1)}, f32[5,1,4,128]{3,2,1,0:T(4,128)S(1)}, u32[]{:S(2)}, u32[]{:S(2)}) collective-permute-start(f32[5,1,4,128]{3,2,1,0:T(4,128)S(1)} %get-tuple-element.18), channel_id=1, source_target_pairs={{0,8},{8,0},{16,24},{24,16},{1,9},{9,1},{17,25},{25,17},{2,10},{10... | collective-permute-start | bytes 30728 | tf_op jit(solution)/shard_map/ppermute | solution.py:21
  44.5 2.2 %collective-permute-start.5 = (f32[5,1,4,128]{3,2,1,0:T(4,128)S(1)}, f32[5,1,4,128]{3,2,1,0:T(4,128)S(1)}, u32[]{:S(2)}, u32[]{:S(2)}) collective-permute-start(f32[5,1,4,128]{3,2,1,0:T(4,128)S(1)} %get-tuple-element.19), channel_id=1, source_target_pairs={{8,16},{16,8},{9,17},{17,9},{10,18},{18,10},{11,19},{19,11},{12,20... | collective-permute-start | bytes 30728 | tf_op jit(solution)/shard_map/ppermute | solution.py:23
  46.9 2.6 %collective-permute-done.5 = f32[5,1,4,128]{3,2,1,0:T(4,128)S(1)} collective-permute-done((f32[5,1,4,128]{3,2,1,0:T(4,128)S(1)}, f32[5,1,4,128]{3,2,1,0:T(4,128)S(1)}, u32[]{:S(2)}, u32[]{:S(2)}) %collective-permute-start.5) | collective-permute-done | bytes 10272 | tf_op jit(solution)/shard_map/ppermute | solution.py:23
  49.8 2.4 %fusion.9 = f32[3,128,128,16]{2,3,1,0:T(8,128)S(1)} fusion(s32[128,128]{1,0:T(8,128)S(1)} %get-tuple-element.7, bf16[1,128,16]{1,2,0:T(8,128)(2,1)S(1)} %get-tuple-element.32, bf16[1,128,16]{1,2,0:T(8,128)(2,1)S(1)} %get-tuple-element.31, bf16[1,128,16]{1,2,0:T(8,128)(2,1)S(1)} %get-tuple-element.30), kind=kOutput, calls=%fused_computation.10 | convolution fusion | flops 203460608 | bytes 3223552 | tf_op jit(solution)/shard_map/srd,kdp->ksrp/dot_general | solution.py:83
  52.7 6.6 %all_to_all.10 = f32[1,128,128]{2,0,1:T(1,128)S(1)} all-to-all(f32[1,128,128]{2,0,1:T(1,128)S(1)} %bitcast.65), channel_id=1, replica_groups=mesh['stream'=4,'cross'=2,'gore'=4] {'stream','cross'}, dimensions={1} | all-to-all | bytes 131072 | tf_op jit(solution)/shard_map/all_to_all | solution.py:167
  (54 shorter events, 3.7 us)
Async XLA Ops:
  0.6 18.1 %copy-start = (f32[4,4,4,128]{3,2,1,0:T(4,128)S(1)}, f32[4,4,4,128]{3,2,1,0:T(4,128)}, u32[]{:S(2)}) copy-start(f32[4,4,4,128]{3,2,1,0:T(4,128)} %param.8) | copy-start | bytes 98308
  0.6 18.1 %copy-start.2 = (f32[4,4,128]{2,1,0:T(4,128)S(1)}, f32[4,4,128]{2,1,0:T(4,128)}, u32[]{:S(2)}) copy-start(f32[4,4,128]{2,1,0:T(4,128)} %param.9) | copy-start | bytes 24580
  0.7 18.1 %copy-start.3 = (f32[4,4,128]{2,1,0:T(4,128)S(1)}, f32[4,4,128]{2,1,0:T(4,128)}, u32[]{:S(2)}) copy-start(f32[4,4,128]{2,1,0:T(4,128)} %param.7) | copy-start | bytes 24580
  1.5 17.5 %collective-permute-start.2 = (f32[6,4,1,128]{3,2,1,0:T(1,128)S(1)}, f32[6,4,1,128]{3,2,1,0:T(1,128)S(1)}, u32[]{:S(2)}, u32[]{:S(2)}) collective-permute-start(f32[6,4,1,128]{3,2,1,0:T(1,128)S(1)} %broadcast_select_fusion.3), channel_id=1, source_target_pairs={{0,4},{4,0},{1,5},{5,1},{2,6},{6,2},{3,7},{7,3},{8,12},{12,8},{9,1... | collective-permute-start | bytes 36872 | tf_op jit(solution)/shard_map/ppermute | solution.py:21
  3.6 15.4 %collective-permute-start.3 = (f32[6,1,4,128]{3,2,1,0:T(4,128)S(1)}, f32[6,1,4,128]{3,2,1,0:T(4,128)S(1)}, u32[]{:S(2)}, u32[]{:S(2)}) collective-permute-start(f32[6,1,4,128]{3,2,1,0:T(4,128)S(1)} %get-tuple-element.16), channel_id=1, source_target_pairs={{0,8},{8,0},{16,24},{24,16},{1,9},{9,1},{17,25},{25,17},{2,10},{10... | collective-permute-start | bytes 36872 | tf_op jit(solution)/shard_map/ppermute | solution.py:21
  4.6 14.5 %collective-permute-start.4 = (f32[6,1,4,128]{3,2,1,0:T(4,128)S(1)}, f32[6,1,4,128]{3,2,1,0:T(4,128)S(1)}, u32[]{:S(2)}, u32[]{:S(2)}) collective-permute-start(f32[6,1,4,128]{3,2,1,0:T(4,128)S(1)} %get-tuple-element.17), channel_id=1, source_target_pairs={{8,16},{16,8},{9,17},{17,9},{10,18},{18,10},{11,19},{19,11},{12,20... | collective-permute-start | bytes 36872 | tf_op jit(solution)/shard_map/ppermute | solution.py:23
  7.7 11.2 %collective-permute-start = (f32[6,4,4,1]{3,2,1,0:T(4,128)S(1)}, f32[6,4,4,1]{3,2,1,0:T(4,128)S(1)}, u32[]{:S(2)}, u32[]{:S(2)}) collective-permute-start(f32[6,4,4,1]{3,2,1,0:T(4,128)S(1)} %get-tuple-element.14), channel_id=1, source_target_pairs={{0,1},{1,0},{2,3},{3,2},{4,5},{5,4},{6,7},{7,6},{8,9},{9,8},{10,11... | collective-permute-start | bytes 1160 | tf_op jit(solution)/shard_map/ppermute | solution.py:21
  9.1 9.8 %collective-permute-start.1 = (f32[6,4,4,1]{3,2,1,0:T(4,128)S(1)}, f32[6,4,4,1]{3,2,1,0:T(4,128)S(1)}, u32[]{:S(2)}, u32[]{:S(2)}) collective-permute-start(f32[6,4,4,1]{3,2,1,0:T(4,128)S(1)} %get-tuple-element.15), channel_id=1, source_target_pairs={{1,2},{2,1},{5,6},{6,5},{9,10},{10,9},{13,14},{14,13},{17,18},{18,... | collective-permute-start | bytes 1160 | tf_op jit(solution)/shard_map/ppermute | solution.py:23
  15.3 11.0 %all-to-all-start = ((f32[128,6,128]{2,1,0:T(8,128)}), f32[128,6,128]{2,1,0:T(8,128)S(1)}, u32[]{:S(2)}, u32[]{:S(2)}) async-start(f32[128,6,128]{2,1,0:T(8,128)} %copy.12), calls=%async_computation | async-start | bytes 1048576 | tf_op jit(solution)/shard_map/all_to_all | solution.py:133
  36.2 10.5 %collective-permute-start.8 = (f32[5,4,4,1]{3,2,1,0:T(4,128)S(1)}, f32[5,4,4,1]{3,2,1,0:T(4,128)S(1)}, u32[]{:S(2)}, u32[]{:S(2)}) collective-permute-start(f32[5,4,4,1]{3,2,1,0:T(4,128)S(1)} %get-tuple-element.20), channel_id=1, source_target_pairs={{1,2},{2,1},{5,6},{6,5},{9,10},{10,9},{13,14},{14,13},{17,18},{18,... | collective-permute-start | bytes 968 | tf_op jit(solution)/shard_map/ppermute | solution.py:23
  36.9 9.8 %collective-permute-start.9 = (f32[5,4,4,1]{3,2,1,0:T(4,128)S(1)}, f32[5,4,4,1]{3,2,1,0:T(4,128)S(1)}, u32[]{:S(2)}, u32[]{:S(2)}) collective-permute-start(f32[5,4,4,1]{3,2,1,0:T(4,128)S(1)} %get-tuple-element.21), channel_id=1, source_target_pairs={{0,1},{1,0},{2,3},{3,2},{4,5},{5,4},{6,7},{7,6},{8,9},{9,8},{10,11... | collective-permute-start | bytes 968 | tf_op jit(solution)/shard_map/ppermute | solution.py:21
  42.4 4.4 %collective-permute-start.7 = (f32[5,4,1,128]{3,2,1,0:T(1,128)S(1)}, f32[5,4,1,128]{3,2,1,0:T(1,128)S(1)}, u32[]{:S(2)}, u32[]{:S(2)}) collective-permute-start(f32[5,4,1,128]{3,2,1,0:T(1,128)S(1)} %broadcast_select_fusion.10), channel_id=1, source_target_pairs={{0,4},{4,0},{1,5},{5,1},{2,6},{6,2},{3,7},{7,3},{8,12},{12,8},{9,1... | collective-permute-start | bytes 30728 | tf_op jit(solution)/shard_map/ppermute | solution.py:21
  43.1 3.8 %collective-permute-start.6 = (f32[5,1,4,128]{3,2,1,0:T(4,128)S(1)}, f32[5,1,4,128]{3,2,1,0:T(4,128)S(1)}, u32[]{:S(2)}, u32[]{:S(2)}) collective-permute-start(f32[5,1,4,128]{3,2,1,0:T(4,128)S(1)} %get-tuple-element.18), channel_id=1, source_target_pairs={{0,8},{8,0},{16,24},{24,16},{1,9},{9,1},{17,25},{25,17},{2,10},{10... | collective-permute-start | bytes 30728 | tf_op jit(solution)/shard_map/ppermute | solution.py:21
  44.5 5.0 %collective-permute-start.5 = (f32[5,1,4,128]{3,2,1,0:T(4,128)S(1)}, f32[5,1,4,128]{3,2,1,0:T(4,128)S(1)}, u32[]{:S(2)}, u32[]{:S(2)}) collective-permute-start(f32[5,1,4,128]{3,2,1,0:T(4,128)S(1)} %get-tuple-element.19), channel_id=1, source_target_pairs={{8,16},{16,8},{9,17},{17,9},{10,18},{18,10},{11,19},{19,11},{12,20... | collective-permute-start | bytes 30728 | tf_op jit(solution)/shard_map/ppermute | solution.py:23
  49.7 3.0 %copy-start.1 = (f32[5,4,4,128]{3,2,1,0:T(4,128)}, f32[5,4,4,128]{3,2,1,0:T(4,128)S(1)}, u32[]{:S(2)}) copy-start(f32[5,4,4,128]{3,2,1,0:T(4,128)S(1)} %fusion.46) | copy-start | bytes 122884

commit v4 on v2

--- a/solution.py
+++ b/solution.py
@@ -11,11 +11,20 @@
     wide = block
     for axis, dim in SIDES:
         count = lax.axis_size(axis)
-        forward = [(i, i + 1) for i in range(count - 1)]
-        backward = [(target, source) for source, target in forward]
+        index = lax.axis_index(axis)
+        odd = index % 2 == 1
         extent = block.shape[dim]
-        low = lax.ppermute(lax.slice_in_dim(block, extent - 1, None, axis=dim), axis, forward)
-        high = lax.ppermute(lax.slice_in_dim(block, 0, 1, axis=dim), axis, backward)
+        last = lax.slice_in_dim(block, extent - 1, None, axis=dim)
+        first = lax.slice_in_dim(block, 0, 1, axis=dim)
+        pairs_a = [(i, i ^ 1) for i in range(count) if (i ^ 1) < count]
+        pairs_b = [(i, j) for i in range(1, count) for j in (i - 1, i + 1) if j >= 1 and j < count and (min(i, j) % 2 == 1)]
+        from_a = lax.ppermute(jnp.where(odd, first, last), axis, pairs_a)
+        if pairs_b:
+            from_b = lax.ppermute(jnp.where(odd, last, first), axis, pairs_b)
+        else:
+            from_b = jnp.zeros_like(from_a)
+        low = jnp.where(odd, from_a, from_b)
+        high = jnp.where(odd, from_b, from_a)
         widths = [(0, 0)] + [(1, 1) if d < dim else (0, 0) for d in range(1, 4)]
         wide = jnp.concatenate([jnp.pad(low, widths), wide, jnp.pad(high, widths)], axis=dim)
     return wide
@@ -89,10 +98,6 @@
     slot_total = blocks * capacity
     faces = slot_total * row_count
 
-    state_visc = face_halo(jnp.concatenate([fluid_state, viscosity[None]], 0))
-    state_pad = state_visc[0:5]
-    visc_pad = state_visc[5]
-
     live_rows = lax.broadcasted_iota(jnp.int32, (tile_count, row_count), 1) < lengths[:, None]
     masked_values = jnp.where(live_rows[None], records, 0.0)
     target = routes[:, 0]
@@ -123,6 +128,12 @@
         "ts,ctr->csr", placement_plan, payload, precision=lax.Precision.HIGHEST
     )
     arrived = lax.all_to_all(outbound, ("stream", "cross"), split_axis=1, concat_axis=1, tiled=True)
+    outbound, state_and_visc = lax.optimization_barrier(
+        (outbound, jnp.concatenate([fluid_state, viscosity[None]], 0))
+    )
+    state_visc = face_halo(state_and_visc)
+    state_pad = state_visc[0:5]
+    visc_pad = state_visc[5]
 
     cells = jnp.round(arrived[5]).astype(jnp.int32).reshape(faces)
     plane = cells // vertical_cells

time: 67.8 us -> 50.8 us (0.75)
  starting transfers between devices: 37 us -> 21.4 us
  waiting for transfers between devices: 4.43 us -> 3.14 us
  blocking collectives: 7.52 us -> 8.55 us
    ppermute x12 -> x10, starting transfers between devices: 31.8 us -> 16.2 us  [the longest x4 8.37 us: face_halo(): from_b = lax.ppermute(jnp.where(odd, last, first), axis, pairs_b)]
    ppermute x12 -> x10, waiting for transfers between devices: 4.43 us -> 3.14 us  [the longest x4 3.12 us: face_halo(): from_b = lax.ppermute(jnp.where(odd, last, first), axis, pairs_b)]
    all_to_all x1, blocking collectives: 7.52 us -> 8.55 us  [shards(): lax.all_to_all(face_pressure.reshape(1, slot_total, row_count), ('stream'...]
    concatenate x2 -> x1, other arithmetic: 1.67 us -> 0.79 us  [shards(): jnp.concatenate([fluid_state, viscosity[None]], 0)]
  transfers between devices with their start and end apart: 13 -> 11, of which waited for: 2 -> 2; matrix products, arithmetic and copies ran while one was open for 3% -> 3% of each run, Pallas kernels for 0% -> 0%
where the time goes in v4:
time: 50.8 us; the launch traced here: 49.9 us
  starting transfers between devices  21.4 us (42%)
  blocking collectives  8.55 us (17%)
  matrix products  7.97 us (16%)
  other arithmetic  6.61 us (13%)
  waiting for transfers between devices  3.14 us (6%)
  local copies, waits for them, and re-layouts  1.21 us (2%)
  between operations  1 us (2%)
    all_to_all x1, blocking collectives, shards(): lax.all_to_all(face_pressure.reshape(1, slot_total, row_count), ('stream'...  8.55 us
    ppermute x4, starting transfers between devices, face_halo(): from_b = lax.ppermute(jnp.where(odd, last, first), axis, pairs_b)  8.37 us
    ppermute x6, starting transfers between devices, face_halo(): from_a = lax.ppermute(jnp.where(odd, first, last), axis, pairs_a)  7.84 us
    all_to_all x1, starting transfers between devices, shards(): lax.all_to_all(outbound, ('stream', 'cross'), split_axis=1, concat_axis=1...  5.22 us
    dot_general x1, matrix products, shards(): jnp.einsum('cpf,fd->cpd', spread, depth_hot.astype(jnp.float32), precisio...  3.97 us
    ppermute x4, waiting for transfers between devices, face_halo(): from_b = lax.ppermute(jnp.where(odd, last, first), axis, pairs_b)  3.12 us
    dot_general x1, matrix products, exact_dot(): jnp.einsum(left + ',k' + right + '->k' + output, onehot, stacked, preferr...  2.4 us
  transfers between devices with their start and end apart: 11, of which 2 were waited for; matrix products, arithmetic and copies ran while one was open for 3% of the time, Pallas kernels for 0%

profile of v4, /device:TPU:1, one launch (start us, length us, event | category | flops | bytes accessed | tf_op | source)
XLA Modules:
  0.0 49.9 jit_solution(16968767982298639690)
XLA Ops:
  0.6 0.7 %iota_compare_fusion.6 = pred[64,128]{1,0:T(8,128)(4,1)S(1)} fusion(s32[64]{0:T(128)} %param.13), kind=kLoop, calls=%fused_computation.133 | loop fusion | flops 8192 | bytes 8448 | tf_op jit(solution)/shard_map/lt | solution.py:101
  1.4 1.0 %broadcast_select_fusion = f32[8,64,128]{2,1,0:T(8,128)S(1)} fusion(f32[8,64,128]{2,1,0:T(8,128)} %param.10, pred[64,128]{1,0:T(8,128)(4,1)S(1)} %iota_compare_fusion.6), kind=kLoop, calls=%fused_computation.26 | loop fusion | flops 65536 | bytes 532480 | tf_op jit(solution)/shard_map/jit(_where)/select_n | solution.py:102
  2.4 0.8 %convert_bitcast_fusion = f32[1,64,128]{2,1,0:T(8,128)S(1)} fusion(s32[64,128]{1,0:T(8,128)} %param.11), kind=kLoop, calls=%fused_computation.132 | loop fusion | flops 8192 | bytes 65536 | tf_op jit(solution)/shard_map/broadcast_in_dim | solution.py:123
  3.1 0.9 %fusion.10 = f32[64]{0:T(128)S(1)} fusion(s32[64]{0:T(128)} %bitcast.99), kind=kOutput, calls=%fused_computation.12 | convolution fusion | flops 71616 | bytes 512 | tf_op jit(solution)/shard_map/dot_general | solution.py:111
  4.0 0.7 %fusion.92 = s32[64]{0:T(128)S(1)} fusion(f32[64]{0:T(128)S(1)} %fusion.10, s32[64,1]{0,1:T(1,128)} %param.12), kind=kLoop, calls=%fused_computation.194 | loop fusion | flops 192 | bytes 768 | tf_op jit(solution)/shard_map/eq | solution.py:117
  4.7 0.5 %convolution_bitcast_fusion.1 = f32[6,128,128]{1,2,0:T(8,128)S(1)} fusion(f32[1,64,128]{2,1,0:T(8,128)S(1)} %convert_bitcast_fusion, f32[4,64,128]{2,1,0:T(8,128)S(1)} %slice.230, f32[1,64,128]{2,1,0:T(8,128)S(1)} %slice_abs_fusion, s32[64]{0:T(128)S(1)} %fusion.92), kind=kOutput, calls=%fused_computation.10 | convolution fusion | flops 75603968 | bytes 590080 | tf_op jit(solution)/shard_map/ts,ctr->csr/dot_general | solution.py:127
  5.2 1.0 %copy.11 = f32[6,128,128]{2,0,1:T(8,128)} copy(f32[6,128,128]{1,2,0:T(8,128)S(1)} %convolution_bitcast_fusion.1) | data formatting | bytes 786432 | tf_op jit(solution)/shard_map/ts,ctr->csr/transpose | solution.py:127
  6.2 5.2 %all-to-all-start = ((f32[6,128,128]{2,0,1:T(8,128)}), f32[6,128,128]{2,0,1:T(8,128)S(1)}, u32[]{:S(2)}, u32[]{:S(2)}) async-start(f32[6,128,128]{2,0,1:T(8,128)} %copy.11), calls=%async_computation | async-start | bytes 1048576 | tf_op jit(solution)/shard_map/all_to_all | solution.py:130
  11.4 0.8 %pad_maximum_fusion.6 = f32[6,4,4,128]{3,2,1,0:T(4,128)S(1)} fusion(f32[1,4,4,128]{3,2,1,0:T(4,128)} %bitcast.97, f32[4,4,4,128]{3,2,1,0:T(4,128)} %param.8, f32[1,4,4,128]{3,2,1,0:T(4,128)} %bitcast.98), kind=kLoop, calls=%fused_computation.44 | loop fusion | flops 24576 | bytes 98304 | tf_op jit(solution)/shard_map/concatenate | solution.py:132
  12.3 0.7 %collective-permute-start.1 = (f32[6,4,4,1]{3,2,1,0:T(4,128)S(1)}, f32[6,4,4,1]{3,2,1,0:T(4,128)S(1)}, u32[]{:S(2)}, u32[]{:S(2)}) collective-permute-start(f32[6,4,4,1]{3,2,1,0:T(4,128)S(1)} %get-tuple-element.18), channel_id=1, source_target_pairs={{1,2},{2,1},{5,6},{6,5},{9,10},{10,9},{13,14},{14,13},{17,18},{18,... | collective-permute-start | bytes 1160 | tf_op jit(solution)/shard_map/ppermute | solution.py:23
  13.0 3.9 %collective-permute-start = (f32[6,4,4,1]{3,2,1,0:T(4,128)S(1)}, f32[6,4,4,1]{3,2,1,0:T(4,128)S(1)}, u32[]{:S(2)}, u32[]{:S(2)}) collective-permute-start(f32[6,4,4,1]{3,2,1,0:T(4,128)S(1)} %get-tuple-element.19), channel_id=1, source_target_pairs={{0,1},{1,0},{2,3},{3,2},{4,5},{5,4},{6,7},{7,6},{8,9},{9,8},{10,11... | collective-permute-start | bytes 1160 | tf_op jit(solution)/shard_map/ppermute | solution.py:21
  16.9 1.4 %collective-permute-start.2 = (f32[6,4,1,128]{3,2,1,0:T(1,128)S(1)}, f32[6,4,1,128]{3,2,1,0:T(1,128)S(1)}, u32[]{:S(2)}, u32[]{:S(2)}) collective-permute-start(f32[6,4,1,128]{3,2,1,0:T(1,128)S(1)} %broadcast_select_fusion.3), channel_id=1, source_target_pairs={{0,4},{4,0},{1,5},{5,1},{2,6},{6,2},{3,7},{7,3},{8,12},{12,8},{9,1... | collective-permute-start | bytes 36872 | tf_op jit(solution)/shard_map/ppermute | solution.py:21
  18.4 1.2 %collective-permute-start.3 = (f32[6,1,4,128]{3,2,1,0:T(4,128)S(1)}, f32[6,1,4,128]{3,2,1,0:T(4,128)S(1)}, u32[]{:S(2)}, u32[]{:S(2)}) collective-permute-start(f32[6,1,4,128]{3,2,1,0:T(4,128)S(1)} %get-tuple-element.16), channel_id=1, source_target_pairs={{0,8},{8,0},{16,24},{24,16},{1,9},{9,1},{17,25},{25,17},{2,10},{10... | collective-permute-start | bytes 36872 | tf_op jit(solution)/shard_map/ppermute | solution.py:21
  19.6 3.0 %collective-permute-start.4 = (f32[6,1,4,128]{3,2,1,0:T(4,128)S(1)}, f32[6,1,4,128]{3,2,1,0:T(4,128)S(1)}, u32[]{:S(2)}, u32[]{:S(2)}) collective-permute-start(f32[6,1,4,128]{3,2,1,0:T(4,128)S(1)} %get-tuple-element.17), channel_id=1, source_target_pairs={{8,16},{16,8},{9,17},{17,9},{10,18},{18,10},{11,19},{19,11},{12,20... | collective-permute-start | bytes 36872 | tf_op jit(solution)/shard_map/ppermute | solution.py:23
  22.7 1.9 %collective-permute-done.4 = f32[6,1,4,128]{3,2,1,0:T(4,128)S(1)} collective-permute-done((f32[6,1,4,128]{3,2,1,0:T(4,128)S(1)}, f32[6,1,4,128]{3,2,1,0:T(4,128)S(1)}, u32[]{:S(2)}, u32[]{:S(2)}) %collective-permute-start.4) | collective-permute-done | bytes 12320 | tf_op jit(solution)/shard_map/ppermute | solution.py:23
  25.2 0.5 fusion.103
  25.7 4.0 %fusion.2 = f32[5,16,128]{2,1,0:T(8,128)S(1)} fusion(s32[16384]{0:T(1024)S(1)} %get-tuple-element.9, f32[5,16,16384]{2,1,0:T(8,128)S(1)} %fusion.103), kind=kOutput, calls=%fused_computation.3 | convolution fusion | flops 2015363072 | bytes 5349376 | tf_op jit(solution)/shard_map/cpf,fd->cpd/dot_general | solution.py:146
  30.0 0.7 %collective-permute-start.8 = (f32[5,4,4,1]{3,2,1,0:T(4,128)S(1)}, f32[5,4,4,1]{3,2,1,0:T(4,128)S(1)}, u32[]{:S(2)}, u32[]{:S(2)}) collective-permute-start(f32[5,4,4,1]{3,2,1,0:T(4,128)S(1)} %get-tuple-element.22), channel_id=1, source_target_pairs={{1,2},{2,1},{5,6},{6,5},{9,10},{10,9},{13,14},{14,13},{17,18},{18,... | collective-permute-start | bytes 968 | tf_op jit(solution)/shard_map/ppermute | solution.py:23
  30.7 1.2 %collective-permute-start.9 = (f32[5,4,4,1]{3,2,1,0:T(4,128)S(1)}, f32[5,4,4,1]{3,2,1,0:T(4,128)S(1)}, u32[]{:S(2)}, u32[]{:S(2)}) collective-permute-start(f32[5,4,4,1]{3,2,1,0:T(4,128)S(1)} %get-tuple-element.23), channel_id=1, source_target_pairs={{0,1},{1,0},{2,3},{3,2},{4,5},{5,4},{6,7},{7,6},{8,9},{9,8},{10,11... | collective-permute-start | bytes 968 | tf_op jit(solution)/shard_map/ppermute | solution.py:21
  32.0 4.1 %collective-permute-start.5 = (f32[5,1,4,128]{3,2,1,0:T(4,128)S(1)}, f32[5,1,4,128]{3,2,1,0:T(4,128)S(1)}, u32[]{:S(2)}, u32[]{:S(2)}) collective-permute-start(f32[5,1,4,128]{3,2,1,0:T(4,128)S(1)} %get-tuple-element.21), channel_id=1, source_target_pairs={{8,16},{16,8},{9,17},{17,9},{10,18},{18,10},{11,19},{19,11},{12,20... | collective-permute-start | bytes 30728 | tf_op jit(solution)/shard_map/ppermute | solution.py:23
  36.2 1.2 %collective-permute-done.5 = f32[5,1,4,128]{3,2,1,0:T(4,128)S(1)} collective-permute-done((f32[5,1,4,128]{3,2,1,0:T(4,128)S(1)}, f32[5,1,4,128]{3,2,1,0:T(4,128)S(1)}, u32[]{:S(2)}, u32[]{:S(2)}) %collective-permute-start.5) | collective-permute-done | bytes 10272 | tf_op jit(solution)/shard_map/ppermute | solution.py:23
  37.7 2.4 %convolution_bitcast_fusion = f32[3,16384,16]{1,2,0:T(8,128)S(1)} fusion(s32[16384]{0:T(1024)S(1)} %get-tuple-element.9, bf16[1,128,16]{1,2,0:T(8,128)(2,1)S(1)} %get-tuple-element.34, bf16[1,128,16]{1,2,0:T(8,128)(2,1)S(1)} %get-tuple-element.33, bf16[1,128,16]{1,2,0:T(8,128)(2,1)S(1)} %get-tuple-element.32), kind=kOutput, calls=%fused_computation | convolution fusion | flops 203436032 | bytes 3223552 | tf_op jit(solution)/shard_map/fd,kdp->kfp/dot_general | solution.py:83
  40.5 8.5 %all_to_all.10 = f32[1,128,128]{2,0,1:T(1,128)S(1)} all-to-all(f32[1,128,128]{2,0,1:T(1,128)S(1)} %bitcast.85), channel_id=1, replica_groups=mesh['stream'=4,'cross'=2,'gore'=4] {'stream','cross'}, dimensions={1} | all-to-all | bytes 131072 | tf_op jit(solution)/shard_map/all_to_all | solution.py:165
  49.3 0.7 %slice_multiply_fusion = f32[3,64,128]{2,1,0:T(8,128)} fusion(f32[8,64,128]{2,1,0:T(8,128)S(1)} %broadcast_select_fusion, f32[64,128]{1,0:T(8,128)S(1)} %fusion.62), kind=kLoop, calls=%fused_computation.27 | loop fusion | flops 24576 | bytes 229376 | tf_op jit(solution)/shard_map/mul | solution.py:175
  (45 shorter events, 2.1 us)
Async XLA Ops:
  6.2 18.7 %all-to-all-start = ((f32[6,128,128]{2,0,1:T(8,128)}), f32[6,128,128]{2,0,1:T(8,128)S(1)}, u32[]{:S(2)}, u32[]{:S(2)}) async-start(f32[6,128,128]{2,0,1:T(8,128)} %copy.11), calls=%async_computation | async-start | bytes 1048576 | tf_op jit(solution)/shard_map/all_to_all | solution.py:130
  12.3 10.2 %collective-permute-start.1 = (f32[6,4,4,1]{3,2,1,0:T(4,128)S(1)}, f32[6,4,4,1]{3,2,1,0:T(4,128)S(1)}, u32[]{:S(2)}, u32[]{:S(2)}) collective-permute-start(f32[6,4,4,1]{3,2,1,0:T(4,128)S(1)} %get-tuple-element.18), channel_id=1, source_target_pairs={{1,2},{2,1},{5,6},{6,5},{9,10},{10,9},{13,14},{14,13},{17,18},{18,... | collective-permute-start | bytes 1160 | tf_op jit(solution)/shard_map/ppermute | solution.py:23
  13.0 9.6 %collective-permute-start = (f32[6,4,4,1]{3,2,1,0:T(4,128)S(1)}, f32[6,4,4,1]{3,2,1,0:T(4,128)S(1)}, u32[]{:S(2)}, u32[]{:S(2)}) collective-permute-start(f32[6,4,4,1]{3,2,1,0:T(4,128)S(1)} %get-tuple-element.19), channel_id=1, source_target_pairs={{0,1},{1,0},{2,3},{3,2},{4,5},{5,4},{6,7},{7,6},{8,9},{9,8},{10,11... | collective-permute-start | bytes 1160 | tf_op jit(solution)/shard_map/ppermute | solution.py:21
  16.9 7.7 %collective-permute-start.2 = (f32[6,4,1,128]{3,2,1,0:T(1,128)S(1)}, f32[6,4,1,128]{3,2,1,0:T(1,128)S(1)}, u32[]{:S(2)}, u32[]{:S(2)}) collective-permute-start(f32[6,4,1,128]{3,2,1,0:T(1,128)S(1)} %broadcast_select_fusion.3), channel_id=1, source_target_pairs={{0,4},{4,0},{1,5},{5,1},{2,6},{6,2},{3,7},{7,3},{8,12},{12,8},{9,1... | collective-permute-start | bytes 36872 | tf_op jit(solution)/shard_map/ppermute | solution.py:21
  18.4 4.3 %collective-permute-start.3 = (f32[6,1,4,128]{3,2,1,0:T(4,128)S(1)}, f32[6,1,4,128]{3,2,1,0:T(4,128)S(1)}, u32[]{:S(2)}, u32[]{:S(2)}) collective-permute-start(f32[6,1,4,128]{3,2,1,0:T(4,128)S(1)} %get-tuple-element.16), channel_id=1, source_target_pairs={{0,8},{8,0},{16,24},{24,16},{1,9},{9,1},{17,25},{25,17},{2,10},{10... | collective-permute-start | bytes 36872 | tf_op jit(solution)/shard_map/ppermute | solution.py:21
  19.6 5.0 %collective-permute-start.4 = (f32[6,1,4,128]{3,2,1,0:T(4,128)S(1)}, f32[6,1,4,128]{3,2,1,0:T(4,128)S(1)}, u32[]{:S(2)}, u32[]{:S(2)}) collective-permute-start(f32[6,1,4,128]{3,2,1,0:T(4,128)S(1)} %get-tuple-element.17), channel_id=1, source_target_pairs={{8,16},{16,8},{9,17},{17,9},{10,18},{18,10},{11,19},{19,11},{12,20... | collective-permute-start | bytes 36872 | tf_op jit(solution)/shard_map/ppermute | solution.py:23
  30.0 6.0 %collective-permute-start.8 = (f32[5,4,4,1]{3,2,1,0:T(4,128)S(1)}, f32[5,4,4,1]{3,2,1,0:T(4,128)S(1)}, u32[]{:S(2)}, u32[]{:S(2)}) collective-permute-start(f32[5,4,4,1]{3,2,1,0:T(4,128)S(1)} %get-tuple-element.22), channel_id=1, source_target_pairs={{1,2},{2,1},{5,6},{6,5},{9,10},{10,9},{13,14},{14,13},{17,18},{18,... | collective-permute-start | bytes 968 | tf_op jit(solution)/shard_map/ppermute | solution.py:23
  30.7 5.4 %collective-permute-start.9 = (f32[5,4,4,1]{3,2,1,0:T(4,128)S(1)}, f32[5,4,4,1]{3,2,1,0:T(4,128)S(1)}, u32[]{:S(2)}, u32[]{:S(2)}) collective-permute-start(f32[5,4,4,1]{3,2,1,0:T(4,128)S(1)} %get-tuple-element.23), channel_id=1, source_target_pairs={{0,1},{1,0},{2,3},{3,2},{4,5},{5,4},{6,7},{7,6},{8,9},{9,8},{10,11... | collective-permute-start | bytes 968 | tf_op jit(solution)/shard_map/ppermute | solution.py:21
  31.9 4.2 %collective-permute-start.7 = (f32[5,4,1,128]{3,2,1,0:T(1,128)S(1)}, f32[5,4,1,128]{3,2,1,0:T(1,128)S(1)}, u32[]{:S(2)}, u32[]{:S(2)}) collective-permute-start(f32[5,4,1,128]{3,2,1,0:T(1,128)S(1)} %broadcast_select_fusion.10), channel_id=1, source_target_pairs={{0,4},{4,0},{1,5},{5,1},{2,6},{6,2},{3,7},{7,3},{8,12},{12,8},{9,1... | collective-permute-start | bytes 30728 | tf_op jit(solution)/shard_map/ppermute | solution.py:21
  32.0 4.2 %collective-permute-start.6 = (f32[5,1,4,128]{3,2,1,0:T(4,128)S(1)}, f32[5,1,4,128]{3,2,1,0:T(4,128)S(1)}, u32[]{:S(2)}, u32[]{:S(2)}) collective-permute-start(f32[5,1,4,128]{3,2,1,0:T(4,128)S(1)} %get-tuple-element.20), channel_id=1, source_target_pairs={{0,8},{8,0},{16,24},{24,16},{1,9},{9,1},{17,25},{25,17},{2,10},{10... | collective-permute-start | bytes 30728 | tf_op jit(solution)/shard_map/ppermute | solution.py:21
  32.0 5.4 %collective-permute-start.5 = (f32[5,1,4,128]{3,2,1,0:T(4,128)S(1)}, f32[5,1,4,128]{3,2,1,0:T(4,128)S(1)}, u32[]{:S(2)}, u32[]{:S(2)}) collective-permute-start(f32[5,1,4,128]{3,2,1,0:T(4,128)S(1)} %get-tuple-element.21), channel_id=1, source_target_pairs={{8,16},{16,8},{9,17},{17,9},{10,18},{18,10},{11,19},{19,11},{12,20... | collective-permute-start | bytes 30728 | tf_op jit(solution)/shard_map/ppermute | solution.py:23
  37.6 12.3 %copy-start = (f32[5,4,4,128]{3,2,1,0:T(4,128)}, f32[5,4,4,128]{3,2,1,0:T(4,128)S(1)}, u32[]{:S(2)}) copy-start(f32[5,4,4,128]{3,2,1,0:T(4,128)S(1)} %fusion.26) | copy-start | bytes 122884

commit v5 on v4

--- a/solution.py
+++ b/solution.py
@@ -159,19 +159,31 @@
         + flat_state[3] * flat_state[3]
     )
     pressure = 0.4 * (flat_state[4] - 0.5 * kinetic / flat_state[0])
-    picked = exact_dot("fd,dp->fp", pressure.T, depth_hot.astype(jnp.bfloat16), False)
-    plane_cols = plane[:, None] == lax.broadcasted_iota(jnp.int32, (faces, plane_count), 1)
-    face_pressure = jnp.sum(jnp.where(plane_cols, picked, 0.0), axis=1)
-    returned = lax.all_to_all(
-        face_pressure.reshape(1, slot_total, row_count),
-        ("stream", "cross"),
-        split_axis=1,
-        concat_axis=1,
-        tiled=True,
-    )
-    home_pressure = jnp.einsum(
-        "ts,sr->tr", placement_plan, returned[0], precision=lax.Precision.HIGHEST
-    )
+    pressure_all = lax.all_gather(pressure, ("stream", "cross"))
+    home_depth = (
+        (cell_ids % vertical_cells)[:, :, None]
+        == lax.broadcasted_iota(jnp.int32, (tile_count, row_count, vertical_cells), 2)
+    ).astype(jnp.bfloat16)
+    home_plane = cell_ids // vertical_cells
+    if blocks * plane_count <= 512:
+        table = pressure_all.reshape(blocks * plane_count, vertical_cells)
+        key = target[:, None] * plane_count + home_plane
+        picked = exact_dot("trd,dq->trq", table.T, home_depth, False)
+        chosen = key[:, :, None] == lax.broadcasted_iota(
+            jnp.int32, (tile_count, row_count, blocks * plane_count), 2
+        )
+    else:
+        tile_table = jnp.einsum(
+            "tb,bq->tq",
+            onehot,
+            pressure_all.reshape(blocks, plane_count * vertical_cells),
+            precision=lax.Precision.HIGHEST,
+        ).reshape(tile_count, plane_count, vertical_cells)
+        picked = exact_dot("trd,tpd->trp", tile_table, home_depth, False)
+        chosen = home_plane[:, :, None] == lax.broadcasted_iota(
+            jnp.int32, (tile_count, row_count, plane_count), 2
+        )
+    home_pressure = jnp.sum(jnp.where(chosen, picked, 0.0), axis=2)
     face_loads = masked_values[5:8] * home_pressure[None]
     return (new_state, face_loads)
 

time: 50.8 us -> 64.7 us (1.27)
  blocking collectives: 8.55 us -> 15.7 us
  waiting for transfers between devices: 3.14 us -> 9.63 us
  other arithmetic: 6.61 us -> 8.25 us
  matrix products: 7.97 us -> 7.28 us
    all_gather x0 -> x1, blocking collectives: none -> 15.7 us  [shards(): pressure_all = lax.all_gather(pressure, ('stream', 'cross'))]
    all_to_all x1 -> x0, blocking collectives: 8.55 us -> none  [shards(): lax.all_to_all(face_pressure.reshape(1, slot_total, row_count), ('stream'...]
    all_to_all x1, waiting for transfers between devices: 0.01 us -> 6.82 us  [shards(): lax.all_to_all(outbound, ('stream', 'cross'), split_axis=1, concat_axis=1...]
    ppermute x6, starting transfers between devices: 7.84 us -> 11.2 us  [face_halo(): from_a = lax.ppermute(jnp.where(odd, first, last), axis, pairs_a)]
    ppermute x4, starting transfers between devices: 8.37 us -> 6.43 us  [face_halo(): from_b = lax.ppermute(jnp.where(odd, last, first), axis, pairs_b)]
    all_to_all x1, starting transfers between devices: 5.22 us -> 3.44 us  [shards(): lax.all_to_all(outbound, ('stream', 'cross'), split_axis=1, concat_axis=1...]
    add x0 -> x2, other arithmetic: none -> 1.58 us  [shards(): key = target[:, None] * plane_count + home_plane]
    reduce_sum x1, other arithmetic: 0.38 us -> 1.86 us  [shards(): home_pressure = jnp.sum(jnp.where(chosen, picked, 0.0), axis=2)]
  transfers between devices with their start and end apart: 11 -> 11, of which waited for: 2 -> 2; matrix products, arithmetic and copies ran while one was open for 3% -> 2% of each run, Pallas kernels for 0% -> 0%
where the time goes in v5:
time: 64.7 us; the launch traced here: 64.2 us
  starting transfers between devices  21.1 us (33%)
  blocking collectives  15.7 us (24%)
  waiting for transfers between devices  9.63 us (15%)
  other arithmetic  8.25 us (13%)
  matrix products  7.28 us (11%)
  local copies, waits for them, and re-layouts  1.23 us (2%)
  between operations  1.03 us (2%)
    all_gather x1, blocking collectives, shards(): pressure_all = lax.all_gather(pressure, ('stream', 'cross'))  15.7 us
    ppermute x6, starting transfers between devices, face_halo(): from_a = lax.ppermute(jnp.where(odd, first, last), axis, pairs_a)  11.2 us
    all_to_all x1, waiting for transfers between devices, shards(): lax.all_to_all(outbound, ('stream', 'cross'), split_axis=1, concat_axis=1...  6.82 us
    ppermute x4, starting transfers between devices, face_halo(): from_b = lax.ppermute(jnp.where(odd, last, first), axis, pairs_b)  6.43 us
    dot_general x1, matrix products, shards(): jnp.einsum('cpf,fd->cpd', spread, depth_hot.astype(jnp.float32), precisio...  3.97 us
    all_to_all x1, starting transfers between devices, shards(): lax.all_to_all(outbound, ('stream', 'cross'), split_axis=1, concat_axis=1...  3.44 us
    ppermute x4, waiting for transfers between devices, face_halo(): from_b = lax.ppermute(jnp.where(odd, last, first), axis, pairs_b)  2.79 us
    dot_general x1, matrix products, exact_dot(): jnp.einsum(left + ',k' + right + '->k' + output, onehot, stacked, preferr...  1.92 us
  transfers between devices with their start and end apart: 11, of which 2 were waited for; matrix products, arithmetic and copies ran while one was open for 2% of the time, Pallas kernels for 0%

profile of v5, /device:TPU:1, one launch (start us, length us, event | category | flops | bytes accessed | tf_op | source)
XLA Modules:
  0.0 64.2 jit_solution(12225087286168825408)
XLA Ops:
  0.6 0.7 %iota_compare_fusion.6 = pred[64,128]{1,0:T(8,128)(4,1)S(1)} fusion(s32[64]{0:T(128)} %param.13), kind=kLoop, calls=%fused_computation.152 | loop fusion | flops 8192 | bytes 8448 | tf_op jit(solution)/shard_map/lt | solution.py:101
  1.4 1.0 %broadcast_select_fusion = f32[8,64,128]{2,1,0:T(8,128)S(1)} fusion(f32[8,64,128]{2,1,0:T(8,128)} %param.10, pred[64,128]{1,0:T(8,128)(4,1)S(1)} %iota_compare_fusion.6), kind=kLoop, calls=%fused_computation.28 | loop fusion | flops 65536 | bytes 532480 | tf_op jit(solution)/shard_map/jit(_where)/select_n | solution.py:102
  2.4 0.9 %fusion.14 = f32[64]{0:T(128)S(1)} fusion(s32[64]{0:T(128)} %bitcast.110), kind=kOutput, calls=%fused_computation.20 | convolution fusion | flops 71616 | bytes 512 | tf_op jit(solution)/shard_map/dot_general | solution.py:111
  3.3 0.7 %multiply_bitcast_fusion = (s32[64]{0:T(128)S(1)}, s32[64]{0:T(128)S(1)}) fusion(s32[64,1]{0,1:T(1,128)} %param.12, f32[64]{0:T(128)S(1)} %fusion.14), kind=kLoop, calls=%fused_computation.201 | loop fusion | flops 192 | bytes 1024 | tf_op jit(solution)/shard_map/add | solution.py:170
  3.9 0.9 %fusion.72 = (s32[64,128]{1,0:T(8,128)S(1)}, f32[1,64,128]{2,1,0:T(8,128)S(1)}, s32[64,128]{1,0:T(8,128)S(1)}) fusion(s32[64,128]{1,0:T(8,128)} %param.11, s32[64]{0:T(128)S(1)} %get-tuple-element.38), kind=kLoop, calls=%fused_computation.146 | loop fusion | flops 172032 | bytes 131328 | tf_op jit(solution)/shard_map/add | solution.py:170
  4.8 0.8 %pad_maximum_fusion.6 = f32[6,4,4,128]{3,2,1,0:T(4,128)S(1)} fusion(f32[1,4,4,128]{3,2,1,0:T(4,128)} %bitcast.108, f32[4,4,4,128]{3,2,1,0:T(4,128)} %param.8, f32[1,4,4,128]{3,2,1,0:T(4,128)} %bitcast.109), kind=kLoop, calls=%fused_computation.58 | loop fusion | flops 24576 | bytes 98304 | tf_op jit(solution)/shard_map/concatenate | solution.py:132
  6.2 2.1 %collective-permute-start.2 = (f32[6,4,1,128]{3,2,1,0:T(1,128)S(1)}, f32[6,4,1,128]{3,2,1,0:T(1,128)S(1)}, u32[]{:S(2)}, u32[]{:S(2)}) collective-permute-start(f32[6,4,1,128]{3,2,1,0:T(1,128)S(1)} %broadcast_select_fusion.3), channel_id=1, source_target_pairs={{0,4},{4,0},{1,5},{5,1},{2,6},{6,2},{3,7},{7,3},{8,12},{12,8},{9,1... | collective-permute-start | bytes 36872 | tf_op jit(solution)/shard_map/ppermute | solution.py:21
  8.4 0.7 %collective-permute-start.1 = (f32[6,4,4,1]{3,2,1,0:T(4,128)S(1)}, f32[6,4,4,1]{3,2,1,0:T(4,128)S(1)}, u32[]{:S(2)}, u32[]{:S(2)}) collective-permute-start(f32[6,4,4,1]{3,2,1,0:T(4,128)S(1)} %get-tuple-element.21), channel_id=1, source_target_pairs={{1,2},{2,1},{5,6},{6,5},{9,10},{10,9},{13,14},{14,13},{17,18},{18,... | collective-permute-start | bytes 1160 | tf_op jit(solution)/shard_map/ppermute | solution.py:23
  9.1 3.9 %collective-permute-start = (f32[6,4,4,1]{3,2,1,0:T(4,128)S(1)}, f32[6,4,4,1]{3,2,1,0:T(4,128)S(1)}, u32[]{:S(2)}, u32[]{:S(2)}) collective-permute-start(f32[6,4,4,1]{3,2,1,0:T(4,128)S(1)} %get-tuple-element.22), channel_id=1, source_target_pairs={{0,1},{1,0},{2,3},{3,2},{4,5},{5,4},{6,7},{7,6},{8,9},{9,8},{10,11... | collective-permute-start | bytes 1160 | tf_op jit(solution)/shard_map/ppermute | solution.py:21
  13.0 1.5 %collective-permute-start.3 = (f32[6,1,4,128]{3,2,1,0:T(4,128)S(1)}, f32[6,1,4,128]{3,2,1,0:T(4,128)S(1)}, u32[]{:S(2)}, u32[]{:S(2)}) collective-permute-start(f32[6,1,4,128]{3,2,1,0:T(4,128)S(1)} %get-tuple-element.19), channel_id=1, source_target_pairs={{0,8},{8,0},{16,24},{24,16},{1,9},{9,1},{17,25},{25,17},{2,10},{10... | collective-permute-start | bytes 36872 | tf_op jit(solution)/shard_map/ppermute | solution.py:21
  14.5 3.0 %collective-permute-start.4 = (f32[6,1,4,128]{3,2,1,0:T(4,128)S(1)}, f32[6,1,4,128]{3,2,1,0:T(4,128)S(1)}, u32[]{:S(2)}, u32[]{:S(2)}) collective-permute-start(f32[6,1,4,128]{3,2,1,0:T(4,128)S(1)} %get-tuple-element.20), channel_id=1, source_target_pairs={{8,16},{16,8},{9,17},{17,9},{10,18},{18,10},{11,19},{19,11},{12,20... | collective-permute-start | bytes 36872 | tf_op jit(solution)/shard_map/ppermute | solution.py:23
  17.5 1.0 %copy.11 = f32[6,128,128]{2,0,1:T(8,128)} copy(f32[6,128,128]{1,2,0:T(8,128)S(1)} %convolution_bitcast_fusion.1) | data formatting | bytes 786432 | tf_op jit(solution)/shard_map/ts,ctr->csr/transpose | solution.py:127
  18.5 3.4 %all-to-all-start = ((f32[6,128,128]{2,0,1:T(8,128)}), f32[6,128,128]{2,0,1:T(8,128)S(1)}, u32[]{:S(2)}, u32[]{:S(2)}) async-start(f32[6,128,128]{2,0,1:T(8,128)} %copy.11), calls=%async_computation | async-start | bytes 1048576 | tf_op jit(solution)/shard_map/all_to_all | solution.py:130
  22.4 6.8 %all-to-all-done = f32[6,128,128]{2,0,1:T(8,128)S(1)} async-done(((f32[6,128,128]{2,0,1:T(8,128)}), f32[6,128,128]{2,0,1:T(8,128)S(1)}, u32[]{:S(2)}, u32[]{:S(2)}) %all-to-all-start) | async-done | bytes 393248 | tf_op jit(solution)/shard_map/all_to_all | solution.py:130
  30.1 4.0 %fusion.1 = f32[5,16,128]{2,1,0:T(8,128)S(1)} fusion(s32[16384]{0:T(1024)S(1)} %get-tuple-element.12, f32[5,16,16384]{2,1,0:T(8,128)S(1)} %fusion.100), kind=kOutput, calls=%fused_computation.2 | convolution fusion | flops 2015363072 | bytes 5349376 | tf_op jit(solution)/shard_map/cpf,fd->cpd/dot_general | solution.py:146
  34.4 0.7 %collective-permute-start.8 = (f32[5,4,4,1]{3,2,1,0:T(4,128)S(1)}, f32[5,4,4,1]{3,2,1,0:T(4,128)S(1)}, u32[]{:S(2)}, u32[]{:S(2)}) collective-permute-start(f32[5,4,4,1]{3,2,1,0:T(4,128)S(1)} %get-tuple-element.25), channel_id=1, source_target_pairs={{1,2},{2,1},{5,6},{6,5},{9,10},{10,9},{13,14},{14,13},{17,18},{18,... | collective-permute-start | bytes 968 | tf_op jit(solution)/shard_map/ppermute | solution.py:23
  35.1 1.3 %collective-permute-start.9 = (f32[5,4,4,1]{3,2,1,0:T(4,128)S(1)}, f32[5,4,4,1]{3,2,1,0:T(4,128)S(1)}, u32[]{:S(2)}, u32[]{:S(2)}) collective-permute-start(f32[5,4,4,1]{3,2,1,0:T(4,128)S(1)} %get-tuple-element.26), channel_id=1, source_target_pairs={{0,1},{1,0},{2,3},{3,2},{4,5},{5,4},{6,7},{7,6},{8,9},{9,8},{10,11... | collective-permute-start | bytes 968 | tf_op jit(solution)/shard_map/ppermute | solution.py:21
  36.4 0.7 %collective-permute-start.7 = (f32[5,4,1,128]{3,2,1,0:T(1,128)S(1)}, f32[5,4,1,128]{3,2,1,0:T(1,128)S(1)}, u32[]{:S(2)}, u32[]{:S(2)}) collective-permute-start(f32[5,4,1,128]{3,2,1,0:T(1,128)S(1)} %broadcast_select_fusion.10), channel_id=1, source_target_pairs={{0,4},{4,0},{1,5},{5,1},{2,6},{6,2},{3,7},{7,3},{8,12},{12,8},{9,1... | collective-permute-start | bytes 30728 | tf_op jit(solution)/shard_map/ppermute | solution.py:21
  37.1 1.7 %collective-permute-start.6 = (f32[5,1,4,128]{3,2,1,0:T(4,128)S(1)}, f32[5,1,4,128]{3,2,1,0:T(4,128)S(1)}, u32[]{:S(2)}, u32[]{:S(2)}) collective-permute-start(f32[5,1,4,128]{3,2,1,0:T(4,128)S(1)} %get-tuple-element.23), channel_id=1, source_target_pairs={{0,8},{8,0},{16,24},{24,16},{1,9},{9,1},{17,25},{25,17},{2,10},{10... | collective-permute-start | bytes 30728 | tf_op jit(solution)/shard_map/ppermute | solution.py:21
  38.8 2.1 %collective-permute-start.5 = (f32[5,1,4,128]{3,2,1,0:T(4,128)S(1)}, f32[5,1,4,128]{3,2,1,0:T(4,128)S(1)}, u32[]{:S(2)}, u32[]{:S(2)}) collective-permute-start(f32[5,1,4,128]{3,2,1,0:T(4,128)S(1)} %get-tuple-element.24), channel_id=1, source_target_pairs={{8,16},{16,8},{9,17},{17,9},{10,18},{18,10},{11,19},{19,11},{12,20... | collective-permute-start | bytes 30728 | tf_op jit(solution)/shard_map/ppermute | solution.py:23
  41.0 2.8 %collective-permute-done.5 = f32[5,1,4,128]{3,2,1,0:T(4,128)S(1)} collective-permute-done((f32[5,1,4,128]{3,2,1,0:T(4,128)S(1)}, f32[5,1,4,128]{3,2,1,0:T(4,128)S(1)}, u32[]{:S(2)}, u32[]{:S(2)}) %collective-permute-start.5) | collective-permute-done | bytes 10272 | tf_op jit(solution)/shard_map/ppermute | solution.py:23
  44.0 15.7 %all_gather.4 = f32[8,16,128]{2,1,0:T(8,128)S(1)} all-gather(f32[1,16,128]{2,1,0:T(8,128)S(1)} %bitcast.107), channel_id=1, replica_groups=mesh['stream'=4,'cross'=2,'gore'=4] {'stream','cross'}, dimensions={0}, use_global_device_ids=true | all-gather | bytes 73728 | tf_op jit(solution)/shard_map/all_gather | solution.py:162
  59.7 1.9 %convolution_bitcast_fusion = f32[3,64,128,128]{2,3,1,0:T(8,128)S(1)} fusion(s32[64,128]{1,0:T(8,128)S(1)} %get-tuple-element.29, bf16[1,128,128]{1,2,0:T(8,128)(2,1)S(1)} %bitcast.102, bf16[1,128,128]{1,2,0:T(8,128)(2,1)S(1)} %bitcast.101, bf16[1,128,128]{1,2,0:T(8,128)(2,1)S(1)} %bitcast.100), kind=kOutput, calls=%fused_computation.4 | convolution fusion | flops 806649856 | bytes 12713984 | tf_op jit(solution)/shard_map/trd,kdq->ktrq/dot_general | solution.py:83
  61.7 1.9 %fusion.6 = f32[64,128]{1,0:T(8,128)S(1)} fusion(f32[3,64,128,128]{2,3,1,0:T(8,128)S(1)} %convolution_bitcast_fusion, s32[64,128]{1,0:T(8,128)S(1)} %get-tuple-element.27), kind=kLoop, calls=%fused_computation.8 | loop fusion | flops 5234688 | bytes 12648448 | tf_op jit(solution)/shard_map/reduce_sum | solution.py:186
  (44 shorter events, 3.1 us)
Async XLA Ops:
  6.2 15.9 %collective-permute-start.2 = (f32[6,4,1,128]{3,2,1,0:T(1,128)S(1)}, f32[6,4,1,128]{3,2,1,0:T(1,128)S(1)}, u32[]{:S(2)}, u32[]{:S(2)}) collective-permute-start(f32[6,4,1,128]{3,2,1,0:T(1,128)S(1)} %broadcast_select_fusion.3), channel_id=1, source_target_pairs={{0,4},{4,0},{1,5},{5,1},{2,6},{6,2},{3,7},{7,3},{8,12},{12,8},{9,1... | collective-permute-start | bytes 36872 | tf_op jit(solution)/shard_map/ppermute | solution.py:21
  8.4 13.6 %collective-permute-start.1 = (f32[6,4,4,1]{3,2,1,0:T(4,128)S(1)}, f32[6,4,4,1]{3,2,1,0:T(4,128)S(1)}, u32[]{:S(2)}, u32[]{:S(2)}) collective-permute-start(f32[6,4,4,1]{3,2,1,0:T(4,128)S(1)} %get-tuple-element.21), channel_id=1, source_target_pairs={{1,2},{2,1},{5,6},{6,5},{9,10},{10,9},{13,14},{14,13},{17,18},{18,... | collective-permute-start | bytes 1160 | tf_op jit(solution)/shard_map/ppermute | solution.py:23
  9.1 12.9 %collective-permute-start = (f32[6,4,4,1]{3,2,1,0:T(4,128)S(1)}, f32[6,4,4,1]{3,2,1,0:T(4,128)S(1)}, u32[]{:S(2)}, u32[]{:S(2)}) collective-permute-start(f32[6,4,4,1]{3,2,1,0:T(4,128)S(1)} %get-tuple-element.22), channel_id=1, source_target_pairs={{0,1},{1,0},{2,3},{3,2},{4,5},{5,4},{6,7},{7,6},{8,9},{9,8},{10,11... | collective-permute-start | bytes 1160 | tf_op jit(solution)/shard_map/ppermute | solution.py:21
  13.0 9.1 %collective-permute-start.3 = (f32[6,1,4,128]{3,2,1,0:T(4,128)S(1)}, f32[6,1,4,128]{3,2,1,0:T(4,128)S(1)}, u32[]{:S(2)}, u32[]{:S(2)}) collective-permute-start(f32[6,1,4,128]{3,2,1,0:T(4,128)S(1)} %get-tuple-element.19), channel_id=1, source_target_pairs={{0,8},{8,0},{16,24},{24,16},{1,9},{9,1},{17,25},{25,17},{2,10},{10... | collective-permute-start | bytes 36872 | tf_op jit(solution)/shard_map/ppermute | solution.py:21
  14.5 7.6 %collective-permute-start.4 = (f32[6,1,4,128]{3,2,1,0:T(4,128)S(1)}, f32[6,1,4,128]{3,2,1,0:T(4,128)S(1)}, u32[]{:S(2)}, u32[]{:S(2)}) collective-permute-start(f32[6,1,4,128]{3,2,1,0:T(4,128)S(1)} %get-tuple-element.20), channel_id=1, source_target_pairs={{8,16},{16,8},{9,17},{17,9},{10,18},{18,10},{11,19},{19,11},{12,20... | collective-permute-start | bytes 36872 | tf_op jit(solution)/shard_map/ppermute | solution.py:23
  18.5 10.7 %all-to-all-start = ((f32[6,128,128]{2,0,1:T(8,128)}), f32[6,128,128]{2,0,1:T(8,128)S(1)}, u32[]{:S(2)}, u32[]{:S(2)}) async-start(f32[6,128,128]{2,0,1:T(8,128)} %copy.11), calls=%async_computation | async-start | bytes 1048576 | tf_op jit(solution)/shard_map/all_to_all | solution.py:130
  34.4 6.5 %collective-permute-start.8 = (f32[5,4,4,1]{3,2,1,0:T(4,128)S(1)}, f32[5,4,4,1]{3,2,1,0:T(4,128)S(1)}, u32[]{:S(2)}, u32[]{:S(2)}) collective-permute-start(f32[5,4,4,1]{3,2,1,0:T(4,128)S(1)} %get-tuple-element.25), channel_id=1, source_target_pairs={{1,2},{2,1},{5,6},{6,5},{9,10},{10,9},{13,14},{14,13},{17,18},{18,... | collective-permute-start | bytes 968 | tf_op jit(solution)/shard_map/ppermute | solution.py:23
  35.1 5.8 %collective-permute-start.9 = (f32[5,4,4,1]{3,2,1,0:T(4,128)S(1)}, f32[5,4,4,1]{3,2,1,0:T(4,128)S(1)}, u32[]{:S(2)}, u32[]{:S(2)}) collective-permute-start(f32[5,4,4,1]{3,2,1,0:T(4,128)S(1)} %get-tuple-element.26), channel_id=1, source_target_pairs={{0,1},{1,0},{2,3},{3,2},{4,5},{5,4},{6,7},{7,6},{8,9},{9,8},{10,11... | collective-permute-start | bytes 968 | tf_op jit(solution)/shard_map/ppermute | solution.py:21
  36.4 4.5 %collective-permute-start.7 = (f32[5,4,1,128]{3,2,1,0:T(1,128)S(1)}, f32[5,4,1,128]{3,2,1,0:T(1,128)S(1)}, u32[]{:S(2)}, u32[]{:S(2)}) collective-permute-start(f32[5,4,1,128]{3,2,1,0:T(1,128)S(1)} %broadcast_select_fusion.10), channel_id=1, source_target_pairs={{0,4},{4,0},{1,5},{5,1},{2,6},{6,2},{3,7},{7,3},{8,12},{12,8},{9,1... | collective-permute-start | bytes 30728 | tf_op jit(solution)/shard_map/ppermute | solution.py:21
  37.1 3.9 %collective-permute-start.6 = (f32[5,1,4,128]{3,2,1,0:T(4,128)S(1)}, f32[5,1,4,128]{3,2,1,0:T(4,128)S(1)}, u32[]{:S(2)}, u32[]{:S(2)}) collective-permute-start(f32[5,1,4,128]{3,2,1,0:T(4,128)S(1)} %get-tuple-element.23), channel_id=1, source_target_pairs={{0,8},{8,0},{16,24},{24,16},{1,9},{9,1},{17,25},{25,17},{2,10},{10... | collective-permute-start | bytes 30728 | tf_op jit(solution)/shard_map/ppermute | solution.py:21
  38.8 5.0 %collective-permute-start.5 = (f32[5,1,4,128]{3,2,1,0:T(4,128)S(1)}, f32[5,1,4,128]{3,2,1,0:T(4,128)S(1)}, u32[]{:S(2)}, u32[]{:S(2)}) collective-permute-start(f32[5,1,4,128]{3,2,1,0:T(4,128)S(1)} %get-tuple-element.24), channel_id=1, source_target_pairs={{8,16},{16,8},{9,17},{17,9},{10,18},{18,10},{11,19},{19,11},{12,20... | collective-permute-start | bytes 30728 | tf_op jit(solution)/shard_map/ppermute | solution.py:23
  44.0 17.7 %copy-start = (f32[5,4,4,128]{3,2,1,0:T(4,128)}, f32[5,4,4,128]{3,2,1,0:T(4,128)S(1)}, u32[]{:S(2)}) copy-start(f32[5,4,4,128]{3,2,1,0:T(4,128)S(1)} %fusion.36) | copy-start | bytes 122884

commit v6 on v4

--- a/solution.py
+++ b/solution.py
@@ -99,7 +99,6 @@
     faces = slot_total * row_count
 
     live_rows = lax.broadcasted_iota(jnp.int32, (tile_count, row_count), 1) < lengths[:, None]
-    masked_values = jnp.where(live_rows[None], records, 0.0)
     target = routes[:, 0]
     onehot = (target[:, None] == lax.broadcasted_iota(jnp.int32, (tile_count, blocks), 1)).astype(
         jnp.float32
@@ -118,16 +117,19 @@
     ).astype(jnp.float32)
     payload = jnp.concatenate(
         [
-            jnp.abs(masked_values[0:1]),
-            masked_values[1:5],
-            cell_ids.astype(jnp.float32)[None],
+            jnp.where(live_rows[:, None], records[0:5].transpose(1, 0, 2), 0.0),
+            cell_ids.astype(jnp.float32)[:, None],
         ],
-        0,
+        1,
     )
+    payload = jnp.concatenate([jnp.abs(payload[:, 0:1]), payload[:, 1:]], 1)
     outbound = jnp.einsum(
-        "ts,ctr->csr", placement_plan, payload, precision=lax.Precision.HIGHEST
-    )
-    arrived = lax.all_to_all(outbound, ("stream", "cross"), split_axis=1, concat_axis=1, tiled=True)
+        "ts,tq->sq",
+        placement_plan,
+        payload.reshape(tile_count, 6 * row_count),
+        precision=lax.Precision.HIGHEST,
+    ).reshape(slot_total, 6, row_count)
+    arrived = lax.all_to_all(outbound, ("stream", "cross"), split_axis=0, concat_axis=0, tiled=True)
     outbound, state_and_visc = lax.optimization_barrier(
         (outbound, jnp.concatenate([fluid_state, viscosity[None]], 0))
     )
@@ -135,14 +137,16 @@
     state_pad = state_visc[0:5]
     visc_pad = state_visc[5]
 
-    cells = jnp.round(arrived[5]).astype(jnp.int32).reshape(faces)
+    cells = jnp.round(arrived[:, 5]).astype(jnp.int32).reshape(faces)
     plane = cells // vertical_cells
     depth = cells % vertical_cells
     depth_hot = (
         depth[:, None] == lax.broadcasted_iota(jnp.int32, (faces, vertical_cells), 1)
     )
     plane_rows = plane[None, :] == lax.broadcasted_iota(jnp.int32, (plane_count, faces), 0)
-    spread = jnp.where(plane_rows[None], arrived[0:5].reshape(5, 1, faces), 0.0)
+    spread = jnp.where(
+        plane_rows[None], arrived[:, 0:5].transpose(1, 0, 2).reshape(5, 1, faces), 0.0
+    )
     source = jnp.einsum(
         "cpf,fd->cpd", spread, depth_hot.astype(jnp.float32), precision=lax.Precision.HIGHEST
     )
@@ -172,7 +176,7 @@
     home_pressure = jnp.einsum(
         "ts,sr->tr", placement_plan, returned[0], precision=lax.Precision.HIGHEST
     )
-    face_loads = masked_values[5:8] * home_pressure[None]
+    face_loads = jnp.where(live_rows[None], records[5:8], 0.0) * home_pressure[None]
     return (new_state, face_loads)
 
 

time: 50.8 us -> 51.6 us (1.016)
  other arithmetic: 6.61 us -> 7.53 us
    dot_general x0 -> x1, local copies, waits for them, and re-layouts: none -> 1.03 us  [shards(): jnp.einsum('ts,tq->sq', placement_plan, payload.reshape(tile_count, 6 * r...]
    transpose x1 -> x0, local copies, waits for them, and re-layouts: 0.99 us -> none  [shards(): jnp.einsum('ts,ctr->csr', placement_plan, payload, precision=lax.Precisio...]
    mul x1, other arithmetic: 0.65 us -> 1.55 us  [shards(): jnp.where(live_rows[None], records[5:8], 0.0) * home_pressure[None]]
where the time goes in v6:
time: 51.6 us; the launch traced here: 50.7 us
  starting transfers between devices  21.4 us (41%)
  blocking collectives  8.55 us (17%)
  matrix products  7.89 us (15%)
  other arithmetic  7.53 us (15%)
  waiting for transfers between devices  3.14 us (6%)
  local copies, waits for them, and re-layouts  1.17 us (2%)
  between operations  1 us (2%)
    all_to_all x1, blocking collectives, shards(): lax.all_to_all(face_pressure.reshape(1, slot_total, row_count), ('stream'...  8.55 us
    ppermute x4, starting transfers between devices, face_halo(): from_b = lax.ppermute(jnp.where(odd, last, first), axis, pairs_b)  8.37 us
    ppermute x6, starting transfers between devices, face_halo(): from_a = lax.ppermute(jnp.where(odd, first, last), axis, pairs_a)  7.84 us
    all_to_all x1, starting transfers between devices, shards(): lax.all_to_all(outbound, ('stream', 'cross'), split_axis=0, concat_axis=0...  5.22 us
    dot_general x1, matrix products, shards(): jnp.einsum('cpf,fd->cpd', spread, depth_hot.astype(jnp.float32), precisio...  3.97 us
    ppermute x4, waiting for transfers between devices, face_halo(): from_b = lax.ppermute(jnp.where(odd, last, first), axis, pairs_b)  3.12 us
    dot_general x1, matrix products, exact_dot(): jnp.einsum(left + ',k' + right + '->k' + output, onehot, stacked, preferr...  2.4 us
    mul x1, other arithmetic, shards(): jnp.where(live_rows[None], records[5:8], 0.0) * home_pressure[None]  1.55 us
  transfers between devices with their start and end apart: 11, of which 2 were waited for; matrix products, arithmetic and copies ran while one was open for 3% of the time, Pallas kernels for 0%

profile of v6, /device:TPU:1, one launch (start us, length us, event | category | flops | bytes accessed | tf_op | source)
XLA Modules:
  0.0 50.7 jit_solution(10012872687860601885)
XLA Ops:
  0.6 0.9 %fusion.10 = f32[64]{0:T(128)S(1)} fusion(s32[64]{0:T(128)} %bitcast.92), kind=kOutput, calls=%fused_computation.11 | convolution fusion | flops 71616 | bytes 512 | tf_op jit(solution)/shard_map/dot_general | solution.py:110
  1.5 0.7 %fusion.92 = s32[64]{0:T(128)S(1)} fusion(f32[64]{0:T(128)S(1)} %fusion.10, s32[64,1]{0,1:T(1,128)} %param.12), kind=kLoop, calls=%fused_computation.196 | loop fusion | flops 192 | bytes 768 | tf_op jit(solution)/shard_map/eq | solution.py:116
  2.2 0.8 %convert_bitcast_fusion = f32[64,1,128]{2,0,1:T(8,128)S(1)} fusion(s32[64,128]{1,0:T(8,128)} %param.11), kind=kLoop, calls=%fused_computation.130 | loop fusion | flops 8192 | bytes 65536 | tf_op jit(solution)/shard_map/broadcast_in_dim | solution.py:121
  2.9 0.7 %iota_compare_fusion.4 = pred[64,128]{1,0:T(8,128)(4,1)S(1)} fusion(s32[64]{0:T(128)} %param.13), kind=kLoop, calls=%fused_computation.131 | loop fusion | flops 8192 | bytes 8448 | tf_op jit(solution)/shard_map/lt | solution.py:101
  3.7 0.9 %select_bitcast_fusion = f32[64,5,128]{2,0,1:T(8,128)S(1)} fusion(f32[8,64,128]{2,1,0:T(8,128)} %param.10, pred[64,128]{1,0:T(8,128)(4,1)S(1)} %iota_compare_fusion.4), kind=kLoop, calls=%fused_computation.28 | loop fusion | flops 40960 | bytes 335872 | tf_op jit(solution)/shard_map/jit(_where)/select_n | solution.py:120
  4.6 0.4 fusion.14
  5.1 1.0 %copy.13 = f32[128,6,128]{2,1,0:T(8,128)} copy(f32[128,6,128]{2,0,1:T(8,128)S(1)} %fusion.14) | data formatting | bytes 786432 | tf_op jit(solution)/shard_map/ts,tq->sq/dot_general | solution.py:126
  6.1 5.2 %all-to-all-start = ((f32[128,6,128]{2,1,0:T(8,128)}), f32[128,6,128]{2,1,0:T(8,128)S(1)}, u32[]{:S(2)}, u32[]{:S(2)}) async-start(f32[128,6,128]{2,1,0:T(8,128)} %copy.13), calls=%async_computation | async-start | bytes 1048576 | tf_op jit(solution)/shard_map/all_to_all | solution.py:132
  11.3 0.8 %pad_maximum_fusion.7 = f32[6,4,4,128]{3,2,1,0:T(4,128)S(1)} fusion(f32[1,4,4,128]{3,2,1,0:T(4,128)} %bitcast.90, f32[4,4,4,128]{3,2,1,0:T(4,128)} %param.8, f32[1,4,4,128]{3,2,1,0:T(4,128)} %bitcast.91), kind=kLoop, calls=%fused_computation.46 | loop fusion | flops 24576 | bytes 98304 | tf_op jit(solution)/shard_map/concatenate | solution.py:134
  12.2 0.7 %collective-permute-start.1 = (f32[6,4,4,1]{3,2,1,0:T(4,128)S(1)}, f32[6,4,4,1]{3,2,1,0:T(4,128)S(1)}, u32[]{:S(2)}, u32[]{:S(2)}) collective-permute-start(f32[6,4,4,1]{3,2,1,0:T(4,128)S(1)} %get-tuple-element.18), channel_id=1, source_target_pairs={{1,2},{2,1},{5,6},{6,5},{9,10},{10,9},{13,14},{14,13},{17,18},{18,... | collective-permute-start | bytes 1160 | tf_op jit(solution)/shard_map/ppermute | solution.py:23
  12.9 3.9 %collective-permute-start = (f32[6,4,4,1]{3,2,1,0:T(4,128)S(1)}, f32[6,4,4,1]{3,2,1,0:T(4,128)S(1)}, u32[]{:S(2)}, u32[]{:S(2)}) collective-permute-start(f32[6,4,4,1]{3,2,1,0:T(4,128)S(1)} %get-tuple-element.19), channel_id=1, source_target_pairs={{0,1},{1,0},{2,3},{3,2},{4,5},{5,4},{6,7},{7,6},{8,9},{9,8},{10,11... | collective-permute-start | bytes 1160 | tf_op jit(solution)/shard_map/ppermute | solution.py:21
  16.8 1.4 %collective-permute-start.2 = (f32[6,4,1,128]{3,2,1,0:T(1,128)S(1)}, f32[6,4,1,128]{3,2,1,0:T(1,128)S(1)}, u32[]{:S(2)}, u32[]{:S(2)}) collective-permute-start(f32[6,4,1,128]{3,2,1,0:T(1,128)S(1)} %broadcast_select_fusion.2), channel_id=1, source_target_pairs={{0,4},{4,0},{1,5},{5,1},{2,6},{6,2},{3,7},{7,3},{8,12},{12,8},{9,1... | collective-permute-start | bytes 36872 | tf_op jit(solution)/shard_map/ppermute | solution.py:21
  18.3 1.2 %collective-permute-start.3 = (f32[6,1,4,128]{3,2,1,0:T(4,128)S(1)}, f32[6,1,4,128]{3,2,1,0:T(4,128)S(1)}, u32[]{:S(2)}, u32[]{:S(2)}) collective-permute-start(f32[6,1,4,128]{3,2,1,0:T(4,128)S(1)} %get-tuple-element.16), channel_id=1, source_target_pairs={{0,8},{8,0},{16,24},{24,16},{1,9},{9,1},{17,25},{25,17},{2,10},{10... | collective-permute-start | bytes 36872 | tf_op jit(solution)/shard_map/ppermute | solution.py:21
  19.5 3.0 %collective-permute-start.4 = (f32[6,1,4,128]{3,2,1,0:T(4,128)S(1)}, f32[6,1,4,128]{3,2,1,0:T(4,128)S(1)}, u32[]{:S(2)}, u32[]{:S(2)}) collective-permute-start(f32[6,1,4,128]{3,2,1,0:T(4,128)S(1)} %get-tuple-element.17), channel_id=1, source_target_pairs={{8,16},{16,8},{9,17},{17,9},{10,18},{18,10},{11,19},{19,11},{12,20... | collective-permute-start | bytes 36872 | tf_op jit(solution)/shard_map/ppermute | solution.py:23
  22.6 1.9 %collective-permute-done.4 = f32[6,1,4,128]{3,2,1,0:T(4,128)S(1)} collective-permute-done((f32[6,1,4,128]{3,2,1,0:T(4,128)S(1)}, f32[6,1,4,128]{3,2,1,0:T(4,128)S(1)}, u32[]{:S(2)}, u32[]{:S(2)}) %collective-permute-start.4) | collective-permute-done | bytes 12320 | tf_op jit(solution)/shard_map/ppermute | solution.py:23
  25.1 0.5 fusion.105
  25.6 4.0 %fusion.2 = f32[5,16,128]{2,1,0:T(8,128)S(1)} fusion(s32[16384]{0:T(1024)S(1)} %get-tuple-element.9, f32[5,16,16384]{2,1,0:T(8,128)S(1)} %fusion.105), kind=kOutput, calls=%fused_computation.3 | convolution fusion | flops 2015363072 | bytes 5349376 | tf_op jit(solution)/shard_map/cpf,fd->cpd/dot_general | solution.py:150
  29.9 0.7 %collective-permute-start.8 = (f32[5,4,4,1]{3,2,1,0:T(4,128)S(1)}, f32[5,4,4,1]{3,2,1,0:T(4,128)S(1)}, u32[]{:S(2)}, u32[]{:S(2)}) collective-permute-start(f32[5,4,4,1]{3,2,1,0:T(4,128)S(1)} %get-tuple-element.22), channel_id=1, source_target_pairs={{1,2},{2,1},{5,6},{6,5},{9,10},{10,9},{13,14},{14,13},{17,18},{18,... | collective-permute-start | bytes 968 | tf_op jit(solution)/shard_map/ppermute | solution.py:23
  30.6 1.2 %collective-permute-start.9 = (f32[5,4,4,1]{3,2,1,0:T(4,128)S(1)}, f32[5,4,4,1]{3,2,1,0:T(4,128)S(1)}, u32[]{:S(2)}, u32[]{:S(2)}) collective-permute-start(f32[5,4,4,1]{3,2,1,0:T(4,128)S(1)} %get-tuple-element.23), channel_id=1, source_target_pairs={{0,1},{1,0},{2,3},{3,2},{4,5},{5,4},{6,7},{7,6},{8,9},{9,8},{10,11... | collective-permute-start | bytes 968 | tf_op jit(solution)/shard_map/ppermute | solution.py:21
  31.9 4.1 %collective-permute-start.5 = (f32[5,1,4,128]{3,2,1,0:T(4,128)S(1)}, f32[5,1,4,128]{3,2,1,0:T(4,128)S(1)}, u32[]{:S(2)}, u32[]{:S(2)}) collective-permute-start(f32[5,1,4,128]{3,2,1,0:T(4,128)S(1)} %get-tuple-element.21), channel_id=1, source_target_pairs={{8,16},{16,8},{9,17},{17,9},{10,18},{18,10},{11,19},{19,11},{12,20... | collective-permute-start | bytes 30728 | tf_op jit(solution)/shard_map/ppermute | solution.py:23
  36.1 1.2 %collective-permute-done.5 = f32[5,1,4,128]{3,2,1,0:T(4,128)S(1)} collective-permute-done((f32[5,1,4,128]{3,2,1,0:T(4,128)S(1)}, f32[5,1,4,128]{3,2,1,0:T(4,128)S(1)}, u32[]{:S(2)}, u32[]{:S(2)}) %collective-permute-start.5) | collective-permute-done | bytes 10272 | tf_op jit(solution)/shard_map/ppermute | solution.py:23
  37.6 2.4 %convolution_bitcast_fusion = f32[3,16384,16]{1,2,0:T(8,128)S(1)} fusion(s32[16384]{0:T(1024)S(1)} %get-tuple-element.9, bf16[1,128,16]{1,2,0:T(8,128)(2,1)S(1)} %get-tuple-element.34, bf16[1,128,16]{1,2,0:T(8,128)(2,1)S(1)} %get-tuple-element.33, bf16[1,128,16]{1,2,0:T(8,128)(2,1)S(1)} %get-tuple-element.32), kind=kOutput, calls=%fused_computation | convolution fusion | flops 203436032 | bytes 3223552 | tf_op jit(solution)/shard_map/fd,kdp->kfp/dot_general | solution.py:83
  40.4 8.5 %all_to_all.10 = f32[1,128,128]{2,0,1:T(1,128)S(1)} all-to-all(f32[1,128,128]{2,0,1:T(1,128)S(1)} %bitcast.78), channel_id=1, replica_groups=mesh['stream'=4,'cross'=2,'gore'=4] {'stream','cross'}, dimensions={1} | all-to-all | bytes 131072 | tf_op jit(solution)/shard_map/all_to_all | solution.py:169
  49.2 1.5 %select_multiply_fusion = f32[3,64,128]{2,1,0:T(8,128)} fusion(f32[8,64,128]{2,1,0:T(8,128)} %param.10, f32[64,128]{1,0:T(8,128)S(1)} %fusion.62, pred[64,128]{1,0:T(8,128)(4,1)S(1)} %iota_compare_fusion.4), kind=kLoop, calls=%fused_computation.29 | loop fusion | flops 49152 | bytes 237568 | tf_op jit(solution)/shard_map/mul | solution.py:179
  (44 shorter events, 2.1 us)
Async XLA Ops:
  6.1 18.7 %all-to-all-start = ((f32[128,6,128]{2,1,0:T(8,128)}), f32[128,6,128]{2,1,0:T(8,128)S(1)}, u32[]{:S(2)}, u32[]{:S(2)}) async-start(f32[128,6,128]{2,1,0:T(8,128)} %copy.13), calls=%async_computation | async-start | bytes 1048576 | tf_op jit(solution)/shard_map/all_to_all | solution.py:132
  12.2 10.2 %collective-permute-start.1 = (f32[6,4,4,1]{3,2,1,0:T(4,128)S(1)}, f32[6,4,4,1]{3,2,1,0:T(4,128)S(1)}, u32[]{:S(2)}, u32[]{:S(2)}) collective-permute-start(f32[6,4,4,1]{3,2,1,0:T(4,128)S(1)} %get-tuple-element.18), channel_id=1, source_target_pairs={{1,2},{2,1},{5,6},{6,5},{9,10},{10,9},{13,14},{14,13},{17,18},{18,... | collective-permute-start | bytes 1160 | tf_op jit(solution)/shard_map/ppermute | solution.py:23
  12.9 9.6 %collective-permute-start = (f32[6,4,4,1]{3,2,1,0:T(4,128)S(1)}, f32[6,4,4,1]{3,2,1,0:T(4,128)S(1)}, u32[]{:S(2)}, u32[]{:S(2)}) collective-permute-start(f32[6,4,4,1]{3,2,1,0:T(4,128)S(1)} %get-tuple-element.19), channel_id=1, source_target_pairs={{0,1},{1,0},{2,3},{3,2},{4,5},{5,4},{6,7},{7,6},{8,9},{9,8},{10,11... | collective-permute-start | bytes 1160 | tf_op jit(solution)/shard_map/ppermute | solution.py:21
  16.8 7.7 %collective-permute-start.2 = (f32[6,4,1,128]{3,2,1,0:T(1,128)S(1)}, f32[6,4,1,128]{3,2,1,0:T(1,128)S(1)}, u32[]{:S(2)}, u32[]{:S(2)}) collective-permute-start(f32[6,4,1,128]{3,2,1,0:T(1,128)S(1)} %broadcast_select_fusion.2), channel_id=1, source_target_pairs={{0,4},{4,0},{1,5},{5,1},{2,6},{6,2},{3,7},{7,3},{8,12},{12,8},{9,1... | collective-permute-start | bytes 36872 | tf_op jit(solution)/shard_map/ppermute | solution.py:21
  18.3 4.3 %collective-permute-start.3 = (f32[6,1,4,128]{3,2,1,0:T(4,128)S(1)}, f32[6,1,4,128]{3,2,1,0:T(4,128)S(1)}, u32[]{:S(2)}, u32[]{:S(2)}) collective-permute-start(f32[6,1,4,128]{3,2,1,0:T(4,128)S(1)} %get-tuple-element.16), channel_id=1, source_target_pairs={{0,8},{8,0},{16,24},{24,16},{1,9},{9,1},{17,25},{25,17},{2,10},{10... | collective-permute-start | bytes 36872 | tf_op jit(solution)/shard_map/ppermute | solution.py:21
  19.5 5.0 %collective-permute-start.4 = (f32[6,1,4,128]{3,2,1,0:T(4,128)S(1)}, f32[6,1,4,128]{3,2,1,0:T(4,128)S(1)}, u32[]{:S(2)}, u32[]{:S(2)}) collective-permute-start(f32[6,1,4,128]{3,2,1,0:T(4,128)S(1)} %get-tuple-element.17), channel_id=1, source_target_pairs={{8,16},{16,8},{9,17},{17,9},{10,18},{18,10},{11,19},{19,11},{12,20... | collective-permute-start | bytes 36872 | tf_op jit(solution)/shard_map/ppermute | solution.py:23
  29.9 6.0 %collective-permute-start.8 = (f32[5,4,4,1]{3,2,1,0:T(4,128)S(1)}, f32[5,4,4,1]{3,2,1,0:T(4,128)S(1)}, u32[]{:S(2)}, u32[]{:S(2)}) collective-permute-start(f32[5,4,4,1]{3,2,1,0:T(4,128)S(1)} %get-tuple-element.22), channel_id=1, source_target_pairs={{1,2},{2,1},{5,6},{6,5},{9,10},{10,9},{13,14},{14,13},{17,18},{18,... | collective-permute-start | bytes 968 | tf_op jit(solution)/shard_map/ppermute | solution.py:23
  30.6 5.4 %collective-permute-start.9 = (f32[5,4,4,1]{3,2,1,0:T(4,128)S(1)}, f32[5,4,4,1]{3,2,1,0:T(4,128)S(1)}, u32[]{:S(2)}, u32[]{:S(2)}) collective-permute-start(f32[5,4,4,1]{3,2,1,0:T(4,128)S(1)} %get-tuple-element.23), channel_id=1, source_target_pairs={{0,1},{1,0},{2,3},{3,2},{4,5},{5,4},{6,7},{7,6},{8,9},{9,8},{10,11... | collective-permute-start | bytes 968 | tf_op jit(solution)/shard_map/ppermute | solution.py:21
  31.8 4.2 %collective-permute-start.7 = (f32[5,4,1,128]{3,2,1,0:T(1,128)S(1)}, f32[5,4,1,128]{3,2,1,0:T(1,128)S(1)}, u32[]{:S(2)}, u32[]{:S(2)}) collective-permute-start(f32[5,4,1,128]{3,2,1,0:T(1,128)S(1)} %broadcast_select_fusion.9), channel_id=1, source_target_pairs={{0,4},{4,0},{1,5},{5,1},{2,6},{6,2},{3,7},{7,3},{8,12},{12,8},{9,1... | collective-permute-start | bytes 30728 | tf_op jit(solution)/shard_map/ppermute | solution.py:21
  31.8 4.2 %collective-permute-start.6 = (f32[5,1,4,128]{3,2,1,0:T(4,128)S(1)}, f32[5,1,4,128]{3,2,1,0:T(4,128)S(1)}, u32[]{:S(2)}, u32[]{:S(2)}) collective-permute-start(f32[5,1,4,128]{3,2,1,0:T(4,128)S(1)} %get-tuple-element.20), channel_id=1, source_target_pairs={{0,8},{8,0},{16,24},{24,16},{1,9},{9,1},{17,25},{25,17},{2,10},{10... | collective-permute-start | bytes 30728 | tf_op jit(solution)/shard_map/ppermute | solution.py:21
  31.9 5.4 %collective-permute-start.5 = (f32[5,1,4,128]{3,2,1,0:T(4,128)S(1)}, f32[5,1,4,128]{3,2,1,0:T(4,128)S(1)}, u32[]{:S(2)}, u32[]{:S(2)}) collective-permute-start(f32[5,1,4,128]{3,2,1,0:T(4,128)S(1)} %get-tuple-element.21), channel_id=1, source_target_pairs={{8,16},{16,8},{9,17},{17,9},{10,18},{18,10},{11,19},{19,11},{12,20... | collective-permute-start | bytes 30728 | tf_op jit(solution)/shard_map/ppermute | solution.py:23
  37.5 13.2 %copy-start = (f32[5,4,4,128]{3,2,1,0:T(4,128)}, f32[5,4,4,128]{3,2,1,0:T(4,128)S(1)}, u32[]{:S(2)}) copy-start(f32[5,4,4,128]{3,2,1,0:T(4,128)S(1)} %fusion.27) | copy-start | bytes 122884

commit v7 on v6

--- a/solution.py
+++ b/solution.py
@@ -100,29 +100,20 @@
 
     live_rows = lax.broadcasted_iota(jnp.int32, (tile_count, row_count), 1) < lengths[:, None]
     target = routes[:, 0]
-    onehot = (target[:, None] == lax.broadcasted_iota(jnp.int32, (tile_count, blocks), 1)).astype(
-        jnp.float32
+    earlier = lax.broadcasted_iota(jnp.int32, (tile_count, tile_count), 1) < lax.broadcasted_iota(
+        jnp.int32, (tile_count, tile_count), 0
     )
-    lower = (
-        lax.broadcasted_iota(jnp.int32, (tile_count, tile_count), 1)
-        < lax.broadcasted_iota(jnp.int32, (tile_count, tile_count), 0)
-    ).astype(jnp.float32)
-    before = jnp.dot(
-        lower, onehot, precision=lax.Precision.HIGHEST, preferred_element_type=jnp.float32
+    slot_rank = jnp.sum(
+        (earlier & (target[None, :] == target[:, None])).astype(jnp.int32), axis=1
     )
-    slot_rank = jnp.sum(before * onehot, axis=1).astype(jnp.int32)
     slot_index = target * capacity + slot_rank
     placement_plan = (
         slot_index[:, None] == lax.broadcasted_iota(jnp.int32, (tile_count, slot_total), 1)
     ).astype(jnp.float32)
+    live_cells = jnp.where(live_rows, cell_ids, -1).astype(jnp.float32)
     payload = jnp.concatenate(
-        [
-            jnp.where(live_rows[:, None], records[0:5].transpose(1, 0, 2), 0.0),
-            cell_ids.astype(jnp.float32)[:, None],
-        ],
-        1,
+        [records[0:5].transpose(1, 0, 2), live_cells[:, None]], 1
     )
-    payload = jnp.concatenate([jnp.abs(payload[:, 0:1]), payload[:, 1:]], 1)
     outbound = jnp.einsum(
         "ts,tq->sq",
         placement_plan,
@@ -144,9 +135,9 @@
         depth[:, None] == lax.broadcasted_iota(jnp.int32, (faces, vertical_cells), 1)
     )
     plane_rows = plane[None, :] == lax.broadcasted_iota(jnp.int32, (plane_count, faces), 0)
-    spread = jnp.where(
-        plane_rows[None], arrived[:, 0:5].transpose(1, 0, 2).reshape(5, 1, faces), 0.0
-    )
+    arrived_values = arrived[:, 0:5].transpose(1, 0, 2).reshape(5, faces)
+    arrived_values = jnp.concatenate([jnp.abs(arrived_values[0:1]), arrived_values[1:5]], 0)
+    spread = jnp.where(plane_rows[None], arrived_values[:, None, :], 0.0)
     source = jnp.einsum(
         "cpf,fd->cpd", spread, depth_hot.astype(jnp.float32), precision=lax.Precision.HIGHEST
     )

time: 51.6 us -> 52.1 us (level)
  blocking collectives: 8.55 us -> 0 us
  waiting for transfers between devices: 3.14 us -> 7.51 us
  starting transfers between devices: 21.4 us -> 25.7 us
  local copies, waits for them, and re-layouts: 1.17 us -> 2.18 us
  matrix products: 7.89 us -> 7.02 us
    all_to_all x1 -> x0, blocking collectives: 8.55 us -> none  [shards(): lax.all_to_all(face_pressure.reshape(1, slot_total, row_count), ('stream'...]
    all_to_all x0 -> x1, waiting for transfers between devices: none -> 4.37 us  [shards(): lax.all_to_all(face_pressure.reshape(1, slot_total, row_count), ('stream'...]
    all_to_all x0 -> x1, starting transfers between devices: none -> 4.3 us  [shards(): lax.all_to_all(face_pressure.reshape(1, slot_total, row_count), ('stream'...]
    transpose x0 -> x2, local copies, waits for them, and re-layouts: none -> 0.96 us  [the longest x1 0.93 us: shards(): records[0:5].transpose(1, 0, 2)]
    select_n x1 -> x0, other arithmetic: 0.93 us -> none  [shards(): jnp.where(live_rows[:, None], records[0:5].transpose(1, 0, 2), 0.0)]
    reduce_sum x0 -> x1, other arithmetic: none -> 0.91 us  [shards(): jnp.sum((earlier & (target[None, :] == target[:, None])).astype(jnp.int32...]
    dot_general x1 -> x0, matrix products: 0.87 us -> none  [shards(): jnp.dot(lower, onehot, precision=lax.Precision.HIGHEST, preferred_element...]
    lt x1, other arithmetic: 0.73 us -> 0.07 us  [shards(): lax.broadcasted_iota(jnp.int32, (tile_count, row_count), 1)]
  transfers between devices with their start and end apart: 11 -> 12, of which waited for: 2 -> 3; matrix products, arithmetic and copies ran while one was open for 3% -> 3% of each run, Pallas kernels for 0% -> 0%
where the time goes in v7:
time: 52.1 us; the launch traced here: 51.2 us
  starting transfers between devices  25.7 us (49%)
  other arithmetic  7.72 us (15%)
  waiting for transfers between devices  7.51 us (14%)
  matrix products  7.02 us (13%)
  local copies, waits for them, and re-layouts  2.18 us (4%)
  between operations  1.02 us (2%)
    ppermute x4, starting transfers between devices, face_halo(): from_b = lax.ppermute(jnp.where(odd, last, first), axis, pairs_b)  8.37 us
    ppermute x6, starting transfers between devices, face_halo(): from_a = lax.ppermute(jnp.where(odd, first, last), axis, pairs_a)  7.84 us
    all_to_all x1, starting transfers between devices, shards(): lax.all_to_all(outbound, ('stream', 'cross'), split_axis=0, concat_axis=0...  5.22 us
    all_to_all x1, waiting for transfers between devices, shards(): lax.all_to_all(face_pressure.reshape(1, slot_total, row_count), ('stream'...  4.37 us
    all_to_all x1, starting transfers between devices, shards(): lax.all_to_all(face_pressure.reshape(1, slot_total, row_count), ('stream'...  4.3 us
    dot_general x1, matrix products, shards(): jnp.einsum('cpf,fd->cpd', spread, depth_hot.astype(jnp.float32), precisio...  3.97 us
    ppermute x4, waiting for transfers between devices, face_halo(): from_b = lax.ppermute(jnp.where(odd, last, first), axis, pairs_b)  3.12 us
    dot_general x1, matrix products, exact_dot(): jnp.einsum(left + ',k' + right + '->k' + output, onehot, stacked, preferr...  2.4 us
  transfers between devices with their start and end apart: 12, of which 3 were waited for; matrix products, arithmetic and copies ran while one was open for 3% of the time, Pallas kernels for 0%

profile of v7, /device:TPU:1, one launch (start us, length us, event | category | flops | bytes accessed | tf_op | source)
XLA Modules:
  0.0 51.2 jit_solution(4578271484463591267)
XLA Ops:
  0.6 0.9 %convert_reduce_fusion = s32[64]{0:T(128)S(1)} fusion(s32[64]{0:T(128)} %bitcast.93), kind=kLoop, calls=%fused_computation.133 | loop fusion | flops 20416 | bytes 512 | tf_op jit(solution)/shard_map/reduce_sum | solution.py:106
  1.5 0.7 %fusion.90 = s32[64]{0:T(128)S(1)} fusion(s32[64]{0:T(128)S(1)} %convert_reduce_fusion, s32[64,1]{0,1:T(1,128)} %param.12), kind=kLoop, calls=%fused_computation.194 | loop fusion | flops 128 | bytes 768 | tf_op jit(solution)/shard_map/eq | solution.py:111
  2.2 0.9 %slice_bitcast_fusion.2 = f32[64,5,128]{2,0,1:T(8,128)S(1)} fusion(f32[8,64,128]{2,1,0:T(8,128)} %param.10), kind=kLoop, calls=%fused_computation.25 | loop fusion | bytes 327680 | tf_op jit(solution)/shard_map/transpose | solution.py:115
  3.1 0.8 %convert_bitcast_fusion = f32[64,1,128]{2,0,1:T(8,128)S(1)} fusion(s32[64,128]{1,0:T(8,128)} %param.11, s32[64]{0:T(128)} %param.13), kind=kLoop, calls=%fused_computation.128 | loop fusion | flops 24576 | bytes 65792 | tf_op jit(solution)/shard_map/broadcast_in_dim | solution.py:115
  4.4 1.0 %copy.16 = f32[128,6,128]{2,1,0:T(8,128)} copy(f32[128,6,128]{2,0,1:T(8,128)S(1)} %fusion.13) | data formatting | bytes 786432 | tf_op jit(solution)/shard_map/ts,tq->sq/dot_general | solution.py:117
  5.5 5.2 %all-to-all-start = ((f32[128,6,128]{2,1,0:T(8,128)}), f32[128,6,128]{2,1,0:T(8,128)S(1)}, u32[]{:S(2)}, u32[]{:S(2)}) async-start(f32[128,6,128]{2,1,0:T(8,128)} %copy.16), calls=%async_computation | async-start | bytes 1048576 | tf_op jit(solution)/shard_map/all_to_all | solution.py:123
  10.7 0.8 %pad_maximum_fusion.7 = f32[6,4,4,128]{3,2,1,0:T(4,128)S(1)} fusion(f32[1,4,4,128]{3,2,1,0:T(4,128)} %bitcast.91, f32[4,4,4,128]{3,2,1,0:T(4,128)} %param.8, f32[1,4,4,128]{3,2,1,0:T(4,128)} %bitcast.92), kind=kLoop, calls=%fused_computation.45 | loop fusion | flops 24576 | bytes 98304 | tf_op jit(solution)/shard_map/concatenate | solution.py:125
  11.6 0.7 %collective-permute-start.1 = (f32[6,4,4,1]{3,2,1,0:T(4,128)S(1)}, f32[6,4,4,1]{3,2,1,0:T(4,128)S(1)}, u32[]{:S(2)}, u32[]{:S(2)}) collective-permute-start(f32[6,4,4,1]{3,2,1,0:T(4,128)S(1)} %get-tuple-element.18), channel_id=1, source_target_pairs={{1,2},{2,1},{5,6},{6,5},{9,10},{10,9},{13,14},{14,13},{17,18},{18,... | collective-permute-start | bytes 1160 | tf_op jit(solution)/shard_map/ppermute | solution.py:23
  12.3 3.9 %collective-permute-start = (f32[6,4,4,1]{3,2,1,0:T(4,128)S(1)}, f32[6,4,4,1]{3,2,1,0:T(4,128)S(1)}, u32[]{:S(2)}, u32[]{:S(2)}) collective-permute-start(f32[6,4,4,1]{3,2,1,0:T(4,128)S(1)} %get-tuple-element.19), channel_id=1, source_target_pairs={{0,1},{1,0},{2,3},{3,2},{4,5},{5,4},{6,7},{7,6},{8,9},{9,8},{10,11... | collective-permute-start | bytes 1160 | tf_op jit(solution)/shard_map/ppermute | solution.py:21
  16.2 1.4 %collective-permute-start.2 = (f32[6,4,1,128]{3,2,1,0:T(1,128)S(1)}, f32[6,4,1,128]{3,2,1,0:T(1,128)S(1)}, u32[]{:S(2)}, u32[]{:S(2)}) collective-permute-start(f32[6,4,1,128]{3,2,1,0:T(1,128)S(1)} %broadcast_select_fusion.2), channel_id=1, source_target_pairs={{0,4},{4,0},{1,5},{5,1},{2,6},{6,2},{3,7},{7,3},{8,12},{12,8},{9,1... | collective-permute-start | bytes 36872 | tf_op jit(solution)/shard_map/ppermute | solution.py:21
  17.6 1.2 %collective-permute-start.3 = (f32[6,1,4,128]{3,2,1,0:T(4,128)S(1)}, f32[6,1,4,128]{3,2,1,0:T(4,128)S(1)}, u32[]{:S(2)}, u32[]{:S(2)}) collective-permute-start(f32[6,1,4,128]{3,2,1,0:T(4,128)S(1)} %get-tuple-element.16), channel_id=1, source_target_pairs={{0,8},{8,0},{16,24},{24,16},{1,9},{9,1},{17,25},{25,17},{2,10},{10... | collective-permute-start | bytes 36872 | tf_op jit(solution)/shard_map/ppermute | solution.py:21
  18.8 3.0 %collective-permute-start.4 = (f32[6,1,4,128]{3,2,1,0:T(4,128)S(1)}, f32[6,1,4,128]{3,2,1,0:T(4,128)S(1)}, u32[]{:S(2)}, u32[]{:S(2)}) collective-permute-start(f32[6,1,4,128]{3,2,1,0:T(4,128)S(1)} %get-tuple-element.17), channel_id=1, source_target_pairs={{8,16},{16,8},{9,17},{17,9},{10,18},{18,10},{11,19},{19,11},{12,20... | collective-permute-start | bytes 36872 | tf_op jit(solution)/shard_map/ppermute | solution.py:23
  21.9 1.9 %collective-permute-done.4 = f32[6,1,4,128]{3,2,1,0:T(4,128)S(1)} collective-permute-done((f32[6,1,4,128]{3,2,1,0:T(4,128)S(1)}, f32[6,1,4,128]{3,2,1,0:T(4,128)S(1)}, u32[]{:S(2)}, u32[]{:S(2)}) %collective-permute-start.4) | collective-permute-done | bytes 12320 | tf_op jit(solution)/shard_map/ppermute | solution.py:23
  24.8 0.5 fusion.100
  25.2 4.0 %fusion.2 = f32[5,16,128]{2,1,0:T(8,128)S(1)} fusion(s32[16384]{0:T(1024)S(1)} %get-tuple-element.9, f32[5,16,16384]{2,1,0:T(8,128)S(1)} %fusion.100), kind=kOutput, calls=%fused_computation.3 | convolution fusion | flops 2015363072 | bytes 5349376 | tf_op jit(solution)/shard_map/cpf,fd->cpd/dot_general | solution.py:141
  29.6 0.7 %collective-permute-start.8 = (f32[5,4,4,1]{3,2,1,0:T(4,128)S(1)}, f32[5,4,4,1]{3,2,1,0:T(4,128)S(1)}, u32[]{:S(2)}, u32[]{:S(2)}) collective-permute-start(f32[5,4,4,1]{3,2,1,0:T(4,128)S(1)} %get-tuple-element.22), channel_id=1, source_target_pairs={{1,2},{2,1},{5,6},{6,5},{9,10},{10,9},{13,14},{14,13},{17,18},{18,... | collective-permute-start | bytes 968 | tf_op jit(solution)/shard_map/ppermute | solution.py:23
  30.3 1.2 %collective-permute-start.9 = (f32[5,4,4,1]{3,2,1,0:T(4,128)S(1)}, f32[5,4,4,1]{3,2,1,0:T(4,128)S(1)}, u32[]{:S(2)}, u32[]{:S(2)}) collective-permute-start(f32[5,4,4,1]{3,2,1,0:T(4,128)S(1)} %get-tuple-element.23), channel_id=1, source_target_pairs={{0,1},{1,0},{2,3},{3,2},{4,5},{5,4},{6,7},{7,6},{8,9},{9,8},{10,11... | collective-permute-start | bytes 968 | tf_op jit(solution)/shard_map/ppermute | solution.py:21
  31.6 4.1 %collective-permute-start.5 = (f32[5,1,4,128]{3,2,1,0:T(4,128)S(1)}, f32[5,1,4,128]{3,2,1,0:T(4,128)S(1)}, u32[]{:S(2)}, u32[]{:S(2)}) collective-permute-start(f32[5,1,4,128]{3,2,1,0:T(4,128)S(1)} %get-tuple-element.21), channel_id=1, source_target_pairs={{8,16},{16,8},{9,17},{17,9},{10,18},{18,10},{11,19},{19,11},{12,20... | collective-permute-start | bytes 30728 | tf_op jit(solution)/shard_map/ppermute | solution.py:23
  35.7 1.2 %collective-permute-done.5 = f32[5,1,4,128]{3,2,1,0:T(4,128)S(1)} collective-permute-done((f32[5,1,4,128]{3,2,1,0:T(4,128)S(1)}, f32[5,1,4,128]{3,2,1,0:T(4,128)S(1)}, u32[]{:S(2)}, u32[]{:S(2)}) %collective-permute-start.5) | collective-permute-done | bytes 10272 | tf_op jit(solution)/shard_map/ppermute | solution.py:23
  37.2 2.4 %convolution_bitcast_fusion = f32[3,16384,16]{1,2,0:T(8,128)S(1)} fusion(s32[16384]{0:T(1024)S(1)} %get-tuple-element.9, bf16[1,128,16]{1,2,0:T(8,128)(2,1)S(1)} %get-tuple-element.34, bf16[1,128,16]{1,2,0:T(8,128)(2,1)S(1)} %get-tuple-element.33, bf16[1,128,16]{1,2,0:T(8,128)(2,1)S(1)} %get-tuple-element.32), kind=kOutput, calls=%fused_computation | convolution fusion | flops 203436032 | bytes 3223552 | tf_op jit(solution)/shard_map/fd,kdp->kfp/dot_general | solution.py:83
  39.7 1.0 %fusion.12 = f32[16384]{0:T(1024)} fusion(f32[3,16384,16]{1,2,0:T(8,128)S(1)} %convolution_bitcast_fusion, s32[16384]{0:T(1024)S(1)} %get-tuple-element.8), kind=kLoop, calls=%fused_computation.13 | loop fusion | flops 1294336 | bytes 3276800 | tf_op jit(solution)/shard_map/reduce_sum | solution.py:159
  40.7 4.3 %all-to-all-start.1 = ((f32[1,128,128]{2,0,1:T(1,128)}), f32[1,128,128]{2,0,1:T(1,128)S(1)}, u32[]{:S(2)}, u32[]{:S(2)}) async-start(f32[1,128,128]{2,0,1:T(1,128)} %bitcast.24), calls=%async_computation.1 | async-start | bytes 131072 | tf_op jit(solution)/shard_map/all_to_all | solution.py:160
  45.0 4.4 %all-to-all-done.1 = f32[1,128,128]{2,0,1:T(1,128)S(1)} async-done(((f32[1,128,128]{2,0,1:T(1,128)}), f32[1,128,128]{2,0,1:T(1,128)S(1)}, u32[]{:S(2)}, u32[]{:S(2)}) %all-to-all-start.1) | async-done | bytes 65568 | tf_op jit(solution)/shard_map/all_to_all | solution.py:160
  49.6 1.6 %select_multiply_fusion = f32[3,64,128]{2,1,0:T(8,128)} fusion(f32[8,64,128]{2,1,0:T(8,128)} %param.10, f32[64,128]{1,0:T(8,128)S(1)} %fusion.60, pred[64,128]{1,0:T(8,128)(4,1)S(1)} %iota_compare_fusion.3), kind=kLoop, calls=%fused_computation.26 | loop fusion | flops 49152 | bytes 237568 | tf_op jit(solution)/shard_map/mul | solution.py:170
  (49 shorter events, 2.5 us)
Async XLA Ops:
  5.5 18.7 %all-to-all-start = ((f32[128,6,128]{2,1,0:T(8,128)}), f32[128,6,128]{2,1,0:T(8,128)S(1)}, u32[]{:S(2)}, u32[]{:S(2)}) async-start(f32[128,6,128]{2,1,0:T(8,128)} %copy.16), calls=%async_computation | async-start | bytes 1048576 | tf_op jit(solution)/shard_map/all_to_all | solution.py:123
  11.6 10.2 %collective-permute-start.1 = (f32[6,4,4,1]{3,2,1,0:T(4,128)S(1)}, f32[6,4,4,1]{3,2,1,0:T(4,128)S(1)}, u32[]{:S(2)}, u32[]{:S(2)}) collective-permute-start(f32[6,4,4,1]{3,2,1,0:T(4,128)S(1)} %get-tuple-element.18), channel_id=1, source_target_pairs={{1,2},{2,1},{5,6},{6,5},{9,10},{10,9},{13,14},{14,13},{17,18},{18,... | collective-permute-start | bytes 1160 | tf_op jit(solution)/shard_map/ppermute | solution.py:23
  12.3 9.6 %collective-permute-start = (f32[6,4,4,1]{3,2,1,0:T(4,128)S(1)}, f32[6,4,4,1]{3,2,1,0:T(4,128)S(1)}, u32[]{:S(2)}, u32[]{:S(2)}) collective-permute-start(f32[6,4,4,1]{3,2,1,0:T(4,128)S(1)} %get-tuple-element.19), channel_id=1, source_target_pairs={{0,1},{1,0},{2,3},{3,2},{4,5},{5,4},{6,7},{7,6},{8,9},{9,8},{10,11... | collective-permute-start | bytes 1160 | tf_op jit(solution)/shard_map/ppermute | solution.py:21
  16.2 7.7 %collective-permute-start.2 = (f32[6,4,1,128]{3,2,1,0:T(1,128)S(1)}, f32[6,4,1,128]{3,2,1,0:T(1,128)S(1)}, u32[]{:S(2)}, u32[]{:S(2)}) collective-permute-start(f32[6,4,1,128]{3,2,1,0:T(1,128)S(1)} %broadcast_select_fusion.2), channel_id=1, source_target_pairs={{0,4},{4,0},{1,5},{5,1},{2,6},{6,2},{3,7},{7,3},{8,12},{12,8},{9,1... | collective-permute-start | bytes 36872 | tf_op jit(solution)/shard_map/ppermute | solution.py:21
  17.6 4.3 %collective-permute-start.3 = (f32[6,1,4,128]{3,2,1,0:T(4,128)S(1)}, f32[6,1,4,128]{3,2,1,0:T(4,128)S(1)}, u32[]{:S(2)}, u32[]{:S(2)}) collective-permute-start(f32[6,1,4,128]{3,2,1,0:T(4,128)S(1)} %get-tuple-element.16), channel_id=1, source_target_pairs={{0,8},{8,0},{16,24},{24,16},{1,9},{9,1},{17,25},{25,17},{2,10},{10... | collective-permute-start | bytes 36872 | tf_op jit(solution)/shard_map/ppermute | solution.py:21
  18.8 5.0 %collective-permute-start.4 = (f32[6,1,4,128]{3,2,1,0:T(4,128)S(1)}, f32[6,1,4,128]{3,2,1,0:T(4,128)S(1)}, u32[]{:S(2)}, u32[]{:S(2)}) collective-permute-start(f32[6,1,4,128]{3,2,1,0:T(4,128)S(1)} %get-tuple-element.17), channel_id=1, source_target_pairs={{8,16},{16,8},{9,17},{17,9},{10,18},{18,10},{11,19},{19,11},{12,20... | collective-permute-start | bytes 36872 | tf_op jit(solution)/shard_map/ppermute | solution.py:23
  29.2 15.7 %copy-start.1 = (s32[64]{0:T(128)S(1)}, s32[64]{0:T(128)}, u32[]{:S(2)}) copy-start(s32[64]{0:T(128)} %param.13) | copy-start | bytes 772
  29.6 6.0 %collective-permute-start.8 = (f32[5,4,4,1]{3,2,1,0:T(4,128)S(1)}, f32[5,4,4,1]{3,2,1,0:T(4,128)S(1)}, u32[]{:S(2)}, u32[]{:S(2)}) collective-permute-start(f32[5,4,4,1]{3,2,1,0:T(4,128)S(1)} %get-tuple-element.22), channel_id=1, source_target_pairs={{1,2},{2,1},{5,6},{6,5},{9,10},{10,9},{13,14},{14,13},{17,18},{18,... | collective-permute-start | bytes 968 | tf_op jit(solution)/shard_map/ppermute | solution.py:23
  30.3 5.4 %collective-permute-start.9 = (f32[5,4,4,1]{3,2,1,0:T(4,128)S(1)}, f32[5,4,4,1]{3,2,1,0:T(4,128)S(1)}, u32[]{:S(2)}, u32[]{:S(2)}) collective-permute-start(f32[5,4,4,1]{3,2,1,0:T(4,128)S(1)} %get-tuple-element.23), channel_id=1, source_target_pairs={{0,1},{1,0},{2,3},{3,2},{4,5},{5,4},{6,7},{7,6},{8,9},{9,8},{10,11... | collective-permute-start | bytes 968 | tf_op jit(solution)/shard_map/ppermute | solution.py:21
  31.5 4.2 %collective-permute-start.7 = (f32[5,4,1,128]{3,2,1,0:T(1,128)S(1)}, f32[5,4,1,128]{3,2,1,0:T(1,128)S(1)}, u32[]{:S(2)}, u32[]{:S(2)}) collective-permute-start(f32[5,4,1,128]{3,2,1,0:T(1,128)S(1)} %broadcast_select_fusion.9), channel_id=1, source_target_pairs={{0,4},{4,0},{1,5},{5,1},{2,6},{6,2},{3,7},{7,3},{8,12},{12,8},{9,1... | collective-permute-start | bytes 30728 | tf_op jit(solution)/shard_map/ppermute | solution.py:21
  31.5 4.2 %collective-permute-start.6 = (f32[5,1,4,128]{3,2,1,0:T(4,128)S(1)}, f32[5,1,4,128]{3,2,1,0:T(4,128)S(1)}, u32[]{:S(2)}, u32[]{:S(2)}) collective-permute-start(f32[5,1,4,128]{3,2,1,0:T(4,128)S(1)} %get-tuple-element.20), channel_id=1, source_target_pairs={{0,8},{8,0},{16,24},{24,16},{1,9},{9,1},{17,25},{25,17},{2,10},{10... | collective-permute-start | bytes 30728 | tf_op jit(solution)/shard_map/ppermute | solution.py:21
  31.6 5.4 %collective-permute-start.5 = (f32[5,1,4,128]{3,2,1,0:T(4,128)S(1)}, f32[5,1,4,128]{3,2,1,0:T(4,128)S(1)}, u32[]{:S(2)}, u32[]{:S(2)}) collective-permute-start(f32[5,1,4,128]{3,2,1,0:T(4,128)S(1)} %get-tuple-element.21), channel_id=1, source_target_pairs={{8,16},{16,8},{9,17},{17,9},{10,18},{18,10},{11,19},{19,11},{12,20... | collective-permute-start | bytes 30728 | tf_op jit(solution)/shard_map/ppermute | solution.py:23
  37.2 14.0 %copy-start = (f32[5,4,4,128]{3,2,1,0:T(4,128)}, f32[5,4,4,128]{3,2,1,0:T(4,128)S(1)}, u32[]{:S(2)}) copy-start(f32[5,4,4,128]{3,2,1,0:T(4,128)S(1)} %fusion.25) | copy-start | bytes 122884
  40.7 8.8 %all-to-all-start.1 = ((f32[1,128,128]{2,0,1:T(1,128)}), f32[1,128,128]{2,0,1:T(1,128)S(1)}, u32[]{:S(2)}, u32[]{:S(2)}) async-start(f32[1,128,128]{2,0,1:T(1,128)} %bitcast.24), calls=%async_computation.1 | async-start | bytes 131072 | tf_op jit(solution)/shard_map/all_to_all | solution.py:160

commit v8 on v7

--- a/solution.py
+++ b/solution.py
@@ -111,31 +111,30 @@
         slot_index[:, None] == lax.broadcasted_iota(jnp.int32, (tile_count, slot_total), 1)
     ).astype(jnp.float32)
     live_cells = jnp.where(live_rows, cell_ids, -1).astype(jnp.float32)
-    payload = jnp.concatenate(
-        [records[0:5].transpose(1, 0, 2), live_cells[:, None]], 1
+    payload = jnp.concatenate([records[0:5], live_cells[None]], 0)
+    outbound = jnp.einsum(
+        "ts,ctr->csr", placement_plan, payload, precision=lax.Precision.HIGHEST
     )
-    outbound = jnp.einsum(
-        "ts,tq->sq",
-        placement_plan,
-        payload.reshape(tile_count, 6 * row_count),
-        precision=lax.Precision.HIGHEST,
-    ).reshape(slot_total, 6, row_count)
-    arrived = lax.all_to_all(outbound, ("stream", "cross"), split_axis=0, concat_axis=0, tiled=True)
-    outbound, state_and_visc = lax.optimization_barrier(
-        (outbound, jnp.concatenate([fluid_state, viscosity[None]], 0))
+    arrived = lax.all_to_all(outbound, ("stream", "cross"), split_axis=1, concat_axis=1, tiled=True)
+    outbound, state_and_visc, load_rows = lax.optimization_barrier(
+        (
+            outbound,
+            jnp.concatenate([fluid_state, viscosity[None]], 0),
+            jnp.where(live_rows[None], records[5:8], 0.0),
+        )
     )
     state_visc = face_halo(state_and_visc)
     state_pad = state_visc[0:5]
     visc_pad = state_visc[5]
 
-    cells = jnp.round(arrived[:, 5]).astype(jnp.int32).reshape(faces)
+    cells = jnp.round(arrived[5]).astype(jnp.int32).reshape(faces)
     plane = cells // vertical_cells
     depth = cells % vertical_cells
     depth_hot = (
         depth[:, None] == lax.broadcasted_iota(jnp.int32, (faces, vertical_cells), 1)
     )
     plane_rows = plane[None, :] == lax.broadcasted_iota(jnp.int32, (plane_count, faces), 0)
-    arrived_values = arrived[:, 0:5].transpose(1, 0, 2).reshape(5, faces)
+    arrived_values = arrived[0:5].reshape(5, faces)
     arrived_values = jnp.concatenate([jnp.abs(arrived_values[0:1]), arrived_values[1:5]], 0)
     spread = jnp.where(plane_rows[None], arrived_values[:, None, :], 0.0)
     source = jnp.einsum(
@@ -167,7 +166,7 @@
     home_pressure = jnp.einsum(
         "ts,sr->tr", placement_plan, returned[0], precision=lax.Precision.HIGHEST
     )
-    face_loads = jnp.where(live_rows[None], records[5:8], 0.0) * home_pressure[None]
+    face_loads = load_rows * home_pressure[None]
     return (new_state, face_loads)
 
 

time: 52.1 us -> 52 us (level)
  blocking collectives: 0 us -> 8.55 us
  waiting for transfers between devices: 7.51 us -> 3.14 us
  starting transfers between devices: 25.7 us -> 21.4 us
    all_to_all x0 -> x1, blocking collectives: none -> 8.55 us  [shards(): lax.all_to_all(face_pressure.reshape(1, slot_total, row_count), ('stream'...]
    all_to_all x2 -> x1, waiting for transfers between devices: 4.38 us -> 0.01 us  [shards(): lax.all_to_all(outbound, ('stream', 'cross'), split_axis=1, concat_axis=1...]
    all_to_all x2 -> x1, starting transfers between devices: 9.52 us -> 5.22 us  [shards(): lax.all_to_all(outbound, ('stream', 'cross'), split_axis=1, concat_axis=1...]
    dot_general x1 -> x0, local copies, waits for them, and re-layouts: 1.04 us -> none  [shards(): jnp.einsum('ts,tq->sq', placement_plan, payload.reshape(tile_count, 6 * r...]
    slice x0 -> x2, local copies, waits for them, and re-layouts: none -> 1.03 us  [the longest x1 0.93 us: shards(): payload = jnp.concatenate([records[0:5], live_cells[None]], 0)]
    select_n x0 -> x1, other arithmetic: none -> 0.91 us  [shards(): jnp.where(live_rows[None], records[5:8], 0.0)]
    mul x1, other arithmetic: 1.55 us -> 0.65 us  [shards(): face_loads = load_rows * home_pressure[None]]
    lt x1, other arithmetic: 0.07 us -> 0.73 us  [shards(): lax.broadcasted_iota(jnp.int32, (tile_count, row_count), 1)]
  transfers between devices with their start and end apart: 12 -> 11, of which waited for: 3 -> 2; matrix products, arithmetic and copies ran while one was open for 3% -> 6% of each run, Pallas kernels for 0% -> 0%
where the time goes in v8:
time: 52 us; the launch traced here: 51.1 us
  starting transfers between devices  21.4 us (41%)
  blocking collectives  8.55 us (16%)
  other arithmetic  7.63 us (15%)
  matrix products  7.11 us (14%)
  waiting for transfers between devices  3.14 us (6%)
  local copies, waits for them, and re-layouts  2.21 us (4%)
  between operations  1.03 us (2%)
    all_to_all x1, blocking collectives, shards(): lax.all_to_all(face_pressure.reshape(1, slot_total, row_count), ('stream'...  8.55 us
    ppermute x4, starting transfers between devices, face_halo(): from_b = lax.ppermute(jnp.where(odd, last, first), axis, pairs_b)  8.42 us
    ppermute x6, starting transfers between devices, face_halo(): from_a = lax.ppermute(jnp.where(odd, first, last), axis, pairs_a)  7.79 us
    all_to_all x1, starting transfers between devices, shards(): lax.all_to_all(outbound, ('stream', 'cross'), split_axis=1, concat_axis=1...  5.22 us
    dot_general x1, matrix products, shards(): jnp.einsum('cpf,fd->cpd', spread, depth_hot.astype(jnp.float32), precisio...  3.98 us
    ppermute x4, waiting for transfers between devices, face_halo(): from_b = lax.ppermute(jnp.where(odd, last, first), axis, pairs_b)  3.12 us
    dot_general x1, matrix products, exact_dot(): jnp.einsum(left + ',k' + right + '->k' + output, onehot, stacked, preferr...  2.4 us
  transfers between devices with their start and end apart: 11, of which 2 were waited for; matrix products, arithmetic and copies ran while one was open for 6% of the time, Pallas kernels for 0%

profile of v8, /device:TPU:1, one launch (start us, length us, event | category | flops | bytes accessed | tf_op | source)
XLA Modules:
  0.0 51.1 jit_solution(12141305638544863209)
XLA Ops:
  0.6 0.9 %slice.190 = f32[5,64,128]{2,1,0:T(8,128)S(1)} slice(f32[8,64,128]{2,1,0:T(8,128)} %param.10), slice={[0:5], [0:64], [0:128]} | slice | bytes 327680 | tf_op jit(solution)/shard_map/slice | solution.py:114
  1.6 0.9 %convert_reduce_fusion = s32[64]{0:T(128)S(1)} fusion(s32[64]{0:T(128)} %bitcast.103), kind=kLoop, calls=%fused_computation.127 | loop fusion | flops 20416 | bytes 512 | tf_op jit(solution)/shard_map/reduce_sum | solution.py:106
  2.5 0.7 %fusion.89 = s32[64]{0:T(128)S(1)} fusion(s32[64]{0:T(128)S(1)} %convert_reduce_fusion, s32[64,1]{0,1:T(1,128)} %param.12), kind=kLoop, calls=%fused_computation.190 | loop fusion | flops 128 | bytes 768 | tf_op jit(solution)/shard_map/eq | solution.py:111
  3.1 0.8 %convert_bitcast_fusion = f32[1,64,128]{2,1,0:T(8,128)S(1)} fusion(s32[64,128]{1,0:T(8,128)} %param.11, s32[64]{0:T(128)} %param.13), kind=kLoop, calls=%fused_computation.129 | loop fusion | flops 24576 | bytes 65792 | tf_op jit(solution)/shard_map/broadcast_in_dim | solution.py:114
  4.0 0.5 %convolution_bitcast_fusion.1 = f32[6,128,128]{1,2,0:T(8,128)S(1)} fusion(f32[1,64,128]{2,1,0:T(8,128)S(1)} %convert_bitcast_fusion, f32[5,64,128]{2,1,0:T(8,128)S(1)} %slice.190, s32[64]{0:T(128)S(1)} %fusion.89), kind=kOutput, calls=%fused_computation.10 | convolution fusion | flops 75554816 | bytes 590080 | tf_op jit(solution)/shard_map/ts,ctr->csr/dot_general | solution.py:115
  4.5 1.0 %copy.15 = f32[6,128,128]{2,0,1:T(8,128)} copy(f32[6,128,128]{1,2,0:T(8,128)S(1)} %convolution_bitcast_fusion.1) | data formatting | bytes 786432 | tf_op jit(solution)/shard_map/ts,ctr->csr/transpose | solution.py:115
  5.5 5.2 %all-to-all-start = ((f32[6,128,128]{2,0,1:T(8,128)}), f32[6,128,128]{2,0,1:T(8,128)S(1)}, u32[]{:S(2)}, u32[]{:S(2)}) async-start(f32[6,128,128]{2,0,1:T(8,128)} %copy.15), calls=%async_computation | async-start | bytes 1048576 | tf_op jit(solution)/shard_map/all_to_all | solution.py:118
  10.7 0.7 %iota_compare_fusion.6 = pred[64,128]{1,0:T(8,128)(4,1)S(1)} fusion(s32[64]{0:T(128)} %param.13), kind=kLoop, calls=%fused_computation.130 | loop fusion | flops 8192 | bytes 8448 | tf_op jit(solution)/shard_map/lt | solution.py:101
  11.5 0.9 %slice_select_fusion = f32[3,64,128]{2,1,0:T(8,128)S(1)} fusion(f32[8,64,128]{2,1,0:T(8,128)} %param.10, pred[64,128]{1,0:T(8,128)(4,1)S(1)} %iota_compare_fusion.6), kind=kLoop, calls=%fused_computation.28 | loop fusion | flops 24576 | bytes 204800 | tf_op jit(solution)/shard_map/jit(_where)/select_n | solution.py:123
  12.4 0.8 %pad_maximum_fusion.7 = f32[6,4,4,128]{3,2,1,0:T(4,128)S(1)} fusion(f32[1,4,4,128]{3,2,1,0:T(4,128)} %bitcast.101, f32[4,4,4,128]{3,2,1,0:T(4,128)} %param.8, f32[1,4,4,128]{3,2,1,0:T(4,128)} %bitcast.102), kind=kLoop, calls=%fused_computation.40 | loop fusion | flops 24576 | bytes 98304 | tf_op jit(solution)/shard_map/concatenate | solution.py:122
  13.3 0.7 %collective-permute-start.1 = (f32[6,4,4,1]{3,2,1,0:T(4,128)S(1)}, f32[6,4,4,1]{3,2,1,0:T(4,128)S(1)}, u32[]{:S(2)}, u32[]{:S(2)}) collective-permute-start(f32[6,4,4,1]{3,2,1,0:T(4,128)S(1)} %get-tuple-element.22), channel_id=1, source_target_pairs={{1,2},{2,1},{5,6},{6,5},{9,10},{10,9},{13,14},{14,13},{17,18},{18,... | collective-permute-start | bytes 1160 | tf_op jit(solution)/shard_map/ppermute | solution.py:23
  14.0 3.9 %collective-permute-start = (f32[6,4,4,1]{3,2,1,0:T(4,128)S(1)}, f32[6,4,4,1]{3,2,1,0:T(4,128)S(1)}, u32[]{:S(2)}, u32[]{:S(2)}) collective-permute-start(f32[6,4,4,1]{3,2,1,0:T(4,128)S(1)} %get-tuple-element.23), channel_id=1, source_target_pairs={{0,1},{1,0},{2,3},{3,2},{4,5},{5,4},{6,7},{7,6},{8,9},{9,8},{10,11... | collective-permute-start | bytes 1160 | tf_op jit(solution)/shard_map/ppermute | solution.py:21
  17.9 1.4 %collective-permute-start.2 = (f32[6,4,1,128]{3,2,1,0:T(1,128)S(1)}, f32[6,4,1,128]{3,2,1,0:T(1,128)S(1)}, u32[]{:S(2)}, u32[]{:S(2)}) collective-permute-start(f32[6,4,1,128]{3,2,1,0:T(1,128)S(1)} %broadcast_select_fusion.2), channel_id=1, source_target_pairs={{0,4},{4,0},{1,5},{5,1},{2,6},{6,2},{3,7},{7,3},{8,12},{12,8},{9,1... | collective-permute-start | bytes 36872 | tf_op jit(solution)/shard_map/ppermute | solution.py:21
  19.3 1.2 %collective-permute-start.3 = (f32[6,1,4,128]{3,2,1,0:T(4,128)S(1)}, f32[6,1,4,128]{3,2,1,0:T(4,128)S(1)}, u32[]{:S(2)}, u32[]{:S(2)}) collective-permute-start(f32[6,1,4,128]{3,2,1,0:T(4,128)S(1)} %get-tuple-element.20), channel_id=1, source_target_pairs={{0,8},{8,0},{16,24},{24,16},{1,9},{9,1},{17,25},{25,17},{2,10},{10... | collective-permute-start | bytes 36872 | tf_op jit(solution)/shard_map/ppermute | solution.py:21
  20.5 3.0 %collective-permute-start.4 = (f32[6,1,4,128]{3,2,1,0:T(4,128)S(1)}, f32[6,1,4,128]{3,2,1,0:T(4,128)S(1)}, u32[]{:S(2)}, u32[]{:S(2)}) collective-permute-start(f32[6,1,4,128]{3,2,1,0:T(4,128)S(1)} %get-tuple-element.21), channel_id=1, source_target_pairs={{8,16},{16,8},{9,17},{17,9},{10,18},{18,10},{11,19},{19,11},{12,20... | collective-permute-start | bytes 36872 | tf_op jit(solution)/shard_map/ppermute | solution.py:23
  23.6 1.9 %collective-permute-done.4 = f32[6,1,4,128]{3,2,1,0:T(4,128)S(1)} collective-permute-done((f32[6,1,4,128]{3,2,1,0:T(4,128)S(1)}, f32[6,1,4,128]{3,2,1,0:T(4,128)S(1)}, u32[]{:S(2)}, u32[]{:S(2)}) %collective-permute-start.4) | collective-permute-done | bytes 12320 | tf_op jit(solution)/shard_map/ppermute | solution.py:23
  26.9 4.0 %fusion.2 = f32[5,16,128]{2,1,0:T(8,128)S(1)} fusion(s32[16384]{0:T(1024)S(1)} %get-tuple-element.13, f32[5,16,16384]{2,1,0:T(8,128)S(1)} %fusion.101), kind=kOutput, calls=%fused_computation.3 | convolution fusion | flops 2015363072 | bytes 5349376 | tf_op jit(solution)/shard_map/cpf,fd->cpd/dot_general | solution.py:140
  31.2 0.7 %collective-permute-start.8 = (f32[5,4,4,1]{3,2,1,0:T(4,128)S(1)}, f32[5,4,4,1]{3,2,1,0:T(4,128)S(1)}, u32[]{:S(2)}, u32[]{:S(2)}) collective-permute-start(f32[5,4,4,1]{3,2,1,0:T(4,128)S(1)} %get-tuple-element.26), channel_id=1, source_target_pairs={{1,2},{2,1},{5,6},{6,5},{9,10},{10,9},{13,14},{14,13},{17,18},{18,... | collective-permute-start | bytes 968 | tf_op jit(solution)/shard_map/ppermute | solution.py:23
  31.9 1.2 %collective-permute-start.9 = (f32[5,4,4,1]{3,2,1,0:T(4,128)S(1)}, f32[5,4,4,1]{3,2,1,0:T(4,128)S(1)}, u32[]{:S(2)}, u32[]{:S(2)}) collective-permute-start(f32[5,4,4,1]{3,2,1,0:T(4,128)S(1)} %get-tuple-element.27), channel_id=1, source_target_pairs={{0,1},{1,0},{2,3},{3,2},{4,5},{5,4},{6,7},{7,6},{8,9},{9,8},{10,11... | collective-permute-start | bytes 968 | tf_op jit(solution)/shard_map/ppermute | solution.py:21
  33.1 4.1 %collective-permute-start.5 = (f32[5,1,4,128]{3,2,1,0:T(4,128)S(1)}, f32[5,1,4,128]{3,2,1,0:T(4,128)S(1)}, u32[]{:S(2)}, u32[]{:S(2)}) collective-permute-start(f32[5,1,4,128]{3,2,1,0:T(4,128)S(1)} %get-tuple-element.25), channel_id=1, source_target_pairs={{8,16},{16,8},{9,17},{17,9},{10,18},{18,10},{11,19},{19,11},{12,20... | collective-permute-start | bytes 30728 | tf_op jit(solution)/shard_map/ppermute | solution.py:23
  37.4 1.2 %collective-permute-done.5 = f32[5,1,4,128]{3,2,1,0:T(4,128)S(1)} collective-permute-done((f32[5,1,4,128]{3,2,1,0:T(4,128)S(1)}, f32[5,1,4,128]{3,2,1,0:T(4,128)S(1)}, u32[]{:S(2)}, u32[]{:S(2)}) %collective-permute-start.5) | collective-permute-done | bytes 10272 | tf_op jit(solution)/shard_map/ppermute | solution.py:23
  38.9 2.4 %convolution_bitcast_fusion = f32[3,16384,16]{1,2,0:T(8,128)S(1)} fusion(s32[16384]{0:T(1024)S(1)} %get-tuple-element.13, bf16[1,128,16]{1,2,0:T(8,128)(2,1)S(1)} %get-tuple-element.38, bf16[1,128,16]{1,2,0:T(8,128)(2,1)S(1)} %get-tuple-element.37, bf16[1,128,16]{1,2,0:T(8,128)(2,1)S(1)} %get-tuple-element.36), kind=kOutput, calls=%fused_computation | convolution fusion | flops 203436032 | bytes 3223552 | tf_op jit(solution)/shard_map/fd,kdp->kfp/dot_general | solution.py:83
  41.7 8.5 %all_to_all.10 = f32[1,128,128]{2,0,1:T(1,128)S(1)} all-to-all(f32[1,128,128]{2,0,1:T(1,128)S(1)} %bitcast.86), channel_id=1, replica_groups=mesh['stream'=4,'cross'=2,'gore'=4] {'stream','cross'}, dimensions={1} | all-to-all | bytes 131072 | tf_op jit(solution)/shard_map/all_to_all | solution.py:159
  50.4 0.7 %broadcast_multiply_fusion = f32[3,64,128]{2,1,0:T(8,128)} fusion(f32[3,64,128]{2,1,0:T(8,128)S(1)} %slice_select_fusion, f32[64,128]{1,0:T(8,128)S(1)} %fusion.59), kind=kLoop, calls=%fused_computation.41 | loop fusion | flops 24576 | bytes 229376 | tf_op jit(solution)/shard_map/mul | solution.py:169
  (46 shorter events, 2.7 us)
Async XLA Ops:
  5.5 20.4 %all-to-all-start = ((f32[6,128,128]{2,0,1:T(8,128)}), f32[6,128,128]{2,0,1:T(8,128)S(1)}, u32[]{:S(2)}, u32[]{:S(2)}) async-start(f32[6,128,128]{2,0,1:T(8,128)} %copy.15), calls=%async_computation | async-start | bytes 1048576 | tf_op jit(solution)/shard_map/all_to_all | solution.py:118
  13.3 10.2 %collective-permute-start.1 = (f32[6,4,4,1]{3,2,1,0:T(4,128)S(1)}, f32[6,4,4,1]{3,2,1,0:T(4,128)S(1)}, u32[]{:S(2)}, u32[]{:S(2)}) collective-permute-start(f32[6,4,4,1]{3,2,1,0:T(4,128)S(1)} %get-tuple-element.22), channel_id=1, source_target_pairs={{1,2},{2,1},{5,6},{6,5},{9,10},{10,9},{13,14},{14,13},{17,18},{18,... | collective-permute-start | bytes 1160 | tf_op jit(solution)/shard_map/ppermute | solution.py:23
  14.0 9.6 %collective-permute-start = (f32[6,4,4,1]{3,2,1,0:T(4,128)S(1)}, f32[6,4,4,1]{3,2,1,0:T(4,128)S(1)}, u32[]{:S(2)}, u32[]{:S(2)}) collective-permute-start(f32[6,4,4,1]{3,2,1,0:T(4,128)S(1)} %get-tuple-element.23), channel_id=1, source_target_pairs={{0,1},{1,0},{2,3},{3,2},{4,5},{5,4},{6,7},{7,6},{8,9},{9,8},{10,11... | collective-permute-start | bytes 1160 | tf_op jit(solution)/shard_map/ppermute | solution.py:21
  17.9 7.7 %collective-permute-start.2 = (f32[6,4,1,128]{3,2,1,0:T(1,128)S(1)}, f32[6,4,1,128]{3,2,1,0:T(1,128)S(1)}, u32[]{:S(2)}, u32[]{:S(2)}) collective-permute-start(f32[6,4,1,128]{3,2,1,0:T(1,128)S(1)} %broadcast_select_fusion.2), channel_id=1, source_target_pairs={{0,4},{4,0},{1,5},{5,1},{2,6},{6,2},{3,7},{7,3},{8,12},{12,8},{9,1... | collective-permute-start | bytes 36872 | tf_op jit(solution)/shard_map/ppermute | solution.py:21
  19.3 4.3 %collective-permute-start.3 = (f32[6,1,4,128]{3,2,1,0:T(4,128)S(1)}, f32[6,1,4,128]{3,2,1,0:T(4,128)S(1)}, u32[]{:S(2)}, u32[]{:S(2)}) collective-permute-start(f32[6,1,4,128]{3,2,1,0:T(4,128)S(1)} %get-tuple-element.20), channel_id=1, source_target_pairs={{0,8},{8,0},{16,24},{24,16},{1,9},{9,1},{17,25},{25,17},{2,10},{10... | collective-permute-start | bytes 36872 | tf_op jit(solution)/shard_map/ppermute | solution.py:21
  20.5 5.0 %collective-permute-start.4 = (f32[6,1,4,128]{3,2,1,0:T(4,128)S(1)}, f32[6,1,4,128]{3,2,1,0:T(4,128)S(1)}, u32[]{:S(2)}, u32[]{:S(2)}) collective-permute-start(f32[6,1,4,128]{3,2,1,0:T(4,128)S(1)} %get-tuple-element.21), channel_id=1, source_target_pairs={{8,16},{16,8},{9,17},{17,9},{10,18},{18,10},{11,19},{19,11},{12,20... | collective-permute-start | bytes 36872 | tf_op jit(solution)/shard_map/ppermute | solution.py:23
  31.2 6.0 %collective-permute-start.8 = (f32[5,4,4,1]{3,2,1,0:T(4,128)S(1)}, f32[5,4,4,1]{3,2,1,0:T(4,128)S(1)}, u32[]{:S(2)}, u32[]{:S(2)}) collective-permute-start(f32[5,4,4,1]{3,2,1,0:T(4,128)S(1)} %get-tuple-element.26), channel_id=1, source_target_pairs={{1,2},{2,1},{5,6},{6,5},{9,10},{10,9},{13,14},{14,13},{17,18},{18,... | collective-permute-start | bytes 968 | tf_op jit(solution)/shard_map/ppermute | solution.py:23
  31.9 5.4 %collective-permute-start.9 = (f32[5,4,4,1]{3,2,1,0:T(4,128)S(1)}, f32[5,4,4,1]{3,2,1,0:T(4,128)S(1)}, u32[]{:S(2)}, u32[]{:S(2)}) collective-permute-start(f32[5,4,4,1]{3,2,1,0:T(4,128)S(1)} %get-tuple-element.27), channel_id=1, source_target_pairs={{0,1},{1,0},{2,3},{3,2},{4,5},{5,4},{6,7},{7,6},{8,9},{9,8},{10,11... | collective-permute-start | bytes 968 | tf_op jit(solution)/shard_map/ppermute | solution.py:21
  33.1 4.2 %collective-permute-start.7 = (f32[5,4,1,128]{3,2,1,0:T(1,128)S(1)}, f32[5,4,1,128]{3,2,1,0:T(1,128)S(1)}, u32[]{:S(2)}, u32[]{:S(2)}) collective-permute-start(f32[5,4,1,128]{3,2,1,0:T(1,128)S(1)} %broadcast_select_fusion.9), channel_id=1, source_target_pairs={{0,4},{4,0},{1,5},{5,1},{2,6},{6,2},{3,7},{7,3},{8,12},{12,8},{9,1... | collective-permute-start | bytes 30728 | tf_op jit(solution)/shard_map/ppermute | solution.py:21
  33.1 4.2 %collective-permute-start.6 = (f32[5,1,4,128]{3,2,1,0:T(4,128)S(1)}, f32[5,1,4,128]{3,2,1,0:T(4,128)S(1)}, u32[]{:S(2)}, u32[]{:S(2)}) collective-permute-start(f32[5,1,4,128]{3,2,1,0:T(4,128)S(1)} %get-tuple-element.24), channel_id=1, source_target_pairs={{0,8},{8,0},{16,24},{24,16},{1,9},{9,1},{17,25},{25,17},{2,10},{10... | collective-permute-start | bytes 30728 | tf_op jit(solution)/shard_map/ppermute | solution.py:21
  33.1 5.5 %collective-permute-start.5 = (f32[5,1,4,128]{3,2,1,0:T(4,128)S(1)}, f32[5,1,4,128]{3,2,1,0:T(4,128)S(1)}, u32[]{:S(2)}, u32[]{:S(2)}) collective-permute-start(f32[5,1,4,128]{3,2,1,0:T(4,128)S(1)} %get-tuple-element.25), channel_id=1, source_target_pairs={{8,16},{16,8},{9,17},{17,9},{10,18},{18,10},{11,19},{19,11},{12,20... | collective-permute-start | bytes 30728 | tf_op jit(solution)/shard_map/ppermute | solution.py:23
  38.8 12.3 %copy-start = (f32[5,4,4,128]{3,2,1,0:T(4,128)}, f32[5,4,4,128]{3,2,1,0:T(4,128)S(1)}, u32[]{:S(2)}) copy-start(f32[5,4,4,128]{3,2,1,0:T(4,128)S(1)} %fusion.23) | copy-start | bytes 122884

commit v9 on v8

--- a/solution.py
+++ b/solution.py
@@ -116,12 +116,8 @@
         "ts,ctr->csr", placement_plan, payload, precision=lax.Precision.HIGHEST
     )
     arrived = lax.all_to_all(outbound, ("stream", "cross"), split_axis=1, concat_axis=1, tiled=True)
-    outbound, state_and_visc, load_rows = lax.optimization_barrier(
-        (
-            outbound,
-            jnp.concatenate([fluid_state, viscosity[None]], 0),
-            jnp.where(live_rows[None], records[5:8], 0.0),
-        )
+    outbound, state_and_visc = lax.optimization_barrier(
+        (outbound, jnp.concatenate([fluid_state, viscosity[None]], 0))
     )
     state_visc = face_halo(state_and_visc)
     state_pad = state_visc[0:5]
@@ -138,7 +134,7 @@
     arrived_values = jnp.concatenate([jnp.abs(arrived_values[0:1]), arrived_values[1:5]], 0)
     spread = jnp.where(plane_rows[None], arrived_values[:, None, :], 0.0)
     source = jnp.einsum(
-        "cpf,fd->cpd", spread, depth_hot.astype(jnp.float32), precision=lax.Precision.HIGHEST
+        "cpf,fd->cpd", spread, depth_hot.astype(jnp.float32), precision=lax.Precision.HIGH
     )
     source = source.reshape(5, cells_x, cells_y, vertical_cells)
 
@@ -166,7 +162,7 @@
     home_pressure = jnp.einsum(
         "ts,sr->tr", placement_plan, returned[0], precision=lax.Precision.HIGHEST
     )
-    face_loads = load_rows * home_pressure[None]
+    face_loads = jnp.where(live_rows[None], records[5:8], 0.0) * home_pressure[None]
     return (new_state, face_loads)
 
 

time: 52 us -> 51.4 us (0.988)
  blocking collectives: 8.55 us -> 0 us
  waiting for transfers between devices: 3.14 us -> 7.51 us
  starting transfers between devices: 21.4 us -> 25.7 us
  matrix products: 7.11 us -> 6.42 us
    all_to_all x1 -> x0, blocking collectives: 8.55 us -> none  [shards(): lax.all_to_all(face_pressure.reshape(1, slot_total, row_count), ('stream'...]
    all_to_all x0 -> x1, waiting for transfers between devices: none -> 4.37 us  [shards(): lax.all_to_all(face_pressure.reshape(1, slot_total, row_count), ('stream'...]
    all_to_all x0 -> x1, starting transfers between devices: none -> 4.3 us  [shards(): lax.all_to_all(face_pressure.reshape(1, slot_total, row_count), ('stream'...]
    select_n x1 -> x0, other arithmetic: 0.91 us -> none  [shards(): jnp.where(live_rows[None], records[5:8], 0.0)]
    mul x1, other arithmetic: 0.65 us -> 1.55 us  [shards(): jnp.where(live_rows[None], records[5:8], 0.0) * home_pressure[None]]
    dot_general x1, matrix products: 3.98 us -> 3.29 us  [shards(): jnp.einsum('cpf,fd->cpd', spread, depth_hot.astype(jnp.float32), precisio...]
    lt x1, other arithmetic: 0.73 us -> 0.07 us  [shards(): lax.broadcasted_iota(jnp.int32, (tile_count, row_count), 1)]
    reduce_sum x1, other arithmetic: 0.38 us -> 1.01 us  [shards(): face_pressure = jnp.sum(jnp.where(plane_cols, picked, 0.0), axis=1)]
  transfers between devices with their start and end apart: 11 -> 12, of which waited for: 2 -> 3; matrix products, arithmetic and copies ran while one was open for 6% -> 3% of each run, Pallas kernels for 0% -> 0%
where the time goes in v9:
time: 51.4 us; the launch traced here: 50.5 us
  starting transfers between devices  25.7 us (50%)
  other arithmetic  7.59 us (15%)
  waiting for transfers between devices  7.51 us (15%)
  matrix products  6.42 us (12%)
  local copies, waits for them, and re-layouts  2.22 us (4%)
  between operations  1.01 us (2%)
    ppermute x4, starting transfers between devices, face_halo(): from_b = lax.ppermute(jnp.where(odd, last, first), axis, pairs_b)  8.37 us
    ppermute x6, starting transfers between devices, face_halo(): from_a = lax.ppermute(jnp.where(odd, first, last), axis, pairs_a)  7.84 us
    all_to_all x1, starting transfers between devices, shards(): lax.all_to_all(outbound, ('stream', 'cross'), split_axis=1, concat_axis=1...  5.22 us
    all_to_all x1, waiting for transfers between devices, shards(): lax.all_to_all(face_pressure.reshape(1, slot_total, row_count), ('stream'...  4.37 us
    all_to_all x1, starting transfers between devices, shards(): lax.all_to_all(face_pressure.reshape(1, slot_total, row_count), ('stream'...  4.3 us
    dot_general x1, matrix products, shards(): jnp.einsum('cpf,fd->cpd', spread, depth_hot.astype(jnp.float32), precisio...  3.29 us
    ppermute x4, waiting for transfers between devices, face_halo(): from_b = lax.ppermute(jnp.where(odd, last, first), axis, pairs_b)  3.12 us
    dot_general x1, matrix products, exact_dot(): jnp.einsum(left + ',k' + right + '->k' + output, onehot, stacked, preferr...  2.4 us
  transfers between devices with their start and end apart: 12, of which 3 were waited for; matrix products, arithmetic and copies ran while one was open for 3% of the time, Pallas kernels for 0%

profile of v9, /device:TPU:1, one launch (start us, length us, event | category | flops | bytes accessed | tf_op | source)
XLA Modules:
  0.0 50.5 jit_solution(15252524938731788700)
XLA Ops:
  0.6 0.9 %slice.190 = f32[5,64,128]{2,1,0:T(8,128)S(1)} slice(f32[8,64,128]{2,1,0:T(8,128)} %param.10), slice={[0:5], [0:64], [0:128]} | slice | bytes 327680 | tf_op jit(solution)/shard_map/slice | solution.py:114
  1.6 0.9 %convert_reduce_fusion = s32[64]{0:T(128)S(1)} fusion(s32[64]{0:T(128)} %bitcast.102), kind=kLoop, calls=%fused_computation.126 | loop fusion | flops 20416 | bytes 512 | tf_op jit(solution)/shard_map/reduce_sum | solution.py:106
  2.5 0.7 %fusion.89 = s32[64]{0:T(128)S(1)} fusion(s32[64]{0:T(128)S(1)} %convert_reduce_fusion, s32[64,1]{0,1:T(1,128)} %param.12), kind=kLoop, calls=%fused_computation.189 | loop fusion | flops 128 | bytes 768 | tf_op jit(solution)/shard_map/eq | solution.py:111
  3.1 0.8 %convert_bitcast_fusion = f32[1,64,128]{2,1,0:T(8,128)S(1)} fusion(s32[64,128]{1,0:T(8,128)} %param.11, s32[64]{0:T(128)} %param.13), kind=kLoop, calls=%fused_computation.128 | loop fusion | flops 24576 | bytes 65792 | tf_op jit(solution)/shard_map/broadcast_in_dim | solution.py:114
  4.0 0.5 %convolution_bitcast_fusion.1 = f32[6,128,128]{1,2,0:T(8,128)S(1)} fusion(f32[1,64,128]{2,1,0:T(8,128)S(1)} %convert_bitcast_fusion, f32[5,64,128]{2,1,0:T(8,128)S(1)} %slice.190, s32[64]{0:T(128)S(1)} %fusion.89), kind=kOutput, calls=%fused_computation.10 | convolution fusion | flops 75554816 | bytes 590080 | tf_op jit(solution)/shard_map/ts,ctr->csr/dot_general | solution.py:115
  4.5 1.0 %copy.15 = f32[6,128,128]{2,0,1:T(8,128)} copy(f32[6,128,128]{1,2,0:T(8,128)S(1)} %convolution_bitcast_fusion.1) | data formatting | bytes 786432 | tf_op jit(solution)/shard_map/ts,ctr->csr/transpose | solution.py:115
  5.5 5.2 %all-to-all-start = ((f32[6,128,128]{2,0,1:T(8,128)}), f32[6,128,128]{2,0,1:T(8,128)S(1)}, u32[]{:S(2)}, u32[]{:S(2)}) async-start(f32[6,128,128]{2,0,1:T(8,128)} %copy.15), calls=%async_computation | async-start | bytes 1048576 | tf_op jit(solution)/shard_map/all_to_all | solution.py:118
  10.7 0.8 %pad_maximum_fusion.7 = f32[6,4,4,128]{3,2,1,0:T(4,128)S(1)} fusion(f32[1,4,4,128]{3,2,1,0:T(4,128)} %bitcast.100, f32[4,4,4,128]{3,2,1,0:T(4,128)} %param.8, f32[1,4,4,128]{3,2,1,0:T(4,128)} %bitcast.101), kind=kLoop, calls=%fused_computation.40 | loop fusion | flops 24576 | bytes 98304 | tf_op jit(solution)/shard_map/concatenate | solution.py:120
  11.6 0.7 %collective-permute-start.1 = (f32[6,4,4,1]{3,2,1,0:T(4,128)S(1)}, f32[6,4,4,1]{3,2,1,0:T(4,128)S(1)}, u32[]{:S(2)}, u32[]{:S(2)}) collective-permute-start(f32[6,4,4,1]{3,2,1,0:T(4,128)S(1)} %get-tuple-element.20), channel_id=1, source_target_pairs={{1,2},{2,1},{5,6},{6,5},{9,10},{10,9},{13,14},{14,13},{17,18},{18,... | collective-permute-start | bytes 1160 | tf_op jit(solution)/shard_map/ppermute | solution.py:23
  12.3 3.9 %collective-permute-start = (f32[6,4,4,1]{3,2,1,0:T(4,128)S(1)}, f32[6,4,4,1]{3,2,1,0:T(4,128)S(1)}, u32[]{:S(2)}, u32[]{:S(2)}) collective-permute-start(f32[6,4,4,1]{3,2,1,0:T(4,128)S(1)} %get-tuple-element.21), channel_id=1, source_target_pairs={{0,1},{1,0},{2,3},{3,2},{4,5},{5,4},{6,7},{7,6},{8,9},{9,8},{10,11... | collective-permute-start | bytes 1160 | tf_op jit(solution)/shard_map/ppermute | solution.py:21
  16.2 1.4 %collective-permute-start.2 = (f32[6,4,1,128]{3,2,1,0:T(1,128)S(1)}, f32[6,4,1,128]{3,2,1,0:T(1,128)S(1)}, u32[]{:S(2)}, u32[]{:S(2)}) collective-permute-start(f32[6,4,1,128]{3,2,1,0:T(1,128)S(1)} %broadcast_select_fusion.2), channel_id=1, source_target_pairs={{0,4},{4,0},{1,5},{5,1},{2,6},{6,2},{3,7},{7,3},{8,12},{12,8},{9,1... | collective-permute-start | bytes 36872 | tf_op jit(solution)/shard_map/ppermute | solution.py:21
  17.7 1.2 %collective-permute-start.3 = (f32[6,1,4,128]{3,2,1,0:T(4,128)S(1)}, f32[6,1,4,128]{3,2,1,0:T(4,128)S(1)}, u32[]{:S(2)}, u32[]{:S(2)}) collective-permute-start(f32[6,1,4,128]{3,2,1,0:T(4,128)S(1)} %get-tuple-element.18), channel_id=1, source_target_pairs={{0,8},{8,0},{16,24},{24,16},{1,9},{9,1},{17,25},{25,17},{2,10},{10... | collective-permute-start | bytes 36872 | tf_op jit(solution)/shard_map/ppermute | solution.py:21
  18.9 3.0 %collective-permute-start.4 = (f32[6,1,4,128]{3,2,1,0:T(4,128)S(1)}, f32[6,1,4,128]{3,2,1,0:T(4,128)S(1)}, u32[]{:S(2)}, u32[]{:S(2)}) collective-permute-start(f32[6,1,4,128]{3,2,1,0:T(4,128)S(1)} %get-tuple-element.19), channel_id=1, source_target_pairs={{8,16},{16,8},{9,17},{17,9},{10,18},{18,10},{11,19},{19,11},{12,20... | collective-permute-start | bytes 36872 | tf_op jit(solution)/shard_map/ppermute | solution.py:23
  22.0 1.9 %collective-permute-done.4 = f32[6,1,4,128]{3,2,1,0:T(4,128)S(1)} collective-permute-done((f32[6,1,4,128]{3,2,1,0:T(4,128)S(1)}, f32[6,1,4,128]{3,2,1,0:T(4,128)S(1)}, u32[]{:S(2)}, u32[]{:S(2)}) %collective-permute-start.4) | collective-permute-done | bytes 12320 | tf_op jit(solution)/shard_map/ppermute | solution.py:23
  25.2 3.3 %fusion.2 = f32[5,16,128]{2,1,0:T(8,128)S(1)} fusion(s32[16384]{0:T(1024)S(1)} %get-tuple-element.11, f32[5,16,16384]{2,1,0:T(8,128)S(1)} %fusion.101), kind=kOutput, calls=%fused_computation.3 | convolution fusion | flops 1008730112 | bytes 5349376 | tf_op jit(solution)/shard_map/cpf,fd->cpd/dot_general | solution.py:136
  28.9 0.7 %collective-permute-start.8 = (f32[5,4,4,1]{3,2,1,0:T(4,128)S(1)}, f32[5,4,4,1]{3,2,1,0:T(4,128)S(1)}, u32[]{:S(2)}, u32[]{:S(2)}) collective-permute-start(f32[5,4,4,1]{3,2,1,0:T(4,128)S(1)} %get-tuple-element.24), channel_id=1, source_target_pairs={{1,2},{2,1},{5,6},{6,5},{9,10},{10,9},{13,14},{14,13},{17,18},{18,... | collective-permute-start | bytes 968 | tf_op jit(solution)/shard_map/ppermute | solution.py:23
  29.6 1.2 %collective-permute-start.9 = (f32[5,4,4,1]{3,2,1,0:T(4,128)S(1)}, f32[5,4,4,1]{3,2,1,0:T(4,128)S(1)}, u32[]{:S(2)}, u32[]{:S(2)}) collective-permute-start(f32[5,4,4,1]{3,2,1,0:T(4,128)S(1)} %get-tuple-element.25), channel_id=1, source_target_pairs={{0,1},{1,0},{2,3},{3,2},{4,5},{5,4},{6,7},{7,6},{8,9},{9,8},{10,11... | collective-permute-start | bytes 968 | tf_op jit(solution)/shard_map/ppermute | solution.py:21
  30.9 4.1 %collective-permute-start.5 = (f32[5,1,4,128]{3,2,1,0:T(4,128)S(1)}, f32[5,1,4,128]{3,2,1,0:T(4,128)S(1)}, u32[]{:S(2)}, u32[]{:S(2)}) collective-permute-start(f32[5,1,4,128]{3,2,1,0:T(4,128)S(1)} %get-tuple-element.23), channel_id=1, source_target_pairs={{8,16},{16,8},{9,17},{17,9},{10,18},{18,10},{11,19},{19,11},{12,20... | collective-permute-start | bytes 30728 | tf_op jit(solution)/shard_map/ppermute | solution.py:23
  35.0 1.2 %collective-permute-done.5 = f32[5,1,4,128]{3,2,1,0:T(4,128)S(1)} collective-permute-done((f32[5,1,4,128]{3,2,1,0:T(4,128)S(1)}, f32[5,1,4,128]{3,2,1,0:T(4,128)S(1)}, u32[]{:S(2)}, u32[]{:S(2)}) %collective-permute-start.5) | collective-permute-done | bytes 10272 | tf_op jit(solution)/shard_map/ppermute | solution.py:23
  36.5 2.4 %convolution_bitcast_fusion = f32[3,16384,16]{1,2,0:T(8,128)S(1)} fusion(s32[16384]{0:T(1024)S(1)} %get-tuple-element.11, bf16[1,128,16]{1,2,0:T(8,128)(2,1)S(1)} %get-tuple-element.36, bf16[1,128,16]{1,2,0:T(8,128)(2,1)S(1)} %get-tuple-element.35, bf16[1,128,16]{1,2,0:T(8,128)(2,1)S(1)} %get-tuple-element.34), kind=kOutput, calls=%fused_computation | convolution fusion | flops 203436032 | bytes 3223552 | tf_op jit(solution)/shard_map/fd,kdp->kfp/dot_general | solution.py:83
  39.0 1.0 %fusion.12 = f32[16384]{0:T(1024)} fusion(f32[3,16384,16]{1,2,0:T(8,128)S(1)} %convolution_bitcast_fusion, s32[16384]{0:T(1024)S(1)} %get-tuple-element.10), kind=kLoop, calls=%fused_computation.14 | loop fusion | flops 1294336 | bytes 3276800 | tf_op jit(solution)/shard_map/reduce_sum | solution.py:154
  40.0 4.3 %all-to-all-start.1 = ((f32[1,128,128]{2,0,1:T(1,128)}), f32[1,128,128]{2,0,1:T(1,128)S(1)}, u32[]{:S(2)}, u32[]{:S(2)}) async-start(f32[1,128,128]{2,0,1:T(1,128)} %bitcast.22), calls=%async_computation.1 | async-start | bytes 131072 | tf_op jit(solution)/shard_map/all_to_all | solution.py:155
  44.3 4.4 %all-to-all-done.1 = f32[1,128,128]{2,0,1:T(1,128)S(1)} async-done(((f32[1,128,128]{2,0,1:T(1,128)}), f32[1,128,128]{2,0,1:T(1,128)S(1)}, u32[]{:S(2)}, u32[]{:S(2)}) %all-to-all-start.1) | async-done | bytes 65568 | tf_op jit(solution)/shard_map/all_to_all | solution.py:155
  48.9 1.6 %select_multiply_fusion = f32[3,64,128]{2,1,0:T(8,128)} fusion(f32[8,64,128]{2,1,0:T(8,128)} %param.10, f32[64,128]{1,0:T(8,128)S(1)} %fusion.59, pred[64,128]{1,0:T(8,128)(4,1)S(1)} %iota_compare_fusion.6), kind=kLoop, calls=%fused_computation.23 | loop fusion | flops 49152 | bytes 237568 | tf_op jit(solution)/shard_map/mul | solution.py:165
  (48 shorter events, 2.4 us)
Async XLA Ops:
  5.5 18.7 %all-to-all-start = ((f32[6,128,128]{2,0,1:T(8,128)}), f32[6,128,128]{2,0,1:T(8,128)S(1)}, u32[]{:S(2)}, u32[]{:S(2)}) async-start(f32[6,128,128]{2,0,1:T(8,128)} %copy.15), calls=%async_computation | async-start | bytes 1048576 | tf_op jit(solution)/shard_map/all_to_all | solution.py:118
  11.6 10.2 %collective-permute-start.1 = (f32[6,4,4,1]{3,2,1,0:T(4,128)S(1)}, f32[6,4,4,1]{3,2,1,0:T(4,128)S(1)}, u32[]{:S(2)}, u32[]{:S(2)}) collective-permute-start(f32[6,4,4,1]{3,2,1,0:T(4,128)S(1)} %get-tuple-element.20), channel_id=1, source_target_pairs={{1,2},{2,1},{5,6},{6,5},{9,10},{10,9},{13,14},{14,13},{17,18},{18,... | collective-permute-start | bytes 1160 | tf_op jit(solution)/shard_map/ppermute | solution.py:23
  12.3 9.6 %collective-permute-start = (f32[6,4,4,1]{3,2,1,0:T(4,128)S(1)}, f32[6,4,4,1]{3,2,1,0:T(4,128)S(1)}, u32[]{:S(2)}, u32[]{:S(2)}) collective-permute-start(f32[6,4,4,1]{3,2,1,0:T(4,128)S(1)} %get-tuple-element.21), channel_id=1, source_target_pairs={{0,1},{1,0},{2,3},{3,2},{4,5},{5,4},{6,7},{7,6},{8,9},{9,8},{10,11... | collective-permute-start | bytes 1160 | tf_op jit(solution)/shard_map/ppermute | solution.py:21
  16.2 7.7 %collective-permute-start.2 = (f32[6,4,1,128]{3,2,1,0:T(1,128)S(1)}, f32[6,4,1,128]{3,2,1,0:T(1,128)S(1)}, u32[]{:S(2)}, u32[]{:S(2)}) collective-permute-start(f32[6,4,1,128]{3,2,1,0:T(1,128)S(1)} %broadcast_select_fusion.2), channel_id=1, source_target_pairs={{0,4},{4,0},{1,5},{5,1},{2,6},{6,2},{3,7},{7,3},{8,12},{12,8},{9,1... | collective-permute-start | bytes 36872 | tf_op jit(solution)/shard_map/ppermute | solution.py:21
  17.7 4.3 %collective-permute-start.3 = (f32[6,1,4,128]{3,2,1,0:T(4,128)S(1)}, f32[6,1,4,128]{3,2,1,0:T(4,128)S(1)}, u32[]{:S(2)}, u32[]{:S(2)}) collective-permute-start(f32[6,1,4,128]{3,2,1,0:T(4,128)S(1)} %get-tuple-element.18), channel_id=1, source_target_pairs={{0,8},{8,0},{16,24},{24,16},{1,9},{9,1},{17,25},{25,17},{2,10},{10... | collective-permute-start | bytes 36872 | tf_op jit(solution)/shard_map/ppermute | solution.py:21
  18.9 5.0 %collective-permute-start.4 = (f32[6,1,4,128]{3,2,1,0:T(4,128)S(1)}, f32[6,1,4,128]{3,2,1,0:T(4,128)S(1)}, u32[]{:S(2)}, u32[]{:S(2)}) collective-permute-start(f32[6,1,4,128]{3,2,1,0:T(4,128)S(1)} %get-tuple-element.19), channel_id=1, source_target_pairs={{8,16},{16,8},{9,17},{17,9},{10,18},{18,10},{11,19},{19,11},{12,20... | collective-permute-start | bytes 36872 | tf_op jit(solution)/shard_map/ppermute | solution.py:23
  28.5 15.7 %copy-start.1 = (s32[64]{0:T(128)S(1)}, s32[64]{0:T(128)}, u32[]{:S(2)}) copy-start(s32[64]{0:T(128)} %param.13) | copy-start | bytes 772
  28.9 6.0 %collective-permute-start.8 = (f32[5,4,4,1]{3,2,1,0:T(4,128)S(1)}, f32[5,4,4,1]{3,2,1,0:T(4,128)S(1)}, u32[]{:S(2)}, u32[]{:S(2)}) collective-permute-start(f32[5,4,4,1]{3,2,1,0:T(4,128)S(1)} %get-tuple-element.24), channel_id=1, source_target_pairs={{1,2},{2,1},{5,6},{6,5},{9,10},{10,9},{13,14},{14,13},{17,18},{18,... | collective-permute-start | bytes 968 | tf_op jit(solution)/shard_map/ppermute | solution.py:23
  29.6 5.4 %collective-permute-start.9 = (f32[5,4,4,1]{3,2,1,0:T(4,128)S(1)}, f32[5,4,4,1]{3,2,1,0:T(4,128)S(1)}, u32[]{:S(2)}, u32[]{:S(2)}) collective-permute-start(f32[5,4,4,1]{3,2,1,0:T(4,128)S(1)} %get-tuple-element.25), channel_id=1, source_target_pairs={{0,1},{1,0},{2,3},{3,2},{4,5},{5,4},{6,7},{7,6},{8,9},{9,8},{10,11... | collective-permute-start | bytes 968 | tf_op jit(solution)/shard_map/ppermute | solution.py:21
  30.8 4.2 %collective-permute-start.7 = (f32[5,4,1,128]{3,2,1,0:T(1,128)S(1)}, f32[5,4,1,128]{3,2,1,0:T(1,128)S(1)}, u32[]{:S(2)}, u32[]{:S(2)}) collective-permute-start(f32[5,4,1,128]{3,2,1,0:T(1,128)S(1)} %broadcast_select_fusion.9), channel_id=1, source_target_pairs={{0,4},{4,0},{1,5},{5,1},{2,6},{6,2},{3,7},{7,3},{8,12},{12,8},{9,1... | collective-permute-start | bytes 30728 | tf_op jit(solution)/shard_map/ppermute | solution.py:21
  30.8 4.2 %collective-permute-start.6 = (f32[5,1,4,128]{3,2,1,0:T(4,128)S(1)}, f32[5,1,4,128]{3,2,1,0:T(4,128)S(1)}, u32[]{:S(2)}, u32[]{:S(2)}) collective-permute-start(f32[5,1,4,128]{3,2,1,0:T(4,128)S(1)} %get-tuple-element.22), channel_id=1, source_target_pairs={{0,8},{8,0},{16,24},{24,16},{1,9},{9,1},{17,25},{25,17},{2,10},{10... | collective-permute-start | bytes 30728 | tf_op jit(solution)/shard_map/ppermute | solution.py:21
  30.9 5.4 %collective-permute-start.5 = (f32[5,1,4,128]{3,2,1,0:T(4,128)S(1)}, f32[5,1,4,128]{3,2,1,0:T(4,128)S(1)}, u32[]{:S(2)}, u32[]{:S(2)}) collective-permute-start(f32[5,1,4,128]{3,2,1,0:T(4,128)S(1)} %get-tuple-element.23), channel_id=1, source_target_pairs={{8,16},{16,8},{9,17},{17,9},{10,18},{18,10},{11,19},{19,11},{12,20... | collective-permute-start | bytes 30728 | tf_op jit(solution)/shard_map/ppermute | solution.py:23
  36.5 14.0 %copy-start = (f32[5,4,4,128]{3,2,1,0:T(4,128)}, f32[5,4,4,128]{3,2,1,0:T(4,128)S(1)}, u32[]{:S(2)}) copy-start(f32[5,4,4,128]{3,2,1,0:T(4,128)S(1)} %fusion.23) | copy-start | bytes 122884
  40.0 8.8 %all-to-all-start.1 = ((f32[1,128,128]{2,0,1:T(1,128)}), f32[1,128,128]{2,0,1:T(1,128)S(1)}, u32[]{:S(2)}, u32[]{:S(2)}) async-start(f32[1,128,128]{2,0,1:T(1,128)} %bitcast.22), calls=%async_computation.1 | async-start | bytes 131072 | tf_op jit(solution)/shard_map/all_to_all | solution.py:155

commit v10 on v9

--- a/solution.py
+++ b/solution.py
@@ -1,6 +1,7 @@
 import jax
 import jax.numpy as jnp
 from jax import lax
+from jax.experimental import pallas as pl
 from jax.sharding import PartitionSpec as P
 
 
@@ -87,6 +88,52 @@
     return terms[0] + terms[1] + terms[2]
 
 
+def make_pack(tile_count, row_count, blocks, capacity):
+    slot_total = blocks * capacity
+
+    def pack_kernel(route_ref, length_ref, cell_ref, record_ref, out_ref):
+        target = route_ref[...]
+        tile_iota_row = lax.broadcasted_iota(jnp.int32, (tile_count, tile_count), 1)
+        tile_iota_col = lax.broadcasted_iota(jnp.int32, (tile_count, tile_count), 0)
+        lengths_col = jnp.sum(
+            jnp.where(tile_iota_row == tile_iota_col, length_ref[...], 0), axis=1, keepdims=True
+        )
+        block_hot = (
+            target == lax.broadcasted_iota(jnp.int32, (tile_count, blocks), 1)
+        ).astype(jnp.float32)
+        same = lax.dot_general(
+            block_hot, block_hot, (((1,), (1,)), ((), ())), preferred_element_type=jnp.float32
+        )
+        rank = jnp.sum(jnp.where(tile_iota_row < tile_iota_col, same, 0.0), axis=1, keepdims=True)
+        slot = target * capacity + rank.astype(jnp.int32)
+        slot_hot = (
+            slot == lax.broadcasted_iota(jnp.int32, (tile_count, slot_total), 1)
+        ).astype(jnp.float32)
+        eye = (
+            lax.broadcasted_iota(jnp.int32, (slot_total, slot_total), 0)
+            == lax.broadcasted_iota(jnp.int32, (slot_total, slot_total), 1)
+        ).astype(jnp.float32)
+        plan = lax.dot_general(
+            eye, slot_hot, (((1,), (1,)), ((), ())), preferred_element_type=jnp.float32
+        )
+        live = lax.broadcasted_iota(jnp.int32, (tile_count, row_count), 1) < lengths_col
+        for comp in range(6):
+            if comp < 5:
+                rows = record_ref[comp]
+            else:
+                rows = jnp.where(live, cell_ref[...], -1).astype(jnp.float32)
+            out_ref[:, comp * row_count:(comp + 1) * row_count] = jnp.dot(
+                plan, rows, precision=lax.Precision.HIGHEST, preferred_element_type=jnp.float32
+            )
+
+    def pack(routes, lengths, cell_ids, records):
+        return pl.pallas_call(
+            pack_kernel,
+            out_shape=jax.ShapeDtypeStruct((slot_total, 6 * row_count), jnp.float32),
+        )(routes, lengths.reshape(1, tile_count), cell_ids, records)
+    return pack
+
+
 def shards(density, momentum_energy, viscosity, records, cell_ids, routes, lengths):
     fluid_state = jnp.concatenate([density[None], momentum_energy], 0)
     cells_x, cells_y, vertical_cells = density.shape
@@ -110,12 +157,9 @@
     placement_plan = (
         slot_index[:, None] == lax.broadcasted_iota(jnp.int32, (tile_count, slot_total), 1)
     ).astype(jnp.float32)
-    live_cells = jnp.where(live_rows, cell_ids, -1).astype(jnp.float32)
-    payload = jnp.concatenate([records[0:5], live_cells[None]], 0)
-    outbound = jnp.einsum(
-        "ts,ctr->csr", placement_plan, payload, precision=lax.Precision.HIGHEST
-    )
-    arrived = lax.all_to_all(outbound, ("stream", "cross"), split_axis=1, concat_axis=1, tiled=True)
+    pack = make_pack(tile_count, row_count, blocks, capacity)
+    outbound = pack(routes, lengths, cell_ids, records)
+    arrived = lax.all_to_all(outbound, ("stream", "cross"), split_axis=0, concat_axis=0, tiled=True)
     outbound, state_and_visc = lax.optimization_barrier(
         (outbound, jnp.concatenate([fluid_state, viscosity[None]], 0))
     )
@@ -123,14 +167,16 @@
     state_pad = state_visc[0:5]
     visc_pad = state_visc[5]
 
-    cells = jnp.round(arrived[5]).astype(jnp.int32).reshape(faces)
+    cells = jnp.round(arrived[:, 5 * row_count:]).astype(jnp.int32).reshape(faces)
     plane = cells // vertical_cells
     depth = cells % vertical_cells
     depth_hot = (
         depth[:, None] == lax.broadcasted_iota(jnp.int32, (faces, vertical_cells), 1)
     )
     plane_rows = plane[None, :] == lax.broadcasted_iota(jnp.int32, (plane_count, faces), 0)
-    arrived_values = arrived[0:5].reshape(5, faces)
+    arrived_values = jnp.stack(
+        [arrived[:, c * row_count:(c + 1) * row_count].reshape(faces) for c in range(5)], 0
+    )
     arrived_values = jnp.concatenate([jnp.abs(arrived_values[0:1]), arrived_values[1:5]], 0)
     spread = jnp.where(plane_rows[None], arrived_values[:, None, :], 0.0)
     source = jnp.einsum(

time: 51.4 us -> 50.8 us (0.988)
  Pallas kernels: 0 us -> 2.7 us
  waiting for transfers between devices: 7.51 us -> 5.93 us
  other arithmetic: 7.59 us -> 6.67 us
  matrix products: 6.42 us -> 5.9 us
    pallas_call x0 -> x1, Pallas kernels: none -> 2.7 us  [pack(): pl.pallas_call(pack_kernel, out_shape=jax.ShapeDtypeStruct((slot_total, 6...]
    ppermute x4, waiting for transfers between devices: 3.12 us -> 1.47 us  [face_halo(): from_b = lax.ppermute(jnp.where(odd, last, first), axis, pairs_b)]
    unnamed x4 -> x5, local copies, waits for them, and re-layouts: 0.01 us -> 1.37 us
    slice x3 -> x0, local copies, waits for them, and re-layouts: 1.1 us -> none  [the longest x1 0.93 us: shards(): payload = jnp.concatenate([records[0:5], live_cells[None]], 0)]
    transpose x1 -> x0, local copies, waits for them, and re-layouts: 1.01 us -> none  [shards(): jnp.einsum('ts,ctr->csr', placement_plan, payload, precision=lax.Precisio...]
    broadcast_in_dim x1 -> x0, other arithmetic: 0.83 us -> none  [shards(): payload = jnp.concatenate([records[0:5], live_cells[None]], 0)]
    eq x1, other arithmetic: 0.67 us -> 0.01 us  [shards(): slot_index[:, None]]
    lt x1, other arithmetic: 0.07 us -> 0.73 us  [shards(): lax.broadcasted_iota(jnp.int32, (tile_count, row_count), 1)]
  transfers between devices with their start and end apart: 12 -> 12, of which waited for: 3 -> 3; matrix products, arithmetic and copies ran while one was open for 3% -> 6% of each run, Pallas kernels for 0% -> 0%
where the time goes in v10:
time: 50.8 us; the launch traced here: 49.9 us
  starting transfers between devices  25.7 us (51%)
  other arithmetic  6.67 us (13%)
  waiting for transfers between devices  5.93 us (12%)
  matrix products  5.9 us (12%)
  Pallas kernels  2.7 us (5%)
  local copies, waits for them, and re-layouts  2.01 us (4%)
  between operations  1 us (2%)
    ppermute x4, starting transfers between devices, face_halo(): from_b = lax.ppermute(jnp.where(odd, last, first), axis, pairs_b)  8.37 us
    ppermute x6, starting transfers between devices, face_halo(): from_a = lax.ppermute(jnp.where(odd, first, last), axis, pairs_a)  7.84 us
    all_to_all x1, starting transfers between devices, shards(): lax.all_to_all(outbound, ('stream', 'cross'), split_axis=0, concat_axis=0...  5.22 us
    all_to_all x1, waiting for transfers between devices, shards(): lax.all_to_all(face_pressure.reshape(1, slot_total, row_count), ('stream'...  4.44 us
    all_to_all x1, starting transfers between devices, shards(): lax.all_to_all(face_pressure.reshape(1, slot_total, row_count), ('stream'...  4.3 us
    dot_general x1, matrix products, shards(): jnp.einsum('cpf,fd->cpd', spread, depth_hot.astype(jnp.float32), precisio...  3.28 us
    pallas_call x1, Pallas kernels, pack(): pl.pallas_call(pack_kernel, out_shape=jax.ShapeDtypeStruct((slot_total, 6...  2.7 us
    dot_general x1, matrix products, exact_dot(): jnp.einsum(left + ',k' + right + '->k' + output, onehot, stacked, preferr...  2.4 us
  transfers between devices with their start and end apart: 12, of which 3 were waited for; matrix products, arithmetic and copies ran while one was open for 6% of the time, Pallas kernels for 0%

profile of v10, /device:TPU:1, one launch (start us, length us, event | category | flops | bytes accessed | tf_op | source)
XLA Modules:
  0.0 49.9 jit_solution(880701270539749758)
XLA Ops:
  0.6 1.4 %copy.11.route_ref = s32[64,1]{1,0:T(8,128)} copy(s32[64,1]{0,1:T(1,128)} %param.12) | data formatting | bytes 512 | tf_op args[5]
  2.0 2.7 %shard_map.86 = f32[128,768]{1,0:T(8,128)} custom-call(s32[64,1]{1,0:T(8,128)} %copy.11.route_ref, s32[1,64]{1,0:T(1,128)} %bitcast.95, s32[64,128]{1,0:T(8,128)} %cell_ref.1, f32[8,64,128]{2,1,0:T(8,128)} %record_ref.1), custom_call_target="tpu_custom_call" | custom-call | tf_op jit(solution)/shard_map/pallas_call | solution.py:130
  4.7 5.2 %all-to-all-start = ((f32[8,16,768]{2,1,0:T(8,128)}), f32[8,16,768]{2,1,0:T(8,128)S(1)}, u32[]{:S(2)}, u32[]{:S(2)}) async-start(f32[8,16,768]{2,1,0:T(8,128)} %bitcast.76), calls=%async_computation | async-start | bytes 786432 | tf_op jit(solution)/shard_map/all_to_all | solution.py:162
  9.9 0.8 %pad_maximum_fusion.6 = f32[6,4,4,128]{3,2,1,0:T(4,128)S(1)} fusion(f32[1,4,4,128]{3,2,1,0:T(4,128)} %bitcast.93, f32[4,4,4,128]{3,2,1,0:T(4,128)} %param.8, f32[1,4,4,128]{3,2,1,0:T(4,128)} %bitcast.94), kind=kLoop, calls=%fused_computation.37 | loop fusion | flops 24576 | bytes 98304 | tf_op jit(solution)/shard_map/concatenate | solution.py:164
  10.8 0.7 %collective-permute-start.1 = (f32[6,4,4,1]{3,2,1,0:T(4,128)S(1)}, f32[6,4,4,1]{3,2,1,0:T(4,128)S(1)}, u32[]{:S(2)}, u32[]{:S(2)}) collective-permute-start(f32[6,4,4,1]{3,2,1,0:T(4,128)S(1)} %get-tuple-element.23), channel_id=1, source_target_pairs={{1,2},{2,1},{5,6},{6,5},{9,10},{10,9},{13,14},{14,13},{17,18},{18,... | collective-permute-start | bytes 1160 | tf_op jit(solution)/shard_map/ppermute | solution.py:24
  11.5 3.9 %collective-permute-start = (f32[6,4,4,1]{3,2,1,0:T(4,128)S(1)}, f32[6,4,4,1]{3,2,1,0:T(4,128)S(1)}, u32[]{:S(2)}, u32[]{:S(2)}) collective-permute-start(f32[6,4,4,1]{3,2,1,0:T(4,128)S(1)} %get-tuple-element.24), channel_id=1, source_target_pairs={{0,1},{1,0},{2,3},{3,2},{4,5},{5,4},{6,7},{7,6},{8,9},{9,8},{10,11... | collective-permute-start | bytes 1160 | tf_op jit(solution)/shard_map/ppermute | solution.py:22
  15.4 1.4 %collective-permute-start.2 = (f32[6,4,1,128]{3,2,1,0:T(1,128)S(1)}, f32[6,4,1,128]{3,2,1,0:T(1,128)S(1)}, u32[]{:S(2)}, u32[]{:S(2)}) collective-permute-start(f32[6,4,1,128]{3,2,1,0:T(1,128)S(1)} %broadcast_select_fusion.2), channel_id=1, source_target_pairs={{0,4},{4,0},{1,5},{5,1},{2,6},{6,2},{3,7},{7,3},{8,12},{12,8},{9,1... | collective-permute-start | bytes 36872 | tf_op jit(solution)/shard_map/ppermute | solution.py:22
  16.9 1.2 %collective-permute-start.3 = (f32[6,1,4,128]{3,2,1,0:T(4,128)S(1)}, f32[6,1,4,128]{3,2,1,0:T(4,128)S(1)}, u32[]{:S(2)}, u32[]{:S(2)}) collective-permute-start(f32[6,1,4,128]{3,2,1,0:T(4,128)S(1)} %get-tuple-element.21), channel_id=1, source_target_pairs={{0,8},{8,0},{16,24},{24,16},{1,9},{9,1},{17,25},{25,17},{2,10},{10... | collective-permute-start | bytes 36872 | tf_op jit(solution)/shard_map/ppermute | solution.py:22
  18.1 3.0 %collective-permute-start.4 = (f32[6,1,4,128]{3,2,1,0:T(4,128)S(1)}, f32[6,1,4,128]{3,2,1,0:T(4,128)S(1)}, u32[]{:S(2)}, u32[]{:S(2)}) collective-permute-start(f32[6,1,4,128]{3,2,1,0:T(4,128)S(1)} %get-tuple-element.22), channel_id=1, source_target_pairs={{8,16},{16,8},{9,17},{17,9},{10,18},{18,10},{11,19},{19,11},{12,20... | collective-permute-start | bytes 36872 | tf_op jit(solution)/shard_map/ppermute | solution.py:24
  21.1 0.7 %iota_compare_fusion.5 = pred[64,128]{1,0:T(8,128)(4,1)S(1)} fusion(s32[64]{0:T(128)} %param.13), kind=kLoop, calls=%fused_computation.122 | loop fusion | flops 8192 | bytes 8448 | tf_op jit(solution)/shard_map/lt | solution.py:148
  21.8 0.9 %convert_reduce_fusion = s32[64]{0:T(128)S(1)} fusion(s32[64]{0:T(128)} %bitcast.96), kind=kLoop, calls=%fused_computation.120 | loop fusion | flops 20416 | bytes 512 | tf_op jit(solution)/shard_map/reduce_sum | solution.py:153
  22.8 0.2 collective-permute-done.4
  23.7 0.5 %concatenate.68 = f32[5,16384]{1,0:T(8,128)S(1)} concatenate(f32[1,16384]{1,0:T(1,128)S(1)} %bitcast.82, f32[1,16384]{1,0:T(1,128)S(1)} %bitcast.81, f32[1,16384]{1,0:T(1,128)S(1)} %bitcast.80, f32[1,16384]{1,0:T(1,128)S(1)} %bitcast.79, f32[1,16384]{1,0:T(1,128)S(1)} %bitcast.78), dimensions={0} | concatenate | bytes 655360 | tf_op jit(solution)/shard_map/concatenate | solution.py:180
  24.2 0.5 fusion.96
  24.7 3.3 %fusion.2 = f32[5,16,128]{2,1,0:T(8,128)S(1)} fusion(s32[16384]{0:T(1024)S(1)} %add_select_fusion, f32[5,16,16384]{2,1,0:T(8,128)S(1)} %fusion.96), kind=kOutput, calls=%fused_computation.3 | convolution fusion | flops 1008730112 | bytes 5349376 | tf_op jit(solution)/shard_map/cpf,fd->cpd/dot_general | solution.py:182
  28.4 0.7 %collective-permute-start.8 = (f32[5,4,4,1]{3,2,1,0:T(4,128)S(1)}, f32[5,4,4,1]{3,2,1,0:T(4,128)S(1)}, u32[]{:S(2)}, u32[]{:S(2)}) collective-permute-start(f32[5,4,4,1]{3,2,1,0:T(4,128)S(1)} %get-tuple-element.27), channel_id=1, source_target_pairs={{1,2},{2,1},{5,6},{6,5},{9,10},{10,9},{13,14},{14,13},{17,18},{18,... | collective-permute-start | bytes 968 | tf_op jit(solution)/shard_map/ppermute | solution.py:24
  29.0 1.2 %collective-permute-start.9 = (f32[5,4,4,1]{3,2,1,0:T(4,128)S(1)}, f32[5,4,4,1]{3,2,1,0:T(4,128)S(1)}, u32[]{:S(2)}, u32[]{:S(2)}) collective-permute-start(f32[5,4,4,1]{3,2,1,0:T(4,128)S(1)} %get-tuple-element.28), channel_id=1, source_target_pairs={{0,1},{1,0},{2,3},{3,2},{4,5},{5,4},{6,7},{7,6},{8,9},{9,8},{10,11... | collective-permute-start | bytes 968 | tf_op jit(solution)/shard_map/ppermute | solution.py:22
  30.3 4.1 %collective-permute-start.5 = (f32[5,1,4,128]{3,2,1,0:T(4,128)S(1)}, f32[5,1,4,128]{3,2,1,0:T(4,128)S(1)}, u32[]{:S(2)}, u32[]{:S(2)}) collective-permute-start(f32[5,1,4,128]{3,2,1,0:T(4,128)S(1)} %get-tuple-element.26), channel_id=1, source_target_pairs={{8,16},{16,8},{9,17},{17,9},{10,18},{18,10},{11,19},{19,11},{12,20... | collective-permute-start | bytes 30728 | tf_op jit(solution)/shard_map/ppermute | solution.py:24
  34.5 1.2 %collective-permute-done.5 = f32[5,1,4,128]{3,2,1,0:T(4,128)S(1)} collective-permute-done((f32[5,1,4,128]{3,2,1,0:T(4,128)S(1)}, f32[5,1,4,128]{3,2,1,0:T(4,128)S(1)}, u32[]{:S(2)}, u32[]{:S(2)}) %collective-permute-start.5) | collective-permute-done | bytes 10272 | tf_op jit(solution)/shard_map/ppermute | solution.py:24
  36.0 2.4 %convolution_bitcast_fusion = f32[3,16384,16]{1,2,0:T(8,128)S(1)} fusion(s32[16384]{0:T(1024)S(1)} %add_select_fusion, bf16[1,128,16]{1,2,0:T(8,128)(2,1)S(1)} %get-tuple-element.39, bf16[1,128,16]{1,2,0:T(8,128)(2,1)S(1)} %get-tuple-element.38, bf16[1,128,16]{1,2,0:T(8,128)(2,1)S(1)} %get-tuple-element.37), kind=kOutput, calls=%fused_computation | convolution fusion | flops 203436032 | bytes 3223552 | tf_op jit(solution)/shard_map/fd,kdp->kfp/dot_general | solution.py:84
  38.4 1.0 %fusion.12 = f32[16384]{0:T(1024)} fusion(f32[3,16384,16]{1,2,0:T(8,128)S(1)} %convolution_bitcast_fusion, s32[16384]{0:T(1024)S(1)} %get-tuple-element.4), kind=kLoop, calls=%fused_computation.13 | loop fusion | flops 1294336 | bytes 3276800 | tf_op jit(solution)/shard_map/reduce_sum | solution.py:200
  39.4 4.3 %all-to-all-start.1 = ((f32[1,128,128]{2,0,1:T(1,128)}), f32[1,128,128]{2,0,1:T(1,128)S(1)}, u32[]{:S(2)}, u32[]{:S(2)}) async-start(f32[1,128,128]{2,0,1:T(1,128)} %bitcast.25), calls=%async_computation.1 | async-start | bytes 131072 | tf_op jit(solution)/shard_map/all_to_all | solution.py:201
  43.7 4.4 %all-to-all-done.1 = f32[1,128,128]{2,0,1:T(1,128)S(1)} async-done(((f32[1,128,128]{2,0,1:T(1,128)}), f32[1,128,128]{2,0,1:T(1,128)S(1)}, u32[]{:S(2)}, u32[]{:S(2)}) %all-to-all-start.1) | async-done | bytes 65568 | tf_op jit(solution)/shard_map/all_to_all | solution.py:201
  48.4 1.5 %select_multiply_fusion = f32[3,64,128]{2,1,0:T(8,128)} fusion(f32[8,64,128]{2,1,0:T(8,128)} %record_ref.1, f32[64,128]{1,0:T(8,128)S(1)} %fusion.58, pred[64,128]{1,0:T(8,128)(4,1)S(1)} %iota_compare_fusion.5), kind=kLoop, calls=%fused_computation.17 | loop fusion | flops 49152 | bytes 237568 | tf_op jit(solution)/shard_map/mul | solution.py:211
  (45 shorter events, 1.6 us)
Async XLA Ops:
  4.7 18.7 %all-to-all-start = ((f32[8,16,768]{2,1,0:T(8,128)}), f32[8,16,768]{2,1,0:T(8,128)S(1)}, u32[]{:S(2)}, u32[]{:S(2)}) async-start(f32[8,16,768]{2,1,0:T(8,128)} %bitcast.76), calls=%async_computation | async-start | bytes 786432 | tf_op jit(solution)/shard_map/all_to_all | solution.py:162
  10.8 11.9 %collective-permute-start.1 = (f32[6,4,4,1]{3,2,1,0:T(4,128)S(1)}, f32[6,4,4,1]{3,2,1,0:T(4,128)S(1)}, u32[]{:S(2)}, u32[]{:S(2)}) collective-permute-start(f32[6,4,4,1]{3,2,1,0:T(4,128)S(1)} %get-tuple-element.23), channel_id=1, source_target_pairs={{1,2},{2,1},{5,6},{6,5},{9,10},{10,9},{13,14},{14,13},{17,18},{18,... | collective-permute-start | bytes 1160 | tf_op jit(solution)/shard_map/ppermute | solution.py:24
  11.5 11.2 %collective-permute-start = (f32[6,4,4,1]{3,2,1,0:T(4,128)S(1)}, f32[6,4,4,1]{3,2,1,0:T(4,128)S(1)}, u32[]{:S(2)}, u32[]{:S(2)}) collective-permute-start(f32[6,4,4,1]{3,2,1,0:T(4,128)S(1)} %get-tuple-element.24), channel_id=1, source_target_pairs={{0,1},{1,0},{2,3},{3,2},{4,5},{5,4},{6,7},{7,6},{8,9},{9,8},{10,11... | collective-permute-start | bytes 1160 | tf_op jit(solution)/shard_map/ppermute | solution.py:22
  15.4 7.7 %collective-permute-start.2 = (f32[6,4,1,128]{3,2,1,0:T(1,128)S(1)}, f32[6,4,1,128]{3,2,1,0:T(1,128)S(1)}, u32[]{:S(2)}, u32[]{:S(2)}) collective-permute-start(f32[6,4,1,128]{3,2,1,0:T(1,128)S(1)} %broadcast_select_fusion.2), channel_id=1, source_target_pairs={{0,4},{4,0},{1,5},{5,1},{2,6},{6,2},{3,7},{7,3},{8,12},{12,8},{9,1... | collective-permute-start | bytes 36872 | tf_op jit(solution)/shard_map/ppermute | solution.py:22
  16.9 5.9 %collective-permute-start.3 = (f32[6,1,4,128]{3,2,1,0:T(4,128)S(1)}, f32[6,1,4,128]{3,2,1,0:T(4,128)S(1)}, u32[]{:S(2)}, u32[]{:S(2)}) collective-permute-start(f32[6,1,4,128]{3,2,1,0:T(4,128)S(1)} %get-tuple-element.21), channel_id=1, source_target_pairs={{0,8},{8,0},{16,24},{24,16},{1,9},{9,1},{17,25},{25,17},{2,10},{10... | collective-permute-start | bytes 36872 | tf_op jit(solution)/shard_map/ppermute | solution.py:22
  18.1 5.0 %collective-permute-start.4 = (f32[6,1,4,128]{3,2,1,0:T(4,128)S(1)}, f32[6,1,4,128]{3,2,1,0:T(4,128)S(1)}, u32[]{:S(2)}, u32[]{:S(2)}) collective-permute-start(f32[6,1,4,128]{3,2,1,0:T(4,128)S(1)} %get-tuple-element.22), channel_id=1, source_target_pairs={{8,16},{16,8},{9,17},{17,9},{10,18},{18,10},{11,19},{19,11},{12,20... | collective-permute-start | bytes 36872 | tf_op jit(solution)/shard_map/ppermute | solution.py:24
  28.0 15.7 %copy-start.1 = (s32[64,1]{0,1:T(1,128)S(1)}, s32[64,1]{0,1:T(1,128)}, u32[]{:S(2)}) copy-start(s32[64,1]{0,1:T(1,128)} %param.12) | copy-start | bytes 772
  28.4 6.0 %collective-permute-start.8 = (f32[5,4,4,1]{3,2,1,0:T(4,128)S(1)}, f32[5,4,4,1]{3,2,1,0:T(4,128)S(1)}, u32[]{:S(2)}, u32[]{:S(2)}) collective-permute-start(f32[5,4,4,1]{3,2,1,0:T(4,128)S(1)} %get-tuple-element.27), channel_id=1, source_target_pairs={{1,2},{2,1},{5,6},{6,5},{9,10},{10,9},{13,14},{14,13},{17,18},{18,... | collective-permute-start | bytes 968 | tf_op jit(solution)/shard_map/ppermute | solution.py:24
  29.0 5.4 %collective-permute-start.9 = (f32[5,4,4,1]{3,2,1,0:T(4,128)S(1)}, f32[5,4,4,1]{3,2,1,0:T(4,128)S(1)}, u32[]{:S(2)}, u32[]{:S(2)}) collective-permute-start(f32[5,4,4,1]{3,2,1,0:T(4,128)S(1)} %get-tuple-element.28), channel_id=1, source_target_pairs={{0,1},{1,0},{2,3},{3,2},{4,5},{5,4},{6,7},{7,6},{8,9},{9,8},{10,11... | collective-permute-start | bytes 968 | tf_op jit(solution)/shard_map/ppermute | solution.py:22
  30.3 4.2 %collective-permute-start.7 = (f32[5,4,1,128]{3,2,1,0:T(1,128)S(1)}, f32[5,4,1,128]{3,2,1,0:T(1,128)S(1)}, u32[]{:S(2)}, u32[]{:S(2)}) collective-permute-start(f32[5,4,1,128]{3,2,1,0:T(1,128)S(1)} %broadcast_select_fusion.9), channel_id=1, source_target_pairs={{0,4},{4,0},{1,5},{5,1},{2,6},{6,2},{3,7},{7,3},{8,12},{12,8},{9,1... | collective-permute-start | bytes 30728 | tf_op jit(solution)/shard_map/ppermute | solution.py:22
  30.3 4.2 %collective-permute-start.6 = (f32[5,1,4,128]{3,2,1,0:T(4,128)S(1)}, f32[5,1,4,128]{3,2,1,0:T(4,128)S(1)}, u32[]{:S(2)}, u32[]{:S(2)}) collective-permute-start(f32[5,1,4,128]{3,2,1,0:T(4,128)S(1)} %get-tuple-element.25), channel_id=1, source_target_pairs={{0,8},{8,0},{16,24},{24,16},{1,9},{9,1},{17,25},{25,17},{2,10},{10... | collective-permute-start | bytes 30728 | tf_op jit(solution)/shard_map/ppermute | solution.py:22
  30.3 5.4 %collective-permute-start.5 = (f32[5,1,4,128]{3,2,1,0:T(4,128)S(1)}, f32[5,1,4,128]{3,2,1,0:T(4,128)S(1)}, u32[]{:S(2)}, u32[]{:S(2)}) collective-permute-start(f32[5,1,4,128]{3,2,1,0:T(4,128)S(1)} %get-tuple-element.26), channel_id=1, source_target_pairs={{8,16},{16,8},{9,17},{17,9},{10,18},{18,10},{11,19},{19,11},{12,20... | collective-permute-start | bytes 30728 | tf_op jit(solution)/shard_map/ppermute | solution.py:24
  36.0 14.0 %copy-start = (f32[5,4,4,128]{3,2,1,0:T(4,128)}, f32[5,4,4,128]{3,2,1,0:T(4,128)S(1)}, u32[]{:S(2)}) copy-start(f32[5,4,4,128]{3,2,1,0:T(4,128)S(1)} %fusion.22) | copy-start | bytes 122884
  39.4 8.8 %all-to-all-start.1 = ((f32[1,128,128]{2,0,1:T(1,128)}), f32[1,128,128]{2,0,1:T(1,128)S(1)}, u32[]{:S(2)}, u32[]{:S(2)}) async-start(f32[1,128,128]{2,0,1:T(1,128)} %bitcast.25), calls=%async_computation.1 | async-start | bytes 131072 | tf_op jit(solution)/shard_map/all_to_all | solution.py:201

commit v11 on v10

--- a/solution.py
+++ b/solution.py
@@ -91,13 +91,12 @@
 def make_pack(tile_count, row_count, blocks, capacity):
     slot_total = blocks * capacity
 
-    def pack_kernel(route_ref, length_ref, cell_ref, record_ref, out_ref):
-        target = route_ref[...]
+    def pack_kernel(route_ref, length_ref, cell_ref, record_ref, out_ref, load_ref):
         tile_iota_row = lax.broadcasted_iota(jnp.int32, (tile_count, tile_count), 1)
         tile_iota_col = lax.broadcasted_iota(jnp.int32, (tile_count, tile_count), 0)
-        lengths_col = jnp.sum(
-            jnp.where(tile_iota_row == tile_iota_col, length_ref[...], 0), axis=1, keepdims=True
-        )
+        diagonal = tile_iota_row == tile_iota_col
+        target = jnp.sum(jnp.where(diagonal, route_ref[...], 0), axis=1, keepdims=True)
+        lengths_col = jnp.sum(jnp.where(diagonal, length_ref[...], 0), axis=1, keepdims=True)
         block_hot = (
             target == lax.broadcasted_iota(jnp.int32, (tile_count, blocks), 1)
         ).astype(jnp.float32)
@@ -117,6 +116,8 @@
             eye, slot_hot, (((1,), (1,)), ((), ())), preferred_element_type=jnp.float32
         )
         live = lax.broadcasted_iota(jnp.int32, (tile_count, row_count), 1) < lengths_col
+        for comp in range(3):
+            load_ref[comp] = jnp.where(live, record_ref[5 + comp], 0.0)
         for comp in range(6):
             if comp < 5:
                 rows = record_ref[comp]
@@ -129,8 +130,11 @@
     def pack(routes, lengths, cell_ids, records):
         return pl.pallas_call(
             pack_kernel,
-            out_shape=jax.ShapeDtypeStruct((slot_total, 6 * row_count), jnp.float32),
-        )(routes, lengths.reshape(1, tile_count), cell_ids, records)
+            out_shape=(
+                jax.ShapeDtypeStruct((slot_total, 6 * row_count), jnp.float32),
+                jax.ShapeDtypeStruct((3, tile_count, row_count), jnp.float32),
+            ),
+        )(routes.reshape(1, tile_count), lengths.reshape(1, tile_count), cell_ids, records)
     return pack
 
 
@@ -145,7 +149,6 @@
     slot_total = blocks * capacity
     faces = slot_total * row_count
 
-    live_rows = lax.broadcasted_iota(jnp.int32, (tile_count, row_count), 1) < lengths[:, None]
     target = routes[:, 0]
     earlier = lax.broadcasted_iota(jnp.int32, (tile_count, tile_count), 1) < lax.broadcasted_iota(
         jnp.int32, (tile_count, tile_count), 0
@@ -158,7 +161,7 @@
         slot_index[:, None] == lax.broadcasted_iota(jnp.int32, (tile_count, slot_total), 1)
     ).astype(jnp.float32)
     pack = make_pack(tile_count, row_count, blocks, capacity)
-    outbound = pack(routes, lengths, cell_ids, records)
+    outbound, load_rows = pack(routes, lengths, cell_ids, records)
     arrived = lax.all_to_all(outbound, ("stream", "cross"), split_axis=0, concat_axis=0, tiled=True)
     outbound, state_and_visc = lax.optimization_barrier(
         (outbound, jnp.concatenate([fluid_state, viscosity[None]], 0))
@@ -208,7 +211,7 @@
     home_pressure = jnp.einsum(
         "ts,sr->tr", placement_plan, returned[0], precision=lax.Precision.HIGHEST
     )
-    face_loads = jnp.where(live_rows[None], records[5:8], 0.0) * home_pressure[None]
+    face_loads = load_rows * home_pressure[None]
     return (new_state, face_loads)
 
 

time: 50.8 us -> 48.5 us (0.955)
  other arithmetic: 6.67 us -> 5.04 us
  local copies, waits for them, and re-layouts: 2.01 us -> 0.66 us
  waiting for transfers between devices: 5.93 us -> 6.67 us
    unnamed x5 -> x6, local copies, waits for them, and re-layouts: 1.37 us -> 0.02 us
    mul x1, other arithmetic: 1.55 us -> 0.65 us  [shards(): face_loads = load_rows * home_pressure[None]]
    ppermute x4, waiting for transfers between devices: 1.47 us -> 2.21 us  [face_halo(): from_b = lax.ppermute(jnp.where(odd, last, first), axis, pairs_b)]
    lt x1 -> x0, other arithmetic: 0.73 us -> none  [shards(): lax.broadcasted_iota(jnp.int32, (tile_count, row_count), 1)]
  transfers between devices with their start and end apart: 12 -> 12, of which waited for: 3 -> 3; matrix products, arithmetic and copies ran while one was open for 6% -> 5% of each run, Pallas kernels for 0% -> 0%
where the time goes in v11:
time: 48.5 us; the launch traced here: 47.7 us
  starting transfers between devices  25.7 us (53%)
  waiting for transfers between devices  6.67 us (14%)
  matrix products  5.9 us (12%)
  other arithmetic  5.04 us (10%)
  Pallas kernels  2.64 us (5%)
  between operations  1.01 us (2%)
  local copies, waits for them, and re-layouts  0.66 us (1%)
    ppermute x4, starting transfers between devices, face_halo(): from_b = lax.ppermute(jnp.where(odd, last, first), axis, pairs_b)  8.43 us
    ppermute x6, starting transfers between devices, face_halo(): from_a = lax.ppermute(jnp.where(odd, first, last), axis, pairs_a)  7.79 us
    all_to_all x1, starting transfers between devices, shards(): lax.all_to_all(outbound, ('stream', 'cross'), split_axis=0, concat_axis=0...  5.22 us
    all_to_all x1, waiting for transfers between devices, shards(): lax.all_to_all(face_pressure.reshape(1, slot_total, row_count), ('stream'...  4.44 us
    all_to_all x1, starting transfers between devices, shards(): lax.all_to_all(face_pressure.reshape(1, slot_total, row_count), ('stream'...  4.3 us
    dot_general x1, matrix products, shards(): jnp.einsum('cpf,fd->cpd', spread, depth_hot.astype(jnp.float32), precisio...  3.29 us
    pallas_call x1, Pallas kernels, pack(): pl.pallas_call(pack_kernel, out_shape=(jax.ShapeDtypeStruct((slot_total,...  2.64 us
    dot_general x1, matrix products, exact_dot(): jnp.einsum(left + ',k' + right + '->k' + output, onehot, stacked, preferr...  2.4 us
  transfers between devices with their start and end apart: 12, of which 3 were waited for; matrix products, arithmetic and copies ran while one was open for 5% of the time, Pallas kernels for 0%

profile of v11, /device:TPU:1, one launch (start us, length us, event | category | flops | bytes accessed | tf_op | source)
XLA Modules:
  0.0 47.7 jit_solution(18084144025696253952)
XLA Ops:
  0.6 2.6 %shard_map.86 = (f32[128,768]{1,0:T(8,128)}, f32[3,64,128]{2,1,0:T(8,128)}) custom-call(s32[1,64]{1,0:T(1,128)} %bitcast.97, s32[1,64]{1,0:T(1,128)} %bitcast.96, s32[64,128]{1,0:T(8,128)} %cell_ref.1, f32[8,64,128]{2,1,0:T(8,128)} %record_ref.1), custom_call_target="tpu_custom_call" | custom-call | tf_op jit(solution)/shard_map/pallas_call | solution.py:131
  3.3 5.2 %all-to-all-start = ((f32[8,16,768]{2,1,0:T(8,128)}), f32[8,16,768]{2,1,0:T(8,128)S(1)}, u32[]{:S(2)}, u32[]{:S(2)}) async-start(f32[8,16,768]{2,1,0:T(8,128)} %bitcast.77), calls=%async_computation | async-start | bytes 786432 | tf_op jit(solution)/shard_map/all_to_all | solution.py:165
  8.5 0.8 %pad_maximum_fusion.6 = f32[6,4,4,128]{3,2,1,0:T(4,128)S(1)} fusion(f32[1,4,4,128]{3,2,1,0:T(4,128)} %bitcast.94, f32[4,4,4,128]{3,2,1,0:T(4,128)} %param.8, f32[1,4,4,128]{3,2,1,0:T(4,128)} %bitcast.95), kind=kLoop, calls=%fused_computation.36 | loop fusion | flops 24576 | bytes 98304 | tf_op jit(solution)/shard_map/concatenate | solution.py:167
  9.4 0.7 %collective-permute-start.1 = (f32[6,4,4,1]{3,2,1,0:T(4,128)S(1)}, f32[6,4,4,1]{3,2,1,0:T(4,128)S(1)}, u32[]{:S(2)}, u32[]{:S(2)}) collective-permute-start(f32[6,4,4,1]{3,2,1,0:T(4,128)S(1)} %get-tuple-element.27), channel_id=1, source_target_pairs={{1,2},{2,1},{5,6},{6,5},{9,10},{10,9},{13,14},{14,13},{17,18},{18,... | collective-permute-start | bytes 1160 | tf_op jit(solution)/shard_map/ppermute | solution.py:24
  10.1 3.9 %collective-permute-start = (f32[6,4,4,1]{3,2,1,0:T(4,128)S(1)}, f32[6,4,4,1]{3,2,1,0:T(4,128)S(1)}, u32[]{:S(2)}, u32[]{:S(2)}) collective-permute-start(f32[6,4,4,1]{3,2,1,0:T(4,128)S(1)} %get-tuple-element.28), channel_id=1, source_target_pairs={{0,1},{1,0},{2,3},{3,2},{4,5},{5,4},{6,7},{7,6},{8,9},{9,8},{10,11... | collective-permute-start | bytes 1160 | tf_op jit(solution)/shard_map/ppermute | solution.py:22
  14.0 1.4 %collective-permute-start.2 = (f32[6,4,1,128]{3,2,1,0:T(1,128)S(1)}, f32[6,4,1,128]{3,2,1,0:T(1,128)S(1)}, u32[]{:S(2)}, u32[]{:S(2)}) collective-permute-start(f32[6,4,1,128]{3,2,1,0:T(1,128)S(1)} %broadcast_select_fusion.2), channel_id=1, source_target_pairs={{0,4},{4,0},{1,5},{5,1},{2,6},{6,2},{3,7},{7,3},{8,12},{12,8},{9,1... | collective-permute-start | bytes 36872 | tf_op jit(solution)/shard_map/ppermute | solution.py:22
  15.4 1.2 %collective-permute-start.3 = (f32[6,1,4,128]{3,2,1,0:T(4,128)S(1)}, f32[6,1,4,128]{3,2,1,0:T(4,128)S(1)}, u32[]{:S(2)}, u32[]{:S(2)}) collective-permute-start(f32[6,1,4,128]{3,2,1,0:T(4,128)S(1)} %get-tuple-element.25), channel_id=1, source_target_pairs={{0,8},{8,0},{16,24},{24,16},{1,9},{9,1},{17,25},{25,17},{2,10},{10... | collective-permute-start | bytes 36872 | tf_op jit(solution)/shard_map/ppermute | solution.py:22
  16.7 3.0 %collective-permute-start.4 = (f32[6,1,4,128]{3,2,1,0:T(4,128)S(1)}, f32[6,1,4,128]{3,2,1,0:T(4,128)S(1)}, u32[]{:S(2)}, u32[]{:S(2)}) collective-permute-start(f32[6,1,4,128]{3,2,1,0:T(4,128)S(1)} %get-tuple-element.26), channel_id=1, source_target_pairs={{8,16},{16,8},{9,17},{17,9},{10,18},{18,10},{11,19},{19,11},{12,20... | collective-permute-start | bytes 36872 | tf_op jit(solution)/shard_map/ppermute | solution.py:24
  19.6 0.9 %convert_reduce_fusion = s32[64]{0:T(128)S(1)} fusion(s32[64]{0:T(128)} %bitcast.98), kind=kLoop, calls=%fused_computation.120 | loop fusion | flops 20416 | bytes 512 | tf_op jit(solution)/shard_map/reduce_sum | solution.py:156
  20.7 1.0 %collective-permute-done.4 = f32[6,1,4,128]{3,2,1,0:T(4,128)S(1)} collective-permute-done((f32[6,1,4,128]{3,2,1,0:T(4,128)S(1)}, f32[6,1,4,128]{3,2,1,0:T(4,128)S(1)}, u32[]{:S(2)}, u32[]{:S(2)}) %collective-permute-start.4) | collective-permute-done | bytes 12320 | tf_op jit(solution)/shard_map/ppermute | solution.py:24
  22.3 0.5 %concatenate.68 = f32[5,16384]{1,0:T(8,128)S(1)} concatenate(f32[1,16384]{1,0:T(1,128)S(1)} %bitcast.83, f32[1,16384]{1,0:T(1,128)S(1)} %bitcast.82, f32[1,16384]{1,0:T(1,128)S(1)} %bitcast.81, f32[1,16384]{1,0:T(1,128)S(1)} %bitcast.80, f32[1,16384]{1,0:T(1,128)S(1)} %bitcast.79), dimensions={0} | concatenate | bytes 655360 | tf_op jit(solution)/shard_map/concatenate | solution.py:183
  22.8 0.5 fusion.96
  23.3 3.3 %fusion.2 = f32[5,16,128]{2,1,0:T(8,128)S(1)} fusion(s32[16384]{0:T(1024)S(1)} %add_select_fusion, f32[5,16,16384]{2,1,0:T(8,128)S(1)} %fusion.96), kind=kOutput, calls=%fused_computation.3 | convolution fusion | flops 1008730112 | bytes 5349376 | tf_op jit(solution)/shard_map/cpf,fd->cpd/dot_general | solution.py:185
  26.6 0.2 fusion.42
  27.0 0.7 %collective-permute-start.8 = (f32[5,4,4,1]{3,2,1,0:T(4,128)S(1)}, f32[5,4,4,1]{3,2,1,0:T(4,128)S(1)}, u32[]{:S(2)}, u32[]{:S(2)}) collective-permute-start(f32[5,4,4,1]{3,2,1,0:T(4,128)S(1)} %get-tuple-element.31), channel_id=1, source_target_pairs={{1,2},{2,1},{5,6},{6,5},{9,10},{10,9},{13,14},{14,13},{17,18},{18,... | collective-permute-start | bytes 968 | tf_op jit(solution)/shard_map/ppermute | solution.py:24
  27.6 1.2 %collective-permute-start.9 = (f32[5,4,4,1]{3,2,1,0:T(4,128)S(1)}, f32[5,4,4,1]{3,2,1,0:T(4,128)S(1)}, u32[]{:S(2)}, u32[]{:S(2)}) collective-permute-start(f32[5,4,4,1]{3,2,1,0:T(4,128)S(1)} %get-tuple-element.32), channel_id=1, source_target_pairs={{0,1},{1,0},{2,3},{3,2},{4,5},{5,4},{6,7},{7,6},{8,9},{9,8},{10,11... | collective-permute-start | bytes 968 | tf_op jit(solution)/shard_map/ppermute | solution.py:22
  28.9 4.1 %collective-permute-start.5 = (f32[5,1,4,128]{3,2,1,0:T(4,128)S(1)}, f32[5,1,4,128]{3,2,1,0:T(4,128)S(1)}, u32[]{:S(2)}, u32[]{:S(2)}) collective-permute-start(f32[5,1,4,128]{3,2,1,0:T(4,128)S(1)} %get-tuple-element.30), channel_id=1, source_target_pairs={{8,16},{16,8},{9,17},{17,9},{10,18},{18,10},{11,19},{19,11},{12,20... | collective-permute-start | bytes 30728 | tf_op jit(solution)/shard_map/ppermute | solution.py:24
  33.1 1.2 %collective-permute-done.5 = f32[5,1,4,128]{3,2,1,0:T(4,128)S(1)} collective-permute-done((f32[5,1,4,128]{3,2,1,0:T(4,128)S(1)}, f32[5,1,4,128]{3,2,1,0:T(4,128)S(1)}, u32[]{:S(2)}, u32[]{:S(2)}) %collective-permute-start.5) | collective-permute-done | bytes 10272 | tf_op jit(solution)/shard_map/ppermute | solution.py:24
  34.3 0.2 fusion.22
  34.6 2.4 %convolution_bitcast_fusion = f32[3,16384,16]{1,2,0:T(8,128)S(1)} fusion(s32[16384]{0:T(1024)S(1)} %add_select_fusion, bf16[1,128,16]{1,2,0:T(8,128)(2,1)S(1)} %get-tuple-element.43, bf16[1,128,16]{1,2,0:T(8,128)(2,1)S(1)} %get-tuple-element.42, bf16[1,128,16]{1,2,0:T(8,128)(2,1)S(1)} %get-tuple-element.41), kind=kOutput, calls=%fused_computation | convolution fusion | flops 203436032 | bytes 3223552 | tf_op jit(solution)/shard_map/fd,kdp->kfp/dot_general | solution.py:84
  37.0 1.0 %fusion.12 = f32[16384]{0:T(1024)} fusion(f32[3,16384,16]{1,2,0:T(8,128)S(1)} %convolution_bitcast_fusion, s32[16384]{0:T(1024)S(1)} %get-tuple-element.8), kind=kLoop, calls=%fused_computation.13 | loop fusion | flops 1294336 | bytes 3276800 | tf_op jit(solution)/shard_map/reduce_sum | solution.py:203
  38.0 4.3 %all-to-all-start.1 = ((f32[1,128,128]{2,0,1:T(1,128)}), f32[1,128,128]{2,0,1:T(1,128)S(1)}, u32[]{:S(2)}, u32[]{:S(2)}) async-start(f32[1,128,128]{2,0,1:T(1,128)} %bitcast.26), calls=%async_computation.1 | async-start | bytes 131072 | tf_op jit(solution)/shard_map/all_to_all | solution.py:204
  42.3 4.4 %all-to-all-done.1 = f32[1,128,128]{2,0,1:T(1,128)S(1)} async-done(((f32[1,128,128]{2,0,1:T(1,128)}), f32[1,128,128]{2,0,1:T(1,128)S(1)}, u32[]{:S(2)}, u32[]{:S(2)}) %all-to-all-start.1) | async-done | bytes 65568 | tf_op jit(solution)/shard_map/all_to_all | solution.py:204
  47.0 0.7 %broadcast_multiply_fusion = f32[3,64,128]{2,1,0:T(8,128)} fusion(f32[3,64,128]{2,1,0:T(8,128)S(1)} %copy-done.1, f32[64,128]{1,0:T(8,128)S(1)} %fusion.58), kind=kLoop, calls=%fused_computation.37 | loop fusion | flops 24576 | bytes 229376 | tf_op jit(solution)/shard_map/mul | solution.py:214
  (45 shorter events, 1.1 us)
Async XLA Ops:
  3.3 18.7 %all-to-all-start = ((f32[8,16,768]{2,1,0:T(8,128)}), f32[8,16,768]{2,1,0:T(8,128)S(1)}, u32[]{:S(2)}, u32[]{:S(2)}) async-start(f32[8,16,768]{2,1,0:T(8,128)} %bitcast.77), calls=%async_computation | async-start | bytes 786432 | tf_op jit(solution)/shard_map/all_to_all | solution.py:165
  9.4 11.2 %collective-permute-start.1 = (f32[6,4,4,1]{3,2,1,0:T(4,128)S(1)}, f32[6,4,4,1]{3,2,1,0:T(4,128)S(1)}, u32[]{:S(2)}, u32[]{:S(2)}) collective-permute-start(f32[6,4,4,1]{3,2,1,0:T(4,128)S(1)} %get-tuple-element.27), channel_id=1, source_target_pairs={{1,2},{2,1},{5,6},{6,5},{9,10},{10,9},{13,14},{14,13},{17,18},{18,... | collective-permute-start | bytes 1160 | tf_op jit(solution)/shard_map/ppermute | solution.py:24
  10.1 10.5 %collective-permute-start = (f32[6,4,4,1]{3,2,1,0:T(4,128)S(1)}, f32[6,4,4,1]{3,2,1,0:T(4,128)S(1)}, u32[]{:S(2)}, u32[]{:S(2)}) collective-permute-start(f32[6,4,4,1]{3,2,1,0:T(4,128)S(1)} %get-tuple-element.28), channel_id=1, source_target_pairs={{0,1},{1,0},{2,3},{3,2},{4,5},{5,4},{6,7},{7,6},{8,9},{9,8},{10,11... | collective-permute-start | bytes 1160 | tf_op jit(solution)/shard_map/ppermute | solution.py:22
  14.0 7.7 %collective-permute-start.2 = (f32[6,4,1,128]{3,2,1,0:T(1,128)S(1)}, f32[6,4,1,128]{3,2,1,0:T(1,128)S(1)}, u32[]{:S(2)}, u32[]{:S(2)}) collective-permute-start(f32[6,4,1,128]{3,2,1,0:T(1,128)S(1)} %broadcast_select_fusion.2), channel_id=1, source_target_pairs={{0,4},{4,0},{1,5},{5,1},{2,6},{6,2},{3,7},{7,3},{8,12},{12,8},{9,1... | collective-permute-start | bytes 36872 | tf_op jit(solution)/shard_map/ppermute | solution.py:22
  15.4 5.2 %collective-permute-start.3 = (f32[6,1,4,128]{3,2,1,0:T(4,128)S(1)}, f32[6,1,4,128]{3,2,1,0:T(4,128)S(1)}, u32[]{:S(2)}, u32[]{:S(2)}) collective-permute-start(f32[6,1,4,128]{3,2,1,0:T(4,128)S(1)} %get-tuple-element.25), channel_id=1, source_target_pairs={{0,8},{8,0},{16,24},{24,16},{1,9},{9,1},{17,25},{25,17},{2,10},{10... | collective-permute-start | bytes 36872 | tf_op jit(solution)/shard_map/ppermute | solution.py:22
  16.7 5.0 %collective-permute-start.4 = (f32[6,1,4,128]{3,2,1,0:T(4,128)S(1)}, f32[6,1,4,128]{3,2,1,0:T(4,128)S(1)}, u32[]{:S(2)}, u32[]{:S(2)}) collective-permute-start(f32[6,1,4,128]{3,2,1,0:T(4,128)S(1)} %get-tuple-element.26), channel_id=1, source_target_pairs={{8,16},{16,8},{9,17},{17,9},{10,18},{18,10},{11,19},{19,11},{12,20... | collective-permute-start | bytes 36872 | tf_op jit(solution)/shard_map/ppermute | solution.py:24
  26.6 15.8 %copy-start.2 = (s32[64,1]{0,1:T(1,128)S(1)}, s32[64,1]{0,1:T(1,128)}, u32[]{:S(2)}) copy-start(s32[64,1]{0,1:T(1,128)} %param.12) | copy-start | bytes 772
  26.6 20.4 %copy-start.1 = (f32[3,64,128]{2,1,0:T(8,128)S(1)}, f32[3,64,128]{2,1,0:T(8,128)}, u32[]{:S(2)}) copy-start(f32[3,64,128]{2,1,0:T(8,128)} %get-tuple-element.7) | copy-start | bytes 294916
  27.0 6.0 %collective-permute-start.8 = (f32[5,4,4,1]{3,2,1,0:T(4,128)S(1)}, f32[5,4,4,1]{3,2,1,0:T(4,128)S(1)}, u32[]{:S(2)}, u32[]{:S(2)}) collective-permute-start(f32[5,4,4,1]{3,2,1,0:T(4,128)S(1)} %get-tuple-element.31), channel_id=1, source_target_pairs={{1,2},{2,1},{5,6},{6,5},{9,10},{10,9},{13,14},{14,13},{17,18},{18,... | collective-permute-start | bytes 968 | tf_op jit(solution)/shard_map/ppermute | solution.py:24
  27.6 5.4 %collective-permute-start.9 = (f32[5,4,4,1]{3,2,1,0:T(4,128)S(1)}, f32[5,4,4,1]{3,2,1,0:T(4,128)S(1)}, u32[]{:S(2)}, u32[]{:S(2)}) collective-permute-start(f32[5,4,4,1]{3,2,1,0:T(4,128)S(1)} %get-tuple-element.32), channel_id=1, source_target_pairs={{0,1},{1,0},{2,3},{3,2},{4,5},{5,4},{6,7},{7,6},{8,9},{9,8},{10,11... | collective-permute-start | bytes 968 | tf_op jit(solution)/shard_map/ppermute | solution.py:22
  28.9 4.2 %collective-permute-start.7 = (f32[5,4,1,128]{3,2,1,0:T(1,128)S(1)}, f32[5,4,1,128]{3,2,1,0:T(1,128)S(1)}, u32[]{:S(2)}, u32[]{:S(2)}) collective-permute-start(f32[5,4,1,128]{3,2,1,0:T(1,128)S(1)} %broadcast_select_fusion.9), channel_id=1, source_target_pairs={{0,4},{4,0},{1,5},{5,1},{2,6},{6,2},{3,7},{7,3},{8,12},{12,8},{9,1... | collective-permute-start | bytes 30728 | tf_op jit(solution)/shard_map/ppermute | solution.py:22
  28.9 4.2 %collective-permute-start.6 = (f32[5,1,4,128]{3,2,1,0:T(4,128)S(1)}, f32[5,1,4,128]{3,2,1,0:T(4,128)S(1)}, u32[]{:S(2)}, u32[]{:S(2)}) collective-permute-start(f32[5,1,4,128]{3,2,1,0:T(4,128)S(1)} %get-tuple-element.29), channel_id=1, source_target_pairs={{0,8},{8,0},{16,24},{24,16},{1,9},{9,1},{17,25},{25,17},{2,10},{10... | collective-permute-start | bytes 30728 | tf_op jit(solution)/shard_map/ppermute | solution.py:22
  28.9 5.5 %collective-permute-start.5 = (f32[5,1,4,128]{3,2,1,0:T(4,128)S(1)}, f32[5,1,4,128]{3,2,1,0:T(4,128)S(1)}, u32[]{:S(2)}, u32[]{:S(2)}) collective-permute-start(f32[5,1,4,128]{3,2,1,0:T(4,128)S(1)} %get-tuple-element.30), channel_id=1, source_target_pairs={{8,16},{16,8},{9,17},{17,9},{10,18},{18,10},{11,19},{19,11},{12,20... | collective-permute-start | bytes 30728 | tf_op jit(solution)/shard_map/ppermute | solution.py:24
  34.6 13.1 %copy-start = (f32[5,4,4,128]{3,2,1,0:T(4,128)}, f32[5,4,4,128]{3,2,1,0:T(4,128)S(1)}, u32[]{:S(2)}) copy-start(f32[5,4,4,128]{3,2,1,0:T(4,128)S(1)} %fusion.22) | copy-start | bytes 122884
  38.0 8.8 %all-to-all-start.1 = ((f32[1,128,128]{2,0,1:T(1,128)}), f32[1,128,128]{2,0,1:T(1,128)S(1)}, u32[]{:S(2)}, u32[]{:S(2)}) async-start(f32[1,128,128]{2,0,1:T(1,128)} %bitcast.26), calls=%async_computation.1 | async-start | bytes 131072 | tf_op jit(solution)/shard_map/all_to_all | solution.py:204

commit v12 on v11

--- a/solution.py
+++ b/solution.py
@@ -91,7 +91,7 @@
 def make_pack(tile_count, row_count, blocks, capacity):
     slot_total = blocks * capacity
 
-    def pack_kernel(route_ref, length_ref, cell_ref, record_ref, out_ref, load_ref):
+    def pack_kernel(route_ref, length_ref, cell_ref, record_ref, out_ref, load_ref, plan_ref):
         tile_iota_row = lax.broadcasted_iota(jnp.int32, (tile_count, tile_count), 1)
         tile_iota_col = lax.broadcasted_iota(jnp.int32, (tile_count, tile_count), 0)
         diagonal = tile_iota_row == tile_iota_col
@@ -108,6 +108,7 @@
         slot_hot = (
             slot == lax.broadcasted_iota(jnp.int32, (tile_count, slot_total), 1)
         ).astype(jnp.float32)
+        plan_ref[...] = slot_hot
         eye = (
             lax.broadcasted_iota(jnp.int32, (slot_total, slot_total), 0)
             == lax.broadcasted_iota(jnp.int32, (slot_total, slot_total), 1)
@@ -119,7 +120,9 @@
         for comp in range(3):
             load_ref[comp] = jnp.where(live, record_ref[5 + comp], 0.0)
         for comp in range(6):
-            if comp < 5:
+            if comp == 0:
+                rows = jnp.abs(record_ref[0])
+            elif comp < 5:
                 rows = record_ref[comp]
             else:
                 rows = jnp.where(live, cell_ref[...], -1).astype(jnp.float32)
@@ -133,6 +136,7 @@
             out_shape=(
                 jax.ShapeDtypeStruct((slot_total, 6 * row_count), jnp.float32),
                 jax.ShapeDtypeStruct((3, tile_count, row_count), jnp.float32),
+                jax.ShapeDtypeStruct((tile_count, slot_total), jnp.float32),
             ),
         )(routes.reshape(1, tile_count), lengths.reshape(1, tile_count), cell_ids, records)
     return pack
@@ -149,19 +153,8 @@
     slot_total = blocks * capacity
     faces = slot_total * row_count
 
-    target = routes[:, 0]
-    earlier = lax.broadcasted_iota(jnp.int32, (tile_count, tile_count), 1) < lax.broadcasted_iota(
-        jnp.int32, (tile_count, tile_count), 0
-    )
-    slot_rank = jnp.sum(
-        (earlier & (target[None, :] == target[:, None])).astype(jnp.int32), axis=1
-    )
-    slot_index = target * capacity + slot_rank
-    placement_plan = (
-        slot_index[:, None] == lax.broadcasted_iota(jnp.int32, (tile_count, slot_total), 1)
-    ).astype(jnp.float32)
     pack = make_pack(tile_count, row_count, blocks, capacity)
-    outbound, load_rows = pack(routes, lengths, cell_ids, records)
+    outbound, load_rows, placement_plan = pack(routes, lengths, cell_ids, records)
     arrived = lax.all_to_all(outbound, ("stream", "cross"), split_axis=0, concat_axis=0, tiled=True)
     outbound, state_and_visc = lax.optimization_barrier(
         (outbound, jnp.concatenate([fluid_state, viscosity[None]], 0))
@@ -180,7 +173,6 @@
     arrived_values = jnp.stack(
         [arrived[:, c * row_count:(c + 1) * row_count].reshape(faces) for c in range(5)], 0
     )
-    arrived_values = jnp.concatenate([jnp.abs(arrived_values[0:1]), arrived_values[1:5]], 0)
     spread = jnp.where(plane_rows[None], arrived_values[:, None, :], 0.0)
     source = jnp.einsum(
         "cpf,fd->cpd", spread, depth_hot.astype(jnp.float32), precision=lax.Precision.HIGH

time: 48.5 us -> 47.5 us (0.979)
  blocking collectives: 0 us -> 8.55 us
  starting transfers between devices: 25.7 us -> 21.4 us
  waiting for transfers between devices: 6.67 us -> 3.14 us
  other arithmetic: 5.04 us -> 3.48 us
    all_to_all x0 -> x1, blocking collectives: none -> 8.55 us  [shards(): lax.all_to_all(face_pressure.reshape(1, slot_total, row_count), ('stream'...]
    all_to_all x1 -> x0, waiting for transfers between devices: 4.44 us -> none  [shards(): lax.all_to_all(face_pressure.reshape(1, slot_total, row_count), ('stream'...]
    all_to_all x1 -> x0, starting transfers between devices: 4.3 us -> none  [shards(): lax.all_to_all(face_pressure.reshape(1, slot_total, row_count), ('stream'...]
    ppermute x4, waiting for transfers between devices: 2.21 us -> 3.12 us  [face_halo(): from_b = lax.ppermute(jnp.where(odd, last, first), axis, pairs_b)]
    reduce_sum x1 -> x0, other arithmetic: 0.91 us -> none  [shards(): jnp.sum((earlier & (target[None, :] == target[:, None])).astype(jnp.int32...]
    reduce_sum x1, other arithmetic: 1 us -> 0.38 us  [shards(): face_pressure = jnp.sum(jnp.where(plane_cols, picked, 0.0), axis=1)]
    another operation x0 -> x1, local copies, waits for them, and re-layouts: none -> 0.55 us  [shards(): jnp.stack([arrived[:, c * row_count:(c + 1) * row_count].reshape(faces) f...]
    concatenate x1 -> x0, local copies, waits for them, and re-layouts: 0.55 us -> none  [shards(): jnp.concatenate([jnp.abs(arrived_values[0:1]), arrived_values[1:5]], 0)]
  transfers between devices with their start and end apart: 12 -> 11, of which waited for: 3 -> 2; matrix products, arithmetic and copies ran while one was open for 5% -> 3% of each run, Pallas kernels for 0% -> 0%
where the time goes in v12:
time: 47.5 us; the launch traced here: 46.8 us
  starting transfers between devices  21.4 us (45%)
  blocking collectives  8.55 us (18%)
  matrix products  5.86 us (12%)
  other arithmetic  3.48 us (7%)
  waiting for transfers between devices  3.14 us (7%)
  Pallas kernels  2.64 us (6%)
  between operations  1.01 us (2%)
  local copies, waits for them, and re-layouts  0.68 us (1%)
    all_to_all x1, blocking collectives, shards(): lax.all_to_all(face_pressure.reshape(1, slot_total, row_count), ('stream'...  8.55 us
    ppermute x4, starting transfers between devices, face_halo(): from_b = lax.ppermute(jnp.where(odd, last, first), axis, pairs_b)  8.42 us
    ppermute x6, starting transfers between devices, face_halo(): from_a = lax.ppermute(jnp.where(odd, first, last), axis, pairs_a)  7.79 us
    all_to_all x1, starting transfers between devices, shards(): lax.all_to_all(outbound, ('stream', 'cross'), split_axis=0, concat_axis=0...  5.22 us
    dot_general x1, matrix products, shards(): jnp.einsum('cpf,fd->cpd', spread, depth_hot.astype(jnp.float32), precisio...  3.28 us
    ppermute x4, waiting for transfers between devices, face_halo(): from_b = lax.ppermute(jnp.where(odd, last, first), axis, pairs_b)  3.12 us
    pallas_call x1, Pallas kernels, pack(): pl.pallas_call(pack_kernel, out_shape=(jax.ShapeDtypeStruct((slot_total,...  2.64 us
    dot_general x1, matrix products, exact_dot(): jnp.einsum(left + ',k' + right + '->k' + output, onehot, stacked, preferr...  2.4 us
  transfers between devices with their start and end apart: 11, of which 2 were waited for; matrix products, arithmetic and copies ran while one was open for 3% of the time, Pallas kernels for 0%

profile of v12, /device:TPU:1, one launch (start us, length us, event | category | flops | bytes accessed | tf_op | source)
XLA Modules:
  0.0 46.8 jit_solution(16930094239931208812)
XLA Ops:
  0.6 2.6 %shard_map.86 = (f32[128,768]{1,0:T(8,128)}, f32[3,64,128]{2,1,0:T(8,128)}, f32[64,128]{1,0:T(8,128)}) custom-call(s32[1,64]{1,0:T(1,128)} %bitcast.91, s32[1,64]{1,0:T(1,128)} %bitcast.92, s32[64,128]{1,0:T(8,128)} %cell_ref.1, f32[8,64,128]{2,1,0:T(8,128)} %record_ref.1), custom_call_target="tpu_custom_call" | custom-call | tf_op jit(solution)/shard_map/pallas_call | solution.py:134
  3.3 5.2 %all-to-all-start = ((f32[8,16,768]{2,1,0:T(8,128)}), f32[8,16,768]{2,1,0:T(8,128)S(1)}, u32[]{:S(2)}, u32[]{:S(2)}) async-start(f32[8,16,768]{2,1,0:T(8,128)} %bitcast.71), calls=%async_computation | async-start | bytes 786432 | tf_op jit(solution)/shard_map/all_to_all | solution.py:158
  8.5 0.8 %pad_maximum_fusion.6 = f32[6,4,4,128]{3,2,1,0:T(4,128)S(1)} fusion(f32[1,4,4,128]{3,2,1,0:T(4,128)} %bitcast.89, f32[4,4,4,128]{3,2,1,0:T(4,128)} %param.8, f32[1,4,4,128]{3,2,1,0:T(4,128)} %bitcast.90), kind=kLoop, calls=%fused_computation.35 | loop fusion | flops 24576 | bytes 98304 | tf_op jit(solution)/shard_map/concatenate | solution.py:160
  9.4 0.7 %collective-permute-start.1 = (f32[6,4,4,1]{3,2,1,0:T(4,128)S(1)}, f32[6,4,4,1]{3,2,1,0:T(4,128)S(1)}, u32[]{:S(2)}, u32[]{:S(2)}) collective-permute-start(f32[6,4,4,1]{3,2,1,0:T(4,128)S(1)} %get-tuple-element.29), channel_id=1, source_target_pairs={{1,2},{2,1},{5,6},{6,5},{9,10},{10,9},{13,14},{14,13},{17,18},{18,... | collective-permute-start | bytes 1160 | tf_op jit(solution)/shard_map/ppermute | solution.py:24
  10.1 3.9 %collective-permute-start = (f32[6,4,4,1]{3,2,1,0:T(4,128)S(1)}, f32[6,4,4,1]{3,2,1,0:T(4,128)S(1)}, u32[]{:S(2)}, u32[]{:S(2)}) collective-permute-start(f32[6,4,4,1]{3,2,1,0:T(4,128)S(1)} %get-tuple-element.30), channel_id=1, source_target_pairs={{0,1},{1,0},{2,3},{3,2},{4,5},{5,4},{6,7},{7,6},{8,9},{9,8},{10,11... | collective-permute-start | bytes 1160 | tf_op jit(solution)/shard_map/ppermute | solution.py:22
  14.0 1.4 %collective-permute-start.2 = (f32[6,4,1,128]{3,2,1,0:T(1,128)S(1)}, f32[6,4,1,128]{3,2,1,0:T(1,128)S(1)}, u32[]{:S(2)}, u32[]{:S(2)}) collective-permute-start(f32[6,4,1,128]{3,2,1,0:T(1,128)S(1)} %broadcast_select_fusion.2), channel_id=1, source_target_pairs={{0,4},{4,0},{1,5},{5,1},{2,6},{6,2},{3,7},{7,3},{8,12},{12,8},{9,1... | collective-permute-start | bytes 36872 | tf_op jit(solution)/shard_map/ppermute | solution.py:22
  15.4 1.2 %collective-permute-start.3 = (f32[6,1,4,128]{3,2,1,0:T(4,128)S(1)}, f32[6,1,4,128]{3,2,1,0:T(4,128)S(1)}, u32[]{:S(2)}, u32[]{:S(2)}) collective-permute-start(f32[6,1,4,128]{3,2,1,0:T(4,128)S(1)} %get-tuple-element.27), channel_id=1, source_target_pairs={{0,8},{8,0},{16,24},{24,16},{1,9},{9,1},{17,25},{25,17},{2,10},{10... | collective-permute-start | bytes 36872 | tf_op jit(solution)/shard_map/ppermute | solution.py:22
  16.6 3.0 %collective-permute-start.4 = (f32[6,1,4,128]{3,2,1,0:T(4,128)S(1)}, f32[6,1,4,128]{3,2,1,0:T(4,128)S(1)}, u32[]{:S(2)}, u32[]{:S(2)}) collective-permute-start(f32[6,1,4,128]{3,2,1,0:T(4,128)S(1)} %get-tuple-element.28), channel_id=1, source_target_pairs={{8,16},{16,8},{9,17},{17,9},{10,18},{18,10},{11,19},{19,11},{12,20... | collective-permute-start | bytes 36872 | tf_op jit(solution)/shard_map/ppermute | solution.py:24
  19.8 1.9 %collective-permute-done.4 = f32[6,1,4,128]{3,2,1,0:T(4,128)S(1)} collective-permute-done((f32[6,1,4,128]{3,2,1,0:T(4,128)S(1)}, f32[6,1,4,128]{3,2,1,0:T(4,128)S(1)}, u32[]{:S(2)}, u32[]{:S(2)}) %collective-permute-start.4) | collective-permute-done | bytes 12320 | tf_op jit(solution)/shard_map/ppermute | solution.py:24
  22.1 0.1 iota_compare_fusion.2
  22.3 0.5 %stack.15 = f32[5,16384]{1,0:T(8,128)S(1)} concatenate(f32[1,16384]{1,0:T(1,128)S(1)} %bitcast.78, f32[1,16384]{1,0:T(1,128)S(1)} %bitcast.77, f32[1,16384]{1,0:T(1,128)S(1)} %bitcast.76, f32[1,16384]{1,0:T(1,128)S(1)} %bitcast.75, f32[1,16384]{1,0:T(1,128)S(1)} %bitcast.74), dimensions={0} | concatenate | bytes 655360 | tf_op jit(solution)/shard_map/stack | solution.py:173
  22.8 0.5 fusion.94
  23.3 3.3 %fusion.2 = f32[5,16,128]{2,1,0:T(8,128)S(1)} fusion(s32[16384]{0:T(1024)S(1)} %add_select_fusion, f32[5,16,16384]{2,1,0:T(8,128)S(1)} %fusion.94), kind=kOutput, calls=%fused_computation.3 | convolution fusion | flops 1008730112 | bytes 5349376 | tf_op jit(solution)/shard_map/cpf,fd->cpd/dot_general | solution.py:177
  26.6 0.2 fusion.42
  26.9 0.7 %collective-permute-start.8 = (f32[5,4,4,1]{3,2,1,0:T(4,128)S(1)}, f32[5,4,4,1]{3,2,1,0:T(4,128)S(1)}, u32[]{:S(2)}, u32[]{:S(2)}) collective-permute-start(f32[5,4,4,1]{3,2,1,0:T(4,128)S(1)} %get-tuple-element.33), channel_id=1, source_target_pairs={{1,2},{2,1},{5,6},{6,5},{9,10},{10,9},{13,14},{14,13},{17,18},{18,... | collective-permute-start | bytes 968 | tf_op jit(solution)/shard_map/ppermute | solution.py:24
  27.6 1.2 %collective-permute-start.9 = (f32[5,4,4,1]{3,2,1,0:T(4,128)S(1)}, f32[5,4,4,1]{3,2,1,0:T(4,128)S(1)}, u32[]{:S(2)}, u32[]{:S(2)}) collective-permute-start(f32[5,4,4,1]{3,2,1,0:T(4,128)S(1)} %get-tuple-element.34), channel_id=1, source_target_pairs={{0,1},{1,0},{2,3},{3,2},{4,5},{5,4},{6,7},{7,6},{8,9},{9,8},{10,11... | collective-permute-start | bytes 968 | tf_op jit(solution)/shard_map/ppermute | solution.py:22
  28.9 4.1 %collective-permute-start.5 = (f32[5,1,4,128]{3,2,1,0:T(4,128)S(1)}, f32[5,1,4,128]{3,2,1,0:T(4,128)S(1)}, u32[]{:S(2)}, u32[]{:S(2)}) collective-permute-start(f32[5,1,4,128]{3,2,1,0:T(4,128)S(1)} %get-tuple-element.32), channel_id=1, source_target_pairs={{8,16},{16,8},{9,17},{17,9},{10,18},{18,10},{11,19},{19,11},{12,20... | collective-permute-start | bytes 30728 | tf_op jit(solution)/shard_map/ppermute | solution.py:24
  33.1 1.2 %collective-permute-done.5 = f32[5,1,4,128]{3,2,1,0:T(4,128)S(1)} collective-permute-done((f32[5,1,4,128]{3,2,1,0:T(4,128)S(1)}, f32[5,1,4,128]{3,2,1,0:T(4,128)S(1)}, u32[]{:S(2)}, u32[]{:S(2)}) %collective-permute-start.5) | collective-permute-done | bytes 10272 | tf_op jit(solution)/shard_map/ppermute | solution.py:24
  34.3 0.2 fusion.22
  34.6 2.4 %convolution_bitcast_fusion = f32[3,16384,16]{1,2,0:T(8,128)S(1)} fusion(s32[16384]{0:T(1024)S(1)} %add_select_fusion, bf16[1,128,16]{1,2,0:T(8,128)(2,1)S(1)} %get-tuple-element.45, bf16[1,128,16]{1,2,0:T(8,128)(2,1)S(1)} %get-tuple-element.44, bf16[1,128,16]{1,2,0:T(8,128)(2,1)S(1)} %get-tuple-element.43), kind=kOutput, calls=%fused_computation | convolution fusion | flops 203436032 | bytes 3223552 | tf_op jit(solution)/shard_map/fd,kdp->kfp/dot_general | solution.py:84
  37.0 0.4 fusion.12
  37.4 8.5 %all_to_all.17 = f32[1,128,128]{2,0,1:T(1,128)S(1)} all-to-all(f32[1,128,128]{2,0,1:T(1,128)S(1)} %bitcast.72), channel_id=1, replica_groups=mesh['stream'=4,'cross'=2,'gore'=4] {'stream','cross'}, dimensions={1} | all-to-all | bytes 131072 | tf_op jit(solution)/shard_map/all_to_all | solution.py:196
  45.9 0.2 fusion.85
  46.1 0.7 %broadcast_multiply_fusion = f32[3,64,128]{2,1,0:T(8,128)} fusion(f32[3,64,128]{2,1,0:T(8,128)S(1)} %copy-done.1, f32[64,128]{1,0:T(8,128)S(1)} %fusion.85), kind=kLoop, calls=%fused_computation.36 | loop fusion | flops 24576 | bytes 229376 | tf_op jit(solution)/shard_map/mul | solution.py:206
  (42 shorter events, 0.8 us)
Async XLA Ops:
  3.3 18.7 %all-to-all-start = ((f32[8,16,768]{2,1,0:T(8,128)}), f32[8,16,768]{2,1,0:T(8,128)S(1)}, u32[]{:S(2)}, u32[]{:S(2)}) async-start(f32[8,16,768]{2,1,0:T(8,128)} %bitcast.71), calls=%async_computation | async-start | bytes 786432 | tf_op jit(solution)/shard_map/all_to_all | solution.py:158
  9.4 10.3 %collective-permute-start.1 = (f32[6,4,4,1]{3,2,1,0:T(4,128)S(1)}, f32[6,4,4,1]{3,2,1,0:T(4,128)S(1)}, u32[]{:S(2)}, u32[]{:S(2)}) collective-permute-start(f32[6,4,4,1]{3,2,1,0:T(4,128)S(1)} %get-tuple-element.29), channel_id=1, source_target_pairs={{1,2},{2,1},{5,6},{6,5},{9,10},{10,9},{13,14},{14,13},{17,18},{18,... | collective-permute-start | bytes 1160 | tf_op jit(solution)/shard_map/ppermute | solution.py:24
  10.1 9.6 %collective-permute-start = (f32[6,4,4,1]{3,2,1,0:T(4,128)S(1)}, f32[6,4,4,1]{3,2,1,0:T(4,128)S(1)}, u32[]{:S(2)}, u32[]{:S(2)}) collective-permute-start(f32[6,4,4,1]{3,2,1,0:T(4,128)S(1)} %get-tuple-element.30), channel_id=1, source_target_pairs={{0,1},{1,0},{2,3},{3,2},{4,5},{5,4},{6,7},{7,6},{8,9},{9,8},{10,11... | collective-permute-start | bytes 1160 | tf_op jit(solution)/shard_map/ppermute | solution.py:22
  14.0 7.7 %collective-permute-start.2 = (f32[6,4,1,128]{3,2,1,0:T(1,128)S(1)}, f32[6,4,1,128]{3,2,1,0:T(1,128)S(1)}, u32[]{:S(2)}, u32[]{:S(2)}) collective-permute-start(f32[6,4,1,128]{3,2,1,0:T(1,128)S(1)} %broadcast_select_fusion.2), channel_id=1, source_target_pairs={{0,4},{4,0},{1,5},{5,1},{2,6},{6,2},{3,7},{7,3},{8,12},{12,8},{9,1... | collective-permute-start | bytes 36872 | tf_op jit(solution)/shard_map/ppermute | solution.py:22
  15.4 4.3 %collective-permute-start.3 = (f32[6,1,4,128]{3,2,1,0:T(4,128)S(1)}, f32[6,1,4,128]{3,2,1,0:T(4,128)S(1)}, u32[]{:S(2)}, u32[]{:S(2)}) collective-permute-start(f32[6,1,4,128]{3,2,1,0:T(4,128)S(1)} %get-tuple-element.27), channel_id=1, source_target_pairs={{0,8},{8,0},{16,24},{24,16},{1,9},{9,1},{17,25},{25,17},{2,10},{10... | collective-permute-start | bytes 36872 | tf_op jit(solution)/shard_map/ppermute | solution.py:22
  16.6 5.0 %collective-permute-start.4 = (f32[6,1,4,128]{3,2,1,0:T(4,128)S(1)}, f32[6,1,4,128]{3,2,1,0:T(4,128)S(1)}, u32[]{:S(2)}, u32[]{:S(2)}) collective-permute-start(f32[6,1,4,128]{3,2,1,0:T(4,128)S(1)} %get-tuple-element.28), channel_id=1, source_target_pairs={{8,16},{16,8},{9,17},{17,9},{10,18},{18,10},{11,19},{19,11},{12,20... | collective-permute-start | bytes 36872 | tf_op jit(solution)/shard_map/ppermute | solution.py:24
  26.6 19.4 %copy-start.2 = (f32[64,128]{1,0:T(8,128)S(1)}, f32[64,128]{1,0:T(8,128)}, u32[]{:S(2)}) copy-start(f32[64,128]{1,0:T(8,128)} %get-tuple-element.9) | copy-start | bytes 98308
  26.6 19.6 %copy-start.1 = (f32[3,64,128]{2,1,0:T(8,128)S(1)}, f32[3,64,128]{2,1,0:T(8,128)}, u32[]{:S(2)}) copy-start(f32[3,64,128]{2,1,0:T(8,128)} %get-tuple-element.8) | copy-start | bytes 294916
  26.9 6.0 %collective-permute-start.8 = (f32[5,4,4,1]{3,2,1,0:T(4,128)S(1)}, f32[5,4,4,1]{3,2,1,0:T(4,128)S(1)}, u32[]{:S(2)}, u32[]{:S(2)}) collective-permute-start(f32[5,4,4,1]{3,2,1,0:T(4,128)S(1)} %get-tuple-element.33), channel_id=1, source_target_pairs={{1,2},{2,1},{5,6},{6,5},{9,10},{10,9},{13,14},{14,13},{17,18},{18,... | collective-permute-start | bytes 968 | tf_op jit(solution)/shard_map/ppermute | solution.py:24
  27.6 5.4 %collective-permute-start.9 = (f32[5,4,4,1]{3,2,1,0:T(4,128)S(1)}, f32[5,4,4,1]{3,2,1,0:T(4,128)S(1)}, u32[]{:S(2)}, u32[]{:S(2)}) collective-permute-start(f32[5,4,4,1]{3,2,1,0:T(4,128)S(1)} %get-tuple-element.34), channel_id=1, source_target_pairs={{0,1},{1,0},{2,3},{3,2},{4,5},{5,4},{6,7},{7,6},{8,9},{9,8},{10,11... | collective-permute-start | bytes 968 | tf_op jit(solution)/shard_map/ppermute | solution.py:22
  28.9 4.2 %collective-permute-start.7 = (f32[5,4,1,128]{3,2,1,0:T(1,128)S(1)}, f32[5,4,1,128]{3,2,1,0:T(1,128)S(1)}, u32[]{:S(2)}, u32[]{:S(2)}) collective-permute-start(f32[5,4,1,128]{3,2,1,0:T(1,128)S(1)} %broadcast_select_fusion.9), channel_id=1, source_target_pairs={{0,4},{4,0},{1,5},{5,1},{2,6},{6,2},{3,7},{7,3},{8,12},{12,8},{9,1... | collective-permute-start | bytes 30728 | tf_op jit(solution)/shard_map/ppermute | solution.py:22
  28.9 4.2 %collective-permute-start.6 = (f32[5,1,4,128]{3,2,1,0:T(4,128)S(1)}, f32[5,1,4,128]{3,2,1,0:T(4,128)S(1)}, u32[]{:S(2)}, u32[]{:S(2)}) collective-permute-start(f32[5,1,4,128]{3,2,1,0:T(4,128)S(1)} %get-tuple-element.31), channel_id=1, source_target_pairs={{0,8},{8,0},{16,24},{24,16},{1,9},{9,1},{17,25},{25,17},{2,10},{10... | collective-permute-start | bytes 30728 | tf_op jit(solution)/shard_map/ppermute | solution.py:22
  28.9 5.5 %collective-permute-start.5 = (f32[5,1,4,128]{3,2,1,0:T(4,128)S(1)}, f32[5,1,4,128]{3,2,1,0:T(4,128)S(1)}, u32[]{:S(2)}, u32[]{:S(2)}) collective-permute-start(f32[5,1,4,128]{3,2,1,0:T(4,128)S(1)} %get-tuple-element.32), channel_id=1, source_target_pairs={{8,16},{16,8},{9,17},{17,9},{10,18},{18,10},{11,19},{19,11},{12,20... | collective-permute-start | bytes 30728 | tf_op jit(solution)/shard_map/ppermute | solution.py:24
  34.5 12.2 %copy-start = (f32[5,4,4,128]{3,2,1,0:T(4,128)}, f32[5,4,4,128]{3,2,1,0:T(4,128)S(1)}, u32[]{:S(2)}) copy-start(f32[5,4,4,128]{3,2,1,0:T(4,128)S(1)} %fusion.22) | copy-start | bytes 122884

commit v13 on v12

--- a/solution.py
+++ b/solution.py
@@ -116,6 +116,7 @@
         plan = lax.dot_general(
             eye, slot_hot, (((1,), (1,)), ((), ())), preferred_element_type=jnp.float32
         )
+        plan_half = plan.astype(jnp.bfloat16)
         live = lax.broadcasted_iota(jnp.int32, (tile_count, row_count), 1) < lengths_col
         for comp in range(3):
             load_ref[comp] = jnp.where(live, record_ref[5 + comp], 0.0)
@@ -126,9 +127,15 @@
                 rows = record_ref[comp]
             else:
                 rows = jnp.where(live, cell_ref[...], -1).astype(jnp.float32)
-            out_ref[:, comp * row_count:(comp + 1) * row_count] = jnp.dot(
-                plan, rows, precision=lax.Precision.HIGHEST, preferred_element_type=jnp.float32
-            )
+            high, rest = split_high(rows)
+            middle, low = split_high(rest)
+            total = None
+            for part in (high, middle, low):
+                term = jnp.dot(
+                    plan_half, part.astype(jnp.bfloat16), preferred_element_type=jnp.float32
+                )
+                total = term if total is None else total + term
+            out_ref[:, comp * row_count:(comp + 1) * row_count] = total
 
     def pack(routes, lengths, cell_ids, records):
         return pl.pallas_call(

time: 47.5 us -> 47.4 us (level)
  no operation moved by 1% of the time
where the time goes in v13:
time: 47.4 us; the launch traced here: 46.6 us
  starting transfers between devices  21.4 us (45%)
  blocking collectives  8.55 us (18%)
  matrix products  5.86 us (12%)
  other arithmetic  3.48 us (7%)
  waiting for transfers between devices  3.14 us (7%)
  Pallas kernels  2.47 us (5%)
  between operations  1.01 us (2%)
  local copies, waits for them, and re-layouts  0.68 us (1%)
    all_to_all x1, blocking collectives, shards(): lax.all_to_all(face_pressure.reshape(1, slot_total, row_count), ('stream'...  8.55 us
    ppermute x4, starting transfers between devices, face_halo(): from_b = lax.ppermute(jnp.where(odd, last, first), axis, pairs_b)  8.42 us
    ppermute x6, starting transfers between devices, face_halo(): from_a = lax.ppermute(jnp.where(odd, first, last), axis, pairs_a)  7.79 us
    all_to_all x1, starting transfers between devices, shards(): lax.all_to_all(outbound, ('stream', 'cross'), split_axis=0, concat_axis=0...  5.23 us
    dot_general x1, matrix products, shards(): jnp.einsum('cpf,fd->cpd', spread, depth_hot.astype(jnp.float32), precisio...  3.28 us
    ppermute x4, waiting for transfers between devices, face_halo(): from_b = lax.ppermute(jnp.where(odd, last, first), axis, pairs_b)  3.12 us
    pallas_call x1, Pallas kernels, pack(): pl.pallas_call(pack_kernel, out_shape=(jax.ShapeDtypeStruct((slot_total,...  2.47 us
    dot_general x1, matrix products, exact_dot(): jnp.einsum(left + ',k' + right + '->k' + output, onehot, stacked, preferr...  2.4 us
  transfers between devices with their start and end apart: 11, of which 2 were waited for; matrix products, arithmetic and copies ran while one was open for 3% of the time, Pallas kernels for 0%

profile of v13, /device:TPU:1, one launch (start us, length us, event | category | flops | bytes accessed | tf_op | source)
XLA Modules:
  0.0 46.6 jit_solution(13228303120142531639)
XLA Ops:
  0.6 2.5 %shard_map.86 = (f32[128,768]{1,0:T(8,128)}, f32[3,64,128]{2,1,0:T(8,128)}, f32[64,128]{1,0:T(8,128)}) custom-call(s32[1,64]{1,0:T(1,128)} %bitcast.91, s32[1,64]{1,0:T(1,128)} %bitcast.92, s32[64,128]{1,0:T(8,128)} %cell_ref.1, f32[8,64,128]{2,1,0:T(8,128)} %record_ref.1), custom_call_target="tpu_custom_call" | custom-call | tf_op jit(solution)/shard_map/pallas_call | solution.py:141
  3.1 5.2 %all-to-all-start = ((f32[8,16,768]{2,1,0:T(8,128)}), f32[8,16,768]{2,1,0:T(8,128)S(1)}, u32[]{:S(2)}, u32[]{:S(2)}) async-start(f32[8,16,768]{2,1,0:T(8,128)} %bitcast.71), calls=%async_computation | async-start | bytes 786432 | tf_op jit(solution)/shard_map/all_to_all | solution.py:165
  8.3 0.8 %pad_maximum_fusion.6 = f32[6,4,4,128]{3,2,1,0:T(4,128)S(1)} fusion(f32[1,4,4,128]{3,2,1,0:T(4,128)} %bitcast.89, f32[4,4,4,128]{3,2,1,0:T(4,128)} %param.8, f32[1,4,4,128]{3,2,1,0:T(4,128)} %bitcast.90), kind=kLoop, calls=%fused_computation.35 | loop fusion | flops 24576 | bytes 98304 | tf_op jit(solution)/shard_map/concatenate | solution.py:167
  9.2 0.7 %collective-permute-start.1 = (f32[6,4,4,1]{3,2,1,0:T(4,128)S(1)}, f32[6,4,4,1]{3,2,1,0:T(4,128)S(1)}, u32[]{:S(2)}, u32[]{:S(2)}) collective-permute-start(f32[6,4,4,1]{3,2,1,0:T(4,128)S(1)} %get-tuple-element.29), channel_id=1, source_target_pairs={{1,2},{2,1},{5,6},{6,5},{9,10},{10,9},{13,14},{14,13},{17,18},{18,... | collective-permute-start | bytes 1160 | tf_op jit(solution)/shard_map/ppermute | solution.py:24
  9.9 3.9 %collective-permute-start = (f32[6,4,4,1]{3,2,1,0:T(4,128)S(1)}, f32[6,4,4,1]{3,2,1,0:T(4,128)S(1)}, u32[]{:S(2)}, u32[]{:S(2)}) collective-permute-start(f32[6,4,4,1]{3,2,1,0:T(4,128)S(1)} %get-tuple-element.30), channel_id=1, source_target_pairs={{0,1},{1,0},{2,3},{3,2},{4,5},{5,4},{6,7},{7,6},{8,9},{9,8},{10,11... | collective-permute-start | bytes 1160 | tf_op jit(solution)/shard_map/ppermute | solution.py:22
  13.8 1.4 %collective-permute-start.2 = (f32[6,4,1,128]{3,2,1,0:T(1,128)S(1)}, f32[6,4,1,128]{3,2,1,0:T(1,128)S(1)}, u32[]{:S(2)}, u32[]{:S(2)}) collective-permute-start(f32[6,4,1,128]{3,2,1,0:T(1,128)S(1)} %broadcast_select_fusion.2), channel_id=1, source_target_pairs={{0,4},{4,0},{1,5},{5,1},{2,6},{6,2},{3,7},{7,3},{8,12},{12,8},{9,1... | collective-permute-start | bytes 36872 | tf_op jit(solution)/shard_map/ppermute | solution.py:22
  15.3 1.2 %collective-permute-start.3 = (f32[6,1,4,128]{3,2,1,0:T(4,128)S(1)}, f32[6,1,4,128]{3,2,1,0:T(4,128)S(1)}, u32[]{:S(2)}, u32[]{:S(2)}) collective-permute-start(f32[6,1,4,128]{3,2,1,0:T(4,128)S(1)} %get-tuple-element.27), channel_id=1, source_target_pairs={{0,8},{8,0},{16,24},{24,16},{1,9},{9,1},{17,25},{25,17},{2,10},{10... | collective-permute-start | bytes 36872 | tf_op jit(solution)/shard_map/ppermute | solution.py:22
  16.5 3.0 %collective-permute-start.4 = (f32[6,1,4,128]{3,2,1,0:T(4,128)S(1)}, f32[6,1,4,128]{3,2,1,0:T(4,128)S(1)}, u32[]{:S(2)}, u32[]{:S(2)}) collective-permute-start(f32[6,1,4,128]{3,2,1,0:T(4,128)S(1)} %get-tuple-element.28), channel_id=1, source_target_pairs={{8,16},{16,8},{9,17},{17,9},{10,18},{18,10},{11,19},{19,11},{12,20... | collective-permute-start | bytes 36872 | tf_op jit(solution)/shard_map/ppermute | solution.py:24
  19.6 1.9 %collective-permute-done.4 = f32[6,1,4,128]{3,2,1,0:T(4,128)S(1)} collective-permute-done((f32[6,1,4,128]{3,2,1,0:T(4,128)S(1)}, f32[6,1,4,128]{3,2,1,0:T(4,128)S(1)}, u32[]{:S(2)}, u32[]{:S(2)}) %collective-permute-start.4) | collective-permute-done | bytes 12320 | tf_op jit(solution)/shard_map/ppermute | solution.py:24
  21.9 0.1 iota_compare_fusion.2
  22.1 0.5 %stack.15 = f32[5,16384]{1,0:T(8,128)S(1)} concatenate(f32[1,16384]{1,0:T(1,128)S(1)} %bitcast.78, f32[1,16384]{1,0:T(1,128)S(1)} %bitcast.77, f32[1,16384]{1,0:T(1,128)S(1)} %bitcast.76, f32[1,16384]{1,0:T(1,128)S(1)} %bitcast.75, f32[1,16384]{1,0:T(1,128)S(1)} %bitcast.74), dimensions={0} | concatenate | bytes 655360 | tf_op jit(solution)/shard_map/stack | solution.py:180
  22.6 0.5 fusion.94
  23.1 3.3 %fusion.2 = f32[5,16,128]{2,1,0:T(8,128)S(1)} fusion(s32[16384]{0:T(1024)S(1)} %add_select_fusion, f32[5,16,16384]{2,1,0:T(8,128)S(1)} %fusion.94), kind=kOutput, calls=%fused_computation.3 | convolution fusion | flops 1008730112 | bytes 5349376 | tf_op jit(solution)/shard_map/cpf,fd->cpd/dot_general | solution.py:184
  26.4 0.2 fusion.42
  26.8 0.7 %collective-permute-start.8 = (f32[5,4,4,1]{3,2,1,0:T(4,128)S(1)}, f32[5,4,4,1]{3,2,1,0:T(4,128)S(1)}, u32[]{:S(2)}, u32[]{:S(2)}) collective-permute-start(f32[5,4,4,1]{3,2,1,0:T(4,128)S(1)} %get-tuple-element.33), channel_id=1, source_target_pairs={{1,2},{2,1},{5,6},{6,5},{9,10},{10,9},{13,14},{14,13},{17,18},{18,... | collective-permute-start | bytes 968 | tf_op jit(solution)/shard_map/ppermute | solution.py:24
  27.5 1.2 %collective-permute-start.9 = (f32[5,4,4,1]{3,2,1,0:T(4,128)S(1)}, f32[5,4,4,1]{3,2,1,0:T(4,128)S(1)}, u32[]{:S(2)}, u32[]{:S(2)}) collective-permute-start(f32[5,4,4,1]{3,2,1,0:T(4,128)S(1)} %get-tuple-element.34), channel_id=1, source_target_pairs={{0,1},{1,0},{2,3},{3,2},{4,5},{5,4},{6,7},{7,6},{8,9},{9,8},{10,11... | collective-permute-start | bytes 968 | tf_op jit(solution)/shard_map/ppermute | solution.py:22
  28.7 4.1 %collective-permute-start.5 = (f32[5,1,4,128]{3,2,1,0:T(4,128)S(1)}, f32[5,1,4,128]{3,2,1,0:T(4,128)S(1)}, u32[]{:S(2)}, u32[]{:S(2)}) collective-permute-start(f32[5,1,4,128]{3,2,1,0:T(4,128)S(1)} %get-tuple-element.32), channel_id=1, source_target_pairs={{8,16},{16,8},{9,17},{17,9},{10,18},{18,10},{11,19},{19,11},{12,20... | collective-permute-start | bytes 30728 | tf_op jit(solution)/shard_map/ppermute | solution.py:24
  32.9 1.2 %collective-permute-done.5 = f32[5,1,4,128]{3,2,1,0:T(4,128)S(1)} collective-permute-done((f32[5,1,4,128]{3,2,1,0:T(4,128)S(1)}, f32[5,1,4,128]{3,2,1,0:T(4,128)S(1)}, u32[]{:S(2)}, u32[]{:S(2)}) %collective-permute-start.5) | collective-permute-done | bytes 10272 | tf_op jit(solution)/shard_map/ppermute | solution.py:24
  34.2 0.2 fusion.22
  34.4 2.4 %convolution_bitcast_fusion = f32[3,16384,16]{1,2,0:T(8,128)S(1)} fusion(s32[16384]{0:T(1024)S(1)} %add_select_fusion, bf16[1,128,16]{1,2,0:T(8,128)(2,1)S(1)} %get-tuple-element.45, bf16[1,128,16]{1,2,0:T(8,128)(2,1)S(1)} %get-tuple-element.44, bf16[1,128,16]{1,2,0:T(8,128)(2,1)S(1)} %get-tuple-element.43), kind=kOutput, calls=%fused_computation | convolution fusion | flops 203436032 | bytes 3223552 | tf_op jit(solution)/shard_map/fd,kdp->kfp/dot_general | solution.py:84
  36.8 0.4 fusion.12
  37.2 8.5 %all_to_all.17 = f32[1,128,128]{2,0,1:T(1,128)S(1)} all-to-all(f32[1,128,128]{2,0,1:T(1,128)S(1)} %bitcast.72), channel_id=1, replica_groups=mesh['stream'=4,'cross'=2,'gore'=4] {'stream','cross'}, dimensions={1} | all-to-all | bytes 131072 | tf_op jit(solution)/shard_map/all_to_all | solution.py:203
  45.8 0.2 fusion.85
  46.0 0.7 %broadcast_multiply_fusion = f32[3,64,128]{2,1,0:T(8,128)} fusion(f32[3,64,128]{2,1,0:T(8,128)S(1)} %copy-done.1, f32[64,128]{1,0:T(8,128)S(1)} %fusion.85), kind=kLoop, calls=%fused_computation.36 | loop fusion | flops 24576 | bytes 229376 | tf_op jit(solution)/shard_map/mul | solution.py:213
  (42 shorter events, 0.8 us)
Async XLA Ops:
  3.1 18.7 %all-to-all-start = ((f32[8,16,768]{2,1,0:T(8,128)}), f32[8,16,768]{2,1,0:T(8,128)S(1)}, u32[]{:S(2)}, u32[]{:S(2)}) async-start(f32[8,16,768]{2,1,0:T(8,128)} %bitcast.71), calls=%async_computation | async-start | bytes 786432 | tf_op jit(solution)/shard_map/all_to_all | solution.py:165
  9.2 10.3 %collective-permute-start.1 = (f32[6,4,4,1]{3,2,1,0:T(4,128)S(1)}, f32[6,4,4,1]{3,2,1,0:T(4,128)S(1)}, u32[]{:S(2)}, u32[]{:S(2)}) collective-permute-start(f32[6,4,4,1]{3,2,1,0:T(4,128)S(1)} %get-tuple-element.29), channel_id=1, source_target_pairs={{1,2},{2,1},{5,6},{6,5},{9,10},{10,9},{13,14},{14,13},{17,18},{18,... | collective-permute-start | bytes 1160 | tf_op jit(solution)/shard_map/ppermute | solution.py:24
  9.9 9.6 %collective-permute-start = (f32[6,4,4,1]{3,2,1,0:T(4,128)S(1)}, f32[6,4,4,1]{3,2,1,0:T(4,128)S(1)}, u32[]{:S(2)}, u32[]{:S(2)}) collective-permute-start(f32[6,4,4,1]{3,2,1,0:T(4,128)S(1)} %get-tuple-element.30), channel_id=1, source_target_pairs={{0,1},{1,0},{2,3},{3,2},{4,5},{5,4},{6,7},{7,6},{8,9},{9,8},{10,11... | collective-permute-start | bytes 1160 | tf_op jit(solution)/shard_map/ppermute | solution.py:22
  13.8 7.7 %collective-permute-start.2 = (f32[6,4,1,128]{3,2,1,0:T(1,128)S(1)}, f32[6,4,1,128]{3,2,1,0:T(1,128)S(1)}, u32[]{:S(2)}, u32[]{:S(2)}) collective-permute-start(f32[6,4,1,128]{3,2,1,0:T(1,128)S(1)} %broadcast_select_fusion.2), channel_id=1, source_target_pairs={{0,4},{4,0},{1,5},{5,1},{2,6},{6,2},{3,7},{7,3},{8,12},{12,8},{9,1... | collective-permute-start | bytes 36872 | tf_op jit(solution)/shard_map/ppermute | solution.py:22
  15.3 4.3 %collective-permute-start.3 = (f32[6,1,4,128]{3,2,1,0:T(4,128)S(1)}, f32[6,1,4,128]{3,2,1,0:T(4,128)S(1)}, u32[]{:S(2)}, u32[]{:S(2)}) collective-permute-start(f32[6,1,4,128]{3,2,1,0:T(4,128)S(1)} %get-tuple-element.27), channel_id=1, source_target_pairs={{0,8},{8,0},{16,24},{24,16},{1,9},{9,1},{17,25},{25,17},{2,10},{10... | collective-permute-start | bytes 36872 | tf_op jit(solution)/shard_map/ppermute | solution.py:22
  16.5 5.0 %collective-permute-start.4 = (f32[6,1,4,128]{3,2,1,0:T(4,128)S(1)}, f32[6,1,4,128]{3,2,1,0:T(4,128)S(1)}, u32[]{:S(2)}, u32[]{:S(2)}) collective-permute-start(f32[6,1,4,128]{3,2,1,0:T(4,128)S(1)} %get-tuple-element.28), channel_id=1, source_target_pairs={{8,16},{16,8},{9,17},{17,9},{10,18},{18,10},{11,19},{19,11},{12,20... | collective-permute-start | bytes 36872 | tf_op jit(solution)/shard_map/ppermute | solution.py:24
  26.4 19.4 %copy-start.2 = (f32[64,128]{1,0:T(8,128)S(1)}, f32[64,128]{1,0:T(8,128)}, u32[]{:S(2)}) copy-start(f32[64,128]{1,0:T(8,128)} %get-tuple-element.9) | copy-start | bytes 98308
  26.4 19.6 %copy-start.1 = (f32[3,64,128]{2,1,0:T(8,128)S(1)}, f32[3,64,128]{2,1,0:T(8,128)}, u32[]{:S(2)}) copy-start(f32[3,64,128]{2,1,0:T(8,128)} %get-tuple-element.8) | copy-start | bytes 294916
  26.8 6.0 %collective-permute-start.8 = (f32[5,4,4,1]{3,2,1,0:T(4,128)S(1)}, f32[5,4,4,1]{3,2,1,0:T(4,128)S(1)}, u32[]{:S(2)}, u32[]{:S(2)}) collective-permute-start(f32[5,4,4,1]{3,2,1,0:T(4,128)S(1)} %get-tuple-element.33), channel_id=1, source_target_pairs={{1,2},{2,1},{5,6},{6,5},{9,10},{10,9},{13,14},{14,13},{17,18},{18,... | collective-permute-start | bytes 968 | tf_op jit(solution)/shard_map/ppermute | solution.py:24
  27.5 5.4 %collective-permute-start.9 = (f32[5,4,4,1]{3,2,1,0:T(4,128)S(1)}, f32[5,4,4,1]{3,2,1,0:T(4,128)S(1)}, u32[]{:S(2)}, u32[]{:S(2)}) collective-permute-start(f32[5,4,4,1]{3,2,1,0:T(4,128)S(1)} %get-tuple-element.34), channel_id=1, source_target_pairs={{0,1},{1,0},{2,3},{3,2},{4,5},{5,4},{6,7},{7,6},{8,9},{9,8},{10,11... | collective-permute-start | bytes 968 | tf_op jit(solution)/shard_map/ppermute | solution.py:22
  28.7 4.2 %collective-permute-start.7 = (f32[5,4,1,128]{3,2,1,0:T(1,128)S(1)}, f32[5,4,1,128]{3,2,1,0:T(1,128)S(1)}, u32[]{:S(2)}, u32[]{:S(2)}) collective-permute-start(f32[5,4,1,128]{3,2,1,0:T(1,128)S(1)} %broadcast_select_fusion.9), channel_id=1, source_target_pairs={{0,4},{4,0},{1,5},{5,1},{2,6},{6,2},{3,7},{7,3},{8,12},{12,8},{9,1... | collective-permute-start | bytes 30728 | tf_op jit(solution)/shard_map/ppermute | solution.py:22
  28.7 4.2 %collective-permute-start.6 = (f32[5,1,4,128]{3,2,1,0:T(4,128)S(1)}, f32[5,1,4,128]{3,2,1,0:T(4,128)S(1)}, u32[]{:S(2)}, u32[]{:S(2)}) collective-permute-start(f32[5,1,4,128]{3,2,1,0:T(4,128)S(1)} %get-tuple-element.31), channel_id=1, source_target_pairs={{0,8},{8,0},{16,24},{24,16},{1,9},{9,1},{17,25},{25,17},{2,10},{10... | collective-permute-start | bytes 30728 | tf_op jit(solution)/shard_map/ppermute | solution.py:22
  28.7 5.5 %collective-permute-start.5 = (f32[5,1,4,128]{3,2,1,0:T(4,128)S(1)}, f32[5,1,4,128]{3,2,1,0:T(4,128)S(1)}, u32[]{:S(2)}, u32[]{:S(2)}) collective-permute-start(f32[5,1,4,128]{3,2,1,0:T(4,128)S(1)} %get-tuple-element.32), channel_id=1, source_target_pairs={{8,16},{16,8},{9,17},{17,9},{10,18},{18,10},{11,19},{19,11},{12,20... | collective-permute-start | bytes 30728 | tf_op jit(solution)/shard_map/ppermute | solution.py:24
  34.4 12.2 %copy-start = (f32[5,4,4,128]{3,2,1,0:T(4,128)}, f32[5,4,4,128]{3,2,1,0:T(4,128)S(1)}, u32[]{:S(2)}) copy-start(f32[5,4,4,128]{3,2,1,0:T(4,128)S(1)} %fusion.22) | copy-start | bytes 122884

commit v14 on v13

--- a/solution.py
+++ b/solution.py
@@ -2,6 +2,7 @@
 import jax.numpy as jnp
 from jax import lax
 from jax.experimental import pallas as pl
+from jax.experimental.pallas import tpu as pltpu
 from jax.sharding import PartitionSpec as P
 
 
@@ -149,6 +150,55 @@
     return pack
 
 
+def make_source(slot_total, row_count, plane_count, vertical_cells):
+    group = 8
+    width = group * row_count
+    rows_out = 15 * plane_count
+
+    def source_kernel(arrived_ref, out_ref, left_ref, right_ref):
+        out_ref[...] = jnp.zeros_like(out_ref)
+        depth_iota = lax.broadcasted_iota(jnp.int32, (vertical_cells, row_count), 0).astype(jnp.float32)
+        plane_iota = lax.broadcasted_iota(jnp.int32, (plane_count, row_count), 0).astype(jnp.float32)
+
+        def body(step, carry):
+            block = arrived_ref[pl.ds(pl.multiple_of(step * group, group), group), :]
+            for g in range(group):
+                row = block[g:g + 1, :]
+                cell = row[:, 5 * row_count:6 * row_count]
+                plane = jnp.floor((cell + 0.5) / vertical_cells)
+                depth = cell - plane * vertical_cells
+                lanes = slice(g * row_count, (g + 1) * row_count)
+                right_ref[:, lanes] = (depth_iota == depth).astype(jnp.bfloat16)
+                hit = plane_iota == plane
+                for comp in range(5):
+                    spread = jnp.where(hit, row[:, comp * row_count:(comp + 1) * row_count], 0.0)
+                    high, rest = split_high(spread)
+                    middle, low = split_high(rest)
+                    for piece, part in enumerate((high, middle, low)):
+                        start = (piece * 5 + comp) * plane_count
+                        left_ref[start:start + plane_count, lanes] = part.astype(jnp.bfloat16)
+            out_ref[...] += lax.dot_general(
+                left_ref[...], right_ref[...], (((1,), (1,)), ((), ())),
+                preferred_element_type=jnp.float32,
+            )
+            return carry
+
+        lax.fori_loop(0, slot_total // group, body, 0)
+
+    def source(arrived):
+        total = pl.pallas_call(
+            source_kernel,
+            out_shape=jax.ShapeDtypeStruct((rows_out, vertical_cells), jnp.float32),
+            scratch_shapes=[
+                pltpu.VMEM((rows_out, width), jnp.bfloat16),
+                pltpu.VMEM((vertical_cells, width), jnp.bfloat16),
+            ],
+        )(arrived)
+        third = 5 * plane_count
+        return total[0:third] + total[third:2 * third] + total[2 * third:]
+    return source
+
+
 def shards(density, momentum_energy, viscosity, records, cell_ids, routes, lengths):
     fluid_state = jnp.concatenate([density[None], momentum_energy], 0)
     cells_x, cells_y, vertical_cells = density.shape
@@ -176,14 +226,7 @@
     depth_hot = (
         depth[:, None] == lax.broadcasted_iota(jnp.int32, (faces, vertical_cells), 1)
     )
-    plane_rows = plane[None, :] == lax.broadcasted_iota(jnp.int32, (plane_count, faces), 0)
-    arrived_values = jnp.stack(
-        [arrived[:, c * row_count:(c + 1) * row_count].reshape(faces) for c in range(5)], 0
-    )
-    spread = jnp.where(plane_rows[None], arrived_values[:, None, :], 0.0)
-    source = jnp.einsum(
-        "cpf,fd->cpd", spread, depth_hot.astype(jnp.float32), precision=lax.Precision.HIGH
-    )
+    source = make_source(slot_total, row_count, plane_count, vertical_cells)(arrived)
     source = source.reshape(5, cells_x, cells_y, vertical_cells)
 
     middle = shifted(state_pad, 1, 0, 0) + viscous(state_pad, visc_pad) + source

time: 47.4 us -> 54.1 us (1.14)
  Pallas kernels: 2.47 us -> 11.1 us
  matrix products: 5.86 us -> 2.58 us
  other arithmetic: 3.48 us -> 4.55 us
    pallas_call x0 -> x1, Pallas kernels: none -> 8.6 us  [source(): pl.pallas_call(source_kernel, out_shape=jax.ShapeDtypeStruct((rows_out, v...]
    dot_general x1 -> x0, matrix products: 3.28 us -> none  [shards(): jnp.einsum('cpf,fd->cpd', spread, depth_hot.astype(jnp.float32), precisio...]
    select_n x1, other arithmetic: 0.03 us -> 0.87 us  [shards(): depth = cells % vertical_cells]
    add x0 -> x1, other arithmetic: none -> 0.83 us  [source(): return total[0:third] + total[third:2 * third] + total[2 * third:]]
    unnamed x6 -> x8, local copies, waits for them, and re-layouts: 0.02 us -> 0.71 us
    another operation x1 -> x0, local copies, waits for them, and re-layouts: 0.55 us -> none  [shards(): jnp.stack([arrived[:, c * row_count:(c + 1) * row_count].reshape(faces) f...]
  transfers between devices with their start and end apart: 11 -> 11, of which waited for: 2 -> 2; matrix products, arithmetic and copies ran while one was open for 3% -> 2% of each run, Pallas kernels for 0% -> 0%
where the time goes in v14:
time: 54.1 us; the launch traced here: 53.2 us
  starting transfers between devices  21.5 us (40%)
  Pallas kernels  11.1 us (21%)
  blocking collectives  8.55 us (16%)
  other arithmetic  4.55 us (8%)
  waiting for transfers between devices  3.14 us (6%)
  matrix products  2.58 us (5%)
  between operations  0.97 us (2%)
  local copies, waits for them, and re-layouts  0.8 us (1%)
    pallas_call x1, Pallas kernels, source(): pl.pallas_call(source_kernel, out_shape=jax.ShapeDtypeStruct((rows_out, v...  8.6 us
    all_to_all x1, blocking collectives, shards(): lax.all_to_all(face_pressure.reshape(1, slot_total, row_count), ('stream'...  8.55 us
    ppermute x4, starting transfers between devices, face_halo(): from_b = lax.ppermute(jnp.where(odd, last, first), axis, pairs_b)  8.43 us
    ppermute x6, starting transfers between devices, face_halo(): from_a = lax.ppermute(jnp.where(odd, first, last), axis, pairs_a)  7.86 us
    all_to_all x1, starting transfers between devices, shards(): lax.all_to_all(outbound, ('stream', 'cross'), split_axis=0, concat_axis=0...  5.23 us
    ppermute x4, waiting for transfers between devices, face_halo(): from_b = lax.ppermute(jnp.where(odd, last, first), axis, pairs_b)  3.12 us
    pallas_call x1, Pallas kernels, pack(): pl.pallas_call(pack_kernel, out_shape=(jax.ShapeDtypeStruct((slot_total,...  2.48 us
    dot_general x1, matrix products, exact_dot(): jnp.einsum(left + ',k' + right + '->k' + output, onehot, stacked, preferr...  2.4 us
  transfers between devices with their start and end apart: 11, of which 2 were waited for; matrix products, arithmetic and copies ran while one was open for 2% of the time, Pallas kernels for 0%

profile of v14, /device:TPU:1, one launch (start us, length us, event | category | flops | bytes accessed | tf_op | source)
XLA Modules:
  0.0 53.2 jit_solution(3373734492938385261)
XLA Ops:
  0.6 2.5 %shard_map.86 = (f32[128,768]{1,0:T(8,128)}, f32[3,64,128]{2,1,0:T(8,128)}, f32[64,128]{1,0:T(8,128)}) custom-call(s32[1,64]{1,0:T(1,128)} %bitcast.76, s32[1,64]{1,0:T(1,128)} %bitcast.77, s32[64,128]{1,0:T(8,128)} %cell_ref.1, f32[8,64,128]{2,1,0:T(8,128)} %record_ref.1), custom_call_target="tpu_custom_call" | custom-call | tf_op jit(solution)/shard_map/pallas_call | solution.py:142
  3.1 5.2 %all-to-all-start = ((f32[8,16,768]{2,1,0:T(8,128)}), f32[8,16,768]{2,1,0:T(8,128)S(1)}, u32[]{:S(2)}, u32[]{:S(2)}) async-start(f32[8,16,768]{2,1,0:T(8,128)} %bitcast.61), calls=%async_computation | async-start | bytes 786432 | tf_op jit(solution)/shard_map/all_to_all | solution.py:215
  8.3 0.8 %pad_maximum_fusion.6 = f32[6,4,4,128]{3,2,1,0:T(4,128)S(1)} fusion(f32[1,4,4,128]{3,2,1,0:T(4,128)} %bitcast.74, f32[4,4,4,128]{3,2,1,0:T(4,128)} %param.8, f32[1,4,4,128]{3,2,1,0:T(4,128)} %bitcast.75), kind=kLoop, calls=%fused_computation.28 | loop fusion | flops 24576 | bytes 98304 | tf_op jit(solution)/shard_map/concatenate | solution.py:217
  9.2 1.4 %collective-permute-start.2 = (f32[6,4,1,128]{3,2,1,0:T(1,128)S(1)}, f32[6,4,1,128]{3,2,1,0:T(1,128)S(1)}, u32[]{:S(2)}, u32[]{:S(2)}) collective-permute-start(f32[6,4,1,128]{3,2,1,0:T(1,128)S(1)} %broadcast_select_fusion.2), channel_id=1, source_target_pairs={{0,4},{4,0},{1,5},{5,1},{2,6},{6,2},{3,7},{7,3},{8,12},{12,8},{9,1... | collective-permute-start | bytes 36872 | tf_op jit(solution)/shard_map/ppermute | solution.py:23
  10.7 0.7 %collective-permute-start.1 = (f32[6,4,4,1]{3,2,1,0:T(4,128)S(1)}, f32[6,4,4,1]{3,2,1,0:T(4,128)S(1)}, u32[]{:S(2)}, u32[]{:S(2)}) collective-permute-start(f32[6,4,4,1]{3,2,1,0:T(4,128)S(1)} %get-tuple-element.24), channel_id=1, source_target_pairs={{1,2},{2,1},{5,6},{6,5},{9,10},{10,9},{13,14},{14,13},{17,18},{18,... | collective-permute-start | bytes 1160 | tf_op jit(solution)/shard_map/ppermute | solution.py:25
  11.4 3.9 %collective-permute-start = (f32[6,4,4,1]{3,2,1,0:T(4,128)S(1)}, f32[6,4,4,1]{3,2,1,0:T(4,128)S(1)}, u32[]{:S(2)}, u32[]{:S(2)}) collective-permute-start(f32[6,4,4,1]{3,2,1,0:T(4,128)S(1)} %get-tuple-element.25), channel_id=1, source_target_pairs={{0,1},{1,0},{2,3},{3,2},{4,5},{5,4},{6,7},{7,6},{8,9},{9,8},{10,11... | collective-permute-start | bytes 1160 | tf_op jit(solution)/shard_map/ppermute | solution.py:23
  15.3 1.2 %collective-permute-start.3 = (f32[6,1,4,128]{3,2,1,0:T(4,128)S(1)}, f32[6,1,4,128]{3,2,1,0:T(4,128)S(1)}, u32[]{:S(2)}, u32[]{:S(2)}) collective-permute-start(f32[6,1,4,128]{3,2,1,0:T(4,128)S(1)} %get-tuple-element.22), channel_id=1, source_target_pairs={{0,8},{8,0},{16,24},{24,16},{1,9},{9,1},{17,25},{25,17},{2,10},{10... | collective-permute-start | bytes 36872 | tf_op jit(solution)/shard_map/ppermute | solution.py:23
  16.5 3.0 %collective-permute-start.4 = (f32[6,1,4,128]{3,2,1,0:T(4,128)S(1)}, f32[6,1,4,128]{3,2,1,0:T(4,128)S(1)}, u32[]{:S(2)}, u32[]{:S(2)}) collective-permute-start(f32[6,1,4,128]{3,2,1,0:T(4,128)S(1)} %get-tuple-element.23), channel_id=1, source_target_pairs={{8,16},{16,8},{9,17},{17,9},{10,18},{18,10},{11,19},{19,11},{12,20... | collective-permute-start | bytes 36872 | tf_op jit(solution)/shard_map/ppermute | solution.py:25
  19.6 1.9 %collective-permute-done.4 = f32[6,1,4,128]{3,2,1,0:T(4,128)S(1)} collective-permute-done((f32[6,1,4,128]{3,2,1,0:T(4,128)S(1)}, f32[6,1,4,128]{3,2,1,0:T(4,128)S(1)}, u32[]{:S(2)}, u32[]{:S(2)}) %collective-permute-start.4) | collective-permute-done | bytes 12320 | tf_op jit(solution)/shard_map/ppermute | solution.py:25
  21.9 0.7 %copy-done = f32[8,16,768]{2,1,0:T(8,128)} copy-done((f32[8,16,768]{2,1,0:T(8,128)}, f32[8,16,768]{2,1,0:T(8,128)S(1)}, u32[]{:S(2)}) %copy-start) | copy-done | bytes 393240
  22.6 8.6 %shard_map.87 = f32[240,128]{1,0:T(8,128)} custom-call(f32[128,768]{1,0:T(8,128)} %bitcast.59), custom_call_target="tpu_custom_call" | custom-call | tf_op jit(solution)/shard_map/pallas_call | solution.py:189
  31.2 0.8 %slice_add_fusion.2 = f32[80,128]{1,0:T(8,128)S(1)} fusion(f32[240,128]{1,0:T(8,128)} %shard_map.87), kind=kLoop, calls=%fused_computation.72 | loop fusion | flops 20480 | bytes 163840 | tf_op jit(solution)/shard_map/add | solution.py:198
  32.0 0.2 fusion.35
  32.4 0.9 %add_select_fusion = s32[16384]{0:T(1024)S(1)} fusion(pred[16384]{0:T(1024)(128)(4,1)S(1)} %get-tuple-element.11, f32[128,768]{1,0:T(8,128)} %bitcast.60), kind=kLoop, calls=%fused_computation.10 | loop fusion | flops 196608 | bytes 147456 | tf_op jit(solution)/shard_map/jit(remainder)/select_n | solution.py:225
  33.2 0.7 %collective-permute-start.8 = (f32[5,4,4,1]{3,2,1,0:T(4,128)S(1)}, f32[5,4,4,1]{3,2,1,0:T(4,128)S(1)}, u32[]{:S(2)}, u32[]{:S(2)}) collective-permute-start(f32[5,4,4,1]{3,2,1,0:T(4,128)S(1)} %get-tuple-element.28), channel_id=1, source_target_pairs={{1,2},{2,1},{5,6},{6,5},{9,10},{10,9},{13,14},{14,13},{17,18},{18,... | collective-permute-start | bytes 968 | tf_op jit(solution)/shard_map/ppermute | solution.py:25
  33.9 1.3 %collective-permute-start.9 = (f32[5,4,4,1]{3,2,1,0:T(4,128)S(1)}, f32[5,4,4,1]{3,2,1,0:T(4,128)S(1)}, u32[]{:S(2)}, u32[]{:S(2)}) collective-permute-start(f32[5,4,4,1]{3,2,1,0:T(4,128)S(1)} %get-tuple-element.29), channel_id=1, source_target_pairs={{0,1},{1,0},{2,3},{3,2},{4,5},{5,4},{6,7},{7,6},{8,9},{9,8},{10,11... | collective-permute-start | bytes 968 | tf_op jit(solution)/shard_map/ppermute | solution.py:23
  35.2 4.1 %collective-permute-start.5 = (f32[5,1,4,128]{3,2,1,0:T(4,128)S(1)}, f32[5,1,4,128]{3,2,1,0:T(4,128)S(1)}, u32[]{:S(2)}, u32[]{:S(2)}) collective-permute-start(f32[5,1,4,128]{3,2,1,0:T(4,128)S(1)} %get-tuple-element.27), channel_id=1, source_target_pairs={{8,16},{16,8},{9,17},{17,9},{10,18},{18,10},{11,19},{19,11},{12,20... | collective-permute-start | bytes 30728 | tf_op jit(solution)/shard_map/ppermute | solution.py:25
  39.5 1.2 %collective-permute-done.5 = f32[5,1,4,128]{3,2,1,0:T(4,128)S(1)} collective-permute-done((f32[5,1,4,128]{3,2,1,0:T(4,128)S(1)}, f32[5,1,4,128]{3,2,1,0:T(4,128)S(1)}, u32[]{:S(2)}, u32[]{:S(2)}) %collective-permute-start.5) | collective-permute-done | bytes 10272 | tf_op jit(solution)/shard_map/ppermute | solution.py:25
  40.7 0.2 fusion.15
  41.0 2.4 %convolution_bitcast_fusion = f32[3,16384,16]{1,2,0:T(8,128)S(1)} fusion(s32[16384]{0:T(1024)S(1)} %add_select_fusion, bf16[1,128,16]{1,2,0:T(8,128)(2,1)S(1)} %get-tuple-element.40, bf16[1,128,16]{1,2,0:T(8,128)(2,1)S(1)} %get-tuple-element.39, bf16[1,128,16]{1,2,0:T(8,128)(2,1)S(1)} %get-tuple-element.38), kind=kOutput, calls=%fused_computation | convolution fusion | flops 203436032 | bytes 3223552 | tf_op jit(solution)/shard_map/fd,kdp->kfp/dot_general | solution.py:85
  43.4 0.4 fusion.5
  43.8 8.5 %all_to_all.16 = f32[1,128,128]{2,0,1:T(1,128)S(1)} all-to-all(f32[1,128,128]{2,0,1:T(1,128)S(1)} %bitcast.62), channel_id=1, replica_groups=mesh['stream'=4,'cross'=2,'gore'=4] {'stream','cross'}, dimensions={1} | all-to-all | bytes 131072 | tf_op jit(solution)/shard_map/all_to_all | solution.py:246
  52.3 0.2 fusion.76
  52.5 0.7 %broadcast_multiply_fusion = f32[3,64,128]{2,1,0:T(8,128)} fusion(f32[3,64,128]{2,1,0:T(8,128)S(1)} %copy-done.2, f32[64,128]{1,0:T(8,128)S(1)} %fusion.76), kind=kLoop, calls=%fused_computation.29 | loop fusion | flops 24576 | bytes 229376 | tf_op jit(solution)/shard_map/mul | solution.py:256
  (41 shorter events, 0.7 us)
Async XLA Ops:
  3.1 18.7 %all-to-all-start = ((f32[8,16,768]{2,1,0:T(8,128)}), f32[8,16,768]{2,1,0:T(8,128)S(1)}, u32[]{:S(2)}, u32[]{:S(2)}) async-start(f32[8,16,768]{2,1,0:T(8,128)} %bitcast.61), calls=%async_computation | async-start | bytes 786432 | tf_op jit(solution)/shard_map/all_to_all | solution.py:215
  9.2 12.3 %collective-permute-start.2 = (f32[6,4,1,128]{3,2,1,0:T(1,128)S(1)}, f32[6,4,1,128]{3,2,1,0:T(1,128)S(1)}, u32[]{:S(2)}, u32[]{:S(2)}) collective-permute-start(f32[6,4,1,128]{3,2,1,0:T(1,128)S(1)} %broadcast_select_fusion.2), channel_id=1, source_target_pairs={{0,4},{4,0},{1,5},{5,1},{2,6},{6,2},{3,7},{7,3},{8,12},{12,8},{9,1... | collective-permute-start | bytes 36872 | tf_op jit(solution)/shard_map/ppermute | solution.py:23
  10.7 8.8 %collective-permute-start.1 = (f32[6,4,4,1]{3,2,1,0:T(4,128)S(1)}, f32[6,4,4,1]{3,2,1,0:T(4,128)S(1)}, u32[]{:S(2)}, u32[]{:S(2)}) collective-permute-start(f32[6,4,4,1]{3,2,1,0:T(4,128)S(1)} %get-tuple-element.24), channel_id=1, source_target_pairs={{1,2},{2,1},{5,6},{6,5},{9,10},{10,9},{13,14},{14,13},{17,18},{18,... | collective-permute-start | bytes 1160 | tf_op jit(solution)/shard_map/ppermute | solution.py:25
  11.4 8.1 %collective-permute-start = (f32[6,4,4,1]{3,2,1,0:T(4,128)S(1)}, f32[6,4,4,1]{3,2,1,0:T(4,128)S(1)}, u32[]{:S(2)}, u32[]{:S(2)}) collective-permute-start(f32[6,4,4,1]{3,2,1,0:T(4,128)S(1)} %get-tuple-element.25), channel_id=1, source_target_pairs={{0,1},{1,0},{2,3},{3,2},{4,5},{5,4},{6,7},{7,6},{8,9},{9,8},{10,11... | collective-permute-start | bytes 1160 | tf_op jit(solution)/shard_map/ppermute | solution.py:23
  15.3 4.3 %collective-permute-start.3 = (f32[6,1,4,128]{3,2,1,0:T(4,128)S(1)}, f32[6,1,4,128]{3,2,1,0:T(4,128)S(1)}, u32[]{:S(2)}, u32[]{:S(2)}) collective-permute-start(f32[6,1,4,128]{3,2,1,0:T(4,128)S(1)} %get-tuple-element.22), channel_id=1, source_target_pairs={{0,8},{8,0},{16,24},{24,16},{1,9},{9,1},{17,25},{25,17},{2,10},{10... | collective-permute-start | bytes 36872 | tf_op jit(solution)/shard_map/ppermute | solution.py:23
  16.5 5.0 %collective-permute-start.4 = (f32[6,1,4,128]{3,2,1,0:T(4,128)S(1)}, f32[6,1,4,128]{3,2,1,0:T(4,128)S(1)}, u32[]{:S(2)}, u32[]{:S(2)}) collective-permute-start(f32[6,1,4,128]{3,2,1,0:T(4,128)S(1)} %get-tuple-element.23), channel_id=1, source_target_pairs={{8,16},{16,8},{9,17},{17,9},{10,18},{18,10},{11,19},{19,11},{12,20... | collective-permute-start | bytes 36872 | tf_op jit(solution)/shard_map/ppermute | solution.py:25
  21.8 0.8 %copy-start = (f32[8,16,768]{2,1,0:T(8,128)}, f32[8,16,768]{2,1,0:T(8,128)S(1)}, u32[]{:S(2)}) copy-start(f32[8,16,768]{2,1,0:T(8,128)S(1)} %all-to-all-done) | copy-start | bytes 1179652
  33.2 6.1 %collective-permute-start.8 = (f32[5,4,4,1]{3,2,1,0:T(4,128)S(1)}, f32[5,4,4,1]{3,2,1,0:T(4,128)S(1)}, u32[]{:S(2)}, u32[]{:S(2)}) collective-permute-start(f32[5,4,4,1]{3,2,1,0:T(4,128)S(1)} %get-tuple-element.28), channel_id=1, source_target_pairs={{1,2},{2,1},{5,6},{6,5},{9,10},{10,9},{13,14},{14,13},{17,18},{18,... | collective-permute-start | bytes 968 | tf_op jit(solution)/shard_map/ppermute | solution.py:25
  33.9 5.4 %collective-permute-start.9 = (f32[5,4,4,1]{3,2,1,0:T(4,128)S(1)}, f32[5,4,4,1]{3,2,1,0:T(4,128)S(1)}, u32[]{:S(2)}, u32[]{:S(2)}) collective-permute-start(f32[5,4,4,1]{3,2,1,0:T(4,128)S(1)} %get-tuple-element.29), channel_id=1, source_target_pairs={{0,1},{1,0},{2,3},{3,2},{4,5},{5,4},{6,7},{7,6},{8,9},{9,8},{10,11... | collective-permute-start | bytes 968 | tf_op jit(solution)/shard_map/ppermute | solution.py:23
  35.2 4.2 %collective-permute-start.7 = (f32[5,4,1,128]{3,2,1,0:T(1,128)S(1)}, f32[5,4,1,128]{3,2,1,0:T(1,128)S(1)}, u32[]{:S(2)}, u32[]{:S(2)}) collective-permute-start(f32[5,4,1,128]{3,2,1,0:T(1,128)S(1)} %broadcast_select_fusion.9), channel_id=1, source_target_pairs={{0,4},{4,0},{1,5},{5,1},{2,6},{6,2},{3,7},{7,3},{8,12},{12,8},{9,1... | collective-permute-start | bytes 30728 | tf_op jit(solution)/shard_map/ppermute | solution.py:23
  35.2 4.2 %collective-permute-start.6 = (f32[5,1,4,128]{3,2,1,0:T(4,128)S(1)}, f32[5,1,4,128]{3,2,1,0:T(4,128)S(1)}, u32[]{:S(2)}, u32[]{:S(2)}) collective-permute-start(f32[5,1,4,128]{3,2,1,0:T(4,128)S(1)} %get-tuple-element.26), channel_id=1, source_target_pairs={{0,8},{8,0},{16,24},{24,16},{1,9},{9,1},{17,25},{25,17},{2,10},{10... | collective-permute-start | bytes 30728 | tf_op jit(solution)/shard_map/ppermute | solution.py:23
  35.2 5.5 %collective-permute-start.5 = (f32[5,1,4,128]{3,2,1,0:T(4,128)S(1)}, f32[5,1,4,128]{3,2,1,0:T(4,128)S(1)}, u32[]{:S(2)}, u32[]{:S(2)}) collective-permute-start(f32[5,1,4,128]{3,2,1,0:T(4,128)S(1)} %get-tuple-element.27), channel_id=1, source_target_pairs={{8,16},{16,8},{9,17},{17,9},{10,18},{18,10},{11,19},{19,11},{12,20... | collective-permute-start | bytes 30728 | tf_op jit(solution)/shard_map/ppermute | solution.py:25
  40.9 2.9 %copy-start.1 = (f32[5,4,4,128]{3,2,1,0:T(4,128)}, f32[5,4,4,128]{3,2,1,0:T(4,128)S(1)}, u32[]{:S(2)}) copy-start(f32[5,4,4,128]{3,2,1,0:T(4,128)S(1)} %fusion.15) | copy-start | bytes 122884
  41.0 11.4 %copy-start.3 = (f32[64,128]{1,0:T(8,128)S(1)}, f32[64,128]{1,0:T(8,128)}, u32[]{:S(2)}) copy-start(f32[64,128]{1,0:T(8,128)} %get-tuple-element.9) | copy-start | bytes 98308
  41.0 11.6 %copy-start.2 = (f32[3,64,128]{2,1,0:T(8,128)S(1)}, f32[3,64,128]{2,1,0:T(8,128)}, u32[]{:S(2)}) copy-start(f32[3,64,128]{2,1,0:T(8,128)} %get-tuple-element.8) | copy-start | bytes 294916

commit v15 on v13

--- a/solution.py
+++ b/solution.py
@@ -65,14 +65,9 @@
     return (high, values - high)
 
 
-def three_bf16(values):
-    first, rest = split_high(values)
-    second, third = split_high(rest)
-    return tuple(part.astype(jnp.bfloat16) for part in (first, second, third))
-
-
 def exact_dot(spec, values, onehot, values_first):
-    stacked = jnp.stack(three_bf16(values), 0)
+    high, rest = split_high(values)
+    stacked = jnp.stack([high.astype(jnp.bfloat16), rest.astype(jnp.bfloat16)], 0)
     left, right = spec.split("->")[0].split(",")
     output = spec.split("->")[1]
     if values_first:
@@ -85,7 +80,7 @@
             left + ",k" + right + "->k" + output, onehot, stacked,
             preferred_element_type=jnp.float32,
         )
-    return terms[0] + terms[1] + terms[2]
+    return terms[0] + terms[1]
 
 
 def make_pack(tile_count, row_count, blocks, capacity):

time: 47.4 us -> 47.3 us (level)
  no operation moved by 1% of the time
where the time goes in v15:
time: 47.3 us; the launch traced here: 46.5 us
  starting transfers between devices  21.4 us (45%)
  blocking collectives  8.55 us (18%)
  matrix products  5.85 us (12%)
  other arithmetic  3.4 us (7%)
  waiting for transfers between devices  3.14 us (7%)
  Pallas kernels  2.47 us (5%)
  between operations  1 us (2%)
  local copies, waits for them, and re-layouts  0.68 us (1%)
    all_to_all x1, blocking collectives, shards(): lax.all_to_all(face_pressure.reshape(1, slot_total, row_count), ('stream'...  8.55 us
    ppermute x4, starting transfers between devices, face_halo(): from_b = lax.ppermute(jnp.where(odd, last, first), axis, pairs_b)  8.42 us
    ppermute x6, starting transfers between devices, face_halo(): from_a = lax.ppermute(jnp.where(odd, first, last), axis, pairs_a)  7.79 us
    all_to_all x1, starting transfers between devices, shards(): lax.all_to_all(outbound, ('stream', 'cross'), split_axis=0, concat_axis=0...  5.23 us
    dot_general x1, matrix products, shards(): jnp.einsum('cpf,fd->cpd', spread, depth_hot.astype(jnp.float32), precisio...  3.29 us
    ppermute x4, waiting for transfers between devices, face_halo(): from_b = lax.ppermute(jnp.where(odd, last, first), axis, pairs_b)  3.12 us
    pallas_call x1, Pallas kernels, pack(): pl.pallas_call(pack_kernel, out_shape=(jax.ShapeDtypeStruct((slot_total,...  2.47 us
    dot_general x1, matrix products, exact_dot(): jnp.einsum(left + ',k' + right + '->k' + output, onehot, stacked, preferr...  2.38 us
  transfers between devices with their start and end apart: 11, of which 2 were waited for; matrix products, arithmetic and copies ran while one was open for 3% of the time, Pallas kernels for 0%

profile of v15, /device:TPU:1, one launch (start us, length us, event | category | flops | bytes accessed | tf_op | source)
XLA Modules:
  0.0 46.5 jit_solution(549063802467054998)
XLA Ops:
  0.6 2.5 %shard_map.86 = (f32[128,768]{1,0:T(8,128)}, f32[3,64,128]{2,1,0:T(8,128)}, f32[64,128]{1,0:T(8,128)}) custom-call(s32[1,64]{1,0:T(1,128)} %bitcast.89, s32[1,64]{1,0:T(1,128)} %bitcast.90, s32[64,128]{1,0:T(8,128)} %cell_ref.1, f32[8,64,128]{2,1,0:T(8,128)} %record_ref.1), custom_call_target="tpu_custom_call" | custom-call | tf_op jit(solution)/shard_map/pallas_call | solution.py:136
  3.1 5.2 %all-to-all-start = ((f32[8,16,768]{2,1,0:T(8,128)}), f32[8,16,768]{2,1,0:T(8,128)S(1)}, u32[]{:S(2)}, u32[]{:S(2)}) async-start(f32[8,16,768]{2,1,0:T(8,128)} %bitcast.69), calls=%async_computation | async-start | bytes 786432 | tf_op jit(solution)/shard_map/all_to_all | solution.py:160
  8.3 0.8 %pad_maximum_fusion.6 = f32[6,4,4,128]{3,2,1,0:T(4,128)S(1)} fusion(f32[1,4,4,128]{3,2,1,0:T(4,128)} %bitcast.87, f32[4,4,4,128]{3,2,1,0:T(4,128)} %param.8, f32[1,4,4,128]{3,2,1,0:T(4,128)} %bitcast.88), kind=kLoop, calls=%fused_computation.34 | loop fusion | flops 24576 | bytes 98304 | tf_op jit(solution)/shard_map/concatenate | solution.py:162
  9.2 0.7 %collective-permute-start.1 = (f32[6,4,4,1]{3,2,1,0:T(4,128)S(1)}, f32[6,4,4,1]{3,2,1,0:T(4,128)S(1)}, u32[]{:S(2)}, u32[]{:S(2)}) collective-permute-start(f32[6,4,4,1]{3,2,1,0:T(4,128)S(1)} %get-tuple-element.29), channel_id=1, source_target_pairs={{1,2},{2,1},{5,6},{6,5},{9,10},{10,9},{13,14},{14,13},{17,18},{18,... | collective-permute-start | bytes 1160 | tf_op jit(solution)/shard_map/ppermute | solution.py:24
  9.9 3.9 %collective-permute-start = (f32[6,4,4,1]{3,2,1,0:T(4,128)S(1)}, f32[6,4,4,1]{3,2,1,0:T(4,128)S(1)}, u32[]{:S(2)}, u32[]{:S(2)}) collective-permute-start(f32[6,4,4,1]{3,2,1,0:T(4,128)S(1)} %get-tuple-element.30), channel_id=1, source_target_pairs={{0,1},{1,0},{2,3},{3,2},{4,5},{5,4},{6,7},{7,6},{8,9},{9,8},{10,11... | collective-permute-start | bytes 1160 | tf_op jit(solution)/shard_map/ppermute | solution.py:22
  13.8 1.4 %collective-permute-start.2 = (f32[6,4,1,128]{3,2,1,0:T(1,128)S(1)}, f32[6,4,1,128]{3,2,1,0:T(1,128)S(1)}, u32[]{:S(2)}, u32[]{:S(2)}) collective-permute-start(f32[6,4,1,128]{3,2,1,0:T(1,128)S(1)} %broadcast_select_fusion.2), channel_id=1, source_target_pairs={{0,4},{4,0},{1,5},{5,1},{2,6},{6,2},{3,7},{7,3},{8,12},{12,8},{9,1... | collective-permute-start | bytes 36872 | tf_op jit(solution)/shard_map/ppermute | solution.py:22
  15.3 1.2 %collective-permute-start.3 = (f32[6,1,4,128]{3,2,1,0:T(4,128)S(1)}, f32[6,1,4,128]{3,2,1,0:T(4,128)S(1)}, u32[]{:S(2)}, u32[]{:S(2)}) collective-permute-start(f32[6,1,4,128]{3,2,1,0:T(4,128)S(1)} %get-tuple-element.27), channel_id=1, source_target_pairs={{0,8},{8,0},{16,24},{24,16},{1,9},{9,1},{17,25},{25,17},{2,10},{10... | collective-permute-start | bytes 36872 | tf_op jit(solution)/shard_map/ppermute | solution.py:22
  16.5 3.0 %collective-permute-start.4 = (f32[6,1,4,128]{3,2,1,0:T(4,128)S(1)}, f32[6,1,4,128]{3,2,1,0:T(4,128)S(1)}, u32[]{:S(2)}, u32[]{:S(2)}) collective-permute-start(f32[6,1,4,128]{3,2,1,0:T(4,128)S(1)} %get-tuple-element.28), channel_id=1, source_target_pairs={{8,16},{16,8},{9,17},{17,9},{10,18},{18,10},{11,19},{19,11},{12,20... | collective-permute-start | bytes 36872 | tf_op jit(solution)/shard_map/ppermute | solution.py:24
  19.6 1.9 %collective-permute-done.4 = f32[6,1,4,128]{3,2,1,0:T(4,128)S(1)} collective-permute-done((f32[6,1,4,128]{3,2,1,0:T(4,128)S(1)}, f32[6,1,4,128]{3,2,1,0:T(4,128)S(1)}, u32[]{:S(2)}, u32[]{:S(2)}) %collective-permute-start.4) | collective-permute-done | bytes 12320 | tf_op jit(solution)/shard_map/ppermute | solution.py:24
  21.9 0.1 iota_compare_fusion.2
  22.1 0.5 %stack.12 = f32[5,16384]{1,0:T(8,128)S(1)} concatenate(f32[1,16384]{1,0:T(1,128)S(1)} %bitcast.76, f32[1,16384]{1,0:T(1,128)S(1)} %bitcast.75, f32[1,16384]{1,0:T(1,128)S(1)} %bitcast.74, f32[1,16384]{1,0:T(1,128)S(1)} %bitcast.73, f32[1,16384]{1,0:T(1,128)S(1)} %bitcast.72), dimensions={0} | concatenate | bytes 655360 | tf_op jit(solution)/shard_map/stack | solution.py:175
  22.6 0.5 fusion.89
  23.1 3.3 %fusion.2 = f32[5,16,128]{2,1,0:T(8,128)S(1)} fusion(s32[16384]{0:T(1024)S(1)} %add_select_fusion, f32[5,16,16384]{2,1,0:T(8,128)S(1)} %fusion.89), kind=kOutput, calls=%fused_computation.3 | convolution fusion | flops 1008730112 | bytes 5349376 | tf_op jit(solution)/shard_map/cpf,fd->cpd/dot_general | solution.py:179
  26.4 0.2 fusion.42
  26.8 0.7 %collective-permute-start.8 = (f32[5,4,4,1]{3,2,1,0:T(4,128)S(1)}, f32[5,4,4,1]{3,2,1,0:T(4,128)S(1)}, u32[]{:S(2)}, u32[]{:S(2)}) collective-permute-start(f32[5,4,4,1]{3,2,1,0:T(4,128)S(1)} %get-tuple-element.33), channel_id=1, source_target_pairs={{1,2},{2,1},{5,6},{6,5},{9,10},{10,9},{13,14},{14,13},{17,18},{18,... | collective-permute-start | bytes 968 | tf_op jit(solution)/shard_map/ppermute | solution.py:24
  27.5 1.2 %collective-permute-start.9 = (f32[5,4,4,1]{3,2,1,0:T(4,128)S(1)}, f32[5,4,4,1]{3,2,1,0:T(4,128)S(1)}, u32[]{:S(2)}, u32[]{:S(2)}) collective-permute-start(f32[5,4,4,1]{3,2,1,0:T(4,128)S(1)} %get-tuple-element.34), channel_id=1, source_target_pairs={{0,1},{1,0},{2,3},{3,2},{4,5},{5,4},{6,7},{7,6},{8,9},{9,8},{10,11... | collective-permute-start | bytes 968 | tf_op jit(solution)/shard_map/ppermute | solution.py:22
  28.7 4.1 %collective-permute-start.5 = (f32[5,1,4,128]{3,2,1,0:T(4,128)S(1)}, f32[5,1,4,128]{3,2,1,0:T(4,128)S(1)}, u32[]{:S(2)}, u32[]{:S(2)}) collective-permute-start(f32[5,1,4,128]{3,2,1,0:T(4,128)S(1)} %get-tuple-element.32), channel_id=1, source_target_pairs={{8,16},{16,8},{9,17},{17,9},{10,18},{18,10},{11,19},{19,11},{12,20... | collective-permute-start | bytes 30728 | tf_op jit(solution)/shard_map/ppermute | solution.py:24
  32.9 1.2 %collective-permute-done.5 = f32[5,1,4,128]{3,2,1,0:T(4,128)S(1)} collective-permute-done((f32[5,1,4,128]{3,2,1,0:T(4,128)S(1)}, f32[5,1,4,128]{3,2,1,0:T(4,128)S(1)}, u32[]{:S(2)}, u32[]{:S(2)}) %collective-permute-start.5) | collective-permute-done | bytes 10272 | tf_op jit(solution)/shard_map/ppermute | solution.py:24
  34.2 0.2 fusion.22
  34.4 2.4 %convolution_bitcast_fusion = f32[2,16384,16]{1,2,0:T(8,128)S(1)} fusion(s32[16384]{0:T(1024)S(1)} %add_select_fusion, bf16[1,128,16]{1,2,0:T(8,128)(2,1)S(1)} %get-tuple-element.44, bf16[1,128,16]{1,2,0:T(8,128)(2,1)S(1)} %get-tuple-element.43), kind=kOutput, calls=%fused_computation | convolution fusion | flops 136318976 | bytes 2170880 | tf_op jit(solution)/shard_map/fd,kdp->kfp/dot_general | solution.py:79
  36.8 0.3 fusion.12
  37.1 8.6 %all_to_all.17 = f32[1,128,128]{2,0,1:T(1,128)S(1)} all-to-all(f32[1,128,128]{2,0,1:T(1,128)S(1)} %bitcast.70), channel_id=1, replica_groups=mesh['stream'=4,'cross'=2,'gore'=4] {'stream','cross'}, dimensions={1} | all-to-all | bytes 131072 | tf_op jit(solution)/shard_map/all_to_all | solution.py:198
  45.7 0.2 fusion.80
  45.9 0.7 %broadcast_multiply_fusion = f32[3,64,128]{2,1,0:T(8,128)} fusion(f32[3,64,128]{2,1,0:T(8,128)S(1)} %copy-done.1, f32[64,128]{1,0:T(8,128)S(1)} %fusion.80), kind=kLoop, calls=%fused_computation.35 | loop fusion | flops 24576 | bytes 229376 | tf_op jit(solution)/shard_map/mul | solution.py:208
  (42 shorter events, 0.8 us)
Async XLA Ops:
  3.1 18.7 %all-to-all-start = ((f32[8,16,768]{2,1,0:T(8,128)}), f32[8,16,768]{2,1,0:T(8,128)S(1)}, u32[]{:S(2)}, u32[]{:S(2)}) async-start(f32[8,16,768]{2,1,0:T(8,128)} %bitcast.69), calls=%async_computation | async-start | bytes 786432 | tf_op jit(solution)/shard_map/all_to_all | solution.py:160
  9.2 10.3 %collective-permute-start.1 = (f32[6,4,4,1]{3,2,1,0:T(4,128)S(1)}, f32[6,4,4,1]{3,2,1,0:T(4,128)S(1)}, u32[]{:S(2)}, u32[]{:S(2)}) collective-permute-start(f32[6,4,4,1]{3,2,1,0:T(4,128)S(1)} %get-tuple-element.29), channel_id=1, source_target_pairs={{1,2},{2,1},{5,6},{6,5},{9,10},{10,9},{13,14},{14,13},{17,18},{18,... | collective-permute-start | bytes 1160 | tf_op jit(solution)/shard_map/ppermute | solution.py:24
  9.9 9.6 %collective-permute-start = (f32[6,4,4,1]{3,2,1,0:T(4,128)S(1)}, f32[6,4,4,1]{3,2,1,0:T(4,128)S(1)}, u32[]{:S(2)}, u32[]{:S(2)}) collective-permute-start(f32[6,4,4,1]{3,2,1,0:T(4,128)S(1)} %get-tuple-element.30), channel_id=1, source_target_pairs={{0,1},{1,0},{2,3},{3,2},{4,5},{5,4},{6,7},{7,6},{8,9},{9,8},{10,11... | collective-permute-start | bytes 1160 | tf_op jit(solution)/shard_map/ppermute | solution.py:22
  13.8 7.7 %collective-permute-start.2 = (f32[6,4,1,128]{3,2,1,0:T(1,128)S(1)}, f32[6,4,1,128]{3,2,1,0:T(1,128)S(1)}, u32[]{:S(2)}, u32[]{:S(2)}) collective-permute-start(f32[6,4,1,128]{3,2,1,0:T(1,128)S(1)} %broadcast_select_fusion.2), channel_id=1, source_target_pairs={{0,4},{4,0},{1,5},{5,1},{2,6},{6,2},{3,7},{7,3},{8,12},{12,8},{9,1... | collective-permute-start | bytes 36872 | tf_op jit(solution)/shard_map/ppermute | solution.py:22
  15.3 4.3 %collective-permute-start.3 = (f32[6,1,4,128]{3,2,1,0:T(4,128)S(1)}, f32[6,1,4,128]{3,2,1,0:T(4,128)S(1)}, u32[]{:S(2)}, u32[]{:S(2)}) collective-permute-start(f32[6,1,4,128]{3,2,1,0:T(4,128)S(1)} %get-tuple-element.27), channel_id=1, source_target_pairs={{0,8},{8,0},{16,24},{24,16},{1,9},{9,1},{17,25},{25,17},{2,10},{10... | collective-permute-start | bytes 36872 | tf_op jit(solution)/shard_map/ppermute | solution.py:22
  16.5 5.0 %collective-permute-start.4 = (f32[6,1,4,128]{3,2,1,0:T(4,128)S(1)}, f32[6,1,4,128]{3,2,1,0:T(4,128)S(1)}, u32[]{:S(2)}, u32[]{:S(2)}) collective-permute-start(f32[6,1,4,128]{3,2,1,0:T(4,128)S(1)} %get-tuple-element.28), channel_id=1, source_target_pairs={{8,16},{16,8},{9,17},{17,9},{10,18},{18,10},{11,19},{19,11},{12,20... | collective-permute-start | bytes 36872 | tf_op jit(solution)/shard_map/ppermute | solution.py:24
  26.4 19.3 %copy-start.2 = (f32[64,128]{1,0:T(8,128)S(1)}, f32[64,128]{1,0:T(8,128)}, u32[]{:S(2)}) copy-start(f32[64,128]{1,0:T(8,128)} %get-tuple-element.9) | copy-start | bytes 98308
  26.4 19.5 %copy-start.1 = (f32[3,64,128]{2,1,0:T(8,128)S(1)}, f32[3,64,128]{2,1,0:T(8,128)}, u32[]{:S(2)}) copy-start(f32[3,64,128]{2,1,0:T(8,128)} %get-tuple-element.8) | copy-start | bytes 294916
  26.8 6.0 %collective-permute-start.8 = (f32[5,4,4,1]{3,2,1,0:T(4,128)S(1)}, f32[5,4,4,1]{3,2,1,0:T(4,128)S(1)}, u32[]{:S(2)}, u32[]{:S(2)}) collective-permute-start(f32[5,4,4,1]{3,2,1,0:T(4,128)S(1)} %get-tuple-element.33), channel_id=1, source_target_pairs={{1,2},{2,1},{5,6},{6,5},{9,10},{10,9},{13,14},{14,13},{17,18},{18,... | collective-permute-start | bytes 968 | tf_op jit(solution)/shard_map/ppermute | solution.py:24
  27.5 5.4 %collective-permute-start.9 = (f32[5,4,4,1]{3,2,1,0:T(4,128)S(1)}, f32[5,4,4,1]{3,2,1,0:T(4,128)S(1)}, u32[]{:S(2)}, u32[]{:S(2)}) collective-permute-start(f32[5,4,4,1]{3,2,1,0:T(4,128)S(1)} %get-tuple-element.34), channel_id=1, source_target_pairs={{0,1},{1,0},{2,3},{3,2},{4,5},{5,4},{6,7},{7,6},{8,9},{9,8},{10,11... | collective-permute-start | bytes 968 | tf_op jit(solution)/shard_map/ppermute | solution.py:22
  28.7 4.2 %collective-permute-start.7 = (f32[5,4,1,128]{3,2,1,0:T(1,128)S(1)}, f32[5,4,1,128]{3,2,1,0:T(1,128)S(1)}, u32[]{:S(2)}, u32[]{:S(2)}) collective-permute-start(f32[5,4,1,128]{3,2,1,0:T(1,128)S(1)} %broadcast_select_fusion.9), channel_id=1, source_target_pairs={{0,4},{4,0},{1,5},{5,1},{2,6},{6,2},{3,7},{7,3},{8,12},{12,8},{9,1... | collective-permute-start | bytes 30728 | tf_op jit(solution)/shard_map/ppermute | solution.py:22
  28.7 4.2 %collective-permute-start.6 = (f32[5,1,4,128]{3,2,1,0:T(4,128)S(1)}, f32[5,1,4,128]{3,2,1,0:T(4,128)S(1)}, u32[]{:S(2)}, u32[]{:S(2)}) collective-permute-start(f32[5,1,4,128]{3,2,1,0:T(4,128)S(1)} %get-tuple-element.31), channel_id=1, source_target_pairs={{0,8},{8,0},{16,24},{24,16},{1,9},{9,1},{17,25},{25,17},{2,10},{10... | collective-permute-start | bytes 30728 | tf_op jit(solution)/shard_map/ppermute | solution.py:22
  28.7 5.5 %collective-permute-start.5 = (f32[5,1,4,128]{3,2,1,0:T(4,128)S(1)}, f32[5,1,4,128]{3,2,1,0:T(4,128)S(1)}, u32[]{:S(2)}, u32[]{:S(2)}) collective-permute-start(f32[5,1,4,128]{3,2,1,0:T(4,128)S(1)} %get-tuple-element.32), channel_id=1, source_target_pairs={{8,16},{16,8},{9,17},{17,9},{10,18},{18,10},{11,19},{19,11},{12,20... | collective-permute-start | bytes 30728 | tf_op jit(solution)/shard_map/ppermute | solution.py:24
  34.4 12.1 %copy-start = (f32[5,4,4,128]{3,2,1,0:T(4,128)}, f32[5,4,4,128]{3,2,1,0:T(4,128)S(1)}, u32[]{:S(2)}) copy-start(f32[5,4,4,128]{3,2,1,0:T(4,128)S(1)} %fusion.22) | copy-start | bytes 122884

commit v16 on v13

--- a/solution.py
+++ b/solution.py
@@ -8,15 +8,17 @@
 SIDES = (("stream", 1), ("cross", 2), ("gore", 3))
 
 
-def face_halo(block):
+def face_halo(block, parts=None):
+    parts = [block] if parts is None else parts
     wide = block
     for axis, dim in SIDES:
         count = lax.axis_size(axis)
         index = lax.axis_index(axis)
         odd = index % 2 == 1
-        extent = block.shape[dim]
-        last = lax.slice_in_dim(block, extent - 1, None, axis=dim)
-        first = lax.slice_in_dim(block, 0, 1, axis=dim)
+        last = jnp.concatenate(
+            [lax.slice_in_dim(part, part.shape[dim] - 1, None, axis=dim) for part in parts], 0
+        )
+        first = jnp.concatenate([lax.slice_in_dim(part, 0, 1, axis=dim) for part in parts], 0)
         pairs_a = [(i, i ^ 1) for i in range(count) if (i ^ 1) < count]
         pairs_b = [(i, j) for i in range(1, count) for j in (i - 1, i + 1) if j >= 1 and j < count and (min(i, j) % 2 == 1)]
         from_a = lax.ppermute(jnp.where(odd, first, last), axis, pairs_a)
@@ -163,10 +165,13 @@
     pack = make_pack(tile_count, row_count, blocks, capacity)
     outbound, load_rows, placement_plan = pack(routes, lengths, cell_ids, records)
     arrived = lax.all_to_all(outbound, ("stream", "cross"), split_axis=0, concat_axis=0, tiled=True)
-    outbound, state_and_visc = lax.optimization_barrier(
-        (outbound, jnp.concatenate([fluid_state, viscosity[None]], 0))
-    )
-    state_visc = face_halo(state_and_visc)
+    outbound, density, momentum_energy, viscosity = lax.optimization_barrier(
+        (outbound, density, momentum_energy, viscosity)
+    )
+    state_visc = face_halo(
+        jnp.concatenate([density[None], momentum_energy, viscosity[None]], 0),
+        [density[None], momentum_energy, viscosity[None]],
+    )
     state_pad = state_visc[0:5]
     visc_pad = state_visc[5]
 

time: 47.4 us -> 55.7 us (1.18)
  local copies, waits for them, and re-layouts: 0.68 us -> 6.95 us
  starting transfers between devices: 21.4 us -> 24.3 us
  waiting for transfers between devices: 3.14 us -> 1.24 us
    slice x0 -> x7, local copies, waits for them, and re-layouts: none -> 3.86 us  [the longest x4 2.3 us: face_halo(): lax.slice_in_dim(part, 0, 1, axis=dim)]
    ppermute x6, starting transfers between devices: 7.79 us -> 10.5 us  [face_halo(): from_a = lax.ppermute(jnp.where(odd, first, last), axis, pairs_a)]
    optimization_barrier x0 -> x2, local copies, waits for them, and re-layouts: none -> 1.95 us  [shards(): lax.optimization_barrier((outbound, density, momentum_energy, viscosity))]
    ppermute x4, waiting for transfers between devices: 3.12 us -> 1.22 us  [face_halo(): from_b = lax.ppermute(jnp.where(odd, last, first), axis, pairs_b)]
  transfers between devices with their start and end apart: 11 -> 11, of which waited for: 2 -> 1; matrix products, arithmetic and copies ran while one was open for 3% -> 14% of each run, Pallas kernels for 0% -> 0%
where the time goes in v16:
time: 55.7 us; the launch traced here: 54.6 us
  starting transfers between devices  24.3 us (44%)
  blocking collectives  9.08 us (16%)
  local copies, waits for them, and re-layouts  6.95 us (12%)
  matrix products  5.87 us (11%)
  other arithmetic  3.55 us (6%)
  Pallas kernels  2.47 us (4%)
  waiting for transfers between devices  1.24 us (2%)
  between operations  1.1 us (2%)
    ppermute x6, starting transfers between devices, face_halo(): from_a = lax.ppermute(jnp.where(odd, first, last), axis, pairs_a)  10.5 us
    all_to_all x1, blocking collectives, shards(): lax.all_to_all(face_pressure.reshape(1, slot_total, row_count), ('stream'...  9.08 us
    ppermute x4, starting transfers between devices, face_halo(): from_b = lax.ppermute(jnp.where(odd, last, first), axis, pairs_b)  8.59 us
    all_to_all x1, starting transfers between devices, shards(): lax.all_to_all(outbound, ('stream', 'cross'), split_axis=0, concat_axis=0...  5.23 us
    dot_general x1, matrix products, shards(): jnp.einsum('cpf,fd->cpd', spread, depth_hot.astype(jnp.float32), precisio...  3.29 us
    pallas_call x1, Pallas kernels, pack(): pl.pallas_call(pack_kernel, out_shape=(jax.ShapeDtypeStruct((slot_total,...  2.47 us
    dot_general x1, matrix products, exact_dot(): jnp.einsum(left + ',k' + right + '->k' + output, onehot, stacked, preferr...  2.4 us
    slice x4, local copies, waits for them, and re-layouts, face_halo(): lax.slice_in_dim(part, 0, 1, axis=dim)  2.3 us
  transfers between devices with their start and end apart: 11, of which 1 were waited for; matrix products, arithmetic and copies ran while one was open for 14% of the time, Pallas kernels for 0%

profile of v16, /device:TPU:1, one launch (start us, length us, event | category | flops | bytes accessed | tf_op | source)
XLA Modules:
  0.0 54.6 jit_solution(8711568613407750315)
XLA Ops:
  0.6 2.5 %shard_map.86 = (f32[128,768]{1,0:T(8,128)}, f32[3,64,128]{2,1,0:T(8,128)}, f32[64,128]{1,0:T(8,128)}) custom-call(s32[1,64]{1,0:T(1,128)} %bitcast.111, s32[1,64]{1,0:T(1,128)} %bitcast.112, s32[64,128]{1,0:T(8,128)} %cell_ref.1, f32[8,64,128]{2,1,0:T(8,128)} %record_ref.1), custom_call_target="tpu_custom_call" | custom-call | tf_op jit(solution)/shard_map/pallas_call | solution.py:143
  3.1 5.2 %all-to-all-start = ((f32[8,16,768]{2,1,0:T(8,128)}), f32[8,16,768]{2,1,0:T(8,128)S(1)}, u32[]{:S(2)}, u32[]{:S(2)}) async-start(f32[8,16,768]{2,1,0:T(8,128)} %bitcast.81), calls=%async_computation | async-start | bytes 786432 | tf_op jit(solution)/shard_map/all_to_all | solution.py:167
  8.3 0.8 %fusion.103 = (f32[1,4,1,128]{3,2,1,0:T(1,128)S(1)}, f32[1,4,1,128]{3,2,1,0:T(1,128)S(1)}) fusion(f32[1,4,4,128]{3,2,1,0:T(4,128)} %bitcast.89), kind=kLoop, calls=%fused_computation.206 | loop fusion | bytes 8192 | tf_op jit(solution)/shard_map/slice | solution.py:19
  9.1 0.8 %copy.40 = f32[4,4,4,128]{3,1,2,0:T(4,128)S(1)} copy(f32[4,4,4,128]{3,2,1,0:T(4,128)} %param.8) | data formatting | bytes 65536 | tf_op jit(solution)/shard_map/optimization_barrier | solution.py:168
  9.9 0.8 %fusion.102 = (f32[1,4,1,128]{3,2,1,0:T(1,128)S(1)}, f32[1,4,1,128]{3,2,1,0:T(1,128)S(1)}) fusion(f32[1,4,4,128]{3,2,1,0:T(4,128)} %bitcast.94), kind=kLoop, calls=%fused_computation.205 | loop fusion | bytes 8192 | tf_op jit(solution)/shard_map/slice | solution.py:19
  10.7 1.4 %collective-permute-start.2 = (f32[6,4,1,128]{3,1,2,0:T(4,128)S(1)}, f32[6,4,1,128]{3,1,2,0:T(4,128)S(1)}, u32[]{:S(2)}, u32[]{:S(2)}) collective-permute-start(f32[6,4,1,128]{3,1,2,0:T(4,128)S(1)} %maximum_select_fusion), channel_id=1, source_target_pairs={{0,4},{4,0},{1,5},{5,1},{2,6},{6,2},{3,7},{7,3},{8,12},{12,8},{9,1... | collective-permute-start | bytes 36872 | tf_op jit(solution)/shard_map/ppermute | solution.py:24
  12.1 0.7 %fusion.100 = (f32[1,1,4,128]{3,2,1,0:T(4,128)S(1)}, f32[1,1,4,128]{3,2,1,0:T(4,128)S(1)}, f32[1,1,4,128]{3,2,1,0:T(4,128)S(1)}, f32[1,1,4,128]{3,2,1,0:T(4,128)S(1)}) fusion(f32[1,4,4,128]{3,2,1,0:T(4,128)} %bitcast.95, f32[1,4,4,128]{3,2,1,0:T(4,128)} %bitcast.90), kind=kLoop, calls=%fused_computation.203 | loop fusion | bytes 16384 | tf_op jit(solution)/shard_map/slice | solution.py:21
  12.9 0.7 %fusion.98 = (f32[4,1,4,128]{3,2,1,0:T(4,128)S(1)}, f32[4,1,4,128]{3,2,1,0:T(4,128)S(1)}) fusion(f32[4,4,4,128]{3,2,1,0:T(4,128)} %param.8), kind=kLoop, calls=%fused_computation.201 | loop fusion | bytes 32768 | tf_op jit(solution)/shard_map/slice | solution.py:21
  13.6 0.7 %collective-permute-start.3 = (f32[6,1,4,128]{3,2,1,0:T(4,128)S(1)}, f32[6,1,4,128]{3,2,1,0:T(4,128)S(1)}, u32[]{:S(2)}, u32[]{:S(2)}) collective-permute-start(f32[6,1,4,128]{3,2,1,0:T(4,128)S(1)} %get-tuple-element.43), channel_id=1, source_target_pairs={{0,8},{8,0},{16,24},{24,16},{1,9},{9,1},{17,25},{25,17},{2,10},{10... | collective-permute-start | bytes 36872 | tf_op jit(solution)/shard_map/ppermute | solution.py:24
  14.3 3.0 %collective-permute-start.4 = (f32[6,1,4,128]{3,2,1,0:T(4,128)S(1)}, f32[6,1,4,128]{3,2,1,0:T(4,128)S(1)}, u32[]{:S(2)}, u32[]{:S(2)}) collective-permute-start(f32[6,1,4,128]{3,2,1,0:T(4,128)S(1)} %get-tuple-element.44), channel_id=1, source_target_pairs={{8,16},{16,8},{9,17},{17,9},{10,18},{18,10},{11,19},{19,11},{12,20... | collective-permute-start | bytes 36872 | tf_op jit(solution)/shard_map/ppermute | solution.py:26
  17.3 0.9 %slice_bitcast_fusion.2 = (f32[1,4,4,1]{0,2,3,1:T(4,128)S(1)}, f32[1,4,4,1]{0,2,3,1:T(4,128)S(1)}, f32[1,4,4,1]{0,2,3,1:T(4,128)S(1)}, f32[1,4,4,1]{0,2,3,1:T(4,128)S(1)}) fusion(f32[1,4,4,128]{3,2,1,0:T(4,128)} %bitcast.91, f32[1,4,4,128]{3,2,1,0:T(4,128)} %bitcast.96), kind=kLoop, calls=%fused_computation.176 | loop fusion | bytes 512 | tf_op jit(solution)/shard_map/slice | solution.py:21
  18.2 1.2 %copy.34 = f32[4,4,4,128]{0,2,3,1:T(4,128)S(1)} copy(f32[4,4,4,128]{3,2,1,0:T(4,128)} %param.8) | data formatting | bytes 65536 | tf_op jit(solution)/shard_map/optimization_barrier | solution.py:168
  19.5 1.4 %collective-permute-start = (f32[6,4,4,1]{0,2,3,1:T(4,128)S(1)}, f32[6,4,4,1]{0,2,3,1:T(4,128)S(1)}, u32[]{:S(2)}, u32[]{:S(2)}) collective-permute-start(f32[6,4,4,1]{0,2,3,1:T(4,128)S(1)} %get-tuple-element.31), channel_id=1, source_target_pairs={{0,1},{1,0},{2,3},{3,2},{4,5},{5,4},{6,7},{7,6},{8,9},{9,8},{10,11... | collective-permute-start | bytes 1160 | tf_op jit(solution)/shard_map/ppermute | solution.py:24
  20.8 0.6 %collective-permute-start.1 = (f32[6,4,4,1]{0,2,3,1:T(4,128)S(1)}, f32[6,4,4,1]{0,2,3,1:T(4,128)S(1)}, u32[]{:S(2)}, u32[]{:S(2)}) collective-permute-start(f32[6,4,4,1]{0,2,3,1:T(4,128)S(1)} %get-tuple-element.32), channel_id=1, source_target_pairs={{1,2},{2,1},{5,6},{6,5},{9,10},{10,9},{13,14},{14,13},{17,18},{18,... | collective-permute-start | bytes 1160 | tf_op jit(solution)/shard_map/ppermute | solution.py:26
  21.5 0.9 %pad_maximum_fusion = f32[6,6,6,130]{3,2,1,0:T(8,128)S(1)} fusion(f32[1,4,4,128]{3,2,1,0:T(4,128)} %bitcast.92, f32[4,4,4,128]{3,2,1,0:T(4,128)} %param.8, f32[1,4,4,128]{3,2,1,0:T(4,128)} %bitcast.97), kind=kLoop, calls=%fused_computation.17 | loop fusion | flops 56160 | bytes 161472 | tf_op jit(solution)/shard_map/concatenate | solution.py:172
  23.5 0.5 stack.15
  24.6 3.3 %fusion.2 = f32[5,16,128]{2,1,0:T(8,128)S(1)} fusion(s32[16384]{0:T(1024)S(1)} %add_select_fusion, f32[5,16,16384]{2,1,0:T(8,128)S(1)} %fusion.113), kind=kOutput, calls=%fused_computation.3 | convolution fusion | flops 1008730112 | bytes 5349376 | tf_op jit(solution)/shard_map/cpf,fd->cpd/dot_general | solution.py:189
  28.3 0.7 %collective-permute-start.8 = (f32[5,4,4,1]{3,2,1,0:T(4,128)S(1)}, f32[5,4,4,1]{3,2,1,0:T(4,128)S(1)}, u32[]{:S(2)}, u32[]{:S(2)}) collective-permute-start(f32[5,4,4,1]{3,2,1,0:T(4,128)S(1)} %get-tuple-element.35), channel_id=1, source_target_pairs={{1,2},{2,1},{5,6},{6,5},{9,10},{10,9},{13,14},{14,13},{17,18},{18,... | collective-permute-start | bytes 968 | tf_op jit(solution)/shard_map/ppermute | solution.py:26
  29.0 6.7 %collective-permute-start.9 = (f32[5,4,4,1]{3,2,1,0:T(4,128)S(1)}, f32[5,4,4,1]{3,2,1,0:T(4,128)S(1)}, u32[]{:S(2)}, u32[]{:S(2)}) collective-permute-start(f32[5,4,4,1]{3,2,1,0:T(4,128)S(1)} %get-tuple-element.36), channel_id=1, source_target_pairs={{0,1},{1,0},{2,3},{3,2},{4,5},{5,4},{6,7},{7,6},{8,9},{9,8},{10,11... | collective-permute-start | bytes 968 | tf_op jit(solution)/shard_map/ppermute | solution.py:24
  35.9 4.3 %collective-permute-start.5 = (f32[5,1,4,128]{3,2,1,0:T(4,128)S(1)}, f32[5,1,4,128]{3,2,1,0:T(4,128)S(1)}, u32[]{:S(2)}, u32[]{:S(2)}) collective-permute-start(f32[5,1,4,128]{3,2,1,0:T(4,128)S(1)} %get-tuple-element.34), channel_id=1, source_target_pairs={{8,16},{16,8},{9,17},{17,9},{10,18},{18,10},{11,19},{19,11},{12,20... | collective-permute-start | bytes 30728 | tf_op jit(solution)/shard_map/ppermute | solution.py:26
  40.4 1.2 %collective-permute-done.5 = f32[5,1,4,128]{3,2,1,0:T(4,128)S(1)} collective-permute-done((f32[5,1,4,128]{3,2,1,0:T(4,128)S(1)}, f32[5,1,4,128]{3,2,1,0:T(4,128)S(1)}, u32[]{:S(2)}, u32[]{:S(2)}) %collective-permute-start.5) | collective-permute-done | bytes 10272 | tf_op jit(solution)/shard_map/ppermute | solution.py:26
  41.9 2.4 %convolution_bitcast_fusion = f32[3,16384,16]{1,2,0:T(8,128)S(1)} fusion(s32[16384]{0:T(1024)S(1)} %add_select_fusion, bf16[1,128,16]{1,2,0:T(8,128)(2,1)S(1)} %get-tuple-element.55, bf16[1,128,16]{1,2,0:T(8,128)(2,1)S(1)} %get-tuple-element.54, bf16[1,128,16]{1,2,0:T(8,128)(2,1)S(1)} %get-tuple-element.53), kind=kOutput, calls=%fused_computation | convolution fusion | flops 203436032 | bytes 3223552 | tf_op jit(solution)/shard_map/fd,kdp->kfp/dot_general | solution.py:86
  44.7 9.1 %all_to_all.17 = f32[1,128,128]{2,0,1:T(1,128)S(1)} all-to-all(f32[1,128,128]{2,0,1:T(1,128)S(1)} %bitcast.82), channel_id=1, replica_groups=mesh['stream'=4,'cross'=2,'gore'=4] {'stream','cross'}, dimensions={1} | all-to-all | bytes 131072 | tf_op jit(solution)/shard_map/all_to_all | solution.py:208
  53.9 0.7 %broadcast_multiply_fusion = f32[3,64,128]{2,1,0:T(8,128)} fusion(f32[3,64,128]{2,1,0:T(8,128)S(1)} %copy-done.4, f32[64,128]{1,0:T(8,128)S(1)} %fusion.104), kind=kLoop, calls=%fused_computation.40 | loop fusion | flops 24576 | bytes 229376 | tf_op jit(solution)/shard_map/mul | solution.py:218
  (59 shorter events, 3.1 us)
Async XLA Ops:
  3.1 20.1 %all-to-all-start = ((f32[8,16,768]{2,1,0:T(8,128)}), f32[8,16,768]{2,1,0:T(8,128)S(1)}, u32[]{:S(2)}, u32[]{:S(2)}) async-start(f32[8,16,768]{2,1,0:T(8,128)} %bitcast.81), calls=%async_computation | async-start | bytes 786432 | tf_op jit(solution)/shard_map/all_to_all | solution.py:167
  10.7 12.2 %collective-permute-start.2 = (f32[6,4,1,128]{3,1,2,0:T(4,128)S(1)}, f32[6,4,1,128]{3,1,2,0:T(4,128)S(1)}, u32[]{:S(2)}, u32[]{:S(2)}) collective-permute-start(f32[6,4,1,128]{3,1,2,0:T(4,128)S(1)} %maximum_select_fusion), channel_id=1, source_target_pairs={{0,4},{4,0},{1,5},{5,1},{2,6},{6,2},{3,7},{7,3},{8,12},{12,8},{9,1... | collective-permute-start | bytes 36872 | tf_op jit(solution)/shard_map/ppermute | solution.py:24
  13.6 9.4 %collective-permute-start.3 = (f32[6,1,4,128]{3,2,1,0:T(4,128)S(1)}, f32[6,1,4,128]{3,2,1,0:T(4,128)S(1)}, u32[]{:S(2)}, u32[]{:S(2)}) collective-permute-start(f32[6,1,4,128]{3,2,1,0:T(4,128)S(1)} %get-tuple-element.43), channel_id=1, source_target_pairs={{0,8},{8,0},{16,24},{24,16},{1,9},{9,1},{17,25},{25,17},{2,10},{10... | collective-permute-start | bytes 36872 | tf_op jit(solution)/shard_map/ppermute | solution.py:24
  14.3 8.7 %collective-permute-start.4 = (f32[6,1,4,128]{3,2,1,0:T(4,128)S(1)}, f32[6,1,4,128]{3,2,1,0:T(4,128)S(1)}, u32[]{:S(2)}, u32[]{:S(2)}) collective-permute-start(f32[6,1,4,128]{3,2,1,0:T(4,128)S(1)} %get-tuple-element.44), channel_id=1, source_target_pairs={{8,16},{16,8},{9,17},{17,9},{10,18},{18,10},{11,19},{19,11},{12,20... | collective-permute-start | bytes 36872 | tf_op jit(solution)/shard_map/ppermute | solution.py:26
  19.5 2.9 %collective-permute-start = (f32[6,4,4,1]{0,2,3,1:T(4,128)S(1)}, f32[6,4,4,1]{0,2,3,1:T(4,128)S(1)}, u32[]{:S(2)}, u32[]{:S(2)}) collective-permute-start(f32[6,4,4,1]{0,2,3,1:T(4,128)S(1)} %get-tuple-element.31), channel_id=1, source_target_pairs={{0,1},{1,0},{2,3},{3,2},{4,5},{5,4},{6,7},{7,6},{8,9},{9,8},{10,11... | collective-permute-start | bytes 1160 | tf_op jit(solution)/shard_map/ppermute | solution.py:24
  20.8 1.6 %collective-permute-start.1 = (f32[6,4,4,1]{0,2,3,1:T(4,128)S(1)}, f32[6,4,4,1]{0,2,3,1:T(4,128)S(1)}, u32[]{:S(2)}, u32[]{:S(2)}) collective-permute-start(f32[6,4,4,1]{0,2,3,1:T(4,128)S(1)} %get-tuple-element.32), channel_id=1, source_target_pairs={{1,2},{2,1},{5,6},{6,5},{9,10},{10,9},{13,14},{14,13},{17,18},{18,... | collective-permute-start | bytes 1160 | tf_op jit(solution)/shard_map/ppermute | solution.py:26
  24.5 3.4 %copy-start = (f32[4,4,4,128]{3,2,1,0:T(4,128)S(1)}, f32[4,4,4,128]{3,2,1,0:T(4,128)}, u32[]{:S(2)}) copy-start(f32[4,4,4,128]{3,2,1,0:T(4,128)} %param.8) | copy-start | bytes 98308
  24.6 3.4 %copy-start.1 = (f32[4,4,128]{2,1,0:T(4,128)S(1)}, f32[4,4,128]{2,1,0:T(4,128)}, u32[]{:S(2)}) copy-start(f32[4,4,128]{2,1,0:T(4,128)} %param.9) | copy-start | bytes 24580
  24.6 3.4 %copy-start.2 = (f32[4,4,128]{2,1,0:T(4,128)S(1)}, f32[4,4,128]{2,1,0:T(4,128)}, u32[]{:S(2)}) copy-start(f32[4,4,128]{2,1,0:T(4,128)} %param.7) | copy-start | bytes 24580
  27.9 25.9 %copy-start.5 = (f32[64,128]{1,0:T(8,128)S(1)}, f32[64,128]{1,0:T(8,128)}, u32[]{:S(2)}) copy-start(f32[64,128]{1,0:T(8,128)} %get-tuple-element.13) | copy-start | bytes 98308
  27.9 26.0 %copy-start.4 = (f32[3,64,128]{2,1,0:T(8,128)S(1)}, f32[3,64,128]{2,1,0:T(8,128)}, u32[]{:S(2)}) copy-start(f32[3,64,128]{2,1,0:T(8,128)} %get-tuple-element.12) | copy-start | bytes 294916
  28.3 12.0 %collective-permute-start.8 = (f32[5,4,4,1]{3,2,1,0:T(4,128)S(1)}, f32[5,4,4,1]{3,2,1,0:T(4,128)S(1)}, u32[]{:S(2)}, u32[]{:S(2)}) collective-permute-start(f32[5,4,4,1]{3,2,1,0:T(4,128)S(1)} %get-tuple-element.35), channel_id=1, source_target_pairs={{1,2},{2,1},{5,6},{6,5},{9,10},{10,9},{13,14},{14,13},{17,18},{18,... | collective-permute-start | bytes 968 | tf_op jit(solution)/shard_map/ppermute | solution.py:26
  29.0 11.3 %collective-permute-start.9 = (f32[5,4,4,1]{3,2,1,0:T(4,128)S(1)}, f32[5,4,4,1]{3,2,1,0:T(4,128)S(1)}, u32[]{:S(2)}, u32[]{:S(2)}) collective-permute-start(f32[5,4,4,1]{3,2,1,0:T(4,128)S(1)} %get-tuple-element.36), channel_id=1, source_target_pairs={{0,1},{1,0},{2,3},{3,2},{4,5},{5,4},{6,7},{7,6},{8,9},{9,8},{10,11... | collective-permute-start | bytes 968 | tf_op jit(solution)/shard_map/ppermute | solution.py:24
  35.7 4.6 %collective-permute-start.7 = (f32[5,4,1,128]{3,2,1,0:T(1,128)S(1)}, f32[5,4,1,128]{3,2,1,0:T(1,128)S(1)}, u32[]{:S(2)}, u32[]{:S(2)}) collective-permute-start(f32[5,4,1,128]{3,2,1,0:T(1,128)S(1)} %broadcast_select_fusion.4), channel_id=1, source_target_pairs={{0,4},{4,0},{1,5},{5,1},{2,6},{6,2},{3,7},{7,3},{8,12},{12,8},{9,1... | collective-permute-start | bytes 30728 | tf_op jit(solution)/shard_map/ppermute | solution.py:24
  35.9 4.4 %collective-permute-start.6 = (f32[5,1,4,128]{3,2,1,0:T(4,128)S(1)}, f32[5,1,4,128]{3,2,1,0:T(4,128)S(1)}, u32[]{:S(2)}, u32[]{:S(2)}) collective-permute-start(f32[5,1,4,128]{3,2,1,0:T(4,128)S(1)} %get-tuple-element.33), channel_id=1, source_target_pairs={{0,8},{8,0},{16,24},{24,16},{1,9},{9,1},{17,25},{25,17},{2,10},{10... | collective-permute-start | bytes 30728 | tf_op jit(solution)/shard_map/ppermute | solution.py:24
  35.9 5.6 %collective-permute-start.5 = (f32[5,1,4,128]{3,2,1,0:T(4,128)S(1)}, f32[5,1,4,128]{3,2,1,0:T(4,128)S(1)}, u32[]{:S(2)}, u32[]{:S(2)}) collective-permute-start(f32[5,1,4,128]{3,2,1,0:T(4,128)S(1)} %get-tuple-element.34), channel_id=1, source_target_pairs={{8,16},{16,8},{9,17},{17,9},{10,18},{18,10},{11,19},{19,11},{12,20... | collective-permute-start | bytes 30728 | tf_op jit(solution)/shard_map/ppermute | solution.py:26
  41.8 12.8 %copy-start.3 = (f32[5,4,4,128]{3,2,1,0:T(4,128)}, f32[5,4,4,128]{3,2,1,0:T(4,128)S(1)}, u32[]{:S(2)}) copy-start(f32[5,4,4,128]{3,2,1,0:T(4,128)S(1)} %fusion.38) | copy-start | bytes 122884

commit v17 on v13

--- a/solution.py
+++ b/solution.py
@@ -149,6 +149,18 @@
     return pack
 
 
+def unpack_kernel(plan_ref, returned_ref, load_ref, out_ref):
+    plan = plan_ref[...].astype(jnp.bfloat16)
+    high, rest = split_high(returned_ref[...])
+    middle, low = split_high(rest)
+    pressure = None
+    for part in (high, middle, low):
+        term = jnp.dot(plan, part.astype(jnp.bfloat16), preferred_element_type=jnp.float32)
+        pressure = term if pressure is None else pressure + term
+    for comp in range(out_ref.shape[0]):
+        out_ref[comp] = load_ref[comp] * pressure
+
+
 def shards(density, momentum_energy, viscosity, records, cell_ids, routes, lengths):
     fluid_state = jnp.concatenate([density[None], momentum_energy], 0)
     cells_x, cells_y, vertical_cells = density.shape
@@ -207,10 +219,9 @@
         concat_axis=1,
         tiled=True,
     )
-    home_pressure = jnp.einsum(
-        "ts,sr->tr", placement_plan, returned[0], precision=lax.Precision.HIGHEST
-    )
-    face_loads = load_rows * home_pressure[None]
+    face_loads = pl.pallas_call(
+        unpack_kernel, out_shape=jax.ShapeDtypeStruct(load_rows.shape, jnp.float32)
+    )(placement_plan, returned[0], load_rows)
     return (new_state, face_loads)
 
 

time: 47.4 us -> 48.4 us (1.021)
  Pallas kernels: 2.47 us -> 4.23 us
  other arithmetic: 3.48 us -> 2.83 us
    pallas_call x0 -> x1, Pallas kernels: none -> 1.76 us  [shards(): pl.pallas_call(unpack_kernel, out_shape=jax.ShapeDtypeStruct(load_rows.sh...]
    mul x1 -> x0, other arithmetic: 0.65 us -> none  [shards(): face_loads = load_rows * home_pressure[None]]
where the time goes in v17:
time: 48.4 us; the launch traced here: 47.6 us
  starting transfers between devices  21.4 us (44%)
  blocking collectives  8.65 us (18%)
  matrix products  5.68 us (12%)
  Pallas kernels  4.23 us (9%)
  waiting for transfers between devices  3.14 us (6%)
  other arithmetic  2.83 us (6%)
  between operations  0.97 us (2%)
  local copies, waits for them, and re-layouts  0.67 us (1%)
    all_to_all x1, blocking collectives, shards(): lax.all_to_all(face_pressure.reshape(1, slot_total, row_count), ('stream'...  8.65 us
    ppermute x4, starting transfers between devices, face_halo(): from_b = lax.ppermute(jnp.where(odd, last, first), axis, pairs_b)  8.42 us
    ppermute x6, starting transfers between devices, face_halo(): from_a = lax.ppermute(jnp.where(odd, first, last), axis, pairs_a)  7.79 us
    all_to_all x1, starting transfers between devices, shards(): lax.all_to_all(outbound, ('stream', 'cross'), split_axis=0, concat_axis=0...  5.22 us
    dot_general x1, matrix products, shards(): jnp.einsum('cpf,fd->cpd', spread, depth_hot.astype(jnp.float32), precisio...  3.28 us
    ppermute x4, waiting for transfers between devices, face_halo(): from_b = lax.ppermute(jnp.where(odd, last, first), axis, pairs_b)  3.12 us
    pallas_call x1, Pallas kernels, pack(): pl.pallas_call(pack_kernel, out_shape=(jax.ShapeDtypeStruct((slot_total,...  2.47 us
    dot_general x1, matrix products, exact_dot(): jnp.einsum(left + ',k' + right + '->k' + output, onehot, stacked, preferr...  2.4 us
  transfers between devices with their start and end apart: 11, of which 2 were waited for; matrix products, arithmetic and copies ran while one was open for 3% of the time, Pallas kernels for 0%

profile of v17, /device:TPU:1, one launch (start us, length us, event | category | flops | bytes accessed | tf_op | source)
XLA Modules:
  0.0 47.6 jit_solution(2363854156053868066)
XLA Ops:
  0.6 2.5 %shard_map.86 = (f32[128,768]{1,0:T(8,128)}, f32[3,64,128]{2,1,0:T(8,128)}, f32[64,128]{1,0:T(8,128)}) custom-call(s32[1,64]{1,0:T(1,128)} %bitcast.89, s32[1,64]{1,0:T(1,128)} %bitcast.90, s32[64,128]{1,0:T(8,128)} %cell_ref.1, f32[8,64,128]{2,1,0:T(8,128)} %record_ref.1), custom_call_target="tpu_custom_call" | custom-call | tf_op jit(solution)/shard_map/pallas_call | solution.py:141
  3.1 5.2 %all-to-all-start = ((f32[8,16,768]{2,1,0:T(8,128)}), f32[8,16,768]{2,1,0:T(8,128)S(1)}, u32[]{:S(2)}, u32[]{:S(2)}) async-start(f32[8,16,768]{2,1,0:T(8,128)} %bitcast.69), calls=%async_computation | async-start | bytes 786432 | tf_op jit(solution)/shard_map/all_to_all | solution.py:177
  8.3 0.8 %pad_maximum_fusion.6 = f32[6,4,4,128]{3,2,1,0:T(4,128)S(1)} fusion(f32[1,4,4,128]{3,2,1,0:T(4,128)} %bitcast.87, f32[4,4,4,128]{3,2,1,0:T(4,128)} %param.8, f32[1,4,4,128]{3,2,1,0:T(4,128)} %bitcast.88), kind=kLoop, calls=%fused_computation.35 | loop fusion | flops 24576 | bytes 98304 | tf_op jit(solution)/shard_map/concatenate | solution.py:179
  9.2 0.7 %collective-permute-start.1 = (f32[6,4,4,1]{3,2,1,0:T(4,128)S(1)}, f32[6,4,4,1]{3,2,1,0:T(4,128)S(1)}, u32[]{:S(2)}, u32[]{:S(2)}) collective-permute-start(f32[6,4,4,1]{3,2,1,0:T(4,128)S(1)} %get-tuple-element.29), channel_id=1, source_target_pairs={{1,2},{2,1},{5,6},{6,5},{9,10},{10,9},{13,14},{14,13},{17,18},{18,... | collective-permute-start | bytes 1160 | tf_op jit(solution)/shard_map/ppermute | solution.py:24
  9.9 3.9 %collective-permute-start = (f32[6,4,4,1]{3,2,1,0:T(4,128)S(1)}, f32[6,4,4,1]{3,2,1,0:T(4,128)S(1)}, u32[]{:S(2)}, u32[]{:S(2)}) collective-permute-start(f32[6,4,4,1]{3,2,1,0:T(4,128)S(1)} %get-tuple-element.30), channel_id=1, source_target_pairs={{0,1},{1,0},{2,3},{3,2},{4,5},{5,4},{6,7},{7,6},{8,9},{9,8},{10,11... | collective-permute-start | bytes 1160 | tf_op jit(solution)/shard_map/ppermute | solution.py:22
  13.8 1.4 %collective-permute-start.2 = (f32[6,4,1,128]{3,2,1,0:T(1,128)S(1)}, f32[6,4,1,128]{3,2,1,0:T(1,128)S(1)}, u32[]{:S(2)}, u32[]{:S(2)}) collective-permute-start(f32[6,4,1,128]{3,2,1,0:T(1,128)S(1)} %broadcast_select_fusion.2), channel_id=1, source_target_pairs={{0,4},{4,0},{1,5},{5,1},{2,6},{6,2},{3,7},{7,3},{8,12},{12,8},{9,1... | collective-permute-start | bytes 36872 | tf_op jit(solution)/shard_map/ppermute | solution.py:22
  15.3 1.2 %collective-permute-start.3 = (f32[6,1,4,128]{3,2,1,0:T(4,128)S(1)}, f32[6,1,4,128]{3,2,1,0:T(4,128)S(1)}, u32[]{:S(2)}, u32[]{:S(2)}) collective-permute-start(f32[6,1,4,128]{3,2,1,0:T(4,128)S(1)} %get-tuple-element.27), channel_id=1, source_target_pairs={{0,8},{8,0},{16,24},{24,16},{1,9},{9,1},{17,25},{25,17},{2,10},{10... | collective-permute-start | bytes 36872 | tf_op jit(solution)/shard_map/ppermute | solution.py:22
  16.5 3.0 %collective-permute-start.4 = (f32[6,1,4,128]{3,2,1,0:T(4,128)S(1)}, f32[6,1,4,128]{3,2,1,0:T(4,128)S(1)}, u32[]{:S(2)}, u32[]{:S(2)}) collective-permute-start(f32[6,1,4,128]{3,2,1,0:T(4,128)S(1)} %get-tuple-element.28), channel_id=1, source_target_pairs={{8,16},{16,8},{9,17},{17,9},{10,18},{18,10},{11,19},{19,11},{12,20... | collective-permute-start | bytes 36872 | tf_op jit(solution)/shard_map/ppermute | solution.py:24
  19.6 1.9 %collective-permute-done.4 = f32[6,1,4,128]{3,2,1,0:T(4,128)S(1)} collective-permute-done((f32[6,1,4,128]{3,2,1,0:T(4,128)S(1)}, f32[6,1,4,128]{3,2,1,0:T(4,128)S(1)}, u32[]{:S(2)}, u32[]{:S(2)}) %collective-permute-start.4) | collective-permute-done | bytes 12320 | tf_op jit(solution)/shard_map/ppermute | solution.py:24
  21.6 0.1 fusion.17
  21.9 0.1 iota_compare_fusion.2
  22.1 0.5 %stack.15 = f32[5,16384]{1,0:T(8,128)S(1)} concatenate(f32[1,16384]{1,0:T(1,128)S(1)} %bitcast.76, f32[1,16384]{1,0:T(1,128)S(1)} %bitcast.75, f32[1,16384]{1,0:T(1,128)S(1)} %bitcast.74, f32[1,16384]{1,0:T(1,128)S(1)} %bitcast.73, f32[1,16384]{1,0:T(1,128)S(1)} %bitcast.72), dimensions={0} | concatenate | bytes 655360 | tf_op jit(solution)/shard_map/stack | solution.py:192
  22.6 0.5 fusion.91
  23.1 3.3 %fusion.2 = f32[5,16,128]{2,1,0:T(8,128)S(1)} fusion(s32[16384]{0:T(1024)S(1)} %add_select_fusion, f32[5,16,16384]{2,1,0:T(8,128)S(1)} %fusion.91), kind=kOutput, calls=%fused_computation.3 | convolution fusion | flops 1008730112 | bytes 5349376 | tf_op jit(solution)/shard_map/cpf,fd->cpd/dot_general | solution.py:196
  26.4 0.2 fusion.42
  26.8 0.7 %collective-permute-start.8 = (f32[5,4,4,1]{3,2,1,0:T(4,128)S(1)}, f32[5,4,4,1]{3,2,1,0:T(4,128)S(1)}, u32[]{:S(2)}, u32[]{:S(2)}) collective-permute-start(f32[5,4,4,1]{3,2,1,0:T(4,128)S(1)} %get-tuple-element.33), channel_id=1, source_target_pairs={{1,2},{2,1},{5,6},{6,5},{9,10},{10,9},{13,14},{14,13},{17,18},{18,... | collective-permute-start | bytes 968 | tf_op jit(solution)/shard_map/ppermute | solution.py:24
  27.4 1.2 %collective-permute-start.9 = (f32[5,4,4,1]{3,2,1,0:T(4,128)S(1)}, f32[5,4,4,1]{3,2,1,0:T(4,128)S(1)}, u32[]{:S(2)}, u32[]{:S(2)}) collective-permute-start(f32[5,4,4,1]{3,2,1,0:T(4,128)S(1)} %get-tuple-element.34), channel_id=1, source_target_pairs={{0,1},{1,0},{2,3},{3,2},{4,5},{5,4},{6,7},{7,6},{8,9},{9,8},{10,11... | collective-permute-start | bytes 968 | tf_op jit(solution)/shard_map/ppermute | solution.py:22
  28.7 4.1 %collective-permute-start.5 = (f32[5,1,4,128]{3,2,1,0:T(4,128)S(1)}, f32[5,1,4,128]{3,2,1,0:T(4,128)S(1)}, u32[]{:S(2)}, u32[]{:S(2)}) collective-permute-start(f32[5,1,4,128]{3,2,1,0:T(4,128)S(1)} %get-tuple-element.32), channel_id=1, source_target_pairs={{8,16},{16,8},{9,17},{17,9},{10,18},{18,10},{11,19},{19,11},{12,20... | collective-permute-start | bytes 30728 | tf_op jit(solution)/shard_map/ppermute | solution.py:24
  32.9 1.2 %collective-permute-done.5 = f32[5,1,4,128]{3,2,1,0:T(4,128)S(1)} collective-permute-done((f32[5,1,4,128]{3,2,1,0:T(4,128)S(1)}, f32[5,1,4,128]{3,2,1,0:T(4,128)S(1)}, u32[]{:S(2)}, u32[]{:S(2)}) %collective-permute-start.5) | collective-permute-done | bytes 10272 | tf_op jit(solution)/shard_map/ppermute | solution.py:24
  34.1 0.2 fusion.22
  34.4 2.4 %convolution_bitcast_fusion = f32[3,16384,16]{1,2,0:T(8,128)S(1)} fusion(s32[16384]{0:T(1024)S(1)} %add_select_fusion, bf16[1,128,16]{1,2,0:T(8,128)(2,1)S(1)} %get-tuple-element.45, bf16[1,128,16]{1,2,0:T(8,128)(2,1)S(1)} %get-tuple-element.44, bf16[1,128,16]{1,2,0:T(8,128)(2,1)S(1)} %get-tuple-element.43), kind=kOutput, calls=%fused_computation | convolution fusion | flops 203436032 | bytes 3223552 | tf_op jit(solution)/shard_map/fd,kdp->kfp/dot_general | solution.py:84
  36.8 0.4 fusion.12
  37.2 8.7 %all_to_all.17 = f32[1,128,128]{2,0,1:T(1,128)} all-to-all(f32[1,128,128]{2,0,1:T(1,128)S(1)} %bitcast.70), channel_id=1, replica_groups=mesh['stream'=4,'cross'=2,'gore'=4] {'stream','cross'}, dimensions={1} | all-to-all | bytes 131072 | tf_op jit(solution)/shard_map/all_to_all | solution.py:215
  45.8 1.8 %shard_map.87 = f32[3,64,128]{2,1,0:T(8,128)} custom-call(f32[64,128]{1,0:T(8,128)} %get-tuple-element.8.plan_ref, f32[128,128]{1,0:T(8,128)} %bitcast.71, f32[3,64,128]{2,1,0:T(8,128)} %get-tuple-element.9.load_ref), custom_call_target="tpu_custom_call" | custom-call | tf_op jit(solution)/shard_map/pallas_call | solution.py:222
  (37 shorter events, 0.7 us)
Async XLA Ops:
  3.1 18.7 %all-to-all-start = ((f32[8,16,768]{2,1,0:T(8,128)}), f32[8,16,768]{2,1,0:T(8,128)S(1)}, u32[]{:S(2)}, u32[]{:S(2)}) async-start(f32[8,16,768]{2,1,0:T(8,128)} %bitcast.69), calls=%async_computation | async-start | bytes 786432 | tf_op jit(solution)/shard_map/all_to_all | solution.py:177
  9.2 10.3 %collective-permute-start.1 = (f32[6,4,4,1]{3,2,1,0:T(4,128)S(1)}, f32[6,4,4,1]{3,2,1,0:T(4,128)S(1)}, u32[]{:S(2)}, u32[]{:S(2)}) collective-permute-start(f32[6,4,4,1]{3,2,1,0:T(4,128)S(1)} %get-tuple-element.29), channel_id=1, source_target_pairs={{1,2},{2,1},{5,6},{6,5},{9,10},{10,9},{13,14},{14,13},{17,18},{18,... | collective-permute-start | bytes 1160 | tf_op jit(solution)/shard_map/ppermute | solution.py:24
  9.9 9.6 %collective-permute-start = (f32[6,4,4,1]{3,2,1,0:T(4,128)S(1)}, f32[6,4,4,1]{3,2,1,0:T(4,128)S(1)}, u32[]{:S(2)}, u32[]{:S(2)}) collective-permute-start(f32[6,4,4,1]{3,2,1,0:T(4,128)S(1)} %get-tuple-element.30), channel_id=1, source_target_pairs={{0,1},{1,0},{2,3},{3,2},{4,5},{5,4},{6,7},{7,6},{8,9},{9,8},{10,11... | collective-permute-start | bytes 1160 | tf_op jit(solution)/shard_map/ppermute | solution.py:22
  13.8 7.7 %collective-permute-start.2 = (f32[6,4,1,128]{3,2,1,0:T(1,128)S(1)}, f32[6,4,1,128]{3,2,1,0:T(1,128)S(1)}, u32[]{:S(2)}, u32[]{:S(2)}) collective-permute-start(f32[6,4,1,128]{3,2,1,0:T(1,128)S(1)} %broadcast_select_fusion.2), channel_id=1, source_target_pairs={{0,4},{4,0},{1,5},{5,1},{2,6},{6,2},{3,7},{7,3},{8,12},{12,8},{9,1... | collective-permute-start | bytes 36872 | tf_op jit(solution)/shard_map/ppermute | solution.py:22
  15.3 4.3 %collective-permute-start.3 = (f32[6,1,4,128]{3,2,1,0:T(4,128)S(1)}, f32[6,1,4,128]{3,2,1,0:T(4,128)S(1)}, u32[]{:S(2)}, u32[]{:S(2)}) collective-permute-start(f32[6,1,4,128]{3,2,1,0:T(4,128)S(1)} %get-tuple-element.27), channel_id=1, source_target_pairs={{0,8},{8,0},{16,24},{24,16},{1,9},{9,1},{17,25},{25,17},{2,10},{10... | collective-permute-start | bytes 36872 | tf_op jit(solution)/shard_map/ppermute | solution.py:22
  16.5 5.0 %collective-permute-start.4 = (f32[6,1,4,128]{3,2,1,0:T(4,128)S(1)}, f32[6,1,4,128]{3,2,1,0:T(4,128)S(1)}, u32[]{:S(2)}, u32[]{:S(2)}) collective-permute-start(f32[6,1,4,128]{3,2,1,0:T(4,128)S(1)} %get-tuple-element.28), channel_id=1, source_target_pairs={{8,16},{16,8},{9,17},{17,9},{10,18},{18,10},{11,19},{19,11},{12,20... | collective-permute-start | bytes 36872 | tf_op jit(solution)/shard_map/ppermute | solution.py:24
  26.8 6.0 %collective-permute-start.8 = (f32[5,4,4,1]{3,2,1,0:T(4,128)S(1)}, f32[5,4,4,1]{3,2,1,0:T(4,128)S(1)}, u32[]{:S(2)}, u32[]{:S(2)}) collective-permute-start(f32[5,4,4,1]{3,2,1,0:T(4,128)S(1)} %get-tuple-element.33), channel_id=1, source_target_pairs={{1,2},{2,1},{5,6},{6,5},{9,10},{10,9},{13,14},{14,13},{17,18},{18,... | collective-permute-start | bytes 968 | tf_op jit(solution)/shard_map/ppermute | solution.py:24
  27.4 5.4 %collective-permute-start.9 = (f32[5,4,4,1]{3,2,1,0:T(4,128)S(1)}, f32[5,4,4,1]{3,2,1,0:T(4,128)S(1)}, u32[]{:S(2)}, u32[]{:S(2)}) collective-permute-start(f32[5,4,4,1]{3,2,1,0:T(4,128)S(1)} %get-tuple-element.34), channel_id=1, source_target_pairs={{0,1},{1,0},{2,3},{3,2},{4,5},{5,4},{6,7},{7,6},{8,9},{9,8},{10,11... | collective-permute-start | bytes 968 | tf_op jit(solution)/shard_map/ppermute | solution.py:22
  28.7 4.2 %collective-permute-start.7 = (f32[5,4,1,128]{3,2,1,0:T(1,128)S(1)}, f32[5,4,1,128]{3,2,1,0:T(1,128)S(1)}, u32[]{:S(2)}, u32[]{:S(2)}) collective-permute-start(f32[5,4,1,128]{3,2,1,0:T(1,128)S(1)} %broadcast_select_fusion.9), channel_id=1, source_target_pairs={{0,4},{4,0},{1,5},{5,1},{2,6},{6,2},{3,7},{7,3},{8,12},{12,8},{9,1... | collective-permute-start | bytes 30728 | tf_op jit(solution)/shard_map/ppermute | solution.py:22
  28.7 4.2 %collective-permute-start.6 = (f32[5,1,4,128]{3,2,1,0:T(4,128)S(1)}, f32[5,1,4,128]{3,2,1,0:T(4,128)S(1)}, u32[]{:S(2)}, u32[]{:S(2)}) collective-permute-start(f32[5,1,4,128]{3,2,1,0:T(4,128)S(1)} %get-tuple-element.31), channel_id=1, source_target_pairs={{0,8},{8,0},{16,24},{24,16},{1,9},{9,1},{17,25},{25,17},{2,10},{10... | collective-permute-start | bytes 30728 | tf_op jit(solution)/shard_map/ppermute | solution.py:22
  28.7 5.5 %collective-permute-start.5 = (f32[5,1,4,128]{3,2,1,0:T(4,128)S(1)}, f32[5,1,4,128]{3,2,1,0:T(4,128)S(1)}, u32[]{:S(2)}, u32[]{:S(2)}) collective-permute-start(f32[5,1,4,128]{3,2,1,0:T(4,128)S(1)} %get-tuple-element.32), channel_id=1, source_target_pairs={{8,16},{16,8},{9,17},{17,9},{10,18},{18,10},{11,19},{19,11},{12,20... | collective-permute-start | bytes 30728 | tf_op jit(solution)/shard_map/ppermute | solution.py:24
  34.4 13.3 %copy-start = (f32[5,4,4,128]{3,2,1,0:T(4,128)}, f32[5,4,4,128]{3,2,1,0:T(4,128)S(1)}, u32[]{:S(2)}) copy-start(f32[5,4,4,128]{3,2,1,0:T(4,128)S(1)} %fusion.22) | copy-start | bytes 122884

commit v18 on v13

--- a/solution.py
+++ b/solution.py
@@ -163,9 +163,7 @@
     pack = make_pack(tile_count, row_count, blocks, capacity)
     outbound, load_rows, placement_plan = pack(routes, lengths, cell_ids, records)
     arrived = lax.all_to_all(outbound, ("stream", "cross"), split_axis=0, concat_axis=0, tiled=True)
-    outbound, state_and_visc = lax.optimization_barrier(
-        (outbound, jnp.concatenate([fluid_state, viscosity[None]], 0))
-    )
+    state_and_visc = jnp.concatenate([fluid_state, viscosity[None]], 0)
     state_visc = face_halo(state_and_visc)
     state_pad = state_visc[0:5]
     visc_pad = state_visc[5]

time: 47.4 us -> 50.3 us (1.061)
  starting transfers between devices: 21.4 us -> 24.7 us
  waiting for transfers between devices: 3.14 us -> 1.33 us
  other arithmetic: 3.48 us -> 4.36 us
    ppermute x6, starting transfers between devices: 7.79 us -> 10.8 us  [face_halo(): from_a = lax.ppermute(jnp.where(odd, first, last), axis, pairs_a)]
    ppermute x4, waiting for transfers between devices: 3.12 us -> 1.22 us  [face_halo(): from_b = lax.ppermute(jnp.where(odd, last, first), axis, pairs_b)]
    concatenate x1 -> x2, other arithmetic: 0.79 us -> 1.67 us  [shards(): state_and_visc = jnp.concatenate([fluid_state, viscosity[None]], 0)]
  transfers between devices with their start and end apart: 11 -> 11, of which waited for: 2 -> 2; matrix products, arithmetic and copies ran while one was open for 3% -> 4% of each run, Pallas kernels for 0% -> 0%
where the time goes in v18:
time: 50.3 us; the launch traced here: 49.5 us
  starting transfers between devices  24.7 us (49%)
  blocking collectives  9.01 us (18%)
  matrix products  5.86 us (12%)
  other arithmetic  4.36 us (9%)
  Pallas kernels  2.49 us (5%)
  waiting for transfers between devices  1.33 us (3%)
  between operations  1.07 us (2%)
  local copies, waits for them, and re-layouts  0.7 us (1%)
    ppermute x6, starting transfers between devices, face_halo(): from_a = lax.ppermute(jnp.where(odd, first, last), axis, pairs_a)  10.8 us
    all_to_all x1, blocking collectives, shards(): lax.all_to_all(face_pressure.reshape(1, slot_total, row_count), ('stream'...  9.01 us
    ppermute x4, starting transfers between devices, face_halo(): from_b = lax.ppermute(jnp.where(odd, last, first), axis, pairs_b)  8.66 us
    all_to_all x1, starting transfers between devices, shards(): lax.all_to_all(outbound, ('stream', 'cross'), split_axis=0, concat_axis=0...  5.23 us
    dot_general x1, matrix products, shards(): jnp.einsum('cpf,fd->cpd', spread, depth_hot.astype(jnp.float32), precisio...  3.28 us
    pallas_call x1, Pallas kernels, pack(): pl.pallas_call(pack_kernel, out_shape=(jax.ShapeDtypeStruct((slot_total,...  2.49 us
    dot_general x1, matrix products, exact_dot(): jnp.einsum(left + ',k' + right + '->k' + output, onehot, stacked, preferr...  2.4 us
    concatenate x2, other arithmetic, shards(): state_and_visc = jnp.concatenate([fluid_state, viscosity[None]], 0)  1.67 us
  transfers between devices with their start and end apart: 11, of which 2 were waited for; matrix products, arithmetic and copies ran while one was open for 4% of the time, Pallas kernels for 0%

profile of v18, /device:TPU:1, one launch (start us, length us, event | category | flops | bytes accessed | tf_op | source)
XLA Modules:
  0.0 49.5 jit_solution(13940740989530308199)
XLA Ops:
  0.6 2.5 %shard_map.86 = (f32[128,768]{1,0:T(8,128)}, f32[3,64,128]{2,1,0:T(8,128)}, f32[64,128]{1,0:T(8,128)}) custom-call(s32[1,64]{1,0:T(1,128)} %bitcast.95, s32[1,64]{1,0:T(1,128)} %bitcast.96, s32[64,128]{1,0:T(8,128)} %cell_ref.1, f32[8,64,128]{2,1,0:T(8,128)} %record_ref.1), custom_call_target="tpu_custom_call" | custom-call | tf_op jit(solution)/shard_map/pallas_call | solution.py:141
  3.1 5.2 %all-to-all-start = ((f32[8,16,768]{2,1,0:T(8,128)}), f32[8,16,768]{2,1,0:T(8,128)S(1)}, u32[]{:S(2)}, u32[]{:S(2)}) async-start(f32[8,16,768]{2,1,0:T(8,128)} %bitcast.71), calls=%async_computation | async-start | bytes 786432 | tf_op jit(solution)/shard_map/all_to_all | solution.py:165
  8.3 0.8 %pad_maximum_fusion.6 = f32[6,4,4,128]{3,2,1,0:T(4,128)S(1)} fusion(f32[1,4,4,128]{3,2,1,0:T(4,128)} %bitcast.83, f32[4,4,4,128]{3,2,1,0:T(4,128)} %param.8, f32[1,4,4,128]{3,2,1,0:T(4,128)} %bitcast.86), kind=kLoop, calls=%fused_computation.40 | loop fusion | flops 24576 | bytes 98304 | tf_op jit(solution)/shard_map/concatenate | solution.py:166
  9.2 1.4 %collective-permute-start.2 = (f32[6,4,1,128]{3,2,1,0:T(1,128)S(1)}, f32[6,4,1,128]{3,2,1,0:T(1,128)S(1)}, u32[]{:S(2)}, u32[]{:S(2)}) collective-permute-start(f32[6,4,1,128]{3,2,1,0:T(1,128)S(1)} %broadcast_select_fusion.2), channel_id=1, source_target_pairs={{0,4},{4,0},{1,5},{5,1},{2,6},{6,2},{3,7},{7,3},{8,12},{12,8},{9,1... | collective-permute-start | bytes 36872 | tf_op jit(solution)/shard_map/ppermute | solution.py:22
  10.6 0.6 %collective-permute-start.3 = (f32[6,1,4,128]{3,2,1,0:T(4,128)S(1)}, f32[6,1,4,128]{3,2,1,0:T(4,128)S(1)}, u32[]{:S(2)}, u32[]{:S(2)}) collective-permute-start(f32[6,1,4,128]{3,2,1,0:T(4,128)S(1)} %get-tuple-element.27), channel_id=1, source_target_pairs={{0,8},{8,0},{16,24},{24,16},{1,9},{9,1},{17,25},{25,17},{2,10},{10... | collective-permute-start | bytes 36872 | tf_op jit(solution)/shard_map/ppermute | solution.py:22
  11.3 3.0 %collective-permute-start.4 = (f32[6,1,4,128]{3,2,1,0:T(4,128)S(1)}, f32[6,1,4,128]{3,2,1,0:T(4,128)S(1)}, u32[]{:S(2)}, u32[]{:S(2)}) collective-permute-start(f32[6,1,4,128]{3,2,1,0:T(4,128)S(1)} %get-tuple-element.28), channel_id=1, source_target_pairs={{8,16},{16,8},{9,17},{17,9},{10,18},{18,10},{11,19},{19,11},{12,20... | collective-permute-start | bytes 36872 | tf_op jit(solution)/shard_map/ppermute | solution.py:24
  14.4 1.4 %collective-permute-start = (f32[6,4,4,1]{3,2,1,0:T(4,128)S(1)}, f32[6,4,4,1]{3,2,1,0:T(4,128)S(1)}, u32[]{:S(2)}, u32[]{:S(2)}) collective-permute-start(f32[6,4,4,1]{3,2,1,0:T(4,128)S(1)} %get-tuple-element.25), channel_id=1, source_target_pairs={{0,1},{1,0},{2,3},{3,2},{4,5},{5,4},{6,7},{7,6},{8,9},{9,8},{10,11... | collective-permute-start | bytes 1160 | tf_op jit(solution)/shard_map/ppermute | solution.py:22
  15.7 0.7 %collective-permute-start.1 = (f32[6,4,4,1]{3,2,1,0:T(4,128)S(1)}, f32[6,4,4,1]{3,2,1,0:T(4,128)S(1)}, u32[]{:S(2)}, u32[]{:S(2)}) collective-permute-start(f32[6,4,4,1]{3,2,1,0:T(4,128)S(1)} %get-tuple-element.26), channel_id=1, source_target_pairs={{1,2},{2,1},{5,6},{6,5},{9,10},{10,9},{13,14},{14,13},{17,18},{18,... | collective-permute-start | bytes 1160 | tf_op jit(solution)/shard_map/ppermute | solution.py:24
  16.4 0.9 %pad_maximum_fusion = f32[6,6,6,130]{3,2,1,0:T(8,128)S(1)} fusion(f32[1,4,4,128]{3,2,1,0:T(4,128)} %bitcast.84, f32[4,4,4,128]{3,2,1,0:T(4,128)} %param.8, f32[1,4,4,128]{3,2,1,0:T(4,128)} %bitcast.87), kind=kLoop, calls=%fused_computation.17 | loop fusion | flops 56160 | bytes 161472 | tf_op jit(solution)/shard_map/concatenate | solution.py:166
  18.1 0.5 %stack.15 = f32[5,16384]{1,0:T(8,128)S(1)} concatenate(f32[1,16384]{1,0:T(1,128)S(1)} %bitcast.78, f32[1,16384]{1,0:T(1,128)S(1)} %bitcast.77, f32[1,16384]{1,0:T(1,128)S(1)} %bitcast.76, f32[1,16384]{1,0:T(1,128)S(1)} %bitcast.75, f32[1,16384]{1,0:T(1,128)S(1)} %bitcast.74), dimensions={0} | concatenate | bytes 655360 | tf_op jit(solution)/shard_map/stack | solution.py:178
  18.6 0.5 fusion.106
  19.1 3.3 %fusion.2 = f32[5,16,128]{2,1,0:T(8,128)S(1)} fusion(s32[16384]{0:T(1024)S(1)} %add_select_fusion, f32[5,16,16384]{2,1,0:T(8,128)S(1)} %fusion.106), kind=kOutput, calls=%fused_computation.3 | convolution fusion | flops 1008730112 | bytes 5349376 | tf_op jit(solution)/shard_map/cpf,fd->cpd/dot_general | solution.py:182
  22.5 0.2 fusion.60
  22.8 0.7 %collective-permute-start.8 = (f32[5,4,4,1]{3,2,1,0:T(4,128)S(1)}, f32[5,4,4,1]{3,2,1,0:T(4,128)S(1)}, u32[]{:S(2)}, u32[]{:S(2)}) collective-permute-start(f32[5,4,4,1]{3,2,1,0:T(4,128)S(1)} %get-tuple-element.31), channel_id=1, source_target_pairs={{1,2},{2,1},{5,6},{6,5},{9,10},{10,9},{13,14},{14,13},{17,18},{18,... | collective-permute-start | bytes 968 | tf_op jit(solution)/shard_map/ppermute | solution.py:24
  23.5 7.1 %collective-permute-start.9 = (f32[5,4,4,1]{3,2,1,0:T(4,128)S(1)}, f32[5,4,4,1]{3,2,1,0:T(4,128)S(1)}, u32[]{:S(2)}, u32[]{:S(2)}) collective-permute-start(f32[5,4,4,1]{3,2,1,0:T(4,128)S(1)} %get-tuple-element.32), channel_id=1, source_target_pairs={{0,1},{1,0},{2,3},{3,2},{4,5},{5,4},{6,7},{7,6},{8,9},{9,8},{10,11... | collective-permute-start | bytes 968 | tf_op jit(solution)/shard_map/ppermute | solution.py:22
  30.6 0.3 collective-permute-start.7
  30.9 4.4 %collective-permute-start.5 = (f32[5,1,4,128]{3,2,1,0:T(4,128)S(1)}, f32[5,1,4,128]{3,2,1,0:T(4,128)S(1)}, u32[]{:S(2)}, u32[]{:S(2)}) collective-permute-start(f32[5,1,4,128]{3,2,1,0:T(4,128)S(1)} %get-tuple-element.30), channel_id=1, source_target_pairs={{8,16},{16,8},{9,17},{17,9},{10,18},{18,10},{11,19},{19,11},{12,20... | collective-permute-start | bytes 30728 | tf_op jit(solution)/shard_map/ppermute | solution.py:24
  35.4 1.2 %collective-permute-done.5 = f32[5,1,4,128]{3,2,1,0:T(4,128)S(1)} collective-permute-done((f32[5,1,4,128]{3,2,1,0:T(4,128)S(1)}, f32[5,1,4,128]{3,2,1,0:T(4,128)S(1)}, u32[]{:S(2)}, u32[]{:S(2)}) %collective-permute-start.5) | collective-permute-done | bytes 10272 | tf_op jit(solution)/shard_map/ppermute | solution.py:24
  36.6 0.2 fusion.38
  36.9 2.4 %convolution_bitcast_fusion = f32[3,16384,16]{1,2,0:T(8,128)S(1)} fusion(s32[16384]{0:T(1024)S(1)} %add_select_fusion, bf16[1,128,16]{1,2,0:T(8,128)(2,1)S(1)} %get-tuple-element.43, bf16[1,128,16]{1,2,0:T(8,128)(2,1)S(1)} %get-tuple-element.42, bf16[1,128,16]{1,2,0:T(8,128)(2,1)S(1)} %get-tuple-element.41), kind=kOutput, calls=%fused_computation | convolution fusion | flops 203436032 | bytes 3223552 | tf_op jit(solution)/shard_map/fd,kdp->kfp/dot_general | solution.py:84
  39.3 0.4 fusion.12
  39.6 9.0 %all_to_all.17 = f32[1,128,128]{2,0,1:T(1,128)S(1)} all-to-all(f32[1,128,128]{2,0,1:T(1,128)S(1)} %bitcast.72), channel_id=1, replica_groups=mesh['stream'=4,'cross'=2,'gore'=4] {'stream','cross'}, dimensions={1} | all-to-all | bytes 131072 | tf_op jit(solution)/shard_map/all_to_all | solution.py:201
  48.7 0.2 fusion.97
  48.9 0.7 %broadcast_multiply_fusion = f32[3,64,128]{2,1,0:T(8,128)} fusion(f32[3,64,128]{2,1,0:T(8,128)S(1)} %copy-done.2, f32[64,128]{1,0:T(8,128)S(1)} %fusion.97), kind=kLoop, calls=%fused_computation.41 | loop fusion | flops 24576 | bytes 229376 | tf_op jit(solution)/shard_map/mul | solution.py:211
  (49 shorter events, 1.0 us)
Async XLA Ops:
  3.1 14.7 %all-to-all-start = ((f32[8,16,768]{2,1,0:T(8,128)}), f32[8,16,768]{2,1,0:T(8,128)S(1)}, u32[]{:S(2)}, u32[]{:S(2)}) async-start(f32[8,16,768]{2,1,0:T(8,128)} %bitcast.71), calls=%async_computation | async-start | bytes 786432 | tf_op jit(solution)/shard_map/all_to_all | solution.py:165
  9.2 8.3 %collective-permute-start.2 = (f32[6,4,1,128]{3,2,1,0:T(1,128)S(1)}, f32[6,4,1,128]{3,2,1,0:T(1,128)S(1)}, u32[]{:S(2)}, u32[]{:S(2)}) collective-permute-start(f32[6,4,1,128]{3,2,1,0:T(1,128)S(1)} %broadcast_select_fusion.2), channel_id=1, source_target_pairs={{0,4},{4,0},{1,5},{5,1},{2,6},{6,2},{3,7},{7,3},{8,12},{12,8},{9,1... | collective-permute-start | bytes 36872 | tf_op jit(solution)/shard_map/ppermute | solution.py:22
  10.6 6.9 %collective-permute-start.3 = (f32[6,1,4,128]{3,2,1,0:T(4,128)S(1)}, f32[6,1,4,128]{3,2,1,0:T(4,128)S(1)}, u32[]{:S(2)}, u32[]{:S(2)}) collective-permute-start(f32[6,1,4,128]{3,2,1,0:T(4,128)S(1)} %get-tuple-element.27), channel_id=1, source_target_pairs={{0,8},{8,0},{16,24},{24,16},{1,9},{9,1},{17,25},{25,17},{2,10},{10... | collective-permute-start | bytes 36872 | tf_op jit(solution)/shard_map/ppermute | solution.py:22
  11.3 6.3 %collective-permute-start.4 = (f32[6,1,4,128]{3,2,1,0:T(4,128)S(1)}, f32[6,1,4,128]{3,2,1,0:T(4,128)S(1)}, u32[]{:S(2)}, u32[]{:S(2)}) collective-permute-start(f32[6,1,4,128]{3,2,1,0:T(4,128)S(1)} %get-tuple-element.28), channel_id=1, source_target_pairs={{8,16},{16,8},{9,17},{17,9},{10,18},{18,10},{11,19},{19,11},{12,20... | collective-permute-start | bytes 36872 | tf_op jit(solution)/shard_map/ppermute | solution.py:24
  14.4 3.0 %collective-permute-start = (f32[6,4,4,1]{3,2,1,0:T(4,128)S(1)}, f32[6,4,4,1]{3,2,1,0:T(4,128)S(1)}, u32[]{:S(2)}, u32[]{:S(2)}) collective-permute-start(f32[6,4,4,1]{3,2,1,0:T(4,128)S(1)} %get-tuple-element.25), channel_id=1, source_target_pairs={{0,1},{1,0},{2,3},{3,2},{4,5},{5,4},{6,7},{7,6},{8,9},{9,8},{10,11... | collective-permute-start | bytes 1160 | tf_op jit(solution)/shard_map/ppermute | solution.py:22
  15.7 1.6 %collective-permute-start.1 = (f32[6,4,4,1]{3,2,1,0:T(4,128)S(1)}, f32[6,4,4,1]{3,2,1,0:T(4,128)S(1)}, u32[]{:S(2)}, u32[]{:S(2)}) collective-permute-start(f32[6,4,4,1]{3,2,1,0:T(4,128)S(1)} %get-tuple-element.26), channel_id=1, source_target_pairs={{1,2},{2,1},{5,6},{6,5},{9,10},{10,9},{13,14},{14,13},{17,18},{18,... | collective-permute-start | bytes 1160 | tf_op jit(solution)/shard_map/ppermute | solution.py:24
  19.1 3.3 %copy-start = (f32[4,4,4,128]{3,2,1,0:T(4,128)S(1)}, f32[4,4,4,128]{3,2,1,0:T(4,128)}, u32[]{:S(2)}) copy-start(f32[4,4,4,128]{3,2,1,0:T(4,128)} %param.8) | copy-start | bytes 98308
  19.1 3.3 %copy-start.3 = (f32[4,4,128]{2,1,0:T(4,128)S(1)}, f32[4,4,128]{2,1,0:T(4,128)}, u32[]{:S(2)}) copy-start(f32[4,4,128]{2,1,0:T(4,128)} %param.9) | copy-start | bytes 24580
  19.1 3.3 %copy-start.4 = (f32[4,4,128]{2,1,0:T(4,128)S(1)}, f32[4,4,128]{2,1,0:T(4,128)}, u32[]{:S(2)}) copy-start(f32[4,4,128]{2,1,0:T(4,128)} %param.7) | copy-start | bytes 24580
  22.4 26.2 %copy-start.5 = (f32[64,128]{1,0:T(8,128)S(1)}, f32[64,128]{1,0:T(8,128)}, u32[]{:S(2)}) copy-start(f32[64,128]{1,0:T(8,128)} %get-tuple-element.7) | copy-start | bytes 98308
  22.4 26.4 %copy-start.2 = (f32[3,64,128]{2,1,0:T(8,128)S(1)}, f32[3,64,128]{2,1,0:T(8,128)}, u32[]{:S(2)}) copy-start(f32[3,64,128]{2,1,0:T(8,128)} %get-tuple-element.6) | copy-start | bytes 294916
  22.8 12.4 %collective-permute-start.8 = (f32[5,4,4,1]{3,2,1,0:T(4,128)S(1)}, f32[5,4,4,1]{3,2,1,0:T(4,128)S(1)}, u32[]{:S(2)}, u32[]{:S(2)}) collective-permute-start(f32[5,4,4,1]{3,2,1,0:T(4,128)S(1)} %get-tuple-element.31), channel_id=1, source_target_pairs={{1,2},{2,1},{5,6},{6,5},{9,10},{10,9},{13,14},{14,13},{17,18},{18,... | collective-permute-start | bytes 968 | tf_op jit(solution)/shard_map/ppermute | solution.py:24
  23.5 11.7 %collective-permute-start.9 = (f32[5,4,4,1]{3,2,1,0:T(4,128)S(1)}, f32[5,4,4,1]{3,2,1,0:T(4,128)S(1)}, u32[]{:S(2)}, u32[]{:S(2)}) collective-permute-start(f32[5,4,4,1]{3,2,1,0:T(4,128)S(1)} %get-tuple-element.32), channel_id=1, source_target_pairs={{0,1},{1,0},{2,3},{3,2},{4,5},{5,4},{6,7},{7,6},{8,9},{9,8},{10,11... | collective-permute-start | bytes 968 | tf_op jit(solution)/shard_map/ppermute | solution.py:22
  30.6 4.7 %collective-permute-start.7 = (f32[5,4,1,128]{3,2,1,0:T(1,128)S(1)}, f32[5,4,1,128]{3,2,1,0:T(1,128)S(1)}, u32[]{:S(2)}, u32[]{:S(2)}) collective-permute-start(f32[5,4,1,128]{3,2,1,0:T(1,128)S(1)} %broadcast_select_fusion.9), channel_id=1, source_target_pairs={{0,4},{4,0},{1,5},{5,1},{2,6},{6,2},{3,7},{7,3},{8,12},{12,8},{9,1... | collective-permute-start | bytes 30728 | tf_op jit(solution)/shard_map/ppermute | solution.py:22
  30.9 4.5 %collective-permute-start.6 = (f32[5,1,4,128]{3,2,1,0:T(4,128)S(1)}, f32[5,1,4,128]{3,2,1,0:T(4,128)S(1)}, u32[]{:S(2)}, u32[]{:S(2)}) collective-permute-start(f32[5,1,4,128]{3,2,1,0:T(4,128)S(1)} %get-tuple-element.29), channel_id=1, source_target_pairs={{0,8},{8,0},{16,24},{24,16},{1,9},{9,1},{17,25},{25,17},{2,10},{10... | collective-permute-start | bytes 30728 | tf_op jit(solution)/shard_map/ppermute | solution.py:22
  30.9 5.7 %collective-permute-start.5 = (f32[5,1,4,128]{3,2,1,0:T(4,128)S(1)}, f32[5,1,4,128]{3,2,1,0:T(4,128)S(1)}, u32[]{:S(2)}, u32[]{:S(2)}) collective-permute-start(f32[5,1,4,128]{3,2,1,0:T(4,128)S(1)} %get-tuple-element.30), channel_id=1, source_target_pairs={{8,16},{16,8},{9,17},{17,9},{10,18},{18,10},{11,19},{19,11},{12,20... | collective-permute-start | bytes 30728 | tf_op jit(solution)/shard_map/ppermute | solution.py:24
  36.8 12.7 %copy-start.1 = (f32[5,4,4,128]{3,2,1,0:T(4,128)}, f32[5,4,4,128]{3,2,1,0:T(4,128)S(1)}, u32[]{:S(2)}) copy-start(f32[5,4,4,128]{3,2,1,0:T(4,128)S(1)} %fusion.38) | copy-start | bytes 122884
